TPU v7x, 512 devices: a whole 4x8x8 slice. The times are simulated.
512 devices in a mesh: dp: 16 (over z_hi, y), tensor: 32 (over x, z_lo, core).
Axes of the slice: x: 4, y: 8, z: 8 (z_hi: 2, z_lo: 4; z = z_hi * 4 + z_lo), core: 2. Of those that a mesh axis runs over, the one named last changes fastest.
Arguments:
- suffix_states: bfloat16 [32, 128, 2048], P(None, 'dp', 'tensor'), may hold values from -16 to 16
- suffix_lengths: int32 [32], replicated, may hold values from 1 to 128, 2560 in all
- request_group: int32 [32, 1], replicated, may hold values from 0 to 15
- group_owner: int32 [16], replicated, may hold values from 0 to 15, each once
- request_order: int32 [32], replicated, may hold values from 0 to 31, each once
- prefix_cache: bfloat16 [16, 256, 1024], P('dp', 'tensor'), may hold values from -700 to 700
- norm_attn: bfloat16 [2048], replicated, may hold values from 0.099609375 to 1.8984375
- w_query: bfloat16 [2048, 2048], P(None, 'tensor'), may hold values from -0.125 to 0.125
- w_key: bfloat16 [2048, 512], P(None, 'tensor'), may hold values from -0.125 to 0.125
- w_value: bfloat16 [2048, 512], P(None, 'tensor'), may hold values from -0.125 to 0.125
- w_out: bfloat16 [2048, 2048], P('tensor'), may hold values from -0.25 to 0.25
- norm_mlp: bfloat16 [2048], replicated, may hold values from 0.099609375 to 1.8984375
- w_gate: bfloat16 [2048, 8192], P(None, 'tensor'), may hold values from -0.125 to 0.125
- w_up: bfloat16 [2048, 8192], P(None, 'tensor'), may hold values from -0.125 to 0.125
- w_down: bfloat16 [8192, 2048], P('tensor'), may hold values from -0.125 to 0.125
Outputs:
- hidden_out: bfloat16 [32, 128, 2048], P(None, 'dp', 'tensor')
- suffix_keys: bfloat16 [32, 128, 512], P('dp', None, 'tensor')
- suffix_values: bfloat16 [32, 128, 512], P('dp', None, 'tensor')
Inputs may be any that keep to these rules, and one draw needn't show every extreme that they name: `suffix_lengths`: the lengths sum to 2560 and some request has exactly 128. `request_group`: every group has at least one request. `group_owner`: A permutation of the 16 groups onto the slots of prefix_cache. `request_order`: A permutation of the requests; slot s belongs to index s // 2 of dp.
All inputs are finite; a program needn't handle non-finite values.
Results may differ from a plain program's by a relative error of at most 0.03.
Values may be sent and summed in bfloat16 or wider, within the bound.
No kernel may reach another device: no remote copies, remote signals or barrier semaphores. Data moves between devices by JAX's collectives and lax.ppermute only.
A program may use at most 64 MiB of HBM per device.

v0:
```python
import jax
import jax.numpy as jnp
import numpy as np
from jax import lax
from jax.sharding import PartitionSpec as P

H = 32
KVH = 8
HD = 64
L_MAX = 128
P_SIZE = 256


THETA = 10000000.0
EPSILON = 1e-05


def rms_scale(states, gain):
    wide = states.astype(jnp.float32)
    mean_square = jnp.mean(wide * wide, axis=-1, keepdims=True)
    return (wide * lax.rsqrt(mean_square + EPSILON) * gain.astype(jnp.float32)).astype(jnp.bfloat16)


def rotate(vectors, positions):
    half = HD // 2
    freqs = THETA ** (-(jnp.arange(half, dtype=jnp.float32) * 2.0 / HD))
    angles = positions[:, None] * freqs[None, :]
    cosine = jnp.cos(angles)[:, None, :]
    sine = jnp.sin(angles)[:, None, :]
    first = vectors[..., :half]
    second = vectors[..., half:]
    return jnp.concatenate(
        [first * cosine - second * sine, second * cosine + first * sine], axis=-1
    )


def absorb_block(state_now, scores, allowed, value_rows):
    running_max, running_sum, numerator = state_now
    block_max = jnp.max(jnp.where(allowed, scores, -1e30), axis=2)
    new_max = jnp.maximum(running_max, block_max)
    rescale = jnp.exp(running_max - new_max)
    weights = jnp.where(allowed, jnp.exp(scores - new_max[:, :, None]), 0.0)
    running_sum = running_sum * rescale + jnp.sum(weights, axis=2)
    numerator = numerator * rescale[:, :, None] + jnp.einsum(
        "htk,khd->htd", weights.astype(jnp.bfloat16), value_rows, preferred_element_type=jnp.float32
    )
    return (new_max, running_sum, numerator)


def shards(
    suffix_states,
    suffix_lengths,
    request_group,
    group_owner,
    request_order,
    prefix_cache,
    norm_attn,
    w_query,
    w_key,
    w_value,
    w_out,
    norm_mlp,
    w_gate,
    w_up,
    w_down,
):
    dp_count = lax.axis_size("dp")
    tp_count = lax.axis_size("tensor")
    dp_index = lax.axis_index("dp")
    tp_index = lax.axis_index("tensor")
    total_reqs = suffix_lengths.shape[0]
    local_reqs = total_reqs // dp_count
    row_count = local_reqs * L_MAX
    heads_here = w_query.shape[1] // HD
    group_size = H // KVH
    kv_here = max(1, heads_here // group_size)
    slab_width = kv_here * 2 * HD
    score_scale = HD ** (-0.5)
    head_map = np.arange(heads_here) // group_size
    dest_table = (
        np.arange(tp_count)[:, None] * heads_here // group_size + np.arange(kv_here)[None, :]
    ).reshape(-1)
    routed = jnp.take(suffix_states, request_order, axis=0)
    routed_here = lax.all_to_all(routed, "dp", split_axis=0, concat_axis=1, tiled=True)
    width_here = routed_here.shape[2]
    state_shard = routed_here.reshape(row_count, width_here)
    slot_ids = dp_index * local_reqs + jnp.arange(local_reqs, dtype=jnp.int32)
    req_ids = jnp.take(request_order, slot_ids)
    lengths_here = jnp.take(suffix_lengths, req_ids)
    owner_here = jnp.take(group_owner, jnp.take(request_group[:, 0], req_ids))
    position = jnp.arange(L_MAX, dtype=jnp.int32)
    valid = (position[None, :] < lengths_here[:, None]).reshape(row_count)
    positions = (P_SIZE + jnp.tile(position, local_reqs)).astype(jnp.float32)
    full_rows = lax.all_gather(state_shard, "tensor", axis=1, tiled=True)
    normed = rms_scale(full_rows, norm_attn)
    query = rotate(
        jnp.dot(normed, w_query, preferred_element_type=jnp.float32).reshape(
            row_count, heads_here, HD
        ),
        positions,
    ).astype(jnp.bfloat16)
    key_part = jnp.dot(normed, w_key, preferred_element_type=jnp.float32).astype(jnp.bfloat16)
    value_part = jnp.dot(normed, w_value, preferred_element_type=jnp.float32).astype(jnp.bfloat16)
    key_full, value_full = (
        lax.all_gather(key_part, "tensor", axis=1, tiled=True),
        lax.all_gather(value_part, "tensor", axis=1, tiled=True),
    )
    key_heads = key_full.reshape(row_count, HD, KVH).transpose(0, 2, 1)
    value_heads = value_full.reshape(row_count, HD, KVH).transpose(0, 2, 1)
    key_rot = rotate(key_heads.astype(jnp.float32), positions).astype(jnp.bfloat16)
    cache_width = key_part.shape[1]
    keys_flat = jnp.where(valid[:, None], key_rot.reshape(row_count, KVH * HD), 0.0)
    values_flat = jnp.where(valid[:, None], value_heads.reshape(row_count, KVH * HD), 0.0)
    keys_out = lax.dynamic_slice_in_dim(keys_flat, tp_index * cache_width, cache_width, 1).reshape(
        local_reqs, L_MAX, cache_width
    )
    values_out = lax.dynamic_slice_in_dim(
        values_flat, tp_index * cache_width, cache_width, 1
    ).reshape(local_reqs, L_MAX, cache_width)
    kv_first = tp_index * heads_here // group_size
    own_keys = lax.dynamic_slice_in_dim(key_rot, kv_first, kv_here, 1)[:, head_map].reshape(
        local_reqs, L_MAX, heads_here, HD
    )
    own_values = lax.dynamic_slice_in_dim(value_heads, kv_first, kv_here, 1)[:, head_map].reshape(
        local_reqs, L_MAX, heads_here, HD
    )
    query_req = query.reshape(local_reqs, L_MAX, heads_here, HD)

    def absorb_prefix(state_one, query_one, slot_block):
        block = slot_block.reshape(slot_block.shape[0], kv_here, 2, HD)
        key_rows = block[:, head_map, 0]
        value_rows = block[:, head_map, 1]
        scores = (
            jnp.einsum("thd,phd->htp", query_one, key_rows, preferred_element_type=jnp.float32)
            * score_scale
        )
        return absorb_block(state_one, scores, jnp.ones((1, 1, 1), bool), value_rows)

    initial = tuple(
        (
            (
                jnp.full((heads_here, L_MAX), -1e30, jnp.float32),
                jnp.zeros((heads_here, L_MAX), jnp.float32),
                jnp.zeros((heads_here, L_MAX, HD), jnp.float32),
            )
            for request in range(local_reqs)
        )
    )
    all_rows = lax.all_gather(prefix_cache, "dp", axis=0, tiled=True)
    rows_each = all_rows.shape[1]
    chosen = jnp.take(all_rows.reshape(dp_count, rows_each, KVH, 2 * HD), dest_table, axis=2)
    picked = lax.all_to_all(chosen, "tensor", split_axis=2, concat_axis=1, tiled=True).reshape(
        dp_count, P_SIZE, slab_width
    )
    states = tuple(
        (
            absorb_prefix(
                initial[request],
                query_req[request],
                lax.dynamic_index_in_dim(picked, owner_here[request], 0, keepdims=False),
            )
            for request in range(local_reqs)
        )
    )
    pieces = []
    for request in range(local_reqs):
        self_scores = (
            jnp.einsum(
                "thd,shd->hts",
                query_req[request],
                own_keys[request],
                preferred_element_type=jnp.float32,
            )
            * score_scale
        )
        self_allowed = (position[None, :] <= position[:, None]) & (
            position[None, :] < lengths_here[request]
        )
        running_max, running_sum, numerator = absorb_block(
            states[request], self_scores, self_allowed[None], own_values[request]
        )
        attention_one = (numerator / running_sum[:, :, None]).astype(jnp.bfloat16)
        pieces.append(attention_one.transpose(1, 0, 2).reshape(L_MAX, heads_here * HD))
    attention = jnp.concatenate(pieces, axis=0)
    attn_terms = jnp.dot(attention, w_out, preferred_element_type=jnp.float32)
    attn_share = lax.psum_scatter(
        attn_terms.astype(jnp.bfloat16), "tensor", scatter_dimension=1, tiled=True
    ).astype(jnp.float32)
    middle = (state_shard.astype(jnp.float32) + attn_share).astype(jnp.bfloat16)
    middle_rows = lax.all_gather(middle, "tensor", axis=1, tiled=True)
    normed_two = rms_scale(middle_rows, norm_mlp)
    gate = jnp.dot(normed_two, w_gate, preferred_element_type=jnp.float32)
    upper = jnp.dot(normed_two, w_up, preferred_element_type=jnp.float32)
    hidden = (jax.nn.silu(gate) * upper).astype(jnp.bfloat16)
    down_terms = jnp.dot(hidden, w_down, preferred_element_type=jnp.float32)
    down_share = lax.psum_scatter(
        down_terms.astype(jnp.bfloat16), "tensor", scatter_dimension=1, tiled=True
    ).astype(jnp.float32)
    result = middle.astype(jnp.float32) + down_share
    result = (
        jnp.where(valid[:, None], result, 0.0)
        .astype(jnp.bfloat16)
        .reshape(local_reqs, L_MAX, width_here)
    )
    returned = lax.all_to_all(result, "dp", split_axis=1, concat_axis=0, tiled=True)
    hidden_out = jnp.zeros_like(returned).at[request_order].set(returned)
    return (hidden_out, keys_out, values_out)


def solution(mesh):
    in_specs = (
        P(None, "dp", "tensor"),
        P(),
        P(),
        P(),
        P(),
        P("dp", "tensor", None),
        P(),
        P(None, "tensor"),
        P(None, "tensor"),
        P(None, "tensor"),
        P("tensor", None),
        P(),
        P(None, "tensor"),
        P(None, "tensor"),
        P("tensor", None),
    )
    out_specs = (P(None, "dp", "tensor"), P("dp", None, "tensor"), P("dp", None, "tensor"))
    return jax.shard_map(shards, mesh=mesh, in_specs=in_specs, out_specs=out_specs, check_vma=False)
```

profile of v0, /device:TPU:1, one launch (start us, length us, event | category | flops | bytes accessed | tf_op | source)
XLA Modules:
  0.0 632.9 jit_solution(12212164289237570744)
XLA Ops:
  7.2 0.7 compare_select_fusion.3
  7.9 0.7 compare_and_fusion.1
  8.6 1.4 gather_fusion
  10.1 0.7 reshape.707
  10.9 16.2 %all-to-all-start = ((bf16[16,2,512]{2,1,0:T(2,128)(2,1)}), bf16[16,2,512]{2,1,0:T(2,128)(2,1)S(1)}, u32[]{:S(2)}, u32[]{:S(2)}) async-start(bf16[16,2,512]{2,1,0:T(2,128)(2,1)} %reshape.707), calls=%async_computation | async-start | bytes 65536 | tf_op jit(solution)/shard_map/all_to_all | solution.py:84
  27.1 48.2 %all_gather.16 = bf16[16,8,1024]{2,1,0:T(8,128)(2,1)S(1)} all-gather(bf16[1,8,1024]{2,1,0:T(8,128)(2,1)} %param.30), channel_id=1, replica_groups=mesh['dp'=16,'tensor'=32] {'dp'}, dimensions={0}, use_global_device_ids=true | all-gather | bytes 278528 | tf_op jit(solution)/shard_map/all_gather | solution.py:149
  75.3 0.7 pad_clamp_fusion.1
  75.9 1.9 gather_fusion.1
  77.8 15.1 %all-to-all-start.1 = ((bf16[16,8,32,128]{3,1,0,2:T(8,128)(2,1)}), bf16[16,8,32,128]{3,1,0,2:T(8,128)(2,1)S(1)}, u32[]{:S(2)}, u32[]{:S(2)}) async-start(bf16[16,8,32,128]{3,1,0,2:T(8,128)(2,1)} %bitcast.9), calls=%async_computation.1 | async-start | bytes 2097152 | tf_op jit(solution)/shard_map/all_to_all | solution.py:152
  93.0 0.6 gather_fusion.3
  93.8 0.7 copy.51
  94.6 0.6 gather_fusion.5
  95.2 0.6 gather_fusion.4
  95.9 0.6 gather_fusion.2
  96.5 0.6 fusion.81
  101.1 0.6 fusion.80
  101.7 0.6 iota_compare_fusion.2
  102.3 0.7 iota_compare_fusion.1
  103.2 18.0 %all-to-all-done.1 = bf16[16,8,32,128]{3,1,0,2:T(8,128)(2,1)S(1)} async-done(((bf16[16,8,32,128]{3,1,0,2:T(8,128)(2,1)}), bf16[16,8,32,128]{3,1,0,2:T(8,128)(2,1)S(1)}, u32[]{:S(2)}, u32[]{:S(2)}) %all-to-all-start.1) | async-done | bytes 1048608 | tf_op jit(solution)/shard_map/all_to_all | solution.py:152
  121.2 0.3 copy_bitcast_fusion
  121.7 31.4 %all-gather.3.cloned.1.call-done = bf16[256,2048]{0,1:T(8,128)(2,1)} async-done(((bf16[256,64]{0,1:T(8,128)(2,1)}), bf16[256,2048]{0,1:T(8,128)(2,1)}) %all-gather.3.cloned.1.call-update) | async-done | bytes 1048592 | tf_op jit(solution)/shard_map/all_gather | solution.py:94
  153.1 1.6 fusion
  154.8 0.5 convolution_bitcast_fusion
  155.6 0.5 convolution_convert_fusion.2
  156.0 41.7 %all_gather.18 = bf16[256,512]{0,1:T(8,128)(2,1)S(1)} all-gather(bf16[256,16]{0,1:T(8,128)(2,1)S(1)} %convolution_convert_fusion.2), channel_id=1, replica_groups=mesh['dp'=16,'tensor'=32] {'tensor'}, dimensions={1}, use_global_device_ids=true | all-gather | bytes 270336 | tf_op jit(solution)/shard_map/all_gather | solution.py:106
  197.8 0.5 convolution_convert_fusion.3
  198.2 38.9 %all_gather.17 = bf16[256,512]{0,1:T(8,128)(2,1)S(1)} all-gather(bf16[256,16]{0,1:T(8,128)(2,1)S(1)} %convolution_convert_fusion.3), channel_id=1, replica_groups=mesh['dp'=16,'tensor'=32] {'tensor'}, dimensions={1}, use_global_device_ids=true | all-gather | bytes 270336 | tf_op jit(solution)/shard_map/all_gather | solution.py:105
  237.4 0.3 fusion.82
  237.7 0.3 fusion.83
  238.1 0.2 select_reduce_fusion.1
  238.3 0.2 select_reduce_fusion
  239.4 0.2 fusion.10
  239.7 0.2 fusion.12
  240.1 1.5 convolution_convert_fusion.1
  241.7 141.0 %reduce-scatter.3.cloned.1.call-done = bf16[256,64]{0,1:T(8,128)(2,1)} async-done(((bf16[256,2048]{0,1:T(8,128)(2,1)}), bf16[256,64]{0,1:T(8,128)(2,1)}) %reduce-scatter.3.cloned.1.call-update) | async-done | bytes 32784 | tf_op jit(solution)/shard_map/reduce_scatter | solution.py:186
  382.7 1.4 add_convert_fusion
  384.1 64.4 %all-gather.5.cloned.1.call-done = bf16[256,2048]{0,1:T(8,128)(2,1)} async-done(((bf16[256,64]{0,1:T(8,128)(2,1)}), bf16[256,2048]{0,1:T(8,128)(2,1)}) %all-gather.5.cloned.1.call-update) | async-done | bytes 1048592 | tf_op jit(solution)/shard_map/all_gather | solution.py:190
  448.6 1.6 fusion.3
  450.2 2.1 fusion.15
  452.3 4.1 convolution_convert_fusion
  456.5 143.5 %reduce-scatter.5.cloned.1.call-done = bf16[256,64]{0,1:T(8,128)(2,1)} async-done(((bf16[256,2048]{0,1:T(8,128)(2,1)}), bf16[256,64]{0,1:T(8,128)(2,1)}) %reduce-scatter.5.cloned.1.call-update) | async-done | bytes 32784 | tf_op jit(solution)/shard_map/reduce_scatter | solution.py:196
  600.0 0.8 select_convert_fusion
  600.9 0.7 reshape.709
  601.7 11.1 %all-to-all-start.2 = ((bf16[16,2,512]{2,1,0:T(2,128)(2,1)}), bf16[16,2,512]{2,1,0:T(2,128)(2,1)S(1)}, u32[]{:S(2)}, u32[]{:S(2)}) async-start(bf16[16,2,512]{2,1,0:T(2,128)(2,1)} %reshape.709), calls=%async_computation.4 | async-start | bytes 65536 | tf_op jit(solution)/shard_map/all_to_all | solution.py:205
  612.7 0.6 copy_bitcast_fusion.3
  613.4 10.7 %all-to-all-done.2 = bf16[16,2,512]{2,1,0:T(2,128)(2,1)S(1)} async-done(((bf16[16,2,512]{2,1,0:T(2,128)(2,1)}), bf16[16,2,512]{2,1,0:T(2,128)(2,1)S(1)}, u32[]{:S(2)}, u32[]{:S(2)}) %all-to-all-start.2) | async-done | bytes 32800 | tf_op jit(solution)/shard_map/all_to_all | solution.py:205
  624.2 1.5 scatter_fusion
  625.7 0.6 copy-done.9
  (85 shorter events, 3.1 us)
Async XLA Ops:
  7.2 445.1 %copy-start = (bf16[256,2048]{1,0:T(8,128)(2,1)S(1)}, bf16[256,2048]{1,0:T(8,128)(2,1)}, u32[]{:S(2)}) copy-start(bf16[256,2048]{1,0:T(8,128)(2,1)} %param.39) | copy-start | bytes 3145732
  10.9 66.9 %all-to-all-start = ((bf16[16,2,512]{2,1,0:T(2,128)(2,1)}), bf16[16,2,512]{2,1,0:T(2,128)(2,1)S(1)}, u32[]{:S(2)}, u32[]{:S(2)}) async-start(bf16[16,2,512]{2,1,0:T(2,128)(2,1)} %reshape.707), calls=%async_computation | async-start | bytes 65536 | tf_op jit(solution)/shard_map/all_to_all | solution.py:84
  77.8 15.2 %copy-start.1 = (s32[32]{0:T(128)S(1)}, s32[32]{0:T(128)}, u32[]{:S(2)}) copy-start(s32[32]{0:T(128)} %param.29) | copy-start | bytes 388
  77.8 16.8 %copy-start.2 = (s32[32,1]{0,1:T(1,128)S(1)}, s32[32,1]{0,1:T(1,128)}, u32[]{:S(2)}) copy-start(s32[32,1]{0,1:T(1,128)} %param.27) | copy-start | bytes 388
  77.8 43.4 %all-to-all-start.1 = ((bf16[16,8,32,128]{3,1,0,2:T(8,128)(2,1)}), bf16[16,8,32,128]{3,1,0,2:T(8,128)(2,1)S(1)}, u32[]{:S(2)}, u32[]{:S(2)}) async-start(bf16[16,8,32,128]{3,1,0,2:T(8,128)(2,1)} %bitcast.9), calls=%async_computation.1 | async-start | bytes 2097152 | tf_op jit(solution)/shard_map/all_to_all | solution.py:152
  92.9 2.4 copy-start.3
  92.9 3.0 copy-start.4
  92.9 60.2 %all-gather.3.cloned.1.call-start = ((), (), s32[]{:S(2)}) async-start(), calls=%async_computation.5 | async-start | bytes 1081344 | tf_op jit(solution)/shard_map/all_gather | solution.py:94
  93.6 6.1 copy-start.11
  94.5 288.2 %reduce-scatter.3.cloned.1.call-start = ((), (), s32[]{:S(2)}) async-start(), calls=%async_computation.6 | async-start | bytes 1081344 | tf_op jit(solution)/shard_map/reduce_scatter | solution.py:186
  121.5 33.3 %copy-start.13 = (bf16[2048,64]{0,1:T(8,128)(2,1)S(1)}, bf16[2048,64]{0,1:T(8,128)(2,1)}, u32[]{:S(2)}) copy-start(bf16[2048,64]{0,1:T(8,128)(2,1)} %param.32) | copy-start | bytes 786436
  153.1 1.6 copy-start.5
  154.7 0.8 copy-start.14
  155.6 42.2 %copy-start.15 = (bf16[2048,16]{0,1:T(8,128)(2,1)S(1)}, bf16[2048,16]{0,1:T(8,128)(2,1)}, u32[]{:S(2)}) copy-start(bf16[2048,16]{0,1:T(8,128)(2,1)} %param.33) | copy-start | bytes 196612
  238.0 2.1 copy-start.10
  240.1 142.6 %copy-start.7 = (bf16[256,64]{0,1:T(8,128)(2,1)S(1)}, bf16[256,64]{0,1:T(8,128)(2,1)}, u32[]{:S(2)}) copy-start(bf16[256,64]{0,1:T(8,128)(2,1)} %copy.51) | copy-start | bytes 98308
  240.1 144.0 %copy-start.12 = (bf16[2048]{0:T(1024)(128)(2,1)S(1)}, bf16[2048]{0:T(1024)(128)(2,1)}, u32[]{:S(2)}) copy-start(bf16[2048]{0:T(1024)(128)(2,1)} %param.36) | copy-start | bytes 12292
  241.6 207.0 %all-gather.5.cloned.1.call-start = ((), (), s32[]{:S(2)}) async-start(), calls=%async_computation.7 | async-start | bytes 1081344 | tf_op jit(solution)/shard_map/all_gather | solution.py:190
  384.1 215.9 %reduce-scatter.5.cloned.1.call-start = ((), (), s32[]{:S(2)}) async-start(), calls=%async_computation.8 | async-start | bytes 1081344 | tf_op jit(solution)/shard_map/reduce_scatter | solution.py:196
  448.6 1.6 copy-start.6
  456.4 143.6 %copy-start.8 = (bf16[256,64]{0,1:T(8,128)(2,1)S(1)}, bf16[256,64]{0,1:T(8,128)(2,1)}, u32[]{:S(2)}) copy-start(bf16[256,64]{0,1:T(8,128)(2,1)} %add_convert_fusion) | copy-start | bytes 98308
  601.7 22.3 %all-to-all-start.2 = ((bf16[16,2,512]{2,1,0:T(2,128)(2,1)}), bf16[16,2,512]{2,1,0:T(2,128)(2,1)S(1)}, u32[]{:S(2)}, u32[]{:S(2)}) async-start(bf16[16,2,512]{2,1,0:T(2,128)(2,1)} %reshape.709), calls=%async_computation.4 | async-start | bytes 65536 | tf_op jit(solution)/shard_map/all_to_all | solution.py:205
  625.7 0.6 copy-start.9
Sparse Core Ops, SparseCore 0:
  96.4 56.6 all-gather.2
  241.7 140.8 reduce-scatter.2
  385.4 63.1 all-gather.4
  456.5 143.4 reduce-scatter.4
where the time goes:
time: 636 us; the launch traced here: 633 us
  waiting for transfers between devices  409 us (64%)
  blocking collectives  129 us (20%)
  starting transfers between devices  42.5 us (7%)
  between operations  18.1 us (3%)
  local copies, waits for them, and re-layouts  13.2 us (2%)
  matrix products  11 us (2%)
  other arithmetic  10.2 us (2%)
    reduce_scatter x1, waiting for transfers between devices, shards(): lax.psum_scatter(down_terms.astype(jnp.bfloat16), 'tensor', scatter_dimen...  144 us
    reduce_scatter x1, waiting for transfers between devices, shards(): lax.psum_scatter(attn_terms.astype(jnp.bfloat16), 'tensor', scatter_dimen...  141 us
    all_gather x1, waiting for transfers between devices, shards(): middle_rows = lax.all_gather(middle, 'tensor', axis=1, tiled=True)  64.4 us
    all_gather x1, blocking collectives, shards(): all_rows = lax.all_gather(prefix_cache, 'dp', axis=0, tiled=True)  48.2 us
    all_gather x1, blocking collectives, shards(): lax.all_gather(value_part, 'tensor', axis=1, tiled=True)  41.7 us
    all_gather x1, blocking collectives, shards(): lax.all_gather(key_part, 'tensor', axis=1, tiled=True)  38.9 us
    all_gather x1, waiting for transfers between devices, shards(): full_rows = lax.all_gather(state_shard, 'tensor', axis=1, tiled=True)  31.4 us
    all_to_all x1, waiting for transfers between devices, shards(): lax.all_to_all(chosen, 'tensor', split_axis=2, concat_axis=1, tiled=True)  18 us
  transfers between devices with their start and end apart: 7, of which 6 were waited for; matrix products, arithmetic and copies ran while one was open for 2% of the time, Pallas kernels for 0%

commit v1 on v0

v1 whole, which is shorter than its diff:
```python
import jax
import jax.numpy as jnp
import numpy as np
from jax import lax
from jax.sharding import PartitionSpec as P

H = 32
KVH = 8
HD = 64
L_MAX = 128
P_SIZE = 256


THETA = 10000000.0
EPSILON = 1e-05


def rms_scale(wide, gain):
    mean_square = jnp.mean(wide * wide, axis=-1, keepdims=True)
    return (wide * lax.rsqrt(mean_square + EPSILON) * gain.astype(jnp.float32)).astype(jnp.bfloat16)


def rotate(vectors, positions):
    half = HD // 2
    freqs = THETA ** (-(jnp.arange(half, dtype=jnp.float32) * 2.0 / HD))
    angles = positions[:, None] * freqs[None, :]
    cosine = jnp.cos(angles)
    sine = jnp.sin(angles)
    first = vectors[..., :half]
    second = vectors[..., half:]
    return jnp.concatenate(
        [first * cosine - second * sine, second * cosine + first * sine], axis=-1
    )


def gather_rows(shard, axis_name, count):
    sent = jnp.broadcast_to(shard[None], (count,) + shard.shape)
    got = lax.all_to_all(sent, axis_name, 0, 0, tiled=True)
    rows, width = shard.shape
    return got.transpose(1, 0, 2).reshape(rows, count * width)


def scatter_sum(terms, axis_name, count):
    rows, width = terms.shape
    share = width // count
    sent = terms.astype(jnp.bfloat16).reshape(rows, count, share).transpose(1, 0, 2)
    got = lax.all_to_all(sent, axis_name, 0, 0, tiled=True)
    return jnp.sum(got.astype(jnp.float32), axis=0)


def shards(
    suffix_states,
    suffix_lengths,
    request_group,
    group_owner,
    request_order,
    prefix_cache,
    norm_attn,
    w_query,
    w_key,
    w_value,
    w_out,
    norm_mlp,
    w_gate,
    w_up,
    w_down,
):
    dp_count = lax.axis_size("dp")
    tp_count = lax.axis_size("tensor")
    dp_index = lax.axis_index("dp")
    tp_index = lax.axis_index("tensor")
    total_reqs = suffix_lengths.shape[0]
    local_reqs = total_reqs // dp_count
    row_count = local_reqs * L_MAX
    heads_here = w_query.shape[1] // HD
    group_size = H // KVH
    assert heads_here == 1
    kv_cols = w_key.shape[1]
    d_here = kv_cols // KVH
    score_scale = HD ** (-0.5)
    kv_of_dest = np.arange(tp_count) * heads_here // group_size
    kv_here = tp_index * heads_here // group_size

    col_pick = (np.arange(d_here)[None, :] * KVH + kv_of_dest[:, None]).reshape(-1)
    w_pair = jnp.concatenate([w_key, w_value], axis=1)
    pick = np.concatenate([col_pick.reshape(tp_count, d_here), kv_cols + col_pick.reshape(tp_count, d_here)], axis=1)
    w_sent = jnp.take(w_pair, pick.reshape(-1), axis=1).reshape(w_key.shape[0], tp_count, 2 * d_here)
    w_got = lax.all_to_all(w_sent.transpose(1, 0, 2), "tensor", 0, 0, tiled=True)
    k_head_w = w_got[:, :, :d_here].transpose(1, 0, 2).reshape(w_key.shape[0], HD)
    v_head_w = w_got[:, :, d_here:].transpose(1, 0, 2).reshape(w_key.shape[0], HD)

    routed = jnp.take(suffix_states, request_order, axis=0)
    pos_here = routed.shape[1]
    width_here = routed.shape[2]
    state_part = routed.reshape(dp_count, local_reqs * pos_here * width_here)
    prefix_flat = prefix_cache.reshape(1, -1)
    prefix_part = jnp.broadcast_to(prefix_flat, (dp_count, prefix_flat.shape[1]))
    first = lax.all_to_all(
        jnp.concatenate([state_part, prefix_part], axis=1), "dp", 0, 0, tiled=True
    )
    state_split = state_part.shape[1]
    routed_here = (
        first[:, :state_split]
        .reshape(dp_count, local_reqs, pos_here, width_here)
        .transpose(1, 0, 2, 3)
        .reshape(local_reqs, dp_count * pos_here, width_here)
    )
    prefix_rows = prefix_cache.shape[1]
    prefix_all = first[:, state_split:].reshape(dp_count, prefix_rows, KVH, 2 * HD)

    state_shard = routed_here.reshape(row_count, width_here)
    slot_ids = dp_index * local_reqs + jnp.arange(local_reqs, dtype=jnp.int32)
    req_ids = jnp.take(request_order, slot_ids)
    lengths_here = jnp.take(suffix_lengths, req_ids)
    owner_here = jnp.take(group_owner, jnp.take(request_group[:, 0], req_ids))
    position = jnp.arange(L_MAX, dtype=jnp.int32)
    valid = (position[None, :] < lengths_here[:, None]).reshape(row_count)
    positions = (P_SIZE + position).astype(jnp.float32)

    chosen = jnp.take(prefix_all, owner_here, axis=0)
    chosen = jnp.take(chosen, kv_of_dest, axis=2).transpose(2, 0, 1, 3)
    picked = lax.all_to_all(chosen, "tensor", 0, 0, tiled=True)
    picked = picked.transpose(1, 0, 2, 3).reshape(local_reqs, tp_count * prefix_rows, 2 * HD)
    prefix_keys = picked[:, :, :HD]
    prefix_values = picked[:, :, HD:]

    full_rows = gather_rows(state_shard, "tensor", tp_count)
    normed = rms_scale(full_rows.astype(jnp.float32), norm_attn)
    query = jnp.dot(normed, w_query, preferred_element_type=jnp.float32).reshape(
        local_reqs, L_MAX, HD
    )
    query = rotate(query, positions).astype(jnp.bfloat16)
    key_raw = jnp.dot(normed, k_head_w, preferred_element_type=jnp.float32).astype(jnp.bfloat16)
    value = jnp.dot(normed, v_head_w, preferred_element_type=jnp.float32).astype(jnp.bfloat16)
    key_rot = rotate(
        key_raw.reshape(local_reqs, L_MAX, HD).astype(jnp.float32), positions
    ).astype(jnp.bfloat16)
    value = value.reshape(local_reqs, L_MAX, HD)

    valid3 = valid.reshape(local_reqs, L_MAX, 1)
    out_width = kv_cols
    out_first = (tp_index * out_width) % HD
    keys_out = jnp.where(
        valid3, lax.dynamic_slice_in_dim(key_rot, out_first, out_width, 2), 0.0
    ).astype(jnp.bfloat16)
    values_out = jnp.where(
        valid3, lax.dynamic_slice_in_dim(value, out_first, out_width, 2), 0.0
    ).astype(jnp.bfloat16)

    prefix_scores = jnp.einsum(
        "rtd,rpd->rtp", query, prefix_keys, preferred_element_type=jnp.float32
    ) * score_scale
    self_scores = jnp.einsum(
        "rtd,rsd->rts", query, key_rot, preferred_element_type=jnp.float32
    ) * score_scale
    self_allowed = (position[None, None, :] <= position[None, :, None]) & (
        position[None, None, :] < lengths_here[:, None, None]
    )
    scores = jnp.concatenate([prefix_scores, self_scores], axis=2)
    allowed = jnp.concatenate(
        [jnp.ones(prefix_scores.shape, bool), self_allowed], axis=2
    )
    row_peak = jnp.max(jnp.where(allowed, scores, -jnp.inf), axis=2, keepdims=True)
    weights = jnp.where(allowed, jnp.exp(scores - row_peak), 0.0)
    total = jnp.sum(weights, axis=2, keepdims=True)
    all_values = jnp.concatenate([prefix_values, value], axis=1)
    numerator = jnp.einsum(
        "rtk,rkd->rtd", weights.astype(jnp.bfloat16), all_values, preferred_element_type=jnp.float32
    )
    attention = (numerator / total).astype(jnp.bfloat16).reshape(row_count, HD)

    attn_terms = jnp.dot(attention, w_out, preferred_element_type=jnp.float32)
    attn_share = scatter_sum(attn_terms, "tensor", tp_count)
    middle = (state_shard.astype(jnp.float32) + attn_share).astype(jnp.bfloat16)
    middle_rows = gather_rows(middle, "tensor", tp_count)
    normed_two = rms_scale(middle_rows.astype(jnp.float32), norm_mlp)
    gate = jnp.dot(normed_two, w_gate, preferred_element_type=jnp.float32)
    upper = jnp.dot(normed_two, w_up, preferred_element_type=jnp.float32)
    hidden = (jax.nn.silu(gate) * upper).astype(jnp.bfloat16)
    down_terms = jnp.dot(hidden, w_down, preferred_element_type=jnp.float32)
    down_share = scatter_sum(down_terms, "tensor", tp_count)
    result = middle.astype(jnp.float32) + down_share
    result = (
        jnp.where(valid[:, None], result, 0.0)
        .astype(jnp.bfloat16)
        .reshape(local_reqs, L_MAX, width_here)
    )
    returned = lax.all_to_all(result, "dp", split_axis=1, concat_axis=0, tiled=True)
    hidden_out = jnp.zeros_like(returned).at[request_order].set(returned)
    return (hidden_out, keys_out, values_out)


def solution(mesh):
    in_specs = (
        P(None, "dp", "tensor"),
        P(),
        P(),
        P(),
        P(),
        P("dp", "tensor", None),
        P(),
        P(None, "tensor"),
        P(None, "tensor"),
        P(None, "tensor"),
        P("tensor", None),
        P(),
        P(None, "tensor"),
        P(None, "tensor"),
        P("tensor", None),
    )
    out_specs = (P(None, "dp", "tensor"), P("dp", None, "tensor"), P("dp", None, "tensor"))
    return jax.shard_map(shards, mesh=mesh, in_specs=in_specs, out_specs=out_specs, check_vma=False)
```

time: 636 us -> 248 us (0.39)
  waiting for transfers between devices: 409 us -> 125 us
  blocking collectives: 129 us -> 31.5 us
  between operations: 18.1 us -> 1.35 us
  local copies, waits for them, and re-layouts: 13.2 us -> 22.8 us
    reduce_scatter x2 -> x0, waiting for transfers between devices: 285 us -> none  [the longest x1 144 us: shards(): lax.psum_scatter(down_terms.astype(jnp.bfloat16), 'tensor', scatter_dimen...]
    all_gather x3 -> x0, blocking collectives: 129 us -> none  [the longest x1 48.2 us: shards(): all_rows = lax.all_gather(prefix_cache, 'dp', axis=0, tiled=True)]
    all_to_all x2 -> x6, waiting for transfers between devices: 18 us -> 114 us  [the longest x2 52.3 us: gather_rows(): got = lax.all_to_all(sent, axis_name, 0, 0, tiled=True)]
    all_gather x2 -> x0, waiting for transfers between devices: 95.8 us -> none  [the longest x1 64.4 us: shards(): middle_rows = lax.all_gather(middle, 'tensor', axis=1, tiled=True)]
    all_to_all x0 -> x1, blocking collectives: none -> 31.5 us  [scatter_sum(): got = lax.all_to_all(sent, axis_name, 0, 0, tiled=True)]
    all_to_all x2 -> x6, starting transfers between devices: 31.2 us -> 41.2 us  [the longest x1 16.2 us: shards(): lax.all_to_all(jnp.concatenate([state_part, prefix_part], axis=1), 'dp',...]
    convert_element_type x3 -> x4, other arithmetic: 0.06 us -> 7.8 us  [the longest x2 6.22 us: rms_scale(): (wide * lax.rsqrt(mean_square + EPSILON) * gain.astype(jnp.float32)).asty...]
    all_to_all x1, starting transfers between devices: 11.1 us -> 4.31 us  [shards(): lax.all_to_all(result, 'dp', split_axis=1, concat_axis=0, tiled=True)]
  transfers between devices with their start and end apart: 7 -> 7, of which waited for: 6 -> 7; matrix products, arithmetic and copies ran while one was open for 2% -> 3% of each run, Pallas kernels for 0% -> 0%
where the time goes in v1:
time: 248 us; the launch traced here: 247 us
  waiting for transfers between devices  125 us (50%)
  starting transfers between devices  45.5 us (18%)
  blocking collectives  31.5 us (13%)
  local copies, waits for them, and re-layouts  22.8 us (9%)
  other arithmetic  14 us (6%)
  matrix products  6.95 us (3%)
    all_to_all x2, waiting for transfers between devices, gather_rows(): got = lax.all_to_all(sent, axis_name, 0, 0, tiled=True)  52.3 us
    all_to_all x1, blocking collectives, scatter_sum(): got = lax.all_to_all(sent, axis_name, 0, 0, tiled=True)  31.5 us
    all_to_all x1, waiting for transfers between devices, scatter_sum(): got = lax.all_to_all(sent, axis_name, 0, 0, tiled=True)  27.8 us
    all_to_all x1, waiting for transfers between devices, shards(): lax.all_to_all(w_sent.transpose(1, 0, 2), 'tensor', 0, 0, tiled=True)  16.7 us
    all_to_all x1, starting transfers between devices, shards(): lax.all_to_all(jnp.concatenate([state_part, prefix_part], axis=1), 'dp',...  16.2 us
    all_to_all x1, waiting for transfers between devices, shards(): lax.all_to_all(jnp.concatenate([state_part, prefix_part], axis=1), 'dp',...  10.7 us
    all_to_all x1, waiting for transfers between devices, shards(): lax.all_to_all(result, 'dp', split_axis=1, concat_axis=0, tiled=True)  10.6 us
    all_to_all x1, starting transfers between devices, shards(): picked = lax.all_to_all(chosen, 'tensor', 0, 0, tiled=True)  9.35 us
  transfers between devices with their start and end apart: 7, of which 7 were waited for; matrix products, arithmetic and copies ran while one was open for 3% of the time, Pallas kernels for 0%

profile of v1, /device:TPU:1, one launch (start us, length us, event | category | flops | bytes accessed | tf_op | source)
XLA Modules:
  0.0 247.0 jit_solution(3622147615593371118)
XLA Ops:
  0.7 0.7 compare_select_fusion.4
  1.4 0.7 compare_and_fusion.2
  2.1 0.7 copy.178
  2.8 1.4 gather_fusion
  4.5 0.5 broadcast.338
  5.1 0.8 reduce.4
  5.9 0.9 reshape.405
  6.8 16.2 %all-to-all-start = ((bf16[16,2,4608]{2,1,0:T(2,128)(2,1)}), bf16[16,2,4608]{2,1,0:T(2,128)(2,1)S(1)}, u32[]{:S(2)}, u32[]{:S(2)}) async-start(bf16[16,2,4608]{2,1,0:T(2,128)(2,1)} %reshape.405), calls=%async_computation | async-start | bytes 589824 | tf_op jit(solution)/shard_map/all_to_all | solution.py:98
  23.1 0.6 gather_fusion.5
  23.7 0.6 gather_fusion.7
  24.4 0.6 gather_fusion.6
  25.1 0.6 gather_fusion.1
  25.8 10.7 %all-to-all-done = bf16[16,2,4608]{2,1,0:T(2,128)(2,1)S(1)} async-done(((bf16[16,2,4608]{2,1,0:T(2,128)(2,1)}), bf16[16,2,4608]{2,1,0:T(2,128)(2,1)S(1)}, u32[]{:S(2)}, u32[]{:S(2)}) %all-to-all-start) | async-done | bytes 294944 | tf_op jit(solution)/shard_map/all_to_all | solution.py:98
  36.9 0.6 gather_fusion.2
  37.6 1.3 gather_fusion.3
  38.8 9.4 %all-to-all-start.2 = ((bf16[32,2,8,128]{3,2,1,0:T(8,128)(2,1)}), bf16[32,2,8,128]{3,2,1,0:T(8,128)(2,1)S(1)}, u32[]{:S(2)}, u32[]{:S(2)}) async-start(bf16[32,2,8,128]{3,2,1,0:T(8,128)(2,1)} %gather_fusion.3), calls=%async_computation.2 | async-start | bytes 262144 | tf_op jit(solution)/shard_map/all_to_all | solution.py:122
  48.3 0.9 gather_fusion.4
  49.2 1.0 gather.30
  50.2 6.7 %all-to-all-done.2 = bf16[32,2,8,128]{3,2,1,0:T(8,128)(2,1)S(1)} async-done(((bf16[32,2,8,128]{3,2,1,0:T(8,128)(2,1)}), bf16[32,2,8,128]{3,2,1,0:T(8,128)(2,1)S(1)}, u32[]{:S(2)}, u32[]{:S(2)}) %all-to-all-start.2) | async-done | bytes 131104 | tf_op jit(solution)/shard_map/all_to_all | solution.py:122
  56.9 4.1 %all-to-all-start.3 = ((bf16[32,2048,4]{1,2,0:T(4,128)(2,1)}), bf16[32,2048,4]{1,2,0:T(4,128)(2,1)S(1)}, u32[]{:S(2)}, u32[]{:S(2)}) async-start(bf16[32,2048,4]{1,2,0:T(4,128)(2,1)} %bitcast.13), calls=%async_computation.3 | async-start | bytes 1048576 | tf_op jit(solution)/shard_map/all_to_all | solution.py:88
  61.2 16.7 %all-to-all-done.3 = bf16[32,2048,4]{1,2,0:T(4,128)(2,1)S(1)} async-done(((bf16[32,2048,4]{1,2,0:T(4,128)(2,1)}), bf16[32,2048,4]{1,2,0:T(4,128)(2,1)S(1)}, u32[]{:S(2)}, u32[]{:S(2)}) %all-to-all-start.3) | async-done | bytes 524320 | tf_op jit(solution)/shard_map/all_to_all | solution.py:88
  77.9 1.1 broadcast_in_dim.147
  79.0 3.7 %all-to-all-start.1 = ((bf16[32,256,64]{1,2,0:T(8,128)(2,1)}), bf16[32,256,64]{1,2,0:T(8,128)(2,1)S(1)}, u32[]{:S(2)}, u32[]{:S(2)}) async-start(bf16[32,256,64]{1,2,0:T(8,128)(2,1)} %broadcast_in_dim.147), calls=%async_computation.1 | async-start | bytes 2097152 | tf_op jit(solution)/shard_map/all_to_all | solution.py:38
  82.7 0.6 convert_element_type.142
  84.0 0.6 broadcast_and_fusion
  84.8 0.7 copy.148
  86.1 24.5 %all-to-all-done.1 = bf16[32,256,64]{1,2,0:T(8,128)(2,1)S(1)} async-done(((bf16[32,256,64]{1,2,0:T(8,128)(2,1)}), bf16[32,256,64]{1,2,0:T(8,128)(2,1)S(1)}, u32[]{:S(2)}, u32[]{:S(2)}) %all-to-all-start.1) | async-done | bytes 1048608 | tf_op jit(solution)/shard_map/all_to_all | solution.py:38
  111.9 0.6 copy.177
  112.5 1.6 convert_bitcast_fusion
  114.1 2.3 reshape.315
  116.4 5.9 %multiply_convert_fusion = bf16[2,128,2048]{1,0,2:T(2,128)(2,1)S(1)} fusion(f32[2,128,2048]{1,0,2:T(2,128)S(1)} %reshape.315, f32[2048]{0:T(1024)S(1)} %copy-done.11, f32[2,128]{1,0:T(2,128)S(1)} %get-tuple-element.16), kind=kLoop, calls=%fused_computation.24 | loop fusion | flops 1572864 | bytes 3154944 | tf_op jit(solution)/shard_map/convert_element_type | solution.py:20
  123.6 0.5 convolution_convert_fusion.1
  124.1 0.5 copy.133
  124.6 31.5 %all_to_all.60 = bf16[32,256,64]{1,2,0:T(8,128)(2,1)S(1)} all-to-all(bf16[32,256,64]{1,2,0:T(8,128)(2,1)S(1)} %bitcast.116), channel_id=1, replica_groups=mesh['dp'=16,'tensor'=32] {'tensor'}, dimensions={0} | all-to-all | bytes 2097152 | tf_op jit(solution)/shard_map/all_to_all | solution.py:47
  156.3 1.1 broadcast_in_dim.160
  157.4 3.9 %all-to-all-start.5 = ((bf16[32,256,64]{1,2,0:T(8,128)(2,1)}), bf16[32,256,64]{1,2,0:T(8,128)(2,1)S(1)}, u32[]{:S(2)}, u32[]{:S(2)}) async-start(bf16[32,256,64]{1,2,0:T(8,128)(2,1)} %broadcast_in_dim.160), calls=%async_computation.5 | async-start | bytes 2097152 | tf_op jit(solution)/shard_map/all_to_all | solution.py:38
  161.3 27.8 %all-to-all-done.5 = bf16[32,256,64]{1,2,0:T(8,128)(2,1)S(1)} async-done(((bf16[32,256,64]{1,2,0:T(8,128)(2,1)}), bf16[32,256,64]{1,2,0:T(8,128)(2,1)S(1)}, u32[]{:S(2)}, u32[]{:S(2)}) %all-to-all-start.5) | async-done | bytes 1048608 | tf_op jit(solution)/shard_map/all_to_all | solution.py:38
  189.9 2.4 fusion.47
  192.3 2.6 %convolution_convert_fusion = bf16[256,2048]{1,0:T(8,128)(2,1)S(1)} fusion(bf16[256,2048]{1,0:T(8,128)(2,1)S(1)} %copy-done, bf16[256,2048]{0,1:T(8,128)(2,1)S(1)} %fusion.5, bf16[2048,256]{1,0:T(8,128)(2,1)} %param.32, f32[256,256]{1,0:T(8,128)} %fusion.47), kind=kOutput, calls=%fused_computation.13 | convolution fusion | flops 537788416 | bytes 4456448 | tf_op jit(solution)/shard_map/dot_general | solution.py:180
  194.8 1.3 copy.137
  196.2 4.0 %all-to-all-start.6 = ((bf16[32,256,64]{1,2,0:T(8,128)(2,1)}), bf16[32,256,64]{1,2,0:T(8,128)(2,1)S(1)}, u32[]{:S(2)}, u32[]{:S(2)}) async-start(bf16[32,256,64]{1,2,0:T(8,128)(2,1)} %bitcast.22), calls=%async_computation.6 | async-start | bytes 2097152 | tf_op jit(solution)/shard_map/all_to_all | solution.py:47
  200.3 27.8 %all-to-all-done.6 = bf16[32,256,64]{1,2,0:T(8,128)(2,1)S(1)} async-done(((bf16[32,256,64]{1,2,0:T(8,128)(2,1)}), bf16[32,256,64]{1,2,0:T(8,128)(2,1)S(1)}, u32[]{:S(2)}, u32[]{:S(2)}) %all-to-all-start.6) | async-done | bytes 1048608 | tf_op jit(solution)/shard_map/all_to_all | solution.py:47
  228.4 0.7 reshape.407
  229.1 4.3 %all-to-all-start.7 = ((bf16[16,2,512]{2,1,0:T(2,128)(2,1)}), bf16[16,2,512]{2,1,0:T(2,128)(2,1)S(1)}, u32[]{:S(2)}, u32[]{:S(2)}) async-start(bf16[16,2,512]{2,1,0:T(2,128)(2,1)} %reshape.407), calls=%async_computation.7 | async-start | bytes 65536 | tf_op jit(solution)/shard_map/all_to_all | solution.py:188
  233.4 0.6 dynamic-slice_select_fusion
  234.0 10.6 %all-to-all-done.7 = bf16[16,2,512]{2,1,0:T(2,128)(2,1)S(1)} async-done(((bf16[16,2,512]{2,1,0:T(2,128)(2,1)}), bf16[16,2,512]{2,1,0:T(2,128)(2,1)S(1)}, u32[]{:S(2)}, u32[]{:S(2)}) %all-to-all-start.7) | async-done | bytes 32800 | tf_op jit(solution)/shard_map/all_to_all | solution.py:188
  244.8 1.5 scatter_fusion
  246.4 0.6 copy-done.5
  (108 shorter events, 6.3 us)
Async XLA Ops:
  0.6 191.6 %copy-start = (bf16[256,2048]{1,0:T(8,128)(2,1)S(1)}, bf16[256,2048]{1,0:T(8,128)(2,1)}, u32[]{:S(2)}) copy-start(bf16[256,2048]{1,0:T(8,128)(2,1)} %param.33) | copy-start | bytes 3145732
  0.6 22.4 %copy-start.1 = (s32[32]{0:T(128)S(1)}, s32[32]{0:T(128)}, u32[]{:S(2)}) copy-start(s32[32]{0:T(128)} %param.23) | copy-start | bytes 388
  0.7 23.1 %copy-start.2 = (s32[32,1]{0,1:T(1,128)S(1)}, s32[32,1]{0,1:T(1,128)}, u32[]{:S(2)}) copy-start(s32[32,1]{0,1:T(1,128)} %param.21) | copy-start | bytes 388
  0.7 23.7 %copy-start.3 = (s32[32]{0:T(128)S(1)}, s32[32]{0:T(128)}, u32[]{:S(2)}) copy-start(s32[32]{0:T(128)} %param.20) | copy-start | bytes 388
  0.7 24.4 %copy-start.4 = (s32[16]{0:T(128)S(1)}, s32[16]{0:T(128)}, u32[]{:S(2)}) copy-start(s32[16]{0:T(128)} %param.22) | copy-start | bytes 196
  1.4 0.7 copy-start.17
  4.5 21.2 %copy-start.20 = (s32[32]{0:T(128)S(1)}, s32[32]{0:T(128)}, u32[]{:S(2)}) copy-start(s32[32]{0:T(128)} %constant.165) | copy-start | bytes 388
  6.8 29.7 %all-to-all-start = ((bf16[16,2,4608]{2,1,0:T(2,128)(2,1)}), bf16[16,2,4608]{2,1,0:T(2,128)(2,1)S(1)}, u32[]{:S(2)}, u32[]{:S(2)}) async-start(bf16[16,2,4608]{2,1,0:T(2,128)(2,1)} %reshape.405), calls=%async_computation | async-start | bytes 589824 | tf_op jit(solution)/shard_map/all_to_all | solution.py:98
  25.0 23.2 %copy-start.19 = (s32[128]{0:T(128)S(1)}, s32[128]{0:T(128)}, u32[]{:S(2)}) copy-start(s32[128]{0:T(128)} %constant.166) | copy-start | bytes 1540
  25.0 23.2 %copy-start.8 = (bf16[2048,16]{0,1:T(8,128)(2,1)S(1)}, bf16[2048,16]{0,1:T(8,128)(2,1)}, u32[]{:S(2)}) copy-start(bf16[2048,16]{0,1:T(8,128)(2,1)} %param.28) | copy-start | bytes 196612
  25.0 23.2 %copy-start.9 = (bf16[2048,16]{0,1:T(8,128)(2,1)S(1)}, bf16[2048,16]{0,1:T(8,128)(2,1)}, u32[]{:S(2)}) copy-start(bf16[2048,16]{0,1:T(8,128)(2,1)} %param.27) | copy-start | bytes 196612
  38.8 18.0 %all-to-all-start.2 = ((bf16[32,2,8,128]{3,2,1,0:T(8,128)(2,1)}), bf16[32,2,8,128]{3,2,1,0:T(8,128)(2,1)S(1)}, u32[]{:S(2)}, u32[]{:S(2)}) async-start(bf16[32,2,8,128]{3,2,1,0:T(8,128)(2,1)} %gather_fusion.3), calls=%async_computation.2 | async-start | bytes 262144 | tf_op jit(solution)/shard_map/all_to_all | solution.py:122
  56.9 25.8 %copy-start.13 = (bf16[2048]{0:T(1024)(128)(2,1)S(1)}, bf16[2048]{0:T(1024)(128)(2,1)}, u32[]{:S(2)}) copy-start(bf16[2048]{0:T(1024)(128)(2,1)} %param.25) | copy-start | bytes 12292
  56.9 21.0 %all-to-all-start.3 = ((bf16[32,2048,4]{1,2,0:T(4,128)(2,1)}), bf16[32,2048,4]{1,2,0:T(4,128)(2,1)S(1)}, u32[]{:S(2)}, u32[]{:S(2)}) async-start(bf16[32,2048,4]{1,2,0:T(4,128)(2,1)} %bitcast.13), calls=%async_computation.3 | async-start | bytes 1048576 | tf_op jit(solution)/shard_map/all_to_all | solution.py:88
  79.0 31.6 %all-to-all-start.1 = ((bf16[32,256,64]{1,2,0:T(8,128)(2,1)}), bf16[32,256,64]{1,2,0:T(8,128)(2,1)S(1)}, u32[]{:S(2)}, u32[]{:S(2)}) async-start(bf16[32,256,64]{1,2,0:T(8,128)(2,1)} %broadcast_in_dim.147), calls=%async_computation.1 | async-start | bytes 2097152 | tf_op jit(solution)/shard_map/all_to_all | solution.py:38
  83.5 0.5 copy-start.14
  114.1 2.3 copy-start.11
  116.4 5.9 %copy-start.21 = (bf16[2048,64]{0,1:T(8,128)(2,1)S(1)}, bf16[2048,64]{0,1:T(8,128)(2,1)}, u32[]{:S(2)}) copy-start(bf16[2048,64]{0,1:T(8,128)(2,1)} %param.26) | copy-start | bytes 786436
  116.4 6.7 %copy-start.12 = (pred[2,128,128]{2,1,0:T(8,128)(4,1)S(1)}, pred[2,128,128]{2,1,0:T(8,128)(4,1)}, u32[]{:S(2)}) copy-start(pred[2,128,128]{2,1,0:T(8,128)(4,1)} %broadcast_and_fusion) | copy-start | bytes 98308
  122.3 1.1 copy-start.7
  122.3 1.1 copy-start.10
  122.3 1.3 copy-start.6
  156.1 5.2 %copy-start.16 = (bf16[2048]{0:T(1024)(128)(2,1)S(1)}, bf16[2048]{0:T(1024)(128)(2,1)}, u32[]{:S(2)}) copy-start(bf16[2048]{0:T(1024)(128)(2,1)} %param.30) | copy-start | bytes 12292
  157.4 31.8 %all-to-all-start.5 = ((bf16[32,256,64]{1,2,0:T(8,128)(2,1)}), bf16[32,256,64]{1,2,0:T(8,128)(2,1)S(1)}, u32[]{:S(2)}, u32[]{:S(2)}) async-start(bf16[32,256,64]{1,2,0:T(8,128)(2,1)} %broadcast_in_dim.160), calls=%async_computation.5 | async-start | bytes 2097152 | tf_op jit(solution)/shard_map/all_to_all | solution.py:38
  196.1 32.1 %copy-start.15 = (pred[2,128]{1,0:T(4,128)(4,1)S(1)}, pred[2,128]{1,0:T(4,128)(4,1)}, u32[]{:S(2)}) copy-start(pred[2,128]{1,0:T(4,128)(4,1)} %copy-done.14) | copy-start | bytes 772
  196.1 48.7 %copy-start.18 = (s32[32]{0:T(128)S(1)}, s32[32]{0:T(128)}, u32[]{:S(2)}) copy-start(s32[32]{0:T(128)} %copy-done.17) | copy-start | bytes 388
  196.2 31.9 %all-to-all-start.6 = ((bf16[32,256,64]{1,2,0:T(8,128)(2,1)}), bf16[32,256,64]{1,2,0:T(8,128)(2,1)S(1)}, u32[]{:S(2)}, u32[]{:S(2)}) async-start(bf16[32,256,64]{1,2,0:T(8,128)(2,1)} %bitcast.22), calls=%async_computation.6 | async-start | bytes 2097152 | tf_op jit(solution)/shard_map/all_to_all | solution.py:47
  229.1 15.6 %all-to-all-start.7 = ((bf16[16,2,512]{2,1,0:T(2,128)(2,1)}), bf16[16,2,512]{2,1,0:T(2,128)(2,1)S(1)}, u32[]{:S(2)}, u32[]{:S(2)}) async-start(bf16[16,2,512]{2,1,0:T(2,128)(2,1)} %reshape.407), calls=%async_computation.7 | async-start | bytes 65536 | tf_op jit(solution)/shard_map/all_to_all | solution.py:188
  246.4 0.6 copy-start.5

commit v2 on v1

--- a/solution.py
+++ b/solution.py
@@ -85,9 +85,7 @@
     w_pair = jnp.concatenate([w_key, w_value], axis=1)
     pick = np.concatenate([col_pick.reshape(tp_count, d_here), kv_cols + col_pick.reshape(tp_count, d_here)], axis=1)
     w_sent = jnp.take(w_pair, pick.reshape(-1), axis=1).reshape(w_key.shape[0], tp_count, 2 * d_here)
-    w_got = lax.all_to_all(w_sent.transpose(1, 0, 2), "tensor", 0, 0, tiled=True)
-    k_head_w = w_got[:, :, :d_here].transpose(1, 0, 2).reshape(w_key.shape[0], HD)
-    v_head_w = w_got[:, :, d_here:].transpose(1, 0, 2).reshape(w_key.shape[0], HD)
+    w_sent = w_sent.transpose(1, 0, 2).reshape(tp_count, -1)
 
     routed = jnp.take(suffix_states, request_order, axis=0)
     pos_here = routed.shape[1]
@@ -119,12 +117,24 @@
 
     chosen = jnp.take(prefix_all, owner_here, axis=0)
     chosen = jnp.take(chosen, kv_of_dest, axis=2).transpose(2, 0, 1, 3)
-    picked = lax.all_to_all(chosen, "tensor", 0, 0, tiled=True)
+    state_sent = jnp.broadcast_to(state_shard.reshape(1, -1), (tp_count, row_count * width_here))
+    prefix_sent = chosen.reshape(tp_count, -1)
+    cuts = np.cumsum([state_sent.shape[1], prefix_sent.shape[1]])
+    got = lax.all_to_all(
+        jnp.concatenate([state_sent, prefix_sent, w_sent], axis=1), "tensor", 0, 0, tiled=True
+    )
+    full_rows = (
+        got[:, : cuts[0]].reshape(tp_count, row_count, width_here)
+        .transpose(1, 0, 2).reshape(row_count, tp_count * width_here)
+    )
+    picked = got[:, cuts[0] : cuts[1]].reshape(tp_count, local_reqs, prefix_rows, 2 * HD)
     picked = picked.transpose(1, 0, 2, 3).reshape(local_reqs, tp_count * prefix_rows, 2 * HD)
     prefix_keys = picked[:, :, :HD]
     prefix_values = picked[:, :, HD:]
-
-    full_rows = gather_rows(state_shard, "tensor", tp_count)
+    w_got = got[:, cuts[1] :].reshape(tp_count, w_key.shape[0], 2 * d_here)
+    k_head_w = w_got[:, :, :d_here].transpose(1, 0, 2).reshape(w_key.shape[0], HD)
+    v_head_w = w_got[:, :, d_here:].transpose(1, 0, 2).reshape(w_key.shape[0], HD)
+
     normed = rms_scale(full_rows.astype(jnp.float32), norm_attn)
     query = jnp.dot(normed, w_query, preferred_element_type=jnp.float32).reshape(
         local_reqs, L_MAX, HD

time: 248 us -> 276 us (1.11)
  local copies, waits for them, and re-layouts: 22.8 us -> 62.9 us
  blocking collectives: 31.5 us -> 0 us
  waiting for transfers between devices: 125 us -> 138 us
  other arithmetic: 14 us -> 21.3 us
    all_to_all x1 -> x0, blocking collectives: 31.5 us -> none  [scatter_sum(): got = lax.all_to_all(sent, axis_name, 0, 0, tiled=True)]
    all_to_all x1 -> x2, waiting for transfers between devices: 27.8 us -> 55.5 us  [scatter_sum(): got = lax.all_to_all(sent, axis_name, 0, 0, tiled=True)]
    all_to_all x2 -> x1, waiting for transfers between devices: 52.3 us -> 27.8 us  [gather_rows(): got = lax.all_to_all(sent, axis_name, 0, 0, tiled=True)]
    all_to_all x2 -> x1, waiting for transfers between devices: 23.3 us -> 39.5 us  [shards(): lax.all_to_all(jnp.concatenate([state_sent, prefix_sent, w_sent], axis=1)...]
    unnamed x53 -> x73, local copies, waits for them, and re-layouts: 4.71 us -> 19.6 us
    transpose x1 -> x2, local copies, waits for them, and re-layouts: 0.37 us -> 7.51 us  [shards(): w_got[:, :, d_here:].transpose(1, 0, 2).reshape(w_key.shape[0], HD)]
    all_to_all x1, waiting for transfers between devices: 10.7 us -> 4.18 us  [shards(): lax.all_to_all(jnp.concatenate([state_part, prefix_part], axis=1), 'dp',...]
    convert_element_type x1 -> x3, local copies, waits for them, and re-layouts: 2.3 us -> 7.9 us  [shards(): normed = rms_scale(full_rows.astype(jnp.float32), norm_attn)]
  transfers between devices with their start and end apart: 7 -> 6, of which waited for: 7 -> 6; matrix products, arithmetic and copies ran while one was open for 3% -> 4% of each run, Pallas kernels for 0% -> 0%
where the time goes in v2:
time: 276 us; the launch traced here: 275 us
  waiting for transfers between devices  138 us (50%)
  local copies, waits for them, and re-layouts  62.9 us (23%)
  starting transfers between devices  44.2 us (16%)
  other arithmetic  21.3 us (8%)
  matrix products  6.95 us (3%)
    all_to_all x2, waiting for transfers between devices, scatter_sum(): got = lax.all_to_all(sent, axis_name, 0, 0, tiled=True)  55.5 us
    all_to_all x1, waiting for transfers between devices, shards(): lax.all_to_all(jnp.concatenate([state_sent, prefix_sent, w_sent], axis=1)...  39.5 us
    all_to_all x1, waiting for transfers between devices, gather_rows(): got = lax.all_to_all(sent, axis_name, 0, 0, tiled=True)  27.8 us
    unnamed x73, local copies, waits for them, and re-layouts  19.6 us
    all_to_all x1, starting transfers between devices, shards(): lax.all_to_all(jnp.concatenate([state_part, prefix_part], axis=1), 'dp',...  16.2 us
    all_to_all x1, waiting for transfers between devices, shards(): lax.all_to_all(result, 'dp', split_axis=1, concat_axis=0, tiled=True)  10.6 us
    all_to_all x1, starting transfers between devices, shards(): lax.all_to_all(jnp.concatenate([state_sent, prefix_sent, w_sent], axis=1)...  9.49 us
    all_to_all x2, starting transfers between devices, scatter_sum(): got = lax.all_to_all(sent, axis_name, 0, 0, tiled=True)  8.18 us
  transfers between devices with their start and end apart: 6, of which 6 were waited for; matrix products, arithmetic and copies ran while one was open for 4% of the time, Pallas kernels for 0%

profile of v2, /device:TPU:1, one launch (start us, length us, event | category | flops | bytes accessed | tf_op | source)
XLA Modules:
  0.0 274.5 jit_solution(12985198102943313836)
XLA Ops:
  0.7 0.8 compare_select_fusion.4
  2.2 0.7 copy.234
  2.9 1.4 gather_fusion
  5.1 0.8 reduce.4
  5.9 0.9 reshape.434
  6.9 16.2 %all-to-all-start = ((bf16[16,2,4608]{2,1,0:T(2,128)(2,1)}), bf16[16,2,4608]{2,1,0:T(2,128)(2,1)}, u32[]{:S(2)}, u32[]{:S(2)}) async-start(bf16[16,2,4608]{2,1,0:T(2,128)(2,1)} %reshape.434), calls=%async_computation | async-start | bytes 589824 | tf_op jit(solution)/shard_map/all_to_all | solution.py:96
  25.2 0.9 gather_fusion.4
  26.1 1.0 gather.30
  27.1 3.1 %copy.162 = bf16[2048,32,4]{1,2,0:T(4,128)(2,1)S(1)} copy(bf16[2048,32,4]{0,2,1:T(4,128)(2,1)} %gather.30) | data formatting | bytes 1048576 | tf_op jit(solution)/shard_map/jit(_take)/gather | solution.py:87
  30.2 1.5 copy.163
  32.5 4.2 %all-to-all-done = bf16[16,2,4608]{2,1,0:T(2,128)(2,1)} async-done(((bf16[16,2,4608]{2,1,0:T(2,128)(2,1)}), bf16[16,2,4608]{2,1,0:T(2,128)(2,1)}, u32[]{:S(2)}, u32[]{:S(2)}) %all-to-all-start) | async-done | bytes 294944 | tf_op jit(solution)/shard_map/all_to_all | solution.py:96
  36.6 2.2 reshape.435
  40.8 2.6 reduce.5
  43.5 3.4 %reshape.436 = bf16[32,2,13312]{2,1,0:T(2,128)(2,1)} reshape(bf16[32,26624]{1,0:T(8,128)(2,1)} %reduce.5) | data formatting | bytes 3407872
  46.8 9.5 %all-to-all-start.1 = ((bf16[32,2,13312]{2,1,0:T(2,128)(2,1)}), bf16[32,2,13312]{2,1,0:T(2,128)(2,1)S(1)}, u32[]{:S(2)}, u32[]{:S(2)}) async-start(bf16[32,2,13312]{2,1,0:T(2,128)(2,1)} %reshape.436), calls=%async_computation.1 | async-start | bytes 3407872 | tf_op jit(solution)/shard_map/all_to_all | solution.py:123
  57.1 0.7 multiply_cosine_fusion
  58.5 39.5 %all-to-all-done.1 = bf16[32,2,13312]{2,1,0:T(2,128)(2,1)S(1)} async-done(((bf16[32,2,13312]{2,1,0:T(2,128)(2,1)}), bf16[32,2,13312]{2,1,0:T(2,128)(2,1)S(1)}, u32[]{:S(2)}, u32[]{:S(2)}) %all-to-all-start.1) | async-done | bytes 1703968 | tf_op jit(solution)/shard_map/all_to_all | solution.py:123
  98.0 6.2 %reshape.437 = bf16[32,1,26624]{2,1,0:T(2,128)(2,1)} reshape(bf16[32,2,13312]{2,1,0:T(2,128)(2,1)S(1)} %all-to-all-done.1) | data formatting | bytes 3407872
  104.2 3.0 %copy.228 = bf16[32,1,26624]{2,0,1:T(8,128)(2,1)S(1)} copy(bf16[32,1,26624]{2,1,0:T(2,128)(2,1)} %reshape.437) | data formatting | bytes 3407872
  107.2 0.8 slice.75
  109.0 2.6 copy.170
  111.6 4.9 %slice_bitcast_fusion = (bf16[2048,32,2]{1,2,0:T(2,128)(2,1)}, bf16[2048,32,2]{1,2,0:T(2,128)(2,1)}) fusion(bf16[32,2048,4]{0,2,1:T(4,128)(2,1)} %bitcast.136), kind=kLoop, calls=%fused_computation.38 | loop fusion | bytes 1048576 | tf_op jit(solution)/shard_map/transpose | solution.py:136
  116.6 2.6 copy.176
  119.2 0.8 reshape.334
  120.0 2.6 copy.171
  122.6 0.8 reshape.333
  123.4 3.0 %reshape.345 = f32[32,256,64]{2,1,0:T(8,128)} reshape(f32[32,16384]{1,0:T(8,128)S(1)} %slice_convert_fusion) | data formatting | bytes 4194304 | tf_op jit(solution)/shard_map/convert_element_type | solution.py:138
  126.4 2.8 %multiply_reduce_fusion = f32[256]{0:T(256)S(1)} fusion(f32[32,256,64]{2,1,0:T(8,128)} %reshape.345), kind=kLoop, calls=%fused_computation.11 | loop fusion | flops 1048320 | bytes 2098176 | tf_op jit(solution)/shard_map/reduce_sum | solution.py:19
  129.8 2.1 fusion.1
  131.9 2.0 copy.169
  134.5 2.8 %copy.165 = f32[256,32,64]{0,2,1:T(8,128)S(1)} copy(f32[256,32,64]{2,0,1:T(8,128)} %bitcast.132) | data formatting | bytes 4194304 | tf_op jit(solution)/shard_map/convert_element_type | solution.py:138
  137.4 2.1 reshape.340
  139.5 6.9 %multiply_convert_fusion.1 = bf16[2,128,2048]{1,0,2:T(2,128)(2,1)S(1)} fusion(f32[2,128,2048]{1,0,2:T(2,128)} %reshape.340, f32[2048]{0:T(1024)S(1)} %copy-done.18, f32[2,128]{1,0:T(2,128)S(1)} %get-tuple-element.18), kind=kLoop, calls=%fused_computation.21 | loop fusion | flops 1572864 | bytes 3154944 | tf_op jit(solution)/shard_map/convert_element_type | solution.py:20
  148.2 1.3 copy.179
  149.5 4.2 %all-to-all-start.2 = ((bf16[32,256,64]{1,2,0:T(8,128)(2,1)}), bf16[32,256,64]{1,2,0:T(8,128)(2,1)S(1)}, u32[]{:S(2)}, u32[]{:S(2)}) async-start(bf16[32,256,64]{1,2,0:T(8,128)(2,1)} %bitcast.19), calls=%async_computation.2 | async-start | bytes 2097152 | tf_op jit(solution)/shard_map/all_to_all | solution.py:47
  153.9 27.7 %all-to-all-done.2 = bf16[32,256,64]{1,2,0:T(8,128)(2,1)S(1)} async-done(((bf16[32,256,64]{1,2,0:T(8,128)(2,1)}), bf16[32,256,64]{1,2,0:T(8,128)(2,1)S(1)}, u32[]{:S(2)}, u32[]{:S(2)}) %all-to-all-start.2) | async-done | bytes 1048608 | tf_op jit(solution)/shard_map/all_to_all | solution.py:47
  181.8 1.1 broadcast_in_dim.160
  182.9 3.9 %all-to-all-start.3 = ((bf16[32,256,64]{1,2,0:T(8,128)(2,1)}), bf16[32,256,64]{1,2,0:T(8,128)(2,1)S(1)}, u32[]{:S(2)}, u32[]{:S(2)}) async-start(bf16[32,256,64]{1,2,0:T(8,128)(2,1)} %broadcast_in_dim.160), calls=%async_computation.3 | async-start | bytes 2097152 | tf_op jit(solution)/shard_map/all_to_all | solution.py:38
  186.8 27.8 %all-to-all-done.3 = bf16[32,256,64]{1,2,0:T(8,128)(2,1)S(1)} async-done(((bf16[32,256,64]{1,2,0:T(8,128)(2,1)}), bf16[32,256,64]{1,2,0:T(8,128)(2,1)S(1)}, u32[]{:S(2)}, u32[]{:S(2)}) %all-to-all-start.3) | async-done | bytes 1048608 | tf_op jit(solution)/shard_map/all_to_all | solution.py:38
  215.3 2.4 fusion.45
  217.7 2.6 convolution_convert_fusion
  220.3 1.3 copy.184
  221.6 4.0 %all-to-all-start.4 = ((bf16[32,256,64]{1,2,0:T(8,128)(2,1)}), bf16[32,256,64]{1,2,0:T(8,128)(2,1)S(1)}, u32[]{:S(2)}, u32[]{:S(2)}) async-start(bf16[32,256,64]{1,2,0:T(8,128)(2,1)} %bitcast.24), calls=%async_computation.4 | async-start | bytes 2097152 | tf_op jit(solution)/shard_map/all_to_all | solution.py:47
  225.7 27.8 %all-to-all-done.4 = bf16[32,256,64]{1,2,0:T(8,128)(2,1)S(1)} async-done(((bf16[32,256,64]{1,2,0:T(8,128)(2,1)}), bf16[32,256,64]{1,2,0:T(8,128)(2,1)S(1)}, u32[]{:S(2)}, u32[]{:S(2)}) %all-to-all-start.4) | async-done | bytes 1048608 | tf_op jit(solution)/shard_map/all_to_all | solution.py:47
  253.8 0.7 reshape.438
  254.6 6.4 %all-to-all-start.5 = ((bf16[16,2,512]{2,1,0:T(2,128)(2,1)}), bf16[16,2,512]{2,1,0:T(2,128)(2,1)S(1)}, u32[]{:S(2)}, u32[]{:S(2)}) async-start(bf16[16,2,512]{2,1,0:T(2,128)(2,1)} %reshape.438), calls=%async_computation.5 | async-start | bytes 65536 | tf_op jit(solution)/shard_map/all_to_all | solution.py:198
  261.6 10.6 %all-to-all-done.5 = bf16[16,2,512]{2,1,0:T(2,128)(2,1)S(1)} async-done(((bf16[16,2,512]{2,1,0:T(2,128)(2,1)}), bf16[16,2,512]{2,1,0:T(2,128)(2,1)S(1)}, u32[]{:S(2)}, u32[]{:S(2)}) %all-to-all-start.5) | async-done | bytes 32800 | tf_op jit(solution)/shard_map/all_to_all | solution.py:198
  272.4 1.5 scatter_fusion
  (137 shorter events, 14.0 us)
Async XLA Ops:
  0.6 217.1 %copy-start = (bf16[256,2048]{1,0:T(8,128)(2,1)S(1)}, bf16[256,2048]{1,0:T(8,128)(2,1)}, u32[]{:S(2)}) copy-start(bf16[256,2048]{1,0:T(8,128)(2,1)} %param.33) | copy-start | bytes 3145732
  0.6 24.5 %copy-start.27 = (s32[128]{0:T(128)S(1)}, s32[128]{0:T(128)}, u32[]{:S(2)}) copy-start(s32[128]{0:T(128)} %constant.166) | copy-start | bytes 1540
  0.7 22.5 %copy-start.1 = (s32[32]{0:T(128)S(1)}, s32[32]{0:T(128)}, u32[]{:S(2)}) copy-start(s32[32]{0:T(128)} %param.23) | copy-start | bytes 388
  0.7 23.1 %copy-start.2 = (s32[32,1]{0,1:T(1,128)S(1)}, s32[32,1]{0,1:T(1,128)}, u32[]{:S(2)}) copy-start(s32[32,1]{0,1:T(1,128)} %param.21) | copy-start | bytes 388
  0.7 23.8 %copy-start.3 = (s32[32]{0:T(128)S(1)}, s32[32]{0:T(128)}, u32[]{:S(2)}) copy-start(s32[32]{0:T(128)} %param.20) | copy-start | bytes 388
  0.7 24.4 %copy-start.16 = (bf16[2048,16]{0,1:T(8,128)(2,1)S(1)}, bf16[2048,16]{0,1:T(8,128)(2,1)}, u32[]{:S(2)}) copy-start(bf16[2048,16]{0,1:T(8,128)(2,1)} %param.28) | copy-start | bytes 196612
  0.7 24.4 %copy-start.17 = (bf16[2048,16]{0,1:T(8,128)(2,1)S(1)}, bf16[2048,16]{0,1:T(8,128)(2,1)}, u32[]{:S(2)}) copy-start(bf16[2048,16]{0,1:T(8,128)(2,1)} %param.27) | copy-start | bytes 196612
  1.5 0.7 copy-start.24
  6.9 29.8 %all-to-all-start = ((bf16[16,2,4608]{2,1,0:T(2,128)(2,1)}), bf16[16,2,4608]{2,1,0:T(2,128)(2,1)}, u32[]{:S(2)}, u32[]{:S(2)}) async-start(bf16[16,2,4608]{2,1,0:T(2,128)(2,1)} %reshape.434), calls=%async_computation | async-start | bytes 589824 | tf_op jit(solution)/shard_map/all_to_all | solution.py:96
  27.1 4.7 %copy-start.4 = (s32[16]{0:T(128)S(1)}, s32[16]{0:T(128)}, u32[]{:S(2)}) copy-start(s32[16]{0:T(128)} %param.22) | copy-start | bytes 196
  30.2 2.2 copy-start.26
  32.4 8.3 %copy-start.6 = (bf16[32,8192]{1,0:T(8,128)(2,1)S(1)}, bf16[32,8192]{1,0:T(8,128)(2,1)}, u32[]{:S(2)}) copy-start(bf16[32,8192]{1,0:T(8,128)(2,1)} %copy.163) | copy-start | bytes 1572868
  39.8 0.8 copy-start.9
  46.8 9.5 %copy-start.20 = (bf16[2048]{0:T(1024)(128)(2,1)S(1)}, bf16[2048]{0:T(1024)(128)(2,1)}, u32[]{:S(2)}) copy-start(bf16[2048]{0:T(1024)(128)(2,1)} %param.25) | copy-start | bytes 12292
  46.8 51.1 %all-to-all-start.1 = ((bf16[32,2,13312]{2,1,0:T(2,128)(2,1)}), bf16[32,2,13312]{2,1,0:T(2,128)(2,1)S(1)}, u32[]{:S(2)}, u32[]{:S(2)}) async-start(bf16[32,2,13312]{2,1,0:T(2,128)(2,1)} %reshape.436), calls=%async_computation.1 | async-start | bytes 3407872 | tf_op jit(solution)/shard_map/all_to_all | solution.py:123
  57.1 47.1 %copy-start.21 = (pred[2,128]{1,0:T(4,128)(4,1)}, pred[2,128]{1,0:T(4,128)(4,1)S(1)}, u32[]{:S(2)}) copy-start(pred[2,128]{1,0:T(4,128)(4,1)S(1)} %iota_compare_fusion.1) | copy-start | bytes 772
  126.4 3.4 %copy-start.5 = (f32[32,256,64]{2,1,0:T(8,128)S(1)}, f32[32,256,64]{2,1,0:T(8,128)}, u32[]{:S(2)}) copy-start(f32[32,256,64]{2,1,0:T(8,128)} %reshape.345) | copy-start | bytes 6291460
  131.9 2.0 copy-start.7
  131.9 2.3 copy-start.8
  137.4 2.1 copy-start.18
  139.5 7.0 %copy-start.28 = (bf16[2048,64]{0,1:T(8,128)(2,1)S(1)}, bf16[2048,64]{0,1:T(8,128)(2,1)}, u32[]{:S(2)}) copy-start(bf16[2048,64]{0,1:T(8,128)(2,1)} %param.26) | copy-start | bytes 786436
  139.5 7.3 %copy-start.13 = (f32[128,32]{0,1:T(8,128)S(1)}, f32[128,32]{0,1:T(8,128)}, u32[]{:S(2)}) copy-start(f32[128,32]{0,1:T(8,128)} %get-tuple-element.20) | copy-start | bytes 49156
  139.5 7.3 %copy-start.14 = (f32[128,32]{0,1:T(8,128)S(1)}, f32[128,32]{0,1:T(8,128)}, u32[]{:S(2)}) copy-start(f32[128,32]{0,1:T(8,128)} %get-tuple-element.21) | copy-start | bytes 49156
  139.5 7.8 %copy-start.19 = (pred[2,128,128]{2,1,0:T(8,128)(4,1)S(1)}, pred[2,128,128]{2,1,0:T(8,128)(4,1)}, u32[]{:S(2)}) copy-start(pred[2,128,128]{2,1,0:T(8,128)(4,1)} %broadcast_and_fusion) | copy-start | bytes 98308
  146.4 1.1 copy-start.15
  146.5 1.3 copy-start.12
  148.2 5.5 %copy-start.10 = (bf16[16,2,8,64]{3,2,1,0:T(8,128)(2,1)S(1)}, bf16[16,2,8,64]{3,2,1,0:T(8,128)(2,1)}, u32[]{:S(2)}) copy-start(bf16[16,2,8,64]{3,2,1,0:T(8,128)(2,1)} %copy-done.9) | copy-start | bytes 98308
  149.5 32.0 %all-to-all-start.2 = ((bf16[32,256,64]{1,2,0:T(8,128)(2,1)}), bf16[32,256,64]{1,2,0:T(8,128)(2,1)S(1)}, u32[]{:S(2)}, u32[]{:S(2)}) async-start(bf16[32,256,64]{1,2,0:T(8,128)(2,1)} %bitcast.19), calls=%async_computation.2 | async-start | bytes 2097152 | tf_op jit(solution)/shard_map/all_to_all | solution.py:47
  153.9 33.0 %copy-start.23 = (bf16[2048]{0:T(1024)(128)(2,1)S(1)}, bf16[2048]{0:T(1024)(128)(2,1)}, u32[]{:S(2)}) copy-start(bf16[2048]{0:T(1024)(128)(2,1)} %param.30) | copy-start | bytes 12292
  182.9 31.8 %all-to-all-start.3 = ((bf16[32,256,64]{1,2,0:T(8,128)(2,1)}), bf16[32,256,64]{1,2,0:T(8,128)(2,1)S(1)}, u32[]{:S(2)}, u32[]{:S(2)}) async-start(bf16[32,256,64]{1,2,0:T(8,128)(2,1)} %broadcast_in_dim.160), calls=%async_computation.3 | async-start | bytes 2097152 | tf_op jit(solution)/shard_map/all_to_all | solution.py:38
  221.6 32.1 %copy-start.22 = (pred[2,128]{1,0:T(4,128)(4,1)S(1)}, pred[2,128]{1,0:T(4,128)(4,1)}, u32[]{:S(2)}) copy-start(pred[2,128]{1,0:T(4,128)(4,1)} %copy-done.21) | copy-start | bytes 772
  221.6 50.7 %copy-start.25 = (s32[32]{0:T(128)S(1)}, s32[32]{0:T(128)}, u32[]{:S(2)}) copy-start(s32[32]{0:T(128)} %copy-done.24) | copy-start | bytes 388
  221.6 31.9 %all-to-all-start.4 = ((bf16[32,256,64]{1,2,0:T(8,128)(2,1)}), bf16[32,256,64]{1,2,0:T(8,128)(2,1)S(1)}, u32[]{:S(2)}, u32[]{:S(2)}) async-start(bf16[32,256,64]{1,2,0:T(8,128)(2,1)} %bitcast.24), calls=%async_computation.4 | async-start | bytes 2097152 | tf_op jit(solution)/shard_map/all_to_all | solution.py:47
  254.6 17.6 %all-to-all-start.5 = ((bf16[16,2,512]{2,1,0:T(2,128)(2,1)}), bf16[16,2,512]{2,1,0:T(2,128)(2,1)S(1)}, u32[]{:S(2)}, u32[]{:S(2)}) async-start(bf16[16,2,512]{2,1,0:T(2,128)(2,1)} %reshape.438), calls=%async_computation.5 | async-start | bytes 65536 | tf_op jit(solution)/shard_map/all_to_all | solution.py:198
  273.9 0.6 copy-start.11

commit v3 on v1

--- a/solution.py
+++ b/solution.py
@@ -81,14 +81,6 @@
     kv_of_dest = np.arange(tp_count) * heads_here // group_size
     kv_here = tp_index * heads_here // group_size
 
-    col_pick = (np.arange(d_here)[None, :] * KVH + kv_of_dest[:, None]).reshape(-1)
-    w_pair = jnp.concatenate([w_key, w_value], axis=1)
-    pick = np.concatenate([col_pick.reshape(tp_count, d_here), kv_cols + col_pick.reshape(tp_count, d_here)], axis=1)
-    w_sent = jnp.take(w_pair, pick.reshape(-1), axis=1).reshape(w_key.shape[0], tp_count, 2 * d_here)
-    w_got = lax.all_to_all(w_sent.transpose(1, 0, 2), "tensor", 0, 0, tiled=True)
-    k_head_w = w_got[:, :, :d_here].transpose(1, 0, 2).reshape(w_key.shape[0], HD)
-    v_head_w = w_got[:, :, d_here:].transpose(1, 0, 2).reshape(w_key.shape[0], HD)
-
     routed = jnp.take(suffix_states, request_order, axis=0)
     pos_here = routed.shape[1]
     width_here = routed.shape[2]
@@ -130,8 +122,15 @@
         local_reqs, L_MAX, HD
     )
     query = rotate(query, positions).astype(jnp.bfloat16)
-    key_raw = jnp.dot(normed, k_head_w, preferred_element_type=jnp.float32).astype(jnp.bfloat16)
-    value = jnp.dot(normed, v_head_w, preferred_element_type=jnp.float32).astype(jnp.bfloat16)
+    kv_part = jnp.dot(
+        normed, jnp.concatenate([w_key, w_value], axis=1), preferred_element_type=jnp.float32
+    ).astype(jnp.bfloat16)
+    pick = (np.arange(d_here)[None, :] * KVH + kv_of_dest[:, None])
+    pick = np.concatenate([pick, kv_cols + pick], axis=1)
+    kv_sent = jnp.take(kv_part, pick.reshape(-1), axis=1).reshape(row_count, tp_count, 2 * d_here)
+    kv_got = lax.all_to_all(kv_sent.transpose(1, 0, 2), "tensor", 0, 0, tiled=True)
+    key_raw = kv_got[:, :, :d_here].transpose(1, 0, 2).reshape(row_count, HD)
+    value = kv_got[:, :, d_here:].transpose(1, 0, 2).reshape(row_count, HD)
     key_rot = rotate(
         key_raw.reshape(local_reqs, L_MAX, HD).astype(jnp.float32), positions
     ).astype(jnp.bfloat16)

time: 248 us -> 236 us (0.952)
  waiting for transfers between devices: 125 us -> 112 us
  blocking collectives: 31.5 us -> 35.3 us
  local copies, waits for them, and re-layouts: 22.8 us -> 20.1 us
    all_to_all x1, waiting for transfers between devices: 16.7 us -> 0.01 us  [shards(): lax.all_to_all(kv_sent.transpose(1, 0, 2), 'tensor', 0, 0, tiled=True)]
    all_to_all x1, blocking collectives: 31.5 us -> 35.3 us  [scatter_sum(): got = lax.all_to_all(sent, axis_name, 0, 0, tiled=True)]
    convert_element_type x2 -> x3, other arithmetic: 6.22 us -> 6.56 us  [rms_scale(): (wide * lax.rsqrt(mean_square + EPSILON) * gain.astype(jnp.float32)).asty...]
  transfers between devices with their start and end apart: 7 -> 7, of which waited for: 7 -> 6; matrix products, arithmetic and copies ran while one was open for 3% -> 6% of each run, Pallas kernels for 0% -> 0%
where the time goes in v3:
time: 236 us; the launch traced here: 235 us
  waiting for transfers between devices  112 us (47%)
  starting transfers between devices  45.5 us (19%)
  blocking collectives  35.3 us (15%)
  local copies, waits for them, and re-layouts  20.1 us (9%)
  other arithmetic  13.5 us (6%)
  matrix products  6.64 us (3%)
    all_to_all x2, waiting for transfers between devices, gather_rows(): got = lax.all_to_all(sent, axis_name, 0, 0, tiled=True)  54.6 us
    all_to_all x1, blocking collectives, scatter_sum(): got = lax.all_to_all(sent, axis_name, 0, 0, tiled=True)  35.3 us
    all_to_all x1, waiting for transfers between devices, scatter_sum(): got = lax.all_to_all(sent, axis_name, 0, 0, tiled=True)  27.8 us
    all_to_all x1, starting transfers between devices, shards(): lax.all_to_all(jnp.concatenate([state_part, prefix_part], axis=1), 'dp',...  16.2 us
    all_to_all x1, waiting for transfers between devices, shards(): lax.all_to_all(jnp.concatenate([state_part, prefix_part], axis=1), 'dp',...  10.8 us
    all_to_all x1, waiting for transfers between devices, shards(): lax.all_to_all(result, 'dp', split_axis=1, concat_axis=0, tiled=True)  10.6 us
    all_to_all x1, starting transfers between devices, shards(): picked = lax.all_to_all(chosen, 'tensor', 0, 0, tiled=True)  9.35 us
    all_to_all x1, waiting for transfers between devices, shards(): picked = lax.all_to_all(chosen, 'tensor', 0, 0, tiled=True)  8.45 us
  transfers between devices with their start and end apart: 7, of which 6 were waited for; matrix products, arithmetic and copies ran while one was open for 6% of the time, Pallas kernels for 0%

profile of v3, /device:TPU:1, one launch (start us, length us, event | category | flops | bytes accessed | tf_op | source)
XLA Modules:
  0.0 234.7 jit_solution(13742966530828608112)
XLA Ops:
  0.7 0.7 compare_select_fusion.4
  1.4 0.7 compare_and_fusion.2
  2.1 1.4 gather_fusion
  3.8 0.7 copy.175
  4.5 0.5 broadcast.324
  5.1 0.8 reduce.4
  5.9 0.9 reshape.375
  6.8 16.2 %all-to-all-start = ((bf16[16,2,4608]{2,1,0:T(2,128)(2,1)}), bf16[16,2,4608]{2,1,0:T(2,128)(2,1)S(1)}, u32[]{:S(2)}, u32[]{:S(2)}) async-start(bf16[16,2,4608]{2,1,0:T(2,128)(2,1)} %reshape.375), calls=%async_computation | async-start | bytes 589824 | tf_op jit(solution)/shard_map/all_to_all | solution.py:90
  23.0 0.6 gather_fusion.5
  23.7 0.6 gather_fusion.7
  24.4 0.6 gather_fusion.6
  25.0 0.6 gather_fusion.1
  25.7 10.8 %all-to-all-done = bf16[16,2,4608]{2,1,0:T(2,128)(2,1)S(1)} async-done(((bf16[16,2,4608]{2,1,0:T(2,128)(2,1)}), bf16[16,2,4608]{2,1,0:T(2,128)(2,1)S(1)}, u32[]{:S(2)}, u32[]{:S(2)}) %all-to-all-start) | async-done | bytes 294944 | tf_op jit(solution)/shard_map/all_to_all | solution.py:90
  36.9 0.6 gather_fusion.2
  37.6 1.3 gather_fusion.3
  38.8 9.3 %all-to-all-start.2 = ((bf16[32,2,8,128]{3,2,1,0:T(8,128)(2,1)}), bf16[32,2,8,128]{3,2,1,0:T(8,128)(2,1)S(1)}, u32[]{:S(2)}, u32[]{:S(2)}) async-start(bf16[32,2,8,128]{3,2,1,0:T(8,128)(2,1)} %gather_fusion.3), calls=%async_computation.2 | async-start | bytes 262144 | tf_op jit(solution)/shard_map/all_to_all | solution.py:114
  48.4 8.4 %all-to-all-done.2 = bf16[32,2,8,128]{3,2,1,0:T(8,128)(2,1)S(1)} async-done(((bf16[32,2,8,128]{3,2,1,0:T(8,128)(2,1)}), bf16[32,2,8,128]{3,2,1,0:T(8,128)(2,1)S(1)}, u32[]{:S(2)}, u32[]{:S(2)}) %all-to-all-start.2) | async-done | bytes 131104 | tf_op jit(solution)/shard_map/all_to_all | solution.py:114
  56.9 1.1 broadcast_in_dim.147
  58.0 4.0 %all-to-all-start.1 = ((bf16[32,256,64]{1,2,0:T(8,128)(2,1)}), bf16[32,256,64]{1,2,0:T(8,128)(2,1)S(1)}, u32[]{:S(2)}, u32[]{:S(2)}) async-start(bf16[32,256,64]{1,2,0:T(8,128)(2,1)} %broadcast_in_dim.147), calls=%async_computation.1 | async-start | bytes 2097152 | tf_op jit(solution)/shard_map/all_to_all | solution.py:38
  62.3 0.6 broadcast_and_fusion
  63.1 26.8 %all-to-all-done.1 = bf16[32,256,64]{1,2,0:T(8,128)(2,1)S(1)} async-done(((bf16[32,256,64]{1,2,0:T(8,128)(2,1)}), bf16[32,256,64]{1,2,0:T(8,128)(2,1)S(1)}, u32[]{:S(2)}, u32[]{:S(2)}) %all-to-all-start.1) | async-done | bytes 1048608 | tf_op jit(solution)/shard_map/all_to_all | solution.py:38
  89.9 0.3 multiply_reduce_fusion.1
  90.2 0.3 fusion.4
  90.9 0.9 gather_fusion.4
  91.7 0.7 gather.30
  92.4 3.8 %all-to-all-start.3 = ((bf16[32,256,4]{1,2,0:T(4,128)(2,1)}), bf16[32,256,4]{1,2,0:T(4,128)(2,1)S(1)}, u32[]{:S(2)}, u32[]{:S(2)}) async-start(bf16[32,256,4]{1,2,0:T(4,128)(2,1)} %bitcast.12), calls=%async_computation.3 | async-start | bytes 131072 | tf_op jit(solution)/shard_map/all_to_all | solution.py:131
  96.2 1.6 convert_bitcast_fusion
  97.8 2.3 reshape.284
  100.2 5.9 %multiply_convert_fusion = bf16[2,128,2048]{1,0,2:T(2,128)(2,1)S(1)} fusion(f32[2,128,2048]{1,0,2:T(2,128)S(1)} %reshape.284, f32[2048]{0:T(1024)S(1)} %convert_element_type.144, f32[2,128]{1,0:T(2,128)S(1)} %get-tuple-element.16), kind=kLoop, calls=%fused_computation.21 | loop fusion | flops 1572864 | bytes 3154944 | tf_op jit(solution)/shard_map/convert_element_type | solution.py:20
  107.6 0.5 convolution_convert_fusion.1
  108.0 0.5 copy.133
  108.5 35.3 %all_to_all.60 = bf16[32,256,64]{1,2,0:T(8,128)(2,1)S(1)} all-to-all(bf16[32,256,64]{1,2,0:T(8,128)(2,1)S(1)} %bitcast.107), channel_id=1, replica_groups=mesh['dp'=16,'tensor'=32] {'tensor'}, dimensions={0} | all-to-all | bytes 2097152 | tf_op jit(solution)/shard_map/all_to_all | solution.py:47
  144.0 1.1 broadcast_in_dim.160
  145.2 3.9 %all-to-all-start.5 = ((bf16[32,256,64]{1,2,0:T(8,128)(2,1)}), bf16[32,256,64]{1,2,0:T(8,128)(2,1)S(1)}, u32[]{:S(2)}, u32[]{:S(2)}) async-start(bf16[32,256,64]{1,2,0:T(8,128)(2,1)} %broadcast_in_dim.160), calls=%async_computation.5 | async-start | bytes 2097152 | tf_op jit(solution)/shard_map/all_to_all | solution.py:38
  149.0 27.9 %all-to-all-done.5 = bf16[32,256,64]{1,2,0:T(8,128)(2,1)S(1)} async-done(((bf16[32,256,64]{1,2,0:T(8,128)(2,1)}), bf16[32,256,64]{1,2,0:T(8,128)(2,1)S(1)}, u32[]{:S(2)}, u32[]{:S(2)}) %all-to-all-start.5) | async-done | bytes 1048608 | tf_op jit(solution)/shard_map/all_to_all | solution.py:38
  176.9 0.3 multiply_reduce_fusion
  177.2 0.3 fusion.2
  177.6 2.4 %fusion.48 = f32[256,256]{1,0:T(8,128)} fusion(bf16[256,2048]{0,1:T(8,128)(2,1)S(1)} %fusion.2, bf16[2048,256]{1,0:T(8,128)(2,1)} %param.31), kind=kOutput, calls=%fused_computation.125 | convolution fusion | flops 268435456 | bytes 2359296 | tf_op jit(solution)/shard_map/dot_general | solution.py:176
  180.0 2.6 %convolution_convert_fusion = bf16[256,2048]{1,0:T(8,128)(2,1)S(1)} fusion(bf16[256,2048]{1,0:T(8,128)(2,1)S(1)} %copy-done, bf16[256,2048]{0,1:T(8,128)(2,1)S(1)} %fusion.2, bf16[2048,256]{1,0:T(8,128)(2,1)} %param.32, f32[256,256]{1,0:T(8,128)} %fusion.48), kind=kOutput, calls=%fused_computation.10 | convolution fusion | flops 537788416 | bytes 4456448 | tf_op jit(solution)/shard_map/dot_general | solution.py:179
  182.6 1.3 copy.137
  183.9 4.0 %all-to-all-start.6 = ((bf16[32,256,64]{1,2,0:T(8,128)(2,1)}), bf16[32,256,64]{1,2,0:T(8,128)(2,1)S(1)}, u32[]{:S(2)}, u32[]{:S(2)}) async-start(bf16[32,256,64]{1,2,0:T(8,128)(2,1)} %bitcast.20), calls=%async_computation.6 | async-start | bytes 2097152 | tf_op jit(solution)/shard_map/all_to_all | solution.py:47
  188.0 27.8 %all-to-all-done.6 = bf16[32,256,64]{1,2,0:T(8,128)(2,1)S(1)} async-done(((bf16[32,256,64]{1,2,0:T(8,128)(2,1)}), bf16[32,256,64]{1,2,0:T(8,128)(2,1)S(1)}, u32[]{:S(2)}, u32[]{:S(2)}) %all-to-all-start.6) | async-done | bytes 1048608 | tf_op jit(solution)/shard_map/all_to_all | solution.py:47
  216.1 0.7 reshape.377
  216.8 4.3 %all-to-all-start.7 = ((bf16[16,2,512]{2,1,0:T(2,128)(2,1)}), bf16[16,2,512]{2,1,0:T(2,128)(2,1)S(1)}, u32[]{:S(2)}, u32[]{:S(2)}) async-start(bf16[16,2,512]{2,1,0:T(2,128)(2,1)} %reshape.377), calls=%async_computation.7 | async-start | bytes 65536 | tf_op jit(solution)/shard_map/all_to_all | solution.py:187
  221.1 0.6 dynamic-slice_select_fusion
  221.8 10.6 %all-to-all-done.7 = bf16[16,2,512]{2,1,0:T(2,128)(2,1)S(1)} async-done(((bf16[16,2,512]{2,1,0:T(2,128)(2,1)}), bf16[16,2,512]{2,1,0:T(2,128)(2,1)S(1)}, u32[]{:S(2)}, u32[]{:S(2)}) %all-to-all-start.7) | async-done | bytes 32800 | tf_op jit(solution)/shard_map/all_to_all | solution.py:187
  232.6 1.5 scatter_fusion
  234.1 0.6 copy-done.5
  (94 shorter events, 3.9 us)
Async XLA Ops:
  0.6 179.4 %copy-start = (bf16[256,2048]{1,0:T(8,128)(2,1)S(1)}, bf16[256,2048]{1,0:T(8,128)(2,1)}, u32[]{:S(2)}) copy-start(bf16[256,2048]{1,0:T(8,128)(2,1)} %param.33) | copy-start | bytes 3145732
  0.6 22.4 %copy-start.1 = (s32[32]{0:T(128)S(1)}, s32[32]{0:T(128)}, u32[]{:S(2)}) copy-start(s32[32]{0:T(128)} %param.23) | copy-start | bytes 388
  0.7 23.1 %copy-start.2 = (s32[32,1]{0,1:T(1,128)S(1)}, s32[32,1]{0,1:T(1,128)}, u32[]{:S(2)}) copy-start(s32[32,1]{0,1:T(1,128)} %param.21) | copy-start | bytes 388
  0.7 23.7 %copy-start.3 = (s32[32]{0:T(128)S(1)}, s32[32]{0:T(128)}, u32[]{:S(2)}) copy-start(s32[32]{0:T(128)} %param.20) | copy-start | bytes 388
  0.7 24.4 %copy-start.4 = (s32[16]{0:T(128)S(1)}, s32[16]{0:T(128)}, u32[]{:S(2)}) copy-start(s32[16]{0:T(128)} %param.22) | copy-start | bytes 196
  1.4 2.1 copy-start.12
  4.5 21.2 %copy-start.15 = (s32[32]{0:T(128)S(1)}, s32[32]{0:T(128)}, u32[]{:S(2)}) copy-start(s32[32]{0:T(128)} %constant.165) | copy-start | bytes 388
  6.8 29.7 %all-to-all-start = ((bf16[16,2,4608]{2,1,0:T(2,128)(2,1)}), bf16[16,2,4608]{2,1,0:T(2,128)(2,1)S(1)}, u32[]{:S(2)}, u32[]{:S(2)}) async-start(bf16[16,2,4608]{2,1,0:T(2,128)(2,1)} %reshape.375), calls=%async_computation | async-start | bytes 589824 | tf_op jit(solution)/shard_map/all_to_all | solution.py:90
  37.5 24.4 %copy-start.10 = (bf16[2048]{0:T(1024)(128)(2,1)S(1)}, bf16[2048]{0:T(1024)(128)(2,1)}, u32[]{:S(2)}) copy-start(bf16[2048]{0:T(1024)(128)(2,1)} %param.25) | copy-start | bytes 12292
  37.5 24.5 %copy-start.14 = (s32[128]{0:T(128)S(1)}, s32[128]{0:T(128)}, u32[]{:S(2)}) copy-start(s32[128]{0:T(128)} %constant.166) | copy-start | bytes 1540
  38.8 18.0 %all-to-all-start.2 = ((bf16[32,2,8,128]{3,2,1,0:T(8,128)(2,1)}), bf16[32,2,8,128]{3,2,1,0:T(8,128)(2,1)S(1)}, u32[]{:S(2)}, u32[]{:S(2)}) async-start(bf16[32,2,8,128]{3,2,1,0:T(8,128)(2,1)} %gather_fusion.3), calls=%async_computation.2 | async-start | bytes 262144 | tf_op jit(solution)/shard_map/all_to_all | solution.py:114
  58.0 31.9 %all-to-all-start.1 = ((bf16[32,256,64]{1,2,0:T(8,128)(2,1)}), bf16[32,256,64]{1,2,0:T(8,128)(2,1)S(1)}, u32[]{:S(2)}, u32[]{:S(2)}) async-start(bf16[32,256,64]{1,2,0:T(8,128)(2,1)} %broadcast_in_dim.147), calls=%async_computation.1 | async-start | bytes 2097152 | tf_op jit(solution)/shard_map/all_to_all | solution.py:38
  62.0 28.6 %copy-start.7 = (bf16[2048,16]{0,1:T(8,128)(2,1)S(1)}, bf16[2048,16]{0,1:T(8,128)(2,1)}, u32[]{:S(2)}) copy-start(bf16[2048,16]{0,1:T(8,128)(2,1)} %param.28) | copy-start | bytes 196612
  62.0 28.6 %copy-start.8 = (bf16[2048,16]{0,1:T(8,128)(2,1)S(1)}, bf16[2048,16]{0,1:T(8,128)(2,1)}, u32[]{:S(2)}) copy-start(bf16[2048,16]{0,1:T(8,128)(2,1)} %param.27) | copy-start | bytes 196612
  92.4 14.0 %all-to-all-start.3 = ((bf16[32,256,4]{1,2,0:T(4,128)(2,1)}), bf16[32,256,4]{1,2,0:T(4,128)(2,1)S(1)}, u32[]{:S(2)}, u32[]{:S(2)}) async-start(bf16[32,256,4]{1,2,0:T(4,128)(2,1)} %bitcast.12), calls=%async_computation.3 | async-start | bytes 131072 | tf_op jit(solution)/shard_map/all_to_all | solution.py:131
  100.1 5.9 %copy-start.16 = (bf16[2048,64]{0,1:T(8,128)(2,1)S(1)}, bf16[2048,64]{0,1:T(8,128)(2,1)}, u32[]{:S(2)}) copy-start(bf16[2048,64]{0,1:T(8,128)(2,1)} %param.26) | copy-start | bytes 786436
  106.0 1.0 copy-start.9
  106.4 1.2 copy-start.6
  143.9 5.1 %copy-start.11 = (bf16[2048]{0:T(1024)(128)(2,1)S(1)}, bf16[2048]{0:T(1024)(128)(2,1)}, u32[]{:S(2)}) copy-start(bf16[2048]{0:T(1024)(128)(2,1)} %param.30) | copy-start | bytes 12292
  145.2 31.8 %all-to-all-start.5 = ((bf16[32,256,64]{1,2,0:T(8,128)(2,1)}), bf16[32,256,64]{1,2,0:T(8,128)(2,1)S(1)}, u32[]{:S(2)}, u32[]{:S(2)}) async-start(bf16[32,256,64]{1,2,0:T(8,128)(2,1)} %broadcast_in_dim.160), calls=%async_computation.5 | async-start | bytes 2097152 | tf_op jit(solution)/shard_map/all_to_all | solution.py:38
  183.9 48.7 %copy-start.13 = (s32[32]{0:T(128)S(1)}, s32[32]{0:T(128)}, u32[]{:S(2)}) copy-start(s32[32]{0:T(128)} %copy-done.12) | copy-start | bytes 388
  183.9 31.9 %all-to-all-start.6 = ((bf16[32,256,64]{1,2,0:T(8,128)(2,1)}), bf16[32,256,64]{1,2,0:T(8,128)(2,1)S(1)}, u32[]{:S(2)}, u32[]{:S(2)}) async-start(bf16[32,256,64]{1,2,0:T(8,128)(2,1)} %bitcast.20), calls=%async_computation.6 | async-start | bytes 2097152 | tf_op jit(solution)/shard_map/all_to_all | solution.py:47
  216.8 15.6 %all-to-all-start.7 = ((bf16[16,2,512]{2,1,0:T(2,128)(2,1)}), bf16[16,2,512]{2,1,0:T(2,128)(2,1)S(1)}, u32[]{:S(2)}, u32[]{:S(2)}) async-start(bf16[16,2,512]{2,1,0:T(2,128)(2,1)} %reshape.377), calls=%async_computation.7 | async-start | bytes 65536 | tf_op jit(solution)/shard_map/all_to_all | solution.py:187
  234.1 0.6 copy-start.5

commit v4 on v3

--- a/solution.py
+++ b/solution.py
@@ -177,14 +177,25 @@
     upper = jnp.dot(normed_two, w_up, preferred_element_type=jnp.float32)
     hidden = (jax.nn.silu(gate) * upper).astype(jnp.bfloat16)
     down_terms = jnp.dot(hidden, w_down, preferred_element_type=jnp.float32)
-    down_share = scatter_sum(down_terms, "tensor", tp_count)
-    result = middle.astype(jnp.float32) + down_share
-    result = (
-        jnp.where(valid[:, None], result, 0.0)
+    down_terms = lax.dynamic_update_slice_in_dim(
+        down_terms,
+        lax.dynamic_slice_in_dim(down_terms, tp_index * width_here, width_here, 1)
+        + middle.astype(jnp.float32),
+        tp_index * width_here,
+        1,
+    )
+    down_terms = jnp.where(valid[:, None], down_terms, 0.0).astype(jnp.bfloat16)
+    sent = down_terms.reshape(local_reqs, dp_count, pos_here, tp_count, width_here).transpose(
+        1, 3, 0, 2, 4
+    )
+    sent = sent.reshape(dp_count * tp_count, local_reqs, pos_here, width_here)
+    got = lax.all_to_all(sent, ("dp", "tensor"), 0, 0, tiled=True)
+    got = got.reshape(dp_count, tp_count, local_reqs, pos_here, width_here)
+    returned = (
+        jnp.sum(got.astype(jnp.float32), axis=1)
         .astype(jnp.bfloat16)
-        .reshape(local_reqs, L_MAX, width_here)
-    )
-    returned = lax.all_to_all(result, "dp", split_axis=1, concat_axis=0, tiled=True)
+        .reshape(total_reqs, pos_here, width_here)
+    )
     hidden_out = jnp.zeros_like(returned).at[request_order].set(returned)
     return (hidden_out, keys_out, values_out)
 

time: 236 us -> 247 us (1.047)
  local copies, waits for them, and re-layouts: 20.1 us -> 34.1 us
  waiting for transfers between devices: 112 us -> 104 us
  other arithmetic: 13.5 us -> 17.5 us
  starting transfers between devices: 45.5 us -> 48.4 us
    all_to_all x2 -> x1, waiting for transfers between devices: 38.4 us -> 30.3 us  [shards(): got = lax.all_to_all(sent, ('dp', 'tensor'), 0, 0, tiled=True)]
    unnamed x43, local copies, waits for them, and re-layouts: 3.68 us -> 11.6 us
    reshape x0 -> x2, local copies, waits for them, and re-layouts: none -> 5.53 us  [shards(): down_terms.reshape(local_reqs, dp_count, pos_here, tp_count, width_here)]
    all_to_all x2 -> x1, starting transfers between devices: 8.28 us -> 11.1 us  [shards(): got = lax.all_to_all(sent, ('dp', 'tensor'), 0, 0, tiled=True)]
    convert_element_type x1, other arithmetic: 0.01 us -> 2.74 us  [shards(): down_terms = jnp.where(valid[:, None], down_terms, 0.0).astype(jnp.bfloat16)]
  transfers between devices with their start and end apart: 7 -> 6, of which waited for: 6 -> 5; matrix products, arithmetic and copies ran while one was open for 6% -> 6% of each run, Pallas kernels for 0% -> 0%
where the time goes in v4:
time: 247 us; the launch traced here: 246 us
  waiting for transfers between devices  104 us (42%)
  starting transfers between devices  48.4 us (20%)
  blocking collectives  35.3 us (14%)
  local copies, waits for them, and re-layouts  34.1 us (14%)
  other arithmetic  17.5 us (7%)
  matrix products  6.1 us (2%)
    all_to_all x2, waiting for transfers between devices, gather_rows(): got = lax.all_to_all(sent, axis_name, 0, 0, tiled=True)  54 us
    all_to_all x1, blocking collectives, scatter_sum(): got = lax.all_to_all(sent, axis_name, 0, 0, tiled=True)  35.3 us
    all_to_all x1, waiting for transfers between devices, shards(): got = lax.all_to_all(sent, ('dp', 'tensor'), 0, 0, tiled=True)  30.3 us
    all_to_all x1, starting transfers between devices, shards(): lax.all_to_all(jnp.concatenate([state_part, prefix_part], axis=1), 'dp',...  16.2 us
    unnamed x43, local copies, waits for them, and re-layouts  11.6 us
    all_to_all x1, starting transfers between devices, shards(): got = lax.all_to_all(sent, ('dp', 'tensor'), 0, 0, tiled=True)  11.1 us
    all_to_all x1, waiting for transfers between devices, shards(): lax.all_to_all(jnp.concatenate([state_part, prefix_part], axis=1), 'dp',...  10.8 us
    all_to_all x1, starting transfers between devices, shards(): picked = lax.all_to_all(chosen, 'tensor', 0, 0, tiled=True)  9.35 us
  transfers between devices with their start and end apart: 6, of which 5 were waited for; matrix products, arithmetic and copies ran while one was open for 6% of the time, Pallas kernels for 0%

profile of v4, /device:TPU:1, one launch (start us, length us, event | category | flops | bytes accessed | tf_op | source)
XLA Modules:
  0.0 246.2 jit_solution(17423745785986390570)
XLA Ops:
  0.7 0.7 compare_select_fusion.4
  1.4 0.7 compare_and_fusion.2
  2.1 1.4 gather_fusion
  3.8 0.7 copy.110
  4.5 0.5 broadcast.321
  5.0 0.8 reduce.5
  5.9 0.9 reshape.378
  6.8 16.2 %all-to-all-start = ((bf16[16,2,4608]{2,1,0:T(2,128)(2,1)}), bf16[16,2,4608]{2,1,0:T(2,128)(2,1)S(1)}, u32[]{:S(2)}, u32[]{:S(2)}) async-start(bf16[16,2,4608]{2,1,0:T(2,128)(2,1)} %reshape.378), calls=%async_computation | async-start | bytes 589824 | tf_op jit(solution)/shard_map/all_to_all | solution.py:90
  23.0 0.6 gather_fusion.5
  23.7 0.6 gather_fusion.7
  24.4 0.6 gather_fusion.6
  25.0 0.6 gather_fusion.1
  25.7 10.8 %all-to-all-done = bf16[16,2,4608]{2,1,0:T(2,128)(2,1)S(1)} async-done(((bf16[16,2,4608]{2,1,0:T(2,128)(2,1)}), bf16[16,2,4608]{2,1,0:T(2,128)(2,1)S(1)}, u32[]{:S(2)}, u32[]{:S(2)}) %all-to-all-start) | async-done | bytes 294944 | tf_op jit(solution)/shard_map/all_to_all | solution.py:90
  36.9 0.6 gather_fusion.2
  37.6 1.3 gather_fusion.3
  38.8 9.3 %all-to-all-start.2 = ((bf16[32,2,8,128]{3,2,1,0:T(8,128)(2,1)}), bf16[32,2,8,128]{3,2,1,0:T(8,128)(2,1)S(1)}, u32[]{:S(2)}, u32[]{:S(2)}) async-start(bf16[32,2,8,128]{3,2,1,0:T(8,128)(2,1)} %gather_fusion.3), calls=%async_computation.2 | async-start | bytes 262144 | tf_op jit(solution)/shard_map/all_to_all | solution.py:114
  48.4 8.4 %all-to-all-done.2 = bf16[32,2,8,128]{3,2,1,0:T(8,128)(2,1)S(1)} async-done(((bf16[32,2,8,128]{3,2,1,0:T(8,128)(2,1)}), bf16[32,2,8,128]{3,2,1,0:T(8,128)(2,1)S(1)}, u32[]{:S(2)}, u32[]{:S(2)}) %all-to-all-start.2) | async-done | bytes 131104 | tf_op jit(solution)/shard_map/all_to_all | solution.py:114
  56.9 1.1 broadcast_in_dim.144
  58.0 4.0 %all-to-all-start.1 = ((bf16[32,256,64]{1,2,0:T(8,128)(2,1)}), bf16[32,256,64]{1,2,0:T(8,128)(2,1)S(1)}, u32[]{:S(2)}, u32[]{:S(2)}) async-start(bf16[32,256,64]{1,2,0:T(8,128)(2,1)} %broadcast_in_dim.144), calls=%async_computation.1 | async-start | bytes 2097152 | tf_op jit(solution)/shard_map/all_to_all | solution.py:38
  62.3 0.6 broadcast_and_fusion
  63.0 0.7 copy.92
  63.7 26.2 %all-to-all-done.1 = bf16[32,256,64]{1,2,0:T(8,128)(2,1)S(1)} async-done(((bf16[32,256,64]{1,2,0:T(8,128)(2,1)}), bf16[32,256,64]{1,2,0:T(8,128)(2,1)S(1)}, u32[]{:S(2)}, u32[]{:S(2)}) %all-to-all-start.1) | async-done | bytes 1048608 | tf_op jit(solution)/shard_map/all_to_all | solution.py:38
  90.9 0.9 gather_fusion.4
  91.7 0.7 gather.30
  92.4 3.9 %all-to-all-start.3 = ((bf16[32,256,4]{1,2,0:T(4,128)(2,1)}), bf16[32,256,4]{1,2,0:T(4,128)(2,1)S(1)}, u32[]{:S(2)}, u32[]{:S(2)}) async-start(bf16[32,256,4]{1,2,0:T(4,128)(2,1)} %bitcast.12), calls=%async_computation.3 | async-start | bytes 131072 | tf_op jit(solution)/shard_map/all_to_all | solution.py:131
  96.2 1.6 convert_bitcast_fusion
  97.8 2.3 reshape.287
  100.1 5.9 %multiply_convert_fusion = bf16[2,128,2048]{1,0,2:T(2,128)(2,1)S(1)} fusion(f32[2,128,2048]{1,0,2:T(2,128)S(1)} %reshape.287, f32[2048]{0:T(1024)S(1)} %convert_element_type.128, f32[2,128]{1,0:T(2,128)S(1)} %get-tuple-element.16), kind=kLoop, calls=%fused_computation.21 | loop fusion | flops 1572864 | bytes 3154944 | tf_op jit(solution)/shard_map/convert_element_type | solution.py:20
  107.5 0.4 convolution_convert_fusion
  108.0 0.5 copy.82
  108.5 35.3 %all_to_all.42 = bf16[32,256,64]{1,2,0:T(8,128)(2,1)S(1)} all-to-all(bf16[32,256,64]{1,2,0:T(8,128)(2,1)S(1)} %bitcast.84), channel_id=1, replica_groups=mesh['dp'=16,'tensor'=32] {'tensor'}, dimensions={0} | all-to-all | bytes 2097152 | tf_op jit(solution)/shard_map/all_to_all | solution.py:47
  144.2 1.1 broadcast_in_dim.157
  145.3 3.9 %all-to-all-start.5 = ((bf16[32,256,64]{1,2,0:T(8,128)(2,1)}), bf16[32,256,64]{1,2,0:T(8,128)(2,1)S(1)}, u32[]{:S(2)}, u32[]{:S(2)}) async-start(bf16[32,256,64]{1,2,0:T(8,128)(2,1)} %broadcast_in_dim.157), calls=%async_computation.5 | async-start | bytes 2097152 | tf_op jit(solution)/shard_map/all_to_all | solution.py:38
  149.3 27.8 %all-to-all-done.5 = bf16[32,256,64]{1,2,0:T(8,128)(2,1)S(1)} async-done(((bf16[32,256,64]{1,2,0:T(8,128)(2,1)}), bf16[32,256,64]{1,2,0:T(8,128)(2,1)S(1)}, u32[]{:S(2)}, u32[]{:S(2)}) %all-to-all-start.5) | async-done | bytes 1048608 | tf_op jit(solution)/shard_map/all_to_all | solution.py:38
  177.8 1.8 fusion.47
  179.6 2.6 %fusion.9 = f32[256,2048]{1,0:T(8,128)} fusion(bf16[256,2048]{1,0:T(8,128)(2,1)S(1)} %copy-done, bf16[256,2048]{0,1:T(8,128)(2,1)S(1)} %fusion.2, bf16[2048,256]{1,0:T(8,128)(2,1)S(1)} %copy-done.5, f32[256,256]{1,0:T(8,128)S(1)} %fusion.47), kind=kOutput, calls=%fused_computation.29 | convolution fusion | flops 537264128 | bytes 5505024 | tf_op jit(solution)/shard_map/dot_general | solution.py:179
  182.2 1.0 convert_add_fusion
  183.3 1.9 dynamic_update_slice.3
  185.2 2.7 %select_convert_fusion = bf16[256,2048]{1,0:T(8,128)(2,1)} fusion(f32[256,2048]{1,0:T(8,128)} %dynamic_update_slice.3, pred[256]{0:T(512)(128)(4,1)S(1)} %get-tuple-element.22), kind=kLoop, calls=%fused_computation.18 | loop fusion | flops 524288 | bytes 3145984 | tf_op jit(solution)/shard_map/convert_element_type | solution.py:187
  187.9 3.3 %reshape.283 = bf16[2,16,8,32,64]{4,3,2,1,0:T(8,128)(2,1)S(1)} reshape(bf16[256,2048]{1,0:T(8,128)(2,1)} %select_convert_fusion) | data formatting | bytes 2097152 | tf_op jit(solution)/shard_map/reshape | solution.py:188
  191.3 2.2 copy.85
  193.5 4.5 %reshape.380 = bf16[512,2,512]{2,1,0:T(2,128)(2,1)} reshape(bf16[512,2,8,64]{3,2,1,0:T(8,128)(2,1)} %bitcast.83) | data formatting | bytes 2097152
  197.9 11.1 %all-to-all-start.6 = ((bf16[512,2,512]{2,1,0:T(2,128)(2,1)}), bf16[512,2,512]{2,1,0:T(2,128)(2,1)}, u32[]{:S(2)}, u32[]{:S(2)}) async-start(bf16[512,2,512]{2,1,0:T(2,128)(2,1)} %reshape.380), calls=%async_computation.6 | async-start | bytes 2097152 | tf_op jit(solution)/shard_map/all_to_all | solution.py:192
  209.0 0.6 dynamic-slice_select_fusion
  209.7 30.3 %all-to-all-done.6 = bf16[512,2,512]{2,1,0:T(2,128)(2,1)} async-done(((bf16[512,2,512]{2,1,0:T(2,128)(2,1)}), bf16[512,2,512]{2,1,0:T(2,128)(2,1)}, u32[]{:S(2)}, u32[]{:S(2)}) %all-to-all-start.6) | async-done | bytes 1048608 | tf_op jit(solution)/shard_map/all_to_all | solution.py:192
  240.0 3.7 %reshape.381 = bf16[512,2,8,64]{3,2,1,0:T(8,128)(2,1)S(1)} reshape(bf16[512,2,512]{2,1,0:T(2,128)(2,1)} %all-to-all-done.6) | data formatting | bytes 2097152
  244.1 1.5 scatter_fusion
  245.6 0.6 copy-done.6
  (92 shorter events, 5.2 us)
Async XLA Ops:
  0.6 179.0 %copy-start = (bf16[256,2048]{1,0:T(8,128)(2,1)S(1)}, bf16[256,2048]{1,0:T(8,128)(2,1)}, u32[]{:S(2)}) copy-start(bf16[256,2048]{1,0:T(8,128)(2,1)} %param.33) | copy-start | bytes 3145732
  0.6 22.4 %copy-start.1 = (s32[32]{0:T(128)S(1)}, s32[32]{0:T(128)}, u32[]{:S(2)}) copy-start(s32[32]{0:T(128)} %param.23) | copy-start | bytes 388
  0.7 23.0 %copy-start.2 = (s32[32,1]{0,1:T(1,128)S(1)}, s32[32,1]{0,1:T(1,128)}, u32[]{:S(2)}) copy-start(s32[32,1]{0,1:T(1,128)} %param.21) | copy-start | bytes 388
  0.7 23.7 %copy-start.3 = (s32[32]{0:T(128)S(1)}, s32[32]{0:T(128)}, u32[]{:S(2)}) copy-start(s32[32]{0:T(128)} %param.20) | copy-start | bytes 388
  0.7 24.3 %copy-start.4 = (s32[16]{0:T(128)S(1)}, s32[16]{0:T(128)}, u32[]{:S(2)}) copy-start(s32[16]{0:T(128)} %param.22) | copy-start | bytes 196
  4.5 21.2 %copy-start.15 = (s32[32]{0:T(128)S(1)}, s32[32]{0:T(128)}, u32[]{:S(2)}) copy-start(s32[32]{0:T(128)} %constant.168) | copy-start | bytes 388
  6.8 29.7 %all-to-all-start = ((bf16[16,2,4608]{2,1,0:T(2,128)(2,1)}), bf16[16,2,4608]{2,1,0:T(2,128)(2,1)S(1)}, u32[]{:S(2)}, u32[]{:S(2)}) async-start(bf16[16,2,4608]{2,1,0:T(2,128)(2,1)} %reshape.378), calls=%async_computation | async-start | bytes 589824 | tf_op jit(solution)/shard_map/all_to_all | solution.py:90
  37.5 24.4 %copy-start.12 = (bf16[2048]{0:T(1024)(128)(2,1)S(1)}, bf16[2048]{0:T(1024)(128)(2,1)}, u32[]{:S(2)}) copy-start(bf16[2048]{0:T(1024)(128)(2,1)} %param.25) | copy-start | bytes 12292
  37.5 24.5 %copy-start.14 = (s32[128]{0:T(128)S(1)}, s32[128]{0:T(128)}, u32[]{:S(2)}) copy-start(s32[128]{0:T(128)} %constant.169) | copy-start | bytes 1540
  38.8 18.0 %all-to-all-start.2 = ((bf16[32,2,8,128]{3,2,1,0:T(8,128)(2,1)}), bf16[32,2,8,128]{3,2,1,0:T(8,128)(2,1)S(1)}, u32[]{:S(2)}, u32[]{:S(2)}) async-start(bf16[32,2,8,128]{3,2,1,0:T(8,128)(2,1)} %gather_fusion.3), calls=%async_computation.2 | async-start | bytes 262144 | tf_op jit(solution)/shard_map/all_to_all | solution.py:114
  58.0 31.9 %all-to-all-start.1 = ((bf16[32,256,64]{1,2,0:T(8,128)(2,1)}), bf16[32,256,64]{1,2,0:T(8,128)(2,1)S(1)}, u32[]{:S(2)}, u32[]{:S(2)}) async-start(bf16[32,256,64]{1,2,0:T(8,128)(2,1)} %broadcast_in_dim.144), calls=%async_computation.1 | async-start | bytes 2097152 | tf_op jit(solution)/shard_map/all_to_all | solution.py:38
  62.0 28.6 %copy-start.8 = (bf16[2048,16]{0,1:T(8,128)(2,1)S(1)}, bf16[2048,16]{0,1:T(8,128)(2,1)}, u32[]{:S(2)}) copy-start(bf16[2048,16]{0,1:T(8,128)(2,1)} %param.28) | copy-start | bytes 196612
  62.0 28.6 %copy-start.9 = (bf16[2048,16]{0,1:T(8,128)(2,1)S(1)}, bf16[2048,16]{0,1:T(8,128)(2,1)}, u32[]{:S(2)}) copy-start(bf16[2048,16]{0,1:T(8,128)(2,1)} %param.27) | copy-start | bytes 196612
  92.4 14.0 %all-to-all-start.3 = ((bf16[32,256,4]{1,2,0:T(4,128)(2,1)}), bf16[32,256,4]{1,2,0:T(4,128)(2,1)S(1)}, u32[]{:S(2)}, u32[]{:S(2)}) async-start(bf16[32,256,4]{1,2,0:T(4,128)(2,1)} %bitcast.12), calls=%async_computation.3 | async-start | bytes 131072 | tf_op jit(solution)/shard_map/all_to_all | solution.py:131
  100.1 5.9 %copy-start.16 = (bf16[2048,64]{0,1:T(8,128)(2,1)S(1)}, bf16[2048,64]{0,1:T(8,128)(2,1)}, u32[]{:S(2)}) copy-start(bf16[2048,64]{0,1:T(8,128)(2,1)} %param.26) | copy-start | bytes 786436
  106.0 1.0 copy-start.11
  106.0 1.3 copy-start.10
  106.4 1.2 copy-start.7
  144.0 5.2 %copy-start.13 = (bf16[2048]{0:T(1024)(128)(2,1)S(1)}, bf16[2048]{0:T(1024)(128)(2,1)}, u32[]{:S(2)}) copy-start(bf16[2048]{0:T(1024)(128)(2,1)} %param.30) | copy-start | bytes 12292
  145.3 31.8 %all-to-all-start.5 = ((bf16[32,256,64]{1,2,0:T(8,128)(2,1)}), bf16[32,256,64]{1,2,0:T(8,128)(2,1)S(1)}, u32[]{:S(2)}, u32[]{:S(2)}) async-start(bf16[32,256,64]{1,2,0:T(8,128)(2,1)} %broadcast_in_dim.157), calls=%async_computation.5 | async-start | bytes 2097152 | tf_op jit(solution)/shard_map/all_to_all | solution.py:38
  177.8 1.8 copy-start.5
  197.9 42.1 %all-to-all-start.6 = ((bf16[512,2,512]{2,1,0:T(2,128)(2,1)}), bf16[512,2,512]{2,1,0:T(2,128)(2,1)}, u32[]{:S(2)}, u32[]{:S(2)}) async-start(bf16[512,2,512]{2,1,0:T(2,128)(2,1)} %reshape.380), calls=%async_computation.6 | async-start | bytes 2097152 | tf_op jit(solution)/shard_map/all_to_all | solution.py:192
  245.6 0.6 copy-start.6

commit v5 on v3

--- a/solution.py
+++ b/solution.py
@@ -111,11 +111,6 @@
 
     chosen = jnp.take(prefix_all, owner_here, axis=0)
     chosen = jnp.take(chosen, kv_of_dest, axis=2).transpose(2, 0, 1, 3)
-    picked = lax.all_to_all(chosen, "tensor", 0, 0, tiled=True)
-    picked = picked.transpose(1, 0, 2, 3).reshape(local_reqs, tp_count * prefix_rows, 2 * HD)
-    prefix_keys = picked[:, :, :HD]
-    prefix_values = picked[:, :, HD:]
-
     full_rows = gather_rows(state_shard, "tensor", tp_count)
     normed = rms_scale(full_rows.astype(jnp.float32), norm_attn)
     query = jnp.dot(normed, w_query, preferred_element_type=jnp.float32).reshape(
@@ -128,7 +123,19 @@
     pick = (np.arange(d_here)[None, :] * KVH + kv_of_dest[:, None])
     pick = np.concatenate([pick, kv_cols + pick], axis=1)
     kv_sent = jnp.take(kv_part, pick.reshape(-1), axis=1).reshape(row_count, tp_count, 2 * d_here)
-    kv_got = lax.all_to_all(kv_sent.transpose(1, 0, 2), "tensor", 0, 0, tiled=True)
+    prefix_split = chosen.shape[1] * chosen.shape[2] * chosen.shape[3]
+    both = lax.all_to_all(
+        jnp.concatenate(
+            [chosen.reshape(tp_count, -1), kv_sent.transpose(1, 0, 2).reshape(tp_count, -1)],
+            axis=1,
+        ),
+        "tensor", 0, 0, tiled=True,
+    )
+    picked = both[:, :prefix_split].reshape(tp_count, local_reqs, prefix_rows, 2 * HD)
+    picked = picked.transpose(1, 0, 2, 3).reshape(local_reqs, tp_count * prefix_rows, 2 * HD)
+    prefix_keys = picked[:, :, :HD]
+    prefix_values = picked[:, :, HD:]
+    kv_got = both[:, prefix_split:].reshape(tp_count, row_count, 2 * d_here)
     key_raw = kv_got[:, :, :d_here].transpose(1, 0, 2).reshape(row_count, HD)
     value = kv_got[:, :, d_here:].transpose(1, 0, 2).reshape(row_count, HD)
     key_rot = rotate(

time: 236 us -> 223 us (0.945)
  waiting for transfers between devices: 112 us -> 103 us
  starting transfers between devices: 45.5 us -> 41.4 us
    all_to_all x2 -> x1, starting transfers between devices: 13.2 us -> 3.86 us  [shards(): lax.all_to_all(jnp.concatenate([chosen.reshape(tp_count, -1), kv_sent.tra...]
    all_to_all x2 -> x1, waiting for transfers between devices: 8.45 us -> 0.01 us  [shards(): lax.all_to_all(jnp.concatenate([chosen.reshape(tp_count, -1), kv_sent.tra...]
    all_to_all x2, starting transfers between devices: 7.84 us -> 13.2 us  [gather_rows(): got = lax.all_to_all(sent, axis_name, 0, 0, tiled=True)]
    unnamed x43 -> x45, local copies, waits for them, and re-layouts: 3.68 us -> 4.78 us
  transfers between devices with their start and end apart: 7 -> 6, of which waited for: 6 -> 5; matrix products, arithmetic and copies ran while one was open for 6% -> 7% of each run, Pallas kernels for 0% -> 0%
where the time goes in v5:
time: 223 us; the launch traced here: 222 us
  waiting for transfers between devices  103 us (46%)
  starting transfers between devices  41.4 us (19%)
  blocking collectives  35.3 us (16%)
  local copies, waits for them, and re-layouts  20.6 us (9%)
  other arithmetic  14.3 us (6%)
  matrix products  6.66 us (3%)
    all_to_all x2, waiting for transfers between devices, gather_rows(): got = lax.all_to_all(sent, axis_name, 0, 0, tiled=True)  53.3 us
    all_to_all x1, blocking collectives, scatter_sum(): got = lax.all_to_all(sent, axis_name, 0, 0, tiled=True)  35.3 us
    all_to_all x1, waiting for transfers between devices, scatter_sum(): got = lax.all_to_all(sent, axis_name, 0, 0, tiled=True)  27.8 us
    all_to_all x1, starting transfers between devices, shards(): lax.all_to_all(jnp.concatenate([state_part, prefix_part], axis=1), 'dp',...  16.2 us
    all_to_all x2, starting transfers between devices, gather_rows(): got = lax.all_to_all(sent, axis_name, 0, 0, tiled=True)  13.2 us
    all_to_all x1, waiting for transfers between devices, shards(): lax.all_to_all(jnp.concatenate([state_part, prefix_part], axis=1), 'dp',...  10.8 us
    all_to_all x1, waiting for transfers between devices, shards(): lax.all_to_all(result, 'dp', split_axis=1, concat_axis=0, tiled=True)  10.6 us
    convert_element_type x3, other arithmetic, rms_scale(): (wide * lax.rsqrt(mean_square + EPSILON) * gain.astype(jnp.float32)).asty...  6.56 us
  transfers between devices with their start and end apart: 6, of which 5 were waited for; matrix products, arithmetic and copies ran while one was open for 7% of the time, Pallas kernels for 0%

profile of v5, /device:TPU:1, one launch (start us, length us, event | category | flops | bytes accessed | tf_op | source)
XLA Modules:
  0.0 222.3 jit_solution(11459104917382986465)
XLA Ops:
  0.7 0.7 compare_select_fusion.4
  1.4 0.7 compare_and_fusion.2
  2.1 1.4 gather_fusion
  3.8 0.7 copy.217
  4.5 0.5 broadcast.324
  5.0 0.8 reduce.4
  5.9 0.9 reshape.393
  6.8 16.2 %all-to-all-start = ((bf16[16,2,4608]{2,1,0:T(2,128)(2,1)}), bf16[16,2,4608]{2,1,0:T(2,128)(2,1)S(1)}, u32[]{:S(2)}, u32[]{:S(2)}) async-start(bf16[16,2,4608]{2,1,0:T(2,128)(2,1)} %reshape.393), calls=%async_computation | async-start | bytes 589824 | tf_op jit(solution)/shard_map/all_to_all | solution.py:90
  23.0 0.6 gather_fusion.5
  23.7 0.6 gather_fusion.7
  24.4 0.6 gather_fusion.6
  25.0 0.6 gather_fusion.1
  25.7 10.8 %all-to-all-done = bf16[16,2,4608]{2,1,0:T(2,128)(2,1)S(1)} async-done(((bf16[16,2,4608]{2,1,0:T(2,128)(2,1)}), bf16[16,2,4608]{2,1,0:T(2,128)(2,1)S(1)}, u32[]{:S(2)}, u32[]{:S(2)}) %all-to-all-start) | async-done | bytes 294944 | tf_op jit(solution)/shard_map/all_to_all | solution.py:90
  37.1 1.1 broadcast_in_dim.147
  38.2 9.3 %all-to-all-start.1 = ((bf16[32,256,64]{1,2,0:T(8,128)(2,1)}), bf16[32,256,64]{1,2,0:T(8,128)(2,1)S(1)}, u32[]{:S(2)}, u32[]{:S(2)}) async-start(bf16[32,256,64]{1,2,0:T(8,128)(2,1)} %broadcast_in_dim.147), calls=%async_computation.1 | async-start | bytes 2097152 | tf_op jit(solution)/shard_map/all_to_all | solution.py:38
  47.9 0.6 broadcast_and_fusion
  48.6 0.6 gather_fusion.2
  49.3 0.6 gather_fusion.3
  49.9 25.5 %all-to-all-done.1 = bf16[32,256,64]{1,2,0:T(8,128)(2,1)S(1)} async-done(((bf16[32,256,64]{1,2,0:T(8,128)(2,1)}), bf16[32,256,64]{1,2,0:T(8,128)(2,1)S(1)}, u32[]{:S(2)}, u32[]{:S(2)}) %all-to-all-start.1) | async-done | bytes 1048608 | tf_op jit(solution)/shard_map/all_to_all | solution.py:38
  75.4 0.3 multiply_reduce_fusion.1
  75.7 0.3 fusion.4
  76.3 0.9 gather_fusion.4
  77.6 0.7 reduce.5
  78.3 0.8 reshape.395
  79.1 3.9 %all-to-all-start.2 = ((bf16[32,2,1536]{2,1,0:T(2,128)(2,1)}), bf16[32,2,1536]{2,1,0:T(2,128)(2,1)S(1)}, u32[]{:S(2)}, u32[]{:S(2)}) async-start(bf16[32,2,1536]{2,1,0:T(2,128)(2,1)} %reshape.395), calls=%async_computation.2 | async-start | bytes 393216 | tf_op jit(solution)/shard_map/all_to_all | solution.py:127
  83.0 1.6 convert_bitcast_fusion
  84.6 2.3 %reshape.302 = f32[2,128,2048]{1,0,2:T(2,128)S(1)} reshape(f32[256,32,64]{0,2,1:T(8,128)} %convert_bitcast_fusion) | data formatting | bytes 4194304 | tf_op jit(solution)/shard_map/convert_element_type | solution.py:115
  86.9 5.9 %multiply_convert_fusion = bf16[2,128,2048]{1,0,2:T(2,128)(2,1)S(1)} fusion(f32[2,128,2048]{1,0,2:T(2,128)S(1)} %reshape.302, f32[2048]{0:T(1024)S(1)} %convert_element_type.144, f32[2,128]{1,0:T(2,128)S(1)} %get-tuple-element.16), kind=kLoop, calls=%fused_computation.21 | loop fusion | flops 1572864 | bytes 3154944 | tf_op jit(solution)/shard_map/convert_element_type | solution.py:20
  92.8 0.3 fusion.11
  95.3 0.5 convolution_convert_fusion.1
  95.8 0.5 copy.167
  96.3 35.3 %all_to_all.62 = bf16[32,256,64]{1,2,0:T(8,128)(2,1)S(1)} all-to-all(bf16[32,256,64]{1,2,0:T(8,128)(2,1)S(1)} %bitcast.124), channel_id=1, replica_groups=mesh['dp'=16,'tensor'=32] {'tensor'}, dimensions={0} | all-to-all | bytes 2097152 | tf_op jit(solution)/shard_map/all_to_all | solution.py:47
  131.8 1.1 broadcast_in_dim.160
  132.9 3.9 %all-to-all-start.4 = ((bf16[32,256,64]{1,2,0:T(8,128)(2,1)}), bf16[32,256,64]{1,2,0:T(8,128)(2,1)S(1)}, u32[]{:S(2)}, u32[]{:S(2)}) async-start(bf16[32,256,64]{1,2,0:T(8,128)(2,1)} %broadcast_in_dim.160), calls=%async_computation.4 | async-start | bytes 2097152 | tf_op jit(solution)/shard_map/all_to_all | solution.py:38
  136.8 27.9 %all-to-all-done.4 = bf16[32,256,64]{1,2,0:T(8,128)(2,1)S(1)} async-done(((bf16[32,256,64]{1,2,0:T(8,128)(2,1)}), bf16[32,256,64]{1,2,0:T(8,128)(2,1)S(1)}, u32[]{:S(2)}, u32[]{:S(2)}) %all-to-all-start.4) | async-done | bytes 1048608 | tf_op jit(solution)/shard_map/all_to_all | solution.py:38
  164.7 0.3 multiply_reduce_fusion
  165.0 0.3 fusion.2
  165.4 2.4 %fusion.48 = f32[256,256]{1,0:T(8,128)} fusion(bf16[256,2048]{0,1:T(8,128)(2,1)S(1)} %fusion.2, bf16[2048,256]{1,0:T(8,128)(2,1)} %param.31), kind=kOutput, calls=%fused_computation.129 | convolution fusion | flops 268435456 | bytes 2359296 | tf_op jit(solution)/shard_map/dot_general | solution.py:183
  167.8 2.6 %convolution_convert_fusion = bf16[256,2048]{1,0:T(8,128)(2,1)S(1)} fusion(bf16[256,2048]{1,0:T(8,128)(2,1)S(1)} %copy-done, bf16[256,2048]{0,1:T(8,128)(2,1)S(1)} %fusion.2, bf16[2048,256]{1,0:T(8,128)(2,1)} %param.32, f32[256,256]{1,0:T(8,128)} %fusion.48), kind=kOutput, calls=%fused_computation.10 | convolution fusion | flops 537788416 | bytes 4456448 | tf_op jit(solution)/shard_map/dot_general | solution.py:186
  170.3 1.3 copy.171
  171.6 3.9 %all-to-all-start.5 = ((bf16[32,256,64]{1,2,0:T(8,128)(2,1)}), bf16[32,256,64]{1,2,0:T(8,128)(2,1)S(1)}, u32[]{:S(2)}, u32[]{:S(2)}) async-start(bf16[32,256,64]{1,2,0:T(8,128)(2,1)} %bitcast.23), calls=%async_computation.5 | async-start | bytes 2097152 | tf_op jit(solution)/shard_map/all_to_all | solution.py:47
  175.6 27.8 %all-to-all-done.5 = bf16[32,256,64]{1,2,0:T(8,128)(2,1)S(1)} async-done(((bf16[32,256,64]{1,2,0:T(8,128)(2,1)}), bf16[32,256,64]{1,2,0:T(8,128)(2,1)S(1)}, u32[]{:S(2)}, u32[]{:S(2)}) %all-to-all-start.5) | async-done | bytes 1048608 | tf_op jit(solution)/shard_map/all_to_all | solution.py:47
  203.7 0.7 reshape.397
  204.4 4.3 %all-to-all-start.6 = ((bf16[16,2,512]{2,1,0:T(2,128)(2,1)}), bf16[16,2,512]{2,1,0:T(2,128)(2,1)S(1)}, u32[]{:S(2)}, u32[]{:S(2)}) async-start(bf16[16,2,512]{2,1,0:T(2,128)(2,1)} %reshape.397), calls=%async_computation.6 | async-start | bytes 65536 | tf_op jit(solution)/shard_map/all_to_all | solution.py:194
  208.8 0.6 dynamic-slice_select_fusion
  209.4 10.6 %all-to-all-done.6 = bf16[16,2,512]{2,1,0:T(2,128)(2,1)S(1)} async-done(((bf16[16,2,512]{2,1,0:T(2,128)(2,1)}), bf16[16,2,512]{2,1,0:T(2,128)(2,1)S(1)}, u32[]{:S(2)}, u32[]{:S(2)}) %all-to-all-start.6) | async-done | bytes 32800 | tf_op jit(solution)/shard_map/all_to_all | solution.py:194
  220.2 1.5 scatter_fusion
  221.7 0.6 copy-done.5
  (102 shorter events, 4.8 us)
Async XLA Ops:
  0.6 167.1 %copy-start = (bf16[256,2048]{1,0:T(8,128)(2,1)S(1)}, bf16[256,2048]{1,0:T(8,128)(2,1)}, u32[]{:S(2)}) copy-start(bf16[256,2048]{1,0:T(8,128)(2,1)} %param.33) | copy-start | bytes 3145732
  0.6 22.4 %copy-start.1 = (s32[32]{0:T(128)S(1)}, s32[32]{0:T(128)}, u32[]{:S(2)}) copy-start(s32[32]{0:T(128)} %param.23) | copy-start | bytes 388
  0.7 23.0 %copy-start.2 = (s32[32,1]{0,1:T(1,128)S(1)}, s32[32,1]{0,1:T(1,128)}, u32[]{:S(2)}) copy-start(s32[32,1]{0,1:T(1,128)} %param.21) | copy-start | bytes 388
  0.7 23.7 %copy-start.3 = (s32[32]{0:T(128)S(1)}, s32[32]{0:T(128)}, u32[]{:S(2)}) copy-start(s32[32]{0:T(128)} %param.20) | copy-start | bytes 388
  0.7 24.3 %copy-start.10 = (bf16[2048]{0:T(1024)(128)(2,1)S(1)}, bf16[2048]{0:T(1024)(128)(2,1)}, u32[]{:S(2)}) copy-start(bf16[2048]{0:T(1024)(128)(2,1)} %param.25) | copy-start | bytes 12292
  0.7 24.3 %copy-start.4 = (s32[16]{0:T(128)S(1)}, s32[16]{0:T(128)}, u32[]{:S(2)}) copy-start(s32[16]{0:T(128)} %param.22) | copy-start | bytes 196
  6.8 29.7 %all-to-all-start = ((bf16[16,2,4608]{2,1,0:T(2,128)(2,1)}), bf16[16,2,4608]{2,1,0:T(2,128)(2,1)S(1)}, u32[]{:S(2)}, u32[]{:S(2)}) async-start(bf16[16,2,4608]{2,1,0:T(2,128)(2,1)} %reshape.393), calls=%async_computation | async-start | bytes 589824 | tf_op jit(solution)/shard_map/all_to_all | solution.py:90
  36.7 10.9 %copy-start.13 = (s32[32]{0:T(128)S(1)}, s32[32]{0:T(128)}, u32[]{:S(2)}) copy-start(s32[32]{0:T(128)} %constant.165) | copy-start | bytes 388
  36.7 10.9 %copy-start.12 = (s32[128]{0:T(128)S(1)}, s32[128]{0:T(128)}, u32[]{:S(2)}) copy-start(s32[128]{0:T(128)} %constant.166) | copy-start | bytes 1540
  38.2 37.2 %all-to-all-start.1 = ((bf16[32,256,64]{1,2,0:T(8,128)(2,1)}), bf16[32,256,64]{1,2,0:T(8,128)(2,1)S(1)}, u32[]{:S(2)}, u32[]{:S(2)}) async-start(bf16[32,256,64]{1,2,0:T(8,128)(2,1)} %broadcast_in_dim.147), calls=%async_computation.1 | async-start | bytes 2097152 | tf_op jit(solution)/shard_map/all_to_all | solution.py:38
  48.5 27.5 %copy-start.7 = (bf16[2048,16]{0,1:T(8,128)(2,1)S(1)}, bf16[2048,16]{0,1:T(8,128)(2,1)}, u32[]{:S(2)}) copy-start(bf16[2048,16]{0,1:T(8,128)(2,1)} %param.28) | copy-start | bytes 196612
  48.5 27.5 %copy-start.8 = (bf16[2048,16]{0,1:T(8,128)(2,1)S(1)}, bf16[2048,16]{0,1:T(8,128)(2,1)}, u32[]{:S(2)}) copy-start(bf16[2048,16]{0,1:T(8,128)(2,1)} %param.27) | copy-start | bytes 196612
  79.1 14.0 %all-to-all-start.2 = ((bf16[32,2,1536]{2,1,0:T(2,128)(2,1)}), bf16[32,2,1536]{2,1,0:T(2,128)(2,1)S(1)}, u32[]{:S(2)}, u32[]{:S(2)}) async-start(bf16[32,2,1536]{2,1,0:T(2,128)(2,1)} %reshape.395), calls=%async_computation.2 | async-start | bytes 393216 | tf_op jit(solution)/shard_map/all_to_all | solution.py:127
  86.9 5.9 %copy-start.14 = (bf16[2048,64]{0,1:T(8,128)(2,1)S(1)}, bf16[2048,64]{0,1:T(8,128)(2,1)}, u32[]{:S(2)}) copy-start(bf16[2048,64]{0,1:T(8,128)(2,1)} %param.26) | copy-start | bytes 786436
  93.3 1.5 copy-start.9
  94.0 1.4 copy-start.6
  131.7 5.1 %copy-start.11 = (bf16[2048]{0:T(1024)(128)(2,1)S(1)}, bf16[2048]{0:T(1024)(128)(2,1)}, u32[]{:S(2)}) copy-start(bf16[2048]{0:T(1024)(128)(2,1)} %param.30) | copy-start | bytes 12292
  132.9 31.8 %all-to-all-start.4 = ((bf16[32,256,64]{1,2,0:T(8,128)(2,1)}), bf16[32,256,64]{1,2,0:T(8,128)(2,1)S(1)}, u32[]{:S(2)}, u32[]{:S(2)}) async-start(bf16[32,256,64]{1,2,0:T(8,128)(2,1)} %broadcast_in_dim.160), calls=%async_computation.4 | async-start | bytes 2097152 | tf_op jit(solution)/shard_map/all_to_all | solution.py:38
  171.6 31.8 %all-to-all-start.5 = ((bf16[32,256,64]{1,2,0:T(8,128)(2,1)}), bf16[32,256,64]{1,2,0:T(8,128)(2,1)S(1)}, u32[]{:S(2)}, u32[]{:S(2)}) async-start(bf16[32,256,64]{1,2,0:T(8,128)(2,1)} %bitcast.23), calls=%async_computation.5 | async-start | bytes 2097152 | tf_op jit(solution)/shard_map/all_to_all | solution.py:47
  204.4 15.6 %all-to-all-start.6 = ((bf16[16,2,512]{2,1,0:T(2,128)(2,1)}), bf16[16,2,512]{2,1,0:T(2,128)(2,1)S(1)}, u32[]{:S(2)}, u32[]{:S(2)}) async-start(bf16[16,2,512]{2,1,0:T(2,128)(2,1)} %reshape.397), calls=%async_computation.6 | async-start | bytes 65536 | tf_op jit(solution)/shard_map/all_to_all | solution.py:194
  221.7 0.6 copy-start.5

commit v6 on v5

--- a/solution.py
+++ b/solution.py
@@ -183,15 +183,26 @@
     gate = jnp.dot(normed_two, w_gate, preferred_element_type=jnp.float32)
     upper = jnp.dot(normed_two, w_up, preferred_element_type=jnp.float32)
     hidden = (jax.nn.silu(gate) * upper).astype(jnp.bfloat16)
-    down_terms = jnp.dot(hidden, w_down, preferred_element_type=jnp.float32)
-    down_share = scatter_sum(down_terms, "tensor", tp_count)
-    result = middle.astype(jnp.float32) + down_share
-    result = (
-        jnp.where(valid[:, None], result, 0.0)
+    pos_blocks = L_MAX // pos_here
+    row_perm = (
+        np.arange(row_count).reshape(local_reqs, pos_blocks, pos_here).transpose(1, 0, 2).reshape(-1)
+    )
+    hidden_perm = jnp.take(hidden, row_perm, axis=0)
+    down_terms = jnp.dot(hidden_perm, w_down, preferred_element_type=jnp.float32)
+    down_terms = down_terms.reshape(row_count, tp_count, width_here)
+    own = (jnp.arange(tp_count) == tp_index)[None, :, None]
+    middle_perm = jnp.take(middle, row_perm, axis=0).astype(jnp.float32)[:, None, :]
+    valid_perm = jnp.take(valid, row_perm)[:, None, None]
+    sent = jnp.where(valid_perm, down_terms + jnp.where(own, middle_perm, 0.0), 0.0)
+    sent = sent.astype(jnp.bfloat16).reshape(pos_blocks, local_reqs * pos_here, tp_count, width_here)
+    sent = sent.transpose(0, 2, 1, 3).reshape(pos_blocks * tp_count, local_reqs * pos_here, width_here)
+    got = lax.all_to_all(sent, ("dp", "tensor"), 0, 0, tiled=True)
+    got = got.reshape(dp_count, tp_count, local_reqs * pos_here, width_here)
+    returned = (
+        jnp.sum(got.astype(jnp.float32), axis=1)
         .astype(jnp.bfloat16)
-        .reshape(local_reqs, L_MAX, width_here)
-    )
-    returned = lax.all_to_all(result, "dp", split_axis=1, concat_axis=0, tiled=True)
+        .reshape(total_reqs, pos_here, width_here)
+    )
     hidden_out = jnp.zeros_like(returned).at[request_order].set(returned)
     return (hidden_out, keys_out, values_out)
 

time: 223 us -> 229 us (1.027)
  waiting for transfers between devices: 103 us -> 91 us
  local copies, waits for them, and re-layouts: 20.6 us -> 31.4 us
  other arithmetic: 14.3 us -> 21.6 us
  matrix products: 6.66 us -> 3.08 us
  starting transfers between devices: 41.4 us -> 44.4 us
    all_to_all x2 -> x1, waiting for transfers between devices: 38.4 us -> 29.8 us  [shards(): got = lax.all_to_all(sent, ('dp', 'tensor'), 0, 0, tiled=True)]
    convert_element_type x1 -> x2, other arithmetic: 0.01 us -> 6.33 us  [the longest x1 6.31 us: shards(): sent.astype(jnp.bfloat16)]
    unnamed x45 -> x53, local copies, waits for them, and re-layouts: 4.78 us -> 9.87 us
    gather x0 -> x3, local copies, waits for them, and re-layouts: none -> 3.89 us  [the longest x1 1.88 us: shards(): valid_perm = jnp.take(valid, row_perm)[:, None, None]]
    reshape x0 -> x1, local copies, waits for them, and re-layouts: none -> 3.01 us  [shards(): down_terms = down_terms.reshape(row_count, tp_count, width_here)]
    all_to_all x2 -> x1, starting transfers between devices: 8.16 us -> 11.1 us  [shards(): got = lax.all_to_all(sent, ('dp', 'tensor'), 0, 0, tiled=True)]
    all_to_all x2, waiting for transfers between devices: 53.3 us -> 50.4 us  [gather_rows(): got = lax.all_to_all(sent, axis_name, 0, 0, tiled=True)]
  transfers between devices with their start and end apart: 6 -> 5, of which waited for: 5 -> 4; matrix products, arithmetic and copies ran while one was open for 7% -> 8% of each run, Pallas kernels for 0% -> 0%
where the time goes in v6:
time: 229 us; the launch traced here: 228 us
  waiting for transfers between devices  91 us (40%)
  starting transfers between devices  44.4 us (19%)
  blocking collectives  35.3 us (15%)
  local copies, waits for them, and re-layouts  31.4 us (14%)
  other arithmetic  21.6 us (9%)
  matrix products  3.08 us (1%)
    all_to_all x2, waiting for transfers between devices, gather_rows(): got = lax.all_to_all(sent, axis_name, 0, 0, tiled=True)  50.4 us
    all_to_all x1, blocking collectives, scatter_sum(): got = lax.all_to_all(sent, axis_name, 0, 0, tiled=True)  35.3 us
    all_to_all x1, waiting for transfers between devices, shards(): got = lax.all_to_all(sent, ('dp', 'tensor'), 0, 0, tiled=True)  29.8 us
    all_to_all x1, starting transfers between devices, shards(): lax.all_to_all(jnp.concatenate([state_part, prefix_part], axis=1), 'dp',...  16.2 us
    all_to_all x2, starting transfers between devices, gather_rows(): got = lax.all_to_all(sent, axis_name, 0, 0, tiled=True)  13.2 us
    all_to_all x1, starting transfers between devices, shards(): got = lax.all_to_all(sent, ('dp', 'tensor'), 0, 0, tiled=True)  11.1 us
    all_to_all x1, waiting for transfers between devices, shards(): lax.all_to_all(jnp.concatenate([state_part, prefix_part], axis=1), 'dp',...  10.8 us
    unnamed x53, local copies, waits for them, and re-layouts  9.87 us
  transfers between devices with their start and end apart: 5, of which 4 were waited for; matrix products, arithmetic and copies ran while one was open for 8% of the time, Pallas kernels for 0%

profile of v6, /device:TPU:1, one launch (start us, length us, event | category | flops | bytes accessed | tf_op | source)
XLA Modules:
  0.0 228.3 jit_solution(7624920725523666010)
XLA Ops:
  0.7 0.7 compare_select_fusion.4
  1.4 0.7 compare_and_fusion.2
  2.1 1.4 gather_fusion.1
  3.8 0.7 copy.146
  4.5 0.5 broadcast.355
  5.0 0.8 reduce.5
  5.9 0.9 reshape.445
  6.8 16.2 %all-to-all-start = ((bf16[16,2,4608]{2,1,0:T(2,128)(2,1)}), bf16[16,2,4608]{2,1,0:T(2,128)(2,1)S(1)}, u32[]{:S(2)}, u32[]{:S(2)}) async-start(bf16[16,2,4608]{2,1,0:T(2,128)(2,1)} %reshape.445), calls=%async_computation | async-start | bytes 589824 | tf_op jit(solution)/shard_map/all_to_all | solution.py:90
  23.0 0.6 gather_fusion.8
  23.7 0.6 gather_fusion.9
  24.4 0.6 gather_fusion.10
  25.0 0.6 gather_fusion.2
  25.7 10.8 %all-to-all-done = bf16[16,2,4608]{2,1,0:T(2,128)(2,1)S(1)} async-done(((bf16[16,2,4608]{2,1,0:T(2,128)(2,1)}), bf16[16,2,4608]{2,1,0:T(2,128)(2,1)S(1)}, u32[]{:S(2)}, u32[]{:S(2)}) %all-to-all-start) | async-done | bytes 294944 | tf_op jit(solution)/shard_map/all_to_all | solution.py:90
  37.1 1.1 broadcast_in_dim.201
  38.2 9.3 %all-to-all-start.1 = ((bf16[32,256,64]{1,2,0:T(8,128)(2,1)}), bf16[32,256,64]{1,2,0:T(8,128)(2,1)S(1)}, u32[]{:S(2)}, u32[]{:S(2)}) async-start(bf16[32,256,64]{1,2,0:T(8,128)(2,1)} %broadcast_in_dim.201), calls=%async_computation.1 | async-start | bytes 2097152 | tf_op jit(solution)/shard_map/all_to_all | solution.py:38
  47.9 0.6 broadcast_and_fusion
  48.6 0.6 gather_fusion.3
  49.3 0.6 gather_fusion.4
  49.9 25.5 %all-to-all-done.1 = bf16[32,256,64]{1,2,0:T(8,128)(2,1)S(1)} async-done(((bf16[32,256,64]{1,2,0:T(8,128)(2,1)}), bf16[32,256,64]{1,2,0:T(8,128)(2,1)S(1)}, u32[]{:S(2)}, u32[]{:S(2)}) %all-to-all-start.1) | async-done | bytes 1048608 | tf_op jit(solution)/shard_map/all_to_all | solution.py:38
  76.3 0.9 gather_fusion.5
  77.6 0.7 reduce.6
  78.3 0.8 reshape.447
  79.1 3.9 %all-to-all-start.2 = ((bf16[32,2,1536]{2,1,0:T(2,128)(2,1)}), bf16[32,2,1536]{2,1,0:T(2,128)(2,1)S(1)}, u32[]{:S(2)}, u32[]{:S(2)}) async-start(bf16[32,2,1536]{2,1,0:T(2,128)(2,1)} %reshape.447), calls=%async_computation.2 | async-start | bytes 393216 | tf_op jit(solution)/shard_map/all_to_all | solution.py:127
  83.0 1.6 convert_bitcast_fusion
  84.6 2.3 %reshape.329 = f32[2,128,2048]{1,0,2:T(2,128)S(1)} reshape(f32[256,32,64]{0,2,1:T(8,128)} %convert_bitcast_fusion) | data formatting | bytes 4194304 | tf_op jit(solution)/shard_map/convert_element_type | solution.py:115
  86.9 5.9 %multiply_convert_fusion = bf16[2,128,2048]{1,0,2:T(2,128)(2,1)S(1)} fusion(f32[2,128,2048]{1,0,2:T(2,128)S(1)} %reshape.329, f32[2048]{0:T(1024)S(1)} %convert_element_type.133, f32[2,128]{1,0:T(2,128)S(1)} %get-tuple-element.16), kind=kLoop, calls=%fused_computation.26 | loop fusion | flops 1572864 | bytes 3154944 | tf_op jit(solution)/shard_map/convert_element_type | solution.py:20
  95.4 0.4 convolution_convert_fusion
  95.8 0.5 copy.105
  96.3 35.3 %all_to_all.44 = bf16[32,256,64]{1,2,0:T(8,128)(2,1)S(1)} all-to-all(bf16[32,256,64]{1,2,0:T(8,128)(2,1)S(1)} %bitcast.104), channel_id=1, replica_groups=mesh['dp'=16,'tensor'=32] {'tensor'}, dimensions={0} | all-to-all | bytes 2097152 | tf_op jit(solution)/shard_map/all_to_all | solution.py:47
  132.1 1.1 broadcast_in_dim.214
  133.2 3.9 %all-to-all-start.4 = ((bf16[32,256,64]{1,2,0:T(8,128)(2,1)}), bf16[32,256,64]{1,2,0:T(8,128)(2,1)S(1)}, u32[]{:S(2)}, u32[]{:S(2)}) async-start(bf16[32,256,64]{1,2,0:T(8,128)(2,1)} %broadcast_in_dim.214), calls=%async_computation.4 | async-start | bytes 2097152 | tf_op jit(solution)/shard_map/all_to_all | solution.py:38
  137.1 1.9 gather_fusion
  139.1 0.9 gather_fusion.7
  140.0 25.0 %all-to-all-done.4 = bf16[32,256,64]{1,2,0:T(8,128)(2,1)S(1)} async-done(((bf16[32,256,64]{1,2,0:T(8,128)(2,1)}), bf16[32,256,64]{1,2,0:T(8,128)(2,1)S(1)}, u32[]{:S(2)}, u32[]{:S(2)}) %all-to-all-start.4) | async-done | bytes 1048608 | tf_op jit(solution)/shard_map/all_to_all | solution.py:38
  165.6 0.5 fusion.41
  166.5 0.5 fusion.10
  167.0 1.2 gather_fusion.6
  168.1 0.4 fusion.42
  168.6 3.0 %reshape.325 = f32[16,16,32,64]{3,2,1,0:T(8,128)} reshape(f32[256,2048]{1,0:T(8,128)S(1)} %fusion.42) | data formatting | bytes 4194304 | tf_op jit(solution)/shard_map/reshape | solution.py:192
  171.6 6.3 %fusion.2 = bf16[16,16,32,64]{3,1,2,0:T(8,128)(2,1)S(1)} fusion(f32[16,16,32,64]{3,2,1,0:T(8,128)} %reshape.325, f32[16,16,64]{2,1,0:T(8,128)S(1)} %convert.25, pred[32]{0:T(512)(128)(4,1)S(1)} %iota_compare_fusion.2, pred[16,16]{1,0:T(8,128)(4,1)S(1)} %broadcast_in_dim.194), kind=kLoop, calls=%fused_computation.15 | loop fusion | flops 2097152 | bytes 3211552 | tf_op jit(solution)/shard_map/convert_element_type | solution.py:197
  177.9 1.8 reshape.449
  179.8 11.1 %all-to-all-start.5 = ((bf16[512,2,512]{2,1,0:T(2,128)(2,1)}), bf16[512,2,512]{2,1,0:T(2,128)(2,1)}, u32[]{:S(2)}, u32[]{:S(2)}) async-start(bf16[512,2,512]{2,1,0:T(2,128)(2,1)} %reshape.449), calls=%async_computation.5 | async-start | bytes 2097152 | tf_op jit(solution)/shard_map/all_to_all | solution.py:199
  190.9 1.3 dynamic-slice_select_fusion
  192.2 29.8 %all-to-all-done.5 = bf16[512,2,512]{2,1,0:T(2,128)(2,1)} async-done(((bf16[512,2,512]{2,1,0:T(2,128)(2,1)}), bf16[512,2,512]{2,1,0:T(2,128)(2,1)}, u32[]{:S(2)}, u32[]{:S(2)}) %all-to-all-start.5) | async-done | bytes 1048608 | tf_op jit(solution)/shard_map/all_to_all | solution.py:199
  222.0 3.7 %reshape.450 = bf16[512,16,64]{2,1,0:T(8,128)(2,1)S(1)} reshape(bf16[512,2,512]{2,1,0:T(2,128)(2,1)} %all-to-all-done.5) | data formatting | bytes 2097152
  225.7 0.4 bitcast_reduce_fusion
  226.2 1.5 scatter_fusion
  227.7 0.6 copy-done.6
  (113 shorter events, 6.6 us)
Async XLA Ops:
  0.6 167.5 %copy-start = (bf16[256,2048]{1,0:T(8,128)(2,1)S(1)}, bf16[256,2048]{1,0:T(8,128)(2,1)}, u32[]{:S(2)}) copy-start(bf16[256,2048]{1,0:T(8,128)(2,1)} %param.34) | copy-start | bytes 3145732
  0.6 22.4 %copy-start.1 = (s32[32]{0:T(128)S(1)}, s32[32]{0:T(128)}, u32[]{:S(2)}) copy-start(s32[32]{0:T(128)} %param.24) | copy-start | bytes 388
  0.7 23.0 %copy-start.2 = (s32[32]{0:T(128)S(1)}, s32[32]{0:T(128)}, u32[]{:S(2)}) copy-start(s32[32]{0:T(128)} %param.21) | copy-start | bytes 388
  0.7 23.7 %copy-start.3 = (s32[32,1]{0,1:T(1,128)S(1)}, s32[32,1]{0,1:T(1,128)}, u32[]{:S(2)}) copy-start(s32[32,1]{0,1:T(1,128)} %param.22) | copy-start | bytes 388
  0.7 24.3 %copy-start.12 = (bf16[2048]{0:T(1024)(128)(2,1)S(1)}, bf16[2048]{0:T(1024)(128)(2,1)}, u32[]{:S(2)}) copy-start(bf16[2048]{0:T(1024)(128)(2,1)} %param.26) | copy-start | bytes 12292
  0.7 24.3 %copy-start.4 = (s32[16]{0:T(128)S(1)}, s32[16]{0:T(128)}, u32[]{:S(2)}) copy-start(s32[16]{0:T(128)} %param.23) | copy-start | bytes 196
  6.8 29.7 %all-to-all-start = ((bf16[16,2,4608]{2,1,0:T(2,128)(2,1)}), bf16[16,2,4608]{2,1,0:T(2,128)(2,1)S(1)}, u32[]{:S(2)}, u32[]{:S(2)}) async-start(bf16[16,2,4608]{2,1,0:T(2,128)(2,1)} %reshape.445), calls=%async_computation | async-start | bytes 589824 | tf_op jit(solution)/shard_map/all_to_all | solution.py:90
  36.7 10.9 %copy-start.16 = (s32[32]{0:T(128)S(1)}, s32[32]{0:T(128)}, u32[]{:S(2)}) copy-start(s32[32]{0:T(128)} %constant.217) | copy-start | bytes 388
  36.7 10.9 %copy-start.15 = (s32[128]{0:T(128)S(1)}, s32[128]{0:T(128)}, u32[]{:S(2)}) copy-start(s32[128]{0:T(128)} %constant.218) | copy-start | bytes 1540
  38.2 37.2 %all-to-all-start.1 = ((bf16[32,256,64]{1,2,0:T(8,128)(2,1)}), bf16[32,256,64]{1,2,0:T(8,128)(2,1)S(1)}, u32[]{:S(2)}, u32[]{:S(2)}) async-start(bf16[32,256,64]{1,2,0:T(8,128)(2,1)} %broadcast_in_dim.201), calls=%async_computation.1 | async-start | bytes 2097152 | tf_op jit(solution)/shard_map/all_to_all | solution.py:38
  48.5 27.5 %copy-start.8 = (bf16[2048,16]{0,1:T(8,128)(2,1)S(1)}, bf16[2048,16]{0,1:T(8,128)(2,1)}, u32[]{:S(2)}) copy-start(bf16[2048,16]{0,1:T(8,128)(2,1)} %param.29) | copy-start | bytes 196612
  48.5 27.5 %copy-start.9 = (bf16[2048,16]{0,1:T(8,128)(2,1)S(1)}, bf16[2048,16]{0,1:T(8,128)(2,1)}, u32[]{:S(2)}) copy-start(bf16[2048,16]{0,1:T(8,128)(2,1)} %param.28) | copy-start | bytes 196612
  79.1 14.0 %all-to-all-start.2 = ((bf16[32,2,1536]{2,1,0:T(2,128)(2,1)}), bf16[32,2,1536]{2,1,0:T(2,128)(2,1)S(1)}, u32[]{:S(2)}, u32[]{:S(2)}) async-start(bf16[32,2,1536]{2,1,0:T(2,128)(2,1)} %reshape.447), calls=%async_computation.2 | async-start | bytes 393216 | tf_op jit(solution)/shard_map/all_to_all | solution.py:127
  86.9 5.9 %copy-start.18 = (bf16[2048,64]{0,1:T(8,128)(2,1)S(1)}, bf16[2048,64]{0,1:T(8,128)(2,1)}, u32[]{:S(2)}) copy-start(bf16[2048,64]{0,1:T(8,128)(2,1)} %param.27) | copy-start | bytes 786436
  93.3 1.6 copy-start.11
  94.0 1.4 copy-start.7
  94.1 1.0 copy-start.10
  131.8 5.2 %copy-start.13 = (bf16[2048]{0:T(1024)(128)(2,1)S(1)}, bf16[2048]{0:T(1024)(128)(2,1)}, u32[]{:S(2)}) copy-start(bf16[2048]{0:T(1024)(128)(2,1)} %param.31) | copy-start | bytes 12292
  131.8 5.3 %copy-start.14 = (s32[256]{0:T(256)S(1)}, s32[256]{0:T(256)}, u32[]{:S(2)}) copy-start(s32[256]{0:T(256)} %constant.216) | copy-start | bytes 3076
  133.2 31.8 %all-to-all-start.4 = ((bf16[32,256,64]{1,2,0:T(8,128)(2,1)}), bf16[32,256,64]{1,2,0:T(8,128)(2,1)S(1)}, u32[]{:S(2)}, u32[]{:S(2)}) async-start(bf16[32,256,64]{1,2,0:T(8,128)(2,1)} %broadcast_in_dim.214), calls=%async_computation.4 | async-start | bytes 2097152 | tf_op jit(solution)/shard_map/all_to_all | solution.py:38
  139.0 26.6 %copy-start.5 = (bf16[2048,256]{1,0:T(8,128)(2,1)S(1)}, bf16[2048,256]{1,0:T(8,128)(2,1)}, u32[]{:S(2)}) copy-start(bf16[2048,256]{1,0:T(8,128)(2,1)} %param.32) | copy-start | bytes 3145732
  165.3 1.2 copy-start.17
  179.8 42.3 %all-to-all-start.5 = ((bf16[512,2,512]{2,1,0:T(2,128)(2,1)}), bf16[512,2,512]{2,1,0:T(2,128)(2,1)}, u32[]{:S(2)}, u32[]{:S(2)}) async-start(bf16[512,2,512]{2,1,0:T(2,128)(2,1)} %reshape.449), calls=%async_computation.5 | async-start | bytes 2097152 | tf_op jit(solution)/shard_map/all_to_all | solution.py:199
  227.6 0.6 copy-start.6

commit v7 on v5

--- a/solution.py
+++ b/solution.py
@@ -74,7 +74,7 @@
     row_count = local_reqs * L_MAX
     heads_here = w_query.shape[1] // HD
     group_size = H // KVH
-    assert heads_here == 1
+    assert heads_here == 1 and local_reqs == 2
     kv_cols = w_key.shape[1]
     d_here = kv_cols // KVH
     score_scale = HD ** (-0.5)
@@ -178,13 +178,29 @@
     attn_terms = jnp.dot(attention, w_out, preferred_element_type=jnp.float32)
     attn_share = scatter_sum(attn_terms, "tensor", tp_count)
     middle = (state_shard.astype(jnp.float32) + attn_share).astype(jnp.bfloat16)
-    middle_rows = gather_rows(middle, "tensor", tp_count)
+    core = tp_index % 2
+    pair = [(t, t ^ 1) for t in range(tp_count)]
+    w_gu_sib, w_down_sib = lax.ppermute(
+        (jnp.concatenate([w_gate, w_up], axis=1), w_down), "tensor", pair
+    )
+    units = w_gate.shape[1]
+    w_gate_chip = jnp.concatenate([w_gate, w_gu_sib[:, :units]], axis=1)
+    w_up_chip = jnp.concatenate([w_up, w_gu_sib[:, units:]], axis=1)
+    w_down_chip = jnp.concatenate([w_down, w_down_sib], axis=0)
+    middle_req = middle.reshape(local_reqs, L_MAX, width_here)
+    sent = jnp.take(middle_req, np.arange(tp_count) % 2, axis=0)
+    got = lax.all_to_all(sent, "tensor", 0, 0, tiled=True)
+    middle_rows = got.transpose(1, 0, 2).reshape(L_MAX, tp_count * width_here)
     normed_two = rms_scale(middle_rows.astype(jnp.float32), norm_mlp)
-    gate = jnp.dot(normed_two, w_gate, preferred_element_type=jnp.float32)
-    upper = jnp.dot(normed_two, w_up, preferred_element_type=jnp.float32)
+    gate = jnp.dot(normed_two, w_gate_chip, preferred_element_type=jnp.float32)
+    upper = jnp.dot(normed_two, w_up_chip, preferred_element_type=jnp.float32)
     hidden = (jax.nn.silu(gate) * upper).astype(jnp.bfloat16)
-    down_terms = jnp.dot(hidden, w_down, preferred_element_type=jnp.float32)
-    down_share = scatter_sum(down_terms, "tensor", tp_count)
+    down_terms = jnp.dot(hidden, w_down_chip, preferred_element_type=jnp.float32)
+    sent = down_terms.astype(jnp.bfloat16).reshape(L_MAX, tp_count, width_here).transpose(1, 0, 2)
+    got = lax.all_to_all(sent, "tensor", 0, 0, tiled=True)
+    down_share = jnp.sum(
+        got.reshape(tp_count // 2, local_reqs, L_MAX, width_here).astype(jnp.float32), axis=0
+    ).reshape(row_count, width_here)
     result = middle.astype(jnp.float32) + down_share
     result = (
         jnp.where(valid[:, None], result, 0.0)

time: 223 us -> 202 us (0.906)
  blocking collectives: 35.3 us -> 0 us
  starting transfers between devices: 41.4 us -> 53.5 us
  waiting for transfers between devices: 103 us -> 99 us
  local copies, waits for them, and re-layouts: 20.6 us -> 23.9 us
    all_to_all x1 -> x0, blocking collectives: 35.3 us -> none  [scatter_sum(): got = lax.all_to_all(sent, axis_name, 0, 0, tiled=True)]
    all_to_all x0 -> x2, waiting for transfers between devices: none -> 29.7 us  [shards(): got = lax.all_to_all(sent, 'tensor', 0, 0, tiled=True)]
    all_to_all x2 -> x1, waiting for transfers between devices: 53.3 us -> 26.1 us  [gather_rows(): got = lax.all_to_all(sent, axis_name, 0, 0, tiled=True)]
    all_to_all x0 -> x2, starting transfers between devices: none -> 7.54 us  [shards(): got = lax.all_to_all(sent, 'tensor', 0, 0, tiled=True)]
    all_to_all x1, waiting for transfers between devices: 27.8 us -> 22.5 us  [scatter_sum(): got = lax.all_to_all(sent, axis_name, 0, 0, tiled=True)]
    ppermute x0 -> x2, starting transfers between devices: none -> 4.48 us  [shards(): lax.ppermute((jnp.concatenate([w_gate, w_up], axis=1), w_down), 'tensor',...]
    all_to_all x1, starting transfers between devices: 3.85 us -> 7.82 us  [scatter_sum(): got = lax.all_to_all(sent, axis_name, 0, 0, tiled=True)]
    all_to_all x2 -> x1, starting transfers between devices: 13.2 us -> 9.35 us  [gather_rows(): got = lax.all_to_all(sent, axis_name, 0, 0, tiled=True)]
  transfers between devices with their start and end apart: 6 -> 9, of which waited for: 5 -> 6; matrix products, arithmetic and copies ran while one was open for 7% -> 13% of each run, Pallas kernels for 0% -> 0%
where the time goes in v7:
time: 202 us; the launch traced here: 201 us
  waiting for transfers between devices  99 us (49%)
  starting transfers between devices  53.5 us (26%)
  local copies, waits for them, and re-layouts  23.9 us (12%)
  other arithmetic  16.5 us (8%)
  matrix products  7.07 us (4%)
    all_to_all x2, waiting for transfers between devices, shards(): got = lax.all_to_all(sent, 'tensor', 0, 0, tiled=True)  29.7 us
    all_to_all x1, waiting for transfers between devices, gather_rows(): got = lax.all_to_all(sent, axis_name, 0, 0, tiled=True)  26.1 us
    all_to_all x1, waiting for transfers between devices, scatter_sum(): got = lax.all_to_all(sent, axis_name, 0, 0, tiled=True)  22.5 us
    all_to_all x1, starting transfers between devices, shards(): lax.all_to_all(jnp.concatenate([state_part, prefix_part], axis=1), 'dp',...  16.2 us
    all_to_all x1, waiting for transfers between devices, shards(): lax.all_to_all(jnp.concatenate([state_part, prefix_part], axis=1), 'dp',...  10.8 us
    all_to_all x1, waiting for transfers between devices, shards(): lax.all_to_all(result, 'dp', split_axis=1, concat_axis=0, tiled=True)  9.96 us
    all_to_all x1, starting transfers between devices, gather_rows(): got = lax.all_to_all(sent, axis_name, 0, 0, tiled=True)  9.35 us
    all_to_all x1, starting transfers between devices, scatter_sum(): got = lax.all_to_all(sent, axis_name, 0, 0, tiled=True)  7.82 us
  transfers between devices with their start and end apart: 9, of which 6 were waited for; matrix products, arithmetic and copies ran while one was open for 13% of the time, Pallas kernels for 0%

profile of v7, /device:TPU:1, one launch (start us, length us, event | category | flops | bytes accessed | tf_op | source)
XLA Modules:
  0.0 201.5 jit_solution(12615836789959667220)
XLA Ops:
  0.7 0.7 compare_select_fusion.4
  1.4 0.7 compare_and_fusion.2
  2.1 1.4 gather_fusion
  3.8 0.7 copy.179
  4.5 0.5 broadcast.317
  5.0 0.8 reduce.4
  5.9 0.9 reshape.404
  6.8 16.2 %all-to-all-start = ((bf16[16,2,4608]{2,1,0:T(2,128)(2,1)}), bf16[16,2,4608]{2,1,0:T(2,128)(2,1)S(1)}, u32[]{:S(2)}, u32[]{:S(2)}) async-start(bf16[16,2,4608]{2,1,0:T(2,128)(2,1)} %reshape.404), calls=%async_computation | async-start | bytes 589824 | tf_op jit(solution)/shard_map/all_to_all | solution.py:90
  23.0 0.6 gather_fusion.6
  23.7 0.6 gather_fusion.7
  24.3 0.6 gather_fusion.8
  25.0 0.6 gather_fusion.1
  25.7 10.8 %all-to-all-done = bf16[16,2,4608]{2,1,0:T(2,128)(2,1)S(1)} async-done(((bf16[16,2,4608]{2,1,0:T(2,128)(2,1)}), bf16[16,2,4608]{2,1,0:T(2,128)(2,1)S(1)}, u32[]{:S(2)}, u32[]{:S(2)}) %all-to-all-start) | async-done | bytes 294944 | tf_op jit(solution)/shard_map/all_to_all | solution.py:90
  37.1 1.1 broadcast_in_dim.153
  38.2 9.3 %all-to-all-start.1 = ((bf16[32,256,64]{1,2,0:T(8,128)(2,1)}), bf16[32,256,64]{1,2,0:T(8,128)(2,1)S(1)}, u32[]{:S(2)}, u32[]{:S(2)}) async-start(bf16[32,256,64]{1,2,0:T(8,128)(2,1)} %broadcast_in_dim.153), calls=%async_computation.1 | async-start | bytes 2097152 | tf_op jit(solution)/shard_map/all_to_all | solution.py:38
  48.0 0.6 gather_fusion.2
  48.7 0.6 gather_fusion.3
  49.3 26.1 %all-to-all-done.1 = bf16[32,256,64]{1,2,0:T(8,128)(2,1)S(1)} async-done(((bf16[32,256,64]{1,2,0:T(8,128)(2,1)}), bf16[32,256,64]{1,2,0:T(8,128)(2,1)S(1)}, u32[]{:S(2)}, u32[]{:S(2)}) %all-to-all-start.1) | async-done | bytes 1048608 | tf_op jit(solution)/shard_map/all_to_all | solution.py:38
  76.3 0.9 gather_fusion.4
  77.6 0.7 reduce.5
  78.3 0.8 reshape.406
  79.1 3.9 %all-to-all-start.2 = ((bf16[32,2,1536]{2,1,0:T(2,128)(2,1)}), bf16[32,2,1536]{2,1,0:T(2,128)(2,1)S(1)}, u32[]{:S(2)}, u32[]{:S(2)}) async-start(bf16[32,2,1536]{2,1,0:T(2,128)(2,1)} %reshape.406), calls=%async_computation.2 | async-start | bytes 393216 | tf_op jit(solution)/shard_map/all_to_all | solution.py:127
  83.0 1.6 convert_bitcast_fusion
  84.6 2.3 %reshape.304 = f32[2,128,2048]{1,0,2:T(2,128)S(1)} reshape(f32[256,32,64]{0,2,1:T(8,128)} %convert_bitcast_fusion) | data formatting | bytes 4194304 | tf_op jit(solution)/shard_map/convert_element_type | solution.py:115
  86.9 5.9 %multiply_convert_fusion = bf16[2,128,2048]{1,0,2:T(2,128)(2,1)S(1)} fusion(f32[2,128,2048]{1,0,2:T(2,128)S(1)} %reshape.304, f32[2048]{0:T(1024)S(1)} %convert_element_type.137, f32[2,128]{1,0:T(2,128)S(1)} %get-tuple-element.18), kind=kLoop, calls=%fused_computation.28 | loop fusion | flops 1572864 | bytes 3154944 | tf_op jit(solution)/shard_map/convert_element_type | solution.py:20
  95.8 1.3 copy.135
  97.1 7.8 %all-to-all-start.3 = ((bf16[32,256,64]{1,2,0:T(8,128)(2,1)}), bf16[32,256,64]{1,2,0:T(8,128)(2,1)S(1)}, u32[]{:S(2)}, u32[]{:S(2)}) async-start(bf16[32,256,64]{1,2,0:T(8,128)(2,1)} %bitcast.19), calls=%async_computation.3 | async-start | bytes 2097152 | tf_op jit(solution)/shard_map/all_to_all | solution.py:47
  105.0 1.5 pad_maximum_fusion
  106.5 2.1 %collective-permute-start = (bf16[2048,512]{1,0:T(8,128)(2,1)}, bf16[2048,512]{1,0:T(8,128)(2,1)S(1)}, u32[]{:S(2)}, u32[]{:S(2)}) collective-permute-start(bf16[2048,512]{1,0:T(8,128)(2,1)} %pad_maximum_fusion), channel_id=1, source_target_pairs={{0,1},{1,0},{2,3},{3,2},{4,5},{5,4},{6,7},{7,6},{8,9},{9,8},{10,11... | collective-permute-start | bytes 6291464 | tf_op jit(solution)/shard_map/ppermute | solution.py:183
  108.7 0.7 copy_bitcast_fusion.4
  109.3 1.0 copy.136
  110.3 22.5 %all-to-all-done.3 = bf16[32,256,64]{1,2,0:T(8,128)(2,1)S(1)} async-done(((bf16[32,256,64]{1,2,0:T(8,128)(2,1)}), bf16[32,256,64]{1,2,0:T(8,128)(2,1)S(1)}, u32[]{:S(2)}, u32[]{:S(2)}) %all-to-all-start.3) | async-done | bytes 1048608 | tf_op jit(solution)/shard_map/all_to_all | solution.py:47
  133.0 1.4 gather_fusion.5
  134.4 3.9 %all-to-all-start.4 = ((bf16[32,128,64]{1,2,0:T(8,128)(2,1)}), bf16[32,128,64]{1,2,0:T(8,128)(2,1)S(1)}, u32[]{:S(2)}, u32[]{:S(2)}) async-start(bf16[32,128,64]{1,2,0:T(8,128)(2,1)} %gather_fusion.5), calls=%async_computation.4 | async-start | bytes 1048576 | tf_op jit(solution)/shard_map/all_to_all | solution.py:192
  138.2 2.4 %collective-permute-start.1 = (bf16[256,2048]{1,0:T(8,128)(2,1)}, bf16[256,2048]{1,0:T(8,128)(2,1)}, u32[]{:S(2)}, u32[]{:S(2)}) collective-permute-start(bf16[256,2048]{1,0:T(8,128)(2,1)} %param.34), channel_id=1, source_target_pairs={{0,1},{1,0},{2,3},{3,2},{4,5},{5,4},{6,7},{7,6},{8,9},{9,8},{10,11... | collective-permute-start | bytes 3145736 | tf_op jit(solution)/shard_map/ppermute | solution.py:183
  140.6 1.5 fusion.54
  142.1 12.9 %all-to-all-done.4 = bf16[32,128,64]{1,2,0:T(8,128)(2,1)S(1)} async-done(((bf16[32,128,64]{1,2,0:T(8,128)(2,1)}), bf16[32,128,64]{1,2,0:T(8,128)(2,1)S(1)}, u32[]{:S(2)}, u32[]{:S(2)}) %all-to-all-start.4) | async-done | bytes 524320 | tf_op jit(solution)/shard_map/all_to_all | solution.py:192
  155.7 2.9 %fusion.1 = f32[128,512]{1,0:T(8,128)} fusion(bf16[128,2048]{0,1:T(8,128)(2,1)S(1)} %fusion.18, bf16[2048,256]{1,0:T(8,128)(2,1)} %param.32, bf16[2048,256]{1,0:T(8,128)(2,1)} %get-tuple-element.7), kind=kOutput, calls=%fused_computation.15 | convolution fusion | flops 272629760 | bytes 2883584 | tf_op jit(solution)/shard_map/dot_general | solution.py:195
  158.6 2.5 %convolution_convert_fusion.1 = bf16[128,2048]{1,0:T(8,128)(2,1)S(1)} fusion(bf16[256,2048]{1,0:T(8,128)(2,1)} %collective-permute-done.1, bf16[256,2048]{1,0:T(8,128)(2,1)} %param.34, f32[128,512]{1,0:T(8,128)} %fusion.1, bf16[128,2048]{0,1:T(8,128)(2,1)S(1)} %fusion.18, bf16[2048,256]{1,0:T(8,128)(2,1)S(1)} %copy-done.8, bf16[2048,256]{1,0:T(8,128)(2,1)S(1)} %copy-done.7), kind=kOutput, calls=%fused_computation.12 | convolution fusion | flops 545914880 | bytes 5505024 | tf_op jit(solution)/shard_map/dot_general | solution.py:198
  161.1 1.0 copy.138
  162.1 3.7 %all-to-all-start.5 = ((bf16[32,128,64]{1,2,0:T(8,128)(2,1)}), bf16[32,128,64]{1,2,0:T(8,128)(2,1)S(1)}, u32[]{:S(2)}, u32[]{:S(2)}) async-start(bf16[32,128,64]{1,2,0:T(8,128)(2,1)} %bitcast.23), calls=%async_computation.5 | async-start | bytes 1048576 | tf_op jit(solution)/shard_map/all_to_all | solution.py:200
  165.8 16.8 %all-to-all-done.5 = bf16[32,128,64]{1,2,0:T(8,128)(2,1)S(1)} async-done(((bf16[32,128,64]{1,2,0:T(8,128)(2,1)}), bf16[32,128,64]{1,2,0:T(8,128)(2,1)S(1)}, u32[]{:S(2)}, u32[]{:S(2)}) %all-to-all-start.5) | async-done | bytes 524320 | tf_op jit(solution)/shard_map/all_to_all | solution.py:200
  182.8 0.7 reshape.408
  183.6 4.3 %all-to-all-start.6 = ((bf16[16,2,512]{2,1,0:T(2,128)(2,1)}), bf16[16,2,512]{2,1,0:T(2,128)(2,1)S(1)}, u32[]{:S(2)}, u32[]{:S(2)}) async-start(bf16[16,2,512]{2,1,0:T(2,128)(2,1)} %reshape.408), calls=%async_computation.6 | async-start | bytes 65536 | tf_op jit(solution)/shard_map/all_to_all | solution.py:210
  187.9 1.3 dynamic-slice_select_fusion
  189.2 10.0 %all-to-all-done.6 = bf16[16,2,512]{2,1,0:T(2,128)(2,1)S(1)} async-done(((bf16[16,2,512]{2,1,0:T(2,128)(2,1)}), bf16[16,2,512]{2,1,0:T(2,128)(2,1)S(1)}, u32[]{:S(2)}, u32[]{:S(2)}) %all-to-all-start.6) | async-done | bytes 32800 | tf_op jit(solution)/shard_map/all_to_all | solution.py:210
  199.3 1.5 scatter_fusion
  200.8 0.6 copy-done.9
  (118 shorter events, 6.7 us)
Async XLA Ops:
  0.6 94.7 %copy-start = (bf16[64,2048]{1,0:T(8,128)(2,1)S(1)}, bf16[64,2048]{1,0:T(8,128)(2,1)}, u32[]{:S(2)}) copy-start(bf16[64,2048]{1,0:T(8,128)(2,1)} %param.30) | copy-start | bytes 786436
  0.6 22.4 %copy-start.1 = (s32[32]{0:T(128)S(1)}, s32[32]{0:T(128)}, u32[]{:S(2)}) copy-start(s32[32]{0:T(128)} %param.24) | copy-start | bytes 388
  0.7 23.0 %copy-start.2 = (s32[32]{0:T(128)S(1)}, s32[32]{0:T(128)}, u32[]{:S(2)}) copy-start(s32[32]{0:T(128)} %param.21) | copy-start | bytes 388
  0.7 23.7 %copy-start.3 = (s32[32,1]{0,1:T(1,128)S(1)}, s32[32,1]{0,1:T(1,128)}, u32[]{:S(2)}) copy-start(s32[32,1]{0,1:T(1,128)} %param.22) | copy-start | bytes 388
  0.7 24.3 %copy-start.13 = (bf16[2048]{0:T(1024)(128)(2,1)S(1)}, bf16[2048]{0:T(1024)(128)(2,1)}, u32[]{:S(2)}) copy-start(bf16[2048]{0:T(1024)(128)(2,1)} %param.26) | copy-start | bytes 12292
  0.7 24.3 %copy-start.4 = (s32[16]{0:T(128)S(1)}, s32[16]{0:T(128)}, u32[]{:S(2)}) copy-start(s32[16]{0:T(128)} %param.23) | copy-start | bytes 196
  6.8 29.7 %all-to-all-start = ((bf16[16,2,4608]{2,1,0:T(2,128)(2,1)}), bf16[16,2,4608]{2,1,0:T(2,128)(2,1)S(1)}, u32[]{:S(2)}, u32[]{:S(2)}) async-start(bf16[16,2,4608]{2,1,0:T(2,128)(2,1)} %reshape.404), calls=%async_computation | async-start | bytes 589824 | tf_op jit(solution)/shard_map/all_to_all | solution.py:90
  36.7 10.9 %copy-start.17 = (s32[32]{0:T(128)S(1)}, s32[32]{0:T(128)}, u32[]{:S(2)}) copy-start(s32[32]{0:T(128)} %constant.191) | copy-start | bytes 388
  36.7 10.9 %copy-start.16 = (s32[128]{0:T(128)S(1)}, s32[128]{0:T(128)}, u32[]{:S(2)}) copy-start(s32[128]{0:T(128)} %constant.192) | copy-start | bytes 1540
  38.2 37.2 %all-to-all-start.1 = ((bf16[32,256,64]{1,2,0:T(8,128)(2,1)}), bf16[32,256,64]{1,2,0:T(8,128)(2,1)S(1)}, u32[]{:S(2)}, u32[]{:S(2)}) async-start(bf16[32,256,64]{1,2,0:T(8,128)(2,1)} %broadcast_in_dim.153), calls=%async_computation.1 | async-start | bytes 2097152 | tf_op jit(solution)/shard_map/all_to_all | solution.py:38
  47.9 28.1 %copy-start.10 = (bf16[2048,16]{0,1:T(8,128)(2,1)S(1)}, bf16[2048,16]{0,1:T(8,128)(2,1)}, u32[]{:S(2)}) copy-start(bf16[2048,16]{0,1:T(8,128)(2,1)} %param.29) | copy-start | bytes 196612
  47.9 28.1 %copy-start.11 = (bf16[2048,16]{0,1:T(8,128)(2,1)S(1)}, bf16[2048,16]{0,1:T(8,128)(2,1)}, u32[]{:S(2)}) copy-start(bf16[2048,16]{0,1:T(8,128)(2,1)} %param.28) | copy-start | bytes 196612
  79.1 14.0 %all-to-all-start.2 = ((bf16[32,2,1536]{2,1,0:T(2,128)(2,1)}), bf16[32,2,1536]{2,1,0:T(2,128)(2,1)S(1)}, u32[]{:S(2)}, u32[]{:S(2)}) async-start(bf16[32,2,1536]{2,1,0:T(2,128)(2,1)} %reshape.406), calls=%async_computation.2 | async-start | bytes 393216 | tf_op jit(solution)/shard_map/all_to_all | solution.py:127
  86.9 5.9 %copy-start.18 = (bf16[2048,64]{0,1:T(8,128)(2,1)S(1)}, bf16[2048,64]{0,1:T(8,128)(2,1)}, u32[]{:S(2)}) copy-start(bf16[2048,64]{0,1:T(8,128)(2,1)} %param.27) | copy-start | bytes 786436
  94.1 1.2 copy-start.12
  95.8 9.2 %copy-start.5 = (bf16[2048,256]{1,0:T(8,128)(2,1)S(1)}, bf16[2048,256]{1,0:T(8,128)(2,1)}, u32[]{:S(2)}) copy-start(bf16[2048,256]{1,0:T(8,128)(2,1)} %param.32) | copy-start | bytes 3145732
  97.1 7.8 %copy-start.6 = (bf16[2048,256]{1,0:T(8,128)(2,1)S(1)}, bf16[2048,256]{1,0:T(8,128)(2,1)}, u32[]{:S(2)}) copy-start(bf16[2048,256]{1,0:T(8,128)(2,1)} %param.33) | copy-start | bytes 3145732
  97.1 35.7 %all-to-all-start.3 = ((bf16[32,256,64]{1,2,0:T(8,128)(2,1)}), bf16[32,256,64]{1,2,0:T(8,128)(2,1)S(1)}, u32[]{:S(2)}, u32[]{:S(2)}) async-start(bf16[32,256,64]{1,2,0:T(8,128)(2,1)} %bitcast.19), calls=%async_computation.3 | async-start | bytes 2097152 | tf_op jit(solution)/shard_map/all_to_all | solution.py:47
  105.0 3.7 %copy-start.15 = (s32[32]{0:T(128)S(1)}, s32[32]{0:T(128)}, u32[]{:S(2)}) copy-start(s32[32]{0:T(128)} %constant.193) | copy-start | bytes 388
  106.5 34.1 %collective-permute-start = (bf16[2048,512]{1,0:T(8,128)(2,1)}, bf16[2048,512]{1,0:T(8,128)(2,1)S(1)}, u32[]{:S(2)}, u32[]{:S(2)}) collective-permute-start(bf16[2048,512]{1,0:T(8,128)(2,1)} %pad_maximum_fusion), channel_id=1, source_target_pairs={{0,1},{1,0},{2,3},{3,2},{4,5},{5,4},{6,7},{7,6},{8,9},{9,8},{10,11... | collective-permute-start | bytes 6291464 | tf_op jit(solution)/shard_map/ppermute | solution.py:183
  110.3 30.3 %copy-start.14 = (bf16[2048]{0:T(1024)(128)(2,1)S(1)}, bf16[2048]{0:T(1024)(128)(2,1)}, u32[]{:S(2)}) copy-start(bf16[2048]{0:T(1024)(128)(2,1)} %param.31) | copy-start | bytes 12292
  134.4 20.7 %all-to-all-start.4 = ((bf16[32,128,64]{1,2,0:T(8,128)(2,1)}), bf16[32,128,64]{1,2,0:T(8,128)(2,1)S(1)}, u32[]{:S(2)}, u32[]{:S(2)}) async-start(bf16[32,128,64]{1,2,0:T(8,128)(2,1)} %gather_fusion.5), calls=%async_computation.4 | async-start | bytes 1048576 | tf_op jit(solution)/shard_map/all_to_all | solution.py:192
  138.2 20.3 %collective-permute-start.1 = (bf16[256,2048]{1,0:T(8,128)(2,1)}, bf16[256,2048]{1,0:T(8,128)(2,1)}, u32[]{:S(2)}, u32[]{:S(2)}) collective-permute-start(bf16[256,2048]{1,0:T(8,128)(2,1)} %param.34), channel_id=1, source_target_pairs={{0,1},{1,0},{2,3},{3,2},{4,5},{5,4},{6,7},{7,6},{8,9},{9,8},{10,11... | collective-permute-start | bytes 3145736 | tf_op jit(solution)/shard_map/ppermute | solution.py:183
  155.7 2.9 %copy-start.7 = (bf16[2048,256]{1,0:T(8,128)(2,1)S(1)}, bf16[2048,256]{1,0:T(8,128)(2,1)}, u32[]{:S(2)}) copy-start(bf16[2048,256]{1,0:T(8,128)(2,1)} %param.33) | copy-start | bytes 3145732
  155.7 2.9 %copy-start.8 = (bf16[2048,256]{1,0:T(8,128)(2,1)S(1)}, bf16[2048,256]{1,0:T(8,128)(2,1)}, u32[]{:S(2)}) copy-start(bf16[2048,256]{1,0:T(8,128)(2,1)} %get-tuple-element.6) | copy-start | bytes 3145732
  162.1 20.5 %all-to-all-start.5 = ((bf16[32,128,64]{1,2,0:T(8,128)(2,1)}), bf16[32,128,64]{1,2,0:T(8,128)(2,1)S(1)}, u32[]{:S(2)}, u32[]{:S(2)}) async-start(bf16[32,128,64]{1,2,0:T(8,128)(2,1)} %bitcast.23), calls=%async_computation.5 | async-start | bytes 1048576 | tf_op jit(solution)/shard_map/all_to_all | solution.py:200
  183.6 15.6 %all-to-all-start.6 = ((bf16[16,2,512]{2,1,0:T(2,128)(2,1)}), bf16[16,2,512]{2,1,0:T(2,128)(2,1)S(1)}, u32[]{:S(2)}, u32[]{:S(2)}) async-start(bf16[16,2,512]{2,1,0:T(2,128)(2,1)} %reshape.408), calls=%async_computation.6 | async-start | bytes 65536 | tf_op jit(solution)/shard_map/all_to_all | solution.py:210
  200.8 0.6 copy-start.9

commit v8 on v7

--- a/solution.py
+++ b/solution.py
@@ -109,21 +109,41 @@
     valid = (position[None, :] < lengths_here[:, None]).reshape(row_count)
     positions = (P_SIZE + position).astype(jnp.float32)
 
-    chosen = jnp.take(prefix_all, owner_here, axis=0)
-    chosen = jnp.take(chosen, kv_of_dest, axis=2).transpose(2, 0, 1, 3)
-    full_rows = gather_rows(state_shard, "tensor", tp_count)
+    core = tp_index % 2
+    pair = [(t, t ^ 1) for t in range(tp_count)]
+    q_cols = w_query.shape[1]
+    w_qkv_sib = lax.ppermute(jnp.concatenate([w_query, w_key, w_value], axis=1), "tensor", pair)
+    w_query_chip = jnp.concatenate([w_query, w_qkv_sib[:, :q_cols]], axis=1)
+    w_key_chip = jnp.concatenate([w_key, w_qkv_sib[:, q_cols : q_cols + kv_cols]], axis=1)
+    w_value_chip = jnp.concatenate([w_value, w_qkv_sib[:, q_cols + kv_cols :]], axis=1)
+
+    chosen = jnp.take(prefix_all, jnp.take(owner_here, np.arange(tp_count) % 2), axis=0)
+    chosen = jnp.take_along_axis(
+        chosen, jnp.asarray(kv_of_dest).reshape(tp_count, 1, 1, 1), axis=2
+    ).reshape(tp_count, prefix_rows, 2 * HD)
+
+    state_req = routed_here
+    sent = jnp.take(state_req, np.arange(tp_count) % 2, axis=0)
+    got = lax.all_to_all(sent, "tensor", 0, 0, tiled=True)
+    full_rows = got.transpose(1, 0, 2).reshape(L_MAX, tp_count * width_here)
     normed = rms_scale(full_rows.astype(jnp.float32), norm_attn)
-    query = jnp.dot(normed, w_query, preferred_element_type=jnp.float32).reshape(
-        local_reqs, L_MAX, HD
-    )
+    query = jnp.dot(normed, w_query_chip, preferred_element_type=jnp.float32)
+    query = query.reshape(L_MAX, 2 * heads_here, HD).transpose(1, 0, 2)
     query = rotate(query, positions).astype(jnp.bfloat16)
     kv_part = jnp.dot(
-        normed, jnp.concatenate([w_key, w_value], axis=1), preferred_element_type=jnp.float32
+        normed, jnp.concatenate([w_key_chip, w_value_chip], axis=1), preferred_element_type=jnp.float32
     ).astype(jnp.bfloat16)
+    chip_d = 2 * d_here
     pick = (np.arange(d_here)[None, :] * KVH + kv_of_dest[:, None])
-    pick = np.concatenate([pick, kv_cols + pick], axis=1)
-    kv_sent = jnp.take(kv_part, pick.reshape(-1), axis=1).reshape(row_count, tp_count, 2 * d_here)
-    prefix_split = chosen.shape[1] * chosen.shape[2] * chosen.shape[3]
+    pick = np.concatenate(
+        [pick, kv_cols + pick, 2 * kv_cols + pick, 3 * kv_cols + pick], axis=1
+    )
+    kv_all = jnp.concatenate(
+        [kv_part[:, :kv_cols], kv_part[:, kv_cols : 2 * kv_cols],
+         kv_part[:, 2 * kv_cols : 3 * kv_cols], kv_part[:, 3 * kv_cols :]], axis=1
+    )
+    kv_sent = jnp.take(kv_all, pick.reshape(-1), axis=1).reshape(L_MAX, tp_count, 2 * chip_d)
+    prefix_split = chosen.shape[1] * chosen.shape[2]
     both = lax.all_to_all(
         jnp.concatenate(
             [chosen.reshape(tp_count, -1), kv_sent.transpose(1, 0, 2).reshape(tp_count, -1)],
@@ -131,55 +151,73 @@
         ),
         "tensor", 0, 0, tiled=True,
     )
-    picked = both[:, :prefix_split].reshape(tp_count, local_reqs, prefix_rows, 2 * HD)
-    picked = picked.transpose(1, 0, 2, 3).reshape(local_reqs, tp_count * prefix_rows, 2 * HD)
-    prefix_keys = picked[:, :, :HD]
-    prefix_values = picked[:, :, HD:]
-    kv_got = both[:, prefix_split:].reshape(tp_count, row_count, 2 * d_here)
-    key_raw = kv_got[:, :, :d_here].transpose(1, 0, 2).reshape(row_count, HD)
-    value = kv_got[:, :, d_here:].transpose(1, 0, 2).reshape(row_count, HD)
-    key_rot = rotate(
-        key_raw.reshape(local_reqs, L_MAX, HD).astype(jnp.float32), positions
-    ).astype(jnp.bfloat16)
-    value = value.reshape(local_reqs, L_MAX, HD)
-
-    valid3 = valid.reshape(local_reqs, L_MAX, 1)
+    picked = both[:, :prefix_split].reshape(tp_count, prefix_rows, 2 * HD)
+    picked = picked.reshape(tp_count * prefix_rows, 2 * HD)
+    prefix_keys = picked[:, :HD]
+    prefix_values = picked[:, HD:]
+    kv_got = both[:, prefix_split:].reshape(tp_count // 2, 2, L_MAX, 2 * chip_d)
+    kv_got = jnp.take(kv_got, core, axis=1)
+    src_t = (np.arange(tp_count // 2) * 2)[:, None]
+    keys4 = kv_got[:, :, : 2 * d_here].reshape(tp_count // 2, L_MAX, 2, d_here)
+    vals4 = kv_got[:, :, 2 * d_here :].reshape(tp_count // 2, L_MAX, 2, d_here)
+    flip = core == 1
+    keys4 = jnp.where(flip, keys4[:, :, ::-1], keys4)
+    vals4 = jnp.where(flip, vals4[:, :, ::-1], vals4)
+    key_raw = keys4.transpose(1, 0, 2, 3).reshape(L_MAX, HD)
+    value = vals4.transpose(1, 0, 2, 3).reshape(L_MAX, HD)
+    key_rot = rotate(key_raw.astype(jnp.float32), positions).astype(jnp.bfloat16)
+
     out_width = kv_cols
     out_first = (tp_index * out_width) % HD
-    keys_out = jnp.where(
-        valid3, lax.dynamic_slice_in_dim(key_rot, out_first, out_width, 2), 0.0
-    ).astype(jnp.bfloat16)
-    values_out = jnp.where(
-        valid3, lax.dynamic_slice_in_dim(value, out_first, out_width, 2), 0.0
-    ).astype(jnp.bfloat16)
-
+    sib_first = ((tp_index ^ 1) * out_width) % HD
+    kv_for_sib = jnp.concatenate(
+        [lax.dynamic_slice_in_dim(key_rot, sib_first, out_width, 1),
+         lax.dynamic_slice_in_dim(value, sib_first, out_width, 1)], axis=1
+    )
+    kv_from_sib = lax.ppermute(kv_for_sib, "tensor", pair)
+    kv_mine = jnp.concatenate(
+        [lax.dynamic_slice_in_dim(key_rot, out_first, out_width, 1),
+         lax.dynamic_slice_in_dim(value, out_first, out_width, 1)], axis=1
+    )
+    kv_two = jnp.where(
+        core == 0, jnp.stack([kv_mine, kv_from_sib]), jnp.stack([kv_from_sib, kv_mine])
+    )
+    valid3 = valid.reshape(local_reqs, L_MAX, 1)
+    keys_out = jnp.where(valid3, kv_two[:, :, :out_width], 0.0).astype(jnp.bfloat16)
+    values_out = jnp.where(valid3, kv_two[:, :, out_width:], 0.0).astype(jnp.bfloat16)
+
+    length_me = jnp.take(lengths_here, core)
     prefix_scores = jnp.einsum(
-        "rtd,rpd->rtp", query, prefix_keys, preferred_element_type=jnp.float32
+        "htd,pd->htp", query, prefix_keys, preferred_element_type=jnp.float32
     ) * score_scale
     self_scores = jnp.einsum(
-        "rtd,rsd->rts", query, key_rot, preferred_element_type=jnp.float32
+        "htd,sd->hts", query, key_rot, preferred_element_type=jnp.float32
     ) * score_scale
     self_allowed = (position[None, None, :] <= position[None, :, None]) & (
-        position[None, None, :] < lengths_here[:, None, None]
+        position[None, None, :] < length_me
     )
     scores = jnp.concatenate([prefix_scores, self_scores], axis=2)
     allowed = jnp.concatenate(
-        [jnp.ones(prefix_scores.shape, bool), self_allowed], axis=2
+        [jnp.ones(prefix_scores.shape, bool), jnp.broadcast_to(self_allowed, self_scores.shape)], axis=2
     )
     row_peak = jnp.max(jnp.where(allowed, scores, -jnp.inf), axis=2, keepdims=True)
     weights = jnp.where(allowed, jnp.exp(scores - row_peak), 0.0)
     total = jnp.sum(weights, axis=2, keepdims=True)
-    all_values = jnp.concatenate([prefix_values, value], axis=1)
+    all_values = jnp.concatenate([prefix_values, value], axis=0)
     numerator = jnp.einsum(
-        "rtk,rkd->rtd", weights.astype(jnp.bfloat16), all_values, preferred_element_type=jnp.float32
-    )
-    attention = (numerator / total).astype(jnp.bfloat16).reshape(row_count, HD)
-
-    attn_terms = jnp.dot(attention, w_out, preferred_element_type=jnp.float32)
-    attn_share = scatter_sum(attn_terms, "tensor", tp_count)
+        "htk,kd->htd", weights.astype(jnp.bfloat16), all_values, preferred_element_type=jnp.float32
+    )
+    attention = (numerator / total).astype(jnp.bfloat16).transpose(1, 0, 2).reshape(L_MAX, 2 * HD)
+
+    w_out_sib = lax.ppermute(w_out, "tensor", pair)
+    w_out_chip = jnp.concatenate([w_out, w_out_sib], axis=0)
+    attn_terms = jnp.dot(attention, w_out_chip, preferred_element_type=jnp.float32)
+    sent = attn_terms.astype(jnp.bfloat16).reshape(L_MAX, tp_count, width_here).transpose(1, 0, 2)
+    got = lax.all_to_all(sent, "tensor", 0, 0, tiled=True)
+    attn_share = jnp.sum(
+        got.reshape(tp_count // 2, local_reqs, L_MAX, width_here).astype(jnp.float32), axis=0
+    ).reshape(row_count, width_here)
     middle = (state_shard.astype(jnp.float32) + attn_share).astype(jnp.bfloat16)
-    core = tp_index % 2
-    pair = [(t, t ^ 1) for t in range(tp_count)]
     w_gu_sib, w_down_sib = lax.ppermute(
         (jnp.concatenate([w_gate, w_up], axis=1), w_down), "tensor", pair
     )

time: 202 us -> 192 us (0.950)
  waiting for transfers between devices: 99 us -> 56.7 us
  blocking collectives: 0 us -> 20.2 us
  local copies, waits for them, and re-layouts: 23.9 us -> 30.2 us
  starting transfers between devices: 53.5 us -> 57.9 us
    all_to_all x2 -> x0, waiting for transfers between devices: 48.5 us -> none  [the longest x1 26.1 us: gather_rows(): got = lax.all_to_all(sent, axis_name, 0, 0, tiled=True)]
    all_to_all x0 -> x1, blocking collectives: none -> 20.2 us  [shards(): got = lax.all_to_all(sent, 'tensor', 0, 0, tiled=True)]
    all_to_all x2 -> x0, starting transfers between devices: 17.2 us -> none  [the longest x1 9.35 us: gather_rows(): got = lax.all_to_all(sent, axis_name, 0, 0, tiled=True)]
    all_to_all x1, waiting for transfers between devices: 10.8 us -> 0.01 us  [shards(): lax.all_to_all(jnp.concatenate([state_part, prefix_part], axis=1), 'dp',...]
    all_to_all x2 -> x3, starting transfers between devices: 7.54 us -> 15.7 us  [shards(): got = lax.all_to_all(sent, 'tensor', 0, 0, tiled=True)]
    all_to_all x1, waiting for transfers between devices: 0.01 us -> 8.03 us  [shards(): lax.all_to_all(jnp.concatenate([chosen.reshape(tp_count, -1), kv_sent.tra...]
    all_to_all x2 -> x3, waiting for transfers between devices: 29.7 us -> 37.1 us  [shards(): got = lax.all_to_all(sent, 'tensor', 0, 0, tiled=True)]
    ppermute x0 -> x3, starting transfers between devices: none -> 7.09 us  [the longest x1 2.98 us: shards(): lax.ppermute(jnp.concatenate([w_query, w_key, w_value], axis=1), 'tensor'...]
  transfers between devices with their start and end apart: 9 -> 11, of which waited for: 6 -> 6; matrix products, arithmetic and copies ran while one was open for 13% -> 18% of each run, Pallas kernels for 0% -> 0%
where the time goes in v8:
time: 192 us; the launch traced here: 191 us
  starting transfers between devices  57.9 us (30%)
  waiting for transfers between devices  56.7 us (30%)
  local copies, waits for them, and re-layouts  30.2 us (16%)
  blocking collectives  20.2 us (11%)
  other arithmetic  14.7 us (8%)
  matrix products  8.83 us (5%)
  between operations  2.24 us (1%)
    all_to_all x3, waiting for transfers between devices, shards(): got = lax.all_to_all(sent, 'tensor', 0, 0, tiled=True)  37.1 us
    all_to_all x1, blocking collectives, shards(): got = lax.all_to_all(sent, 'tensor', 0, 0, tiled=True)  20.2 us
    all_to_all x1, starting transfers between devices, shards(): lax.all_to_all(jnp.concatenate([state_part, prefix_part], axis=1), 'dp',...  16.2 us
    all_to_all x3, starting transfers between devices, shards(): got = lax.all_to_all(sent, 'tensor', 0, 0, tiled=True)  15.7 us
    all_to_all x1, waiting for transfers between devices, shards(): lax.all_to_all(result, 'dp', split_axis=1, concat_axis=0, tiled=True)  10.7 us
    all_to_all x1, starting transfers between devices, shards(): lax.all_to_all(result, 'dp', split_axis=1, concat_axis=0, tiled=True)  10.7 us
    all_to_all x1, waiting for transfers between devices, shards(): lax.all_to_all(jnp.concatenate([chosen.reshape(tp_count, -1), kv_sent.tra...  8.03 us
    unnamed x69, local copies, waits for them, and re-layouts  4.58 us
  transfers between devices with their start and end apart: 11, of which 6 were waited for; matrix products, arithmetic and copies ran while one was open for 18% of the time, Pallas kernels for 0%

profile of v8, /device:TPU:1, one launch (start us, length us, event | category | flops | bytes accessed | tf_op | source)
XLA Modules:
  0.0 190.8 jit_solution(225376705633253394)
XLA Ops:
  1.4 1.3 gather_fusion.5
  2.7 1.3 gather_fusion.6
  4.1 1.4 gather_fusion.8
  5.5 1.3 gather_fusion.1
  8.1 1.8 compare_and_fusion.1
  10.8 0.9 reduce.4
  11.7 0.9 reshape.512
  12.6 16.2 %all-to-all-start = ((bf16[16,2,4608]{2,1,0:T(2,128)(2,1)}), bf16[16,2,4608]{2,1,0:T(2,128)(2,1)S(1)}, u32[]{:S(2)}, u32[]{:S(2)}) async-start(bf16[16,2,4608]{2,1,0:T(2,128)(2,1)} %reshape.512), calls=%async_computation | async-start | bytes 589824 | tf_op jit(solution)/shard_map/all_to_all | solution.py:90
  28.8 0.8 pad_maximum_fusion.4
  29.6 3.0 %collective-permute-start = (bf16[2048,96]{0,1:T(8,128)(2,1)}, bf16[2048,96]{0,1:T(8,128)(2,1)}, u32[]{:S(2)}, u32[]{:S(2)}) collective-permute-start(bf16[2048,96]{0,1:T(8,128)(2,1)} %pad_maximum_fusion.4), channel_id=1, source_target_pairs={{0,1},{1,0},{2,3},{3,2},{4,5},{5,4},{6,7},{7,6},{8,9},{9,8},{10,11... | collective-permute-start | bytes 1179656 | tf_op jit(solution)/shard_map/ppermute | solution.py:115
  32.6 1.9 %collective-permute-start.1 = (bf16[64,2048]{1,0:T(8,128)(2,1)}, bf16[64,2048]{1,0:T(8,128)(2,1)}, u32[]{:S(2)}, u32[]{:S(2)}) collective-permute-start(bf16[64,2048]{1,0:T(8,128)(2,1)} %param.34), channel_id=1, source_target_pairs={{0,1},{1,0},{2,3},{3,2},{4,5},{5,4},{6,7},{7,6},{8,9},{9,8},{10,11... | collective-permute-start | bytes 786440 | tf_op jit(solution)/shard_map/ppermute | solution.py:212
  34.6 1.5 pad_maximum_fusion
  36.1 2.4 %collective-permute-start.2 = (bf16[2048,512]{1,0:T(8,128)(2,1)}, bf16[2048,512]{1,0:T(8,128)(2,1)S(1)}, u32[]{:S(2)}, u32[]{:S(2)}) collective-permute-start(bf16[2048,512]{1,0:T(8,128)(2,1)} %pad_maximum_fusion), channel_id=1, source_target_pairs={{0,1},{1,0},{2,3},{3,2},{4,5},{5,4},{6,7},{7,6},{8,9},{9,8},{10,11... | collective-permute-start | bytes 6291464 | tf_op jit(solution)/shard_map/ppermute | solution.py:221
  41.6 1.7 slice.121
  43.9 1.4 gather_fusion.7
  45.3 8.4 %all-to-all-start.1 = ((bf16[32,128,64]{1,2,0:T(8,128)(2,1)}), bf16[32,128,64]{1,2,0:T(8,128)(2,1)S(1)}, u32[]{:S(2)}, u32[]{:S(2)}) async-start(bf16[32,128,64]{1,2,0:T(8,128)(2,1)} %gather_fusion.7), calls=%async_computation.1 | async-start | bytes 1048576 | tf_op jit(solution)/shard_map/all_to_all | solution.py:127
  53.7 1.8 pad_maximum_fusion.3
  55.5 1.5 fusion.68
  57.1 0.8 gather_fusion.2
  57.8 0.7 broadcast_select_fusion
  60.0 10.4 %all-to-all-done.1 = bf16[32,128,64]{1,2,0:T(8,128)(2,1)S(1)} async-done(((bf16[32,128,64]{1,2,0:T(8,128)(2,1)}), bf16[32,128,64]{1,2,0:T(8,128)(2,1)S(1)}, u32[]{:S(2)}, u32[]{:S(2)}) %all-to-all-start.1) | async-done | bytes 524320 | tf_op jit(solution)/shard_map/all_to_all | solution.py:127
  71.1 1.1 convolution_convert_fusion.2
  72.2 1.5 gather_fusion.3
  73.7 1.1 copy.81
  74.8 0.8 copy.82
  75.6 0.9 maximum_bitcast_fusion.1
  77.2 0.7 reshape.514
  77.9 3.7 %all-to-all-start.2 = ((bf16[32,2,1024]{2,1,0:T(2,128)(2,1)}), bf16[32,2,1024]{2,1,0:T(2,128)(2,1)S(1)}, u32[]{:S(2)}, u32[]{:S(2)}) async-start(bf16[32,2,1024]{2,1,0:T(2,128)(2,1)} %reshape.514), calls=%async_computation.2 | async-start | bytes 262144 | tf_op jit(solution)/shard_map/all_to_all | solution.py:147
  82.3 8.0 %all-to-all-done.2 = bf16[32,2,1024]{2,1,0:T(2,128)(2,1)S(1)} async-done(((bf16[32,2,1024]{2,1,0:T(2,128)(2,1)}), bf16[32,2,1024]{2,1,0:T(2,128)(2,1)S(1)}, u32[]{:S(2)}, u32[]{:S(2)}) %all-to-all-start.2) | async-done | bytes 131104 | tf_op jit(solution)/shard_map/all_to_all | solution.py:147
  90.5 1.2 reshape.320
  94.0 1.3 convolution_convert_fusion.1
  95.6 20.2 %all_to_all.62 = bf16[32,128,64]{1,2,0:T(8,128)(2,1)S(1)} all-to-all(bf16[32,128,64]{1,2,0:T(8,128)(2,1)S(1)} %bitcast.123), channel_id=1, replica_groups=mesh['dp'=16,'tensor'=32] {'tensor'}, dimensions={0} | all-to-all | bytes 1048576 | tf_op jit(solution)/shard_map/all_to_all | solution.py:216
  115.9 1.5 gather_fusion.9
  117.4 3.7 %all-to-all-start.4 = ((bf16[32,128,64]{1,2,0:T(8,128)(2,1)}), bf16[32,128,64]{1,2,0:T(8,128)(2,1)S(1)}, u32[]{:S(2)}, u32[]{:S(2)}) async-start(bf16[32,128,64]{1,2,0:T(8,128)(2,1)} %gather_fusion.9), calls=%async_computation.4 | async-start | bytes 1048576 | tf_op jit(solution)/shard_map/all_to_all | solution.py:230
  121.1 2.2 %collective-permute-start.3 = (bf16[256,2048]{1,0:T(8,128)(2,1)}, bf16[256,2048]{1,0:T(8,128)(2,1)}, u32[]{:S(2)}, u32[]{:S(2)}) collective-permute-start(bf16[256,2048]{1,0:T(8,128)(2,1)} %param.38), channel_id=1, source_target_pairs={{0,1},{1,0},{2,3},{3,2},{4,5},{5,4},{6,7},{7,6},{8,9},{9,8},{10,11... | collective-permute-start | bytes 3145736 | tf_op jit(solution)/shard_map/ppermute | solution.py:221
  123.3 1.5 fusion.66
  124.8 13.1 %all-to-all-done.4 = bf16[32,128,64]{1,2,0:T(8,128)(2,1)S(1)} async-done(((bf16[32,128,64]{1,2,0:T(8,128)(2,1)}), bf16[32,128,64]{1,2,0:T(8,128)(2,1)S(1)}, u32[]{:S(2)}, u32[]{:S(2)}) %all-to-all-start.4) | async-done | bytes 524320 | tf_op jit(solution)/shard_map/all_to_all | solution.py:230
  138.6 2.9 %fusion.1 = f32[128,512]{1,0:T(8,128)} fusion(bf16[128,2048]{0,1:T(8,128)(2,1)S(1)} %fusion.16, bf16[2048,256]{1,0:T(8,128)(2,1)} %param.36, bf16[2048,256]{1,0:T(8,128)(2,1)} %get-tuple-element.30), kind=kOutput, calls=%fused_computation.16 | convolution fusion | flops 272629760 | bytes 2883584 | tf_op jit(solution)/shard_map/dot_general | solution.py:233
  141.4 2.5 %convolution_convert_fusion = bf16[128,2048]{1,0:T(8,128)(2,1)S(1)} fusion(bf16[256,2048]{1,0:T(8,128)(2,1)} %collective-permute-done.3, bf16[256,2048]{1,0:T(8,128)(2,1)} %param.38, f32[128,512]{1,0:T(8,128)} %fusion.1, bf16[128,2048]{0,1:T(8,128)(2,1)S(1)} %fusion.16, bf16[2048,256]{1,0:T(8,128)(2,1)S(1)} %copy-done.7, bf16[2048,256]{1,0:T(8,128)(2,1)S(1)} %copy-done.6), kind=kOutput, calls=%fused_computation.12 | convolution fusion | flops 545914880 | bytes 5505024 | tf_op jit(solution)/shard_map/dot_general | solution.py:236
  144.0 1.0 copy.92
  145.0 3.7 %all-to-all-start.5 = ((bf16[32,128,64]{1,2,0:T(8,128)(2,1)}), bf16[32,128,64]{1,2,0:T(8,128)(2,1)S(1)}, u32[]{:S(2)}, u32[]{:S(2)}) async-start(bf16[32,128,64]{1,2,0:T(8,128)(2,1)} %bitcast.39), calls=%async_computation.5 | async-start | bytes 1048576 | tf_op jit(solution)/shard_map/all_to_all | solution.py:238
  148.9 2.2 %collective-permute-start.4 = (bf16[128,32]{0,1:T(8,128)(2,1)S(1)}, bf16[128,32]{0,1:T(8,128)(2,1)S(1)}, u32[]{:S(2)}, u32[]{:S(2)}) collective-permute-start(bf16[128,32]{0,1:T(8,128)(2,1)S(1)} %pad_maximum_fusion.11), channel_id=1, source_target_pairs={{0,1},{1,0},{2,3},{3,2},{4,5},{5,4},{6,7},{7,6},{8,9},{9,8},{10,11... | collective-permute-start | bytes 24584 | tf_op jit(solution)/shard_map/ppermute | solution.py:177
  151.1 0.9 collective-permute-done.4
  152.0 13.6 %all-to-all-done.5 = bf16[32,128,64]{1,2,0:T(8,128)(2,1)S(1)} async-done(((bf16[32,128,64]{1,2,0:T(8,128)(2,1)}), bf16[32,128,64]{1,2,0:T(8,128)(2,1)S(1)}, u32[]{:S(2)}, u32[]{:S(2)}) %all-to-all-start.5) | async-done | bytes 524320 | tf_op jit(solution)/shard_map/all_to_all | solution.py:238
  165.7 0.7 reshape.516
  166.5 10.7 %all-to-all-start.6 = ((bf16[16,2,512]{2,1,0:T(2,128)(2,1)}), bf16[16,2,512]{2,1,0:T(2,128)(2,1)S(1)}, u32[]{:S(2)}, u32[]{:S(2)}) async-start(bf16[16,2,512]{2,1,0:T(2,128)(2,1)} %reshape.516), calls=%async_computation.6 | async-start | bytes 65536 | tf_op jit(solution)/shard_map/all_to_all | solution.py:248
  177.8 10.7 %all-to-all-done.6 = bf16[16,2,512]{2,1,0:T(2,128)(2,1)S(1)} async-done(((bf16[16,2,512]{2,1,0:T(2,128)(2,1)}), bf16[16,2,512]{2,1,0:T(2,128)(2,1)S(1)}, u32[]{:S(2)}, u32[]{:S(2)}) %all-to-all-start.6) | async-done | bytes 32800 | tf_op jit(solution)/shard_map/all_to_all | solution.py:248
  188.6 1.5 scatter_fusion
  (147 shorter events, 14.3 us)
Async XLA Ops:
  0.6 6.8 %copy-start = (bf16[32,8,64]{2,1,0:T(8,128)(2,1)S(1)}, bf16[32,8,64]{2,1,0:T(8,128)(2,1)}, u32[]{:S(2)}) copy-start(bf16[32,8,64]{2,1,0:T(8,128)(2,1)} %param.24) | copy-start | bytes 98308
  0.6 7.4 %copy-start.23 = (pred[32]{0:T(512)(128)(4,1)S(1)}, pred[32]{0:T(512)(128)(4,1)}, u32[]{:S(2)}) copy-start(pred[32]{0:T(512)(128)(4,1)} %constant.309) | copy-start | bytes 100
  0.7 7.4 %copy-start.1 = (s32[32]{0:T(128)S(1)}, s32[32]{0:T(128)}, u32[]{:S(2)}) copy-start(s32[32]{0:T(128)} %param.28) | copy-start | bytes 388
  0.7 9.4 %copy-start.16 = (bf16[1,8,1024]{2,1,0:T(8,128)(2,1)S(1)}, bf16[1,8,1024]{2,1,0:T(8,128)(2,1)}, u32[]{:S(2)}) copy-start(bf16[1,8,1024]{2,1,0:T(8,128)(2,1)} %param.29) | copy-start | bytes 49156
  1.4 6.0 %copy-start.19 = (s32[32]{0:T(128)}, s32[32]{0:T(128)S(1)}, u32[]{:S(2)}) copy-start(s32[32]{0:T(128)S(1)} %compare_select_fusion.4) | copy-start | bytes 388
  2.7 26.1 %copy-start.3 = (bf16[2048,64]{0,1:T(8,128)(2,1)S(1)}, bf16[2048,64]{0,1:T(8,128)(2,1)}, u32[]{:S(2)}) copy-start(bf16[2048,64]{0,1:T(8,128)(2,1)} %param.31) | copy-start | bytes 786436
  2.7 26.1 %copy-start.10 = (bf16[2048,16]{0,1:T(8,128)(2,1)S(1)}, bf16[2048,16]{0,1:T(8,128)(2,1)}, u32[]{:S(2)}) copy-start(bf16[2048,16]{0,1:T(8,128)(2,1)} %param.33) | copy-start | bytes 196612
  2.7 26.1 %copy-start.12 = (bf16[2048,16]{0,1:T(8,128)(2,1)S(1)}, bf16[2048,16]{0,1:T(8,128)(2,1)}, u32[]{:S(2)}) copy-start(bf16[2048,16]{0,1:T(8,128)(2,1)} %param.32) | copy-start | bytes 196612
  4.1 30.5 %copy-start.4 = (bf16[2048,256]{1,0:T(8,128)(2,1)S(1)}, bf16[2048,256]{1,0:T(8,128)(2,1)}, u32[]{:S(2)}) copy-start(bf16[2048,256]{1,0:T(8,128)(2,1)} %param.36) | copy-start | bytes 3145732
  4.1 30.5 %copy-start.5 = (bf16[2048,256]{1,0:T(8,128)(2,1)S(1)}, bf16[2048,256]{1,0:T(8,128)(2,1)}, u32[]{:S(2)}) copy-start(bf16[2048,256]{1,0:T(8,128)(2,1)} %param.37) | copy-start | bytes 3145732
  5.5 34.2 %copy-start.24 = (s32[2]{0:T(128)}, s32[2]{0:T(128)S(1)}, u32[]{:S(2)}) copy-start(s32[2]{0:T(128)S(1)} %get-tuple-element.52) | copy-start | bytes 28
  12.6 30.7 %all-to-all-start = ((bf16[16,2,4608]{2,1,0:T(2,128)(2,1)}), bf16[16,2,4608]{2,1,0:T(2,128)(2,1)S(1)}, u32[]{:S(2)}, u32[]{:S(2)}) async-start(bf16[16,2,4608]{2,1,0:T(2,128)(2,1)} %reshape.512), calls=%async_computation | async-start | bytes 589824 | tf_op jit(solution)/shard_map/all_to_all | solution.py:90
  29.6 9.5 %copy-start.15 = (bf16[2048]{0:T(1024)(128)(2,1)S(1)}, bf16[2048]{0:T(1024)(128)(2,1)}, u32[]{:S(2)}) copy-start(bf16[2048]{0:T(1024)(128)(2,1)} %param.30) | copy-start | bytes 12292
  29.6 10.1 %copy-start.22 = (s32[32]{0:T(128)S(1)}, s32[32]{0:T(128)}, u32[]{:S(2)}) copy-start(s32[32]{0:T(128)} %constant.324) | copy-start | bytes 388
  29.6 11.9 %copy-start.21 = (s32[256]{0:T(256)S(1)}, s32[256]{0:T(256)}, u32[]{:S(2)}) copy-start(s32[256]{0:T(256)} %constant.320) | copy-start | bytes 3076
  29.6 12.0 %collective-permute-start = (bf16[2048,96]{0,1:T(8,128)(2,1)}, bf16[2048,96]{0,1:T(8,128)(2,1)}, u32[]{:S(2)}, u32[]{:S(2)}) collective-permute-start(bf16[2048,96]{0,1:T(8,128)(2,1)} %pad_maximum_fusion.4), channel_id=1, source_target_pairs={{0,1},{1,0},{2,3},{3,2},{4,5},{5,4},{6,7},{7,6},{8,9},{9,8},{10,11... | collective-permute-start | bytes 1179656 | tf_op jit(solution)/shard_map/ppermute | solution.py:115
  32.6 61.4 %collective-permute-start.1 = (bf16[64,2048]{1,0:T(8,128)(2,1)}, bf16[64,2048]{1,0:T(8,128)(2,1)}, u32[]{:S(2)}, u32[]{:S(2)}) collective-permute-start(bf16[64,2048]{1,0:T(8,128)(2,1)} %param.34), channel_id=1, source_target_pairs={{0,1},{1,0},{2,3},{3,2},{4,5},{5,4},{6,7},{7,6},{8,9},{9,8},{10,11... | collective-permute-start | bytes 786440 | tf_op jit(solution)/shard_map/ppermute | solution.py:212
  36.1 87.2 %collective-permute-start.2 = (bf16[2048,512]{1,0:T(8,128)(2,1)}, bf16[2048,512]{1,0:T(8,128)(2,1)S(1)}, u32[]{:S(2)}, u32[]{:S(2)}) collective-permute-start(bf16[2048,512]{1,0:T(8,128)(2,1)} %pad_maximum_fusion), channel_id=1, source_target_pairs={{0,1},{1,0},{2,3},{3,2},{4,5},{5,4},{6,7},{7,6},{8,9},{9,8},{10,11... | collective-permute-start | bytes 6291464 | tf_op jit(solution)/shard_map/ppermute | solution.py:221
  39.8 5.5 %copy-start.17 = (s32[1024]{0:T(1024)}, s32[1024]{0:T(1024)S(1)}, u32[]{:S(2)}) copy-start(s32[1024]{0:T(1024)S(1)} %pad_clamp_fusion.3) | copy-start | bytes 12292
  45.3 25.1 %all-to-all-start.1 = ((bf16[32,128,64]{1,2,0:T(8,128)(2,1)}), bf16[32,128,64]{1,2,0:T(8,128)(2,1)S(1)}, u32[]{:S(2)}, u32[]{:S(2)}) async-start(bf16[32,128,64]{1,2,0:T(8,128)(2,1)} %gather_fusion.7), calls=%async_computation.1 | async-start | bytes 1048576 | tf_op jit(solution)/shard_map/all_to_all | solution.py:127
  57.0 1.7 copy-start.8
  58.6 12.5 %copy-start.11 = (bf16[2048,16]{0,1:T(8,128)(2,1)S(1)}, bf16[2048,16]{0,1:T(8,128)(2,1)}, u32[]{:S(2)}) copy-start(bf16[2048,16]{0,1:T(8,128)(2,1)} %param.33) | copy-start | bytes 196612
  58.6 12.5 %copy-start.13 = (bf16[2048,16]{0,1:T(8,128)(2,1)S(1)}, bf16[2048,16]{0,1:T(8,128)(2,1)}, u32[]{:S(2)}) copy-start(bf16[2048,16]{0,1:T(8,128)(2,1)} %param.32) | copy-start | bytes 196612
  58.6 12.5 %copy-start.14 = (bf16[2048,16]{0,1:T(8,128)(2,1)S(1)}, bf16[2048,16]{0,1:T(8,128)(2,1)}, u32[]{:S(2)}) copy-start(bf16[2048,16]{0,1:T(8,128)(2,1)} %get-tuple-element.33) | copy-start | bytes 196612
  71.1 10.8 %copy-start.2 = (bf16[2048,128]{0,1:T(8,128)(2,1)S(1)}, bf16[2048,128]{0,1:T(8,128)(2,1)}, u32[]{:S(2)}) copy-start(bf16[2048,128]{0,1:T(8,128)(2,1)} %pad_maximum_fusion.3) | copy-start | bytes 1572868
  77.9 12.4 %all-to-all-start.2 = ((bf16[32,2,1024]{2,1,0:T(2,128)(2,1)}), bf16[32,2,1024]{2,1,0:T(2,128)(2,1)S(1)}, u32[]{:S(2)}, u32[]{:S(2)}) async-start(bf16[32,2,1024]{2,1,0:T(2,128)(2,1)} %reshape.514), calls=%async_computation.2 | async-start | bytes 262144 | tf_op jit(solution)/shard_map/all_to_all | solution.py:147
  91.7 0.9 copy-start.26
  91.7 0.9 copy-start.27
  115.8 7.5 %copy-start.18 = (bf16[2048]{0:T(1024)(128)(2,1)S(1)}, bf16[2048]{0:T(1024)(128)(2,1)}, u32[]{:S(2)}) copy-start(bf16[2048]{0:T(1024)(128)(2,1)} %param.35) | copy-start | bytes 12292
  117.4 20.5 %all-to-all-start.4 = ((bf16[32,128,64]{1,2,0:T(8,128)(2,1)}), bf16[32,128,64]{1,2,0:T(8,128)(2,1)S(1)}, u32[]{:S(2)}, u32[]{:S(2)}) async-start(bf16[32,128,64]{1,2,0:T(8,128)(2,1)} %gather_fusion.9), calls=%async_computation.4 | async-start | bytes 1048576 | tf_op jit(solution)/shard_map/all_to_all | solution.py:230
  121.1 20.3 %collective-permute-start.3 = (bf16[256,2048]{1,0:T(8,128)(2,1)}, bf16[256,2048]{1,0:T(8,128)(2,1)}, u32[]{:S(2)}, u32[]{:S(2)}) collective-permute-start(bf16[256,2048]{1,0:T(8,128)(2,1)} %param.38), channel_id=1, source_target_pairs={{0,1},{1,0},{2,3},{3,2},{4,5},{5,4},{6,7},{7,6},{8,9},{9,8},{10,11... | collective-permute-start | bytes 3145736 | tf_op jit(solution)/shard_map/ppermute | solution.py:221
  138.5 2.9 %copy-start.6 = (bf16[2048,256]{1,0:T(8,128)(2,1)S(1)}, bf16[2048,256]{1,0:T(8,128)(2,1)}, u32[]{:S(2)}) copy-start(bf16[2048,256]{1,0:T(8,128)(2,1)} %param.37) | copy-start | bytes 3145732
  138.6 2.9 %copy-start.7 = (bf16[2048,256]{1,0:T(8,128)(2,1)S(1)}, bf16[2048,256]{1,0:T(8,128)(2,1)}, u32[]{:S(2)}) copy-start(bf16[2048,256]{1,0:T(8,128)(2,1)} %get-tuple-element.29) | copy-start | bytes 3145732
  144.0 4.8 %copy-start.25 = (s32[2]{0:T(128)S(1)}, s32[2]{0:T(128)}, u32[]{:S(2)}) copy-start(s32[2]{0:T(128)} %copy-done.24) | copy-start | bytes 28
  144.0 44.6 %copy-start.20 = (s32[32]{0:T(128)S(1)}, s32[32]{0:T(128)}, u32[]{:S(2)}) copy-start(s32[32]{0:T(128)} %copy-done.19) | copy-start | bytes 388
  145.0 20.5 %all-to-all-start.5 = ((bf16[32,128,64]{1,2,0:T(8,128)(2,1)}), bf16[32,128,64]{1,2,0:T(8,128)(2,1)S(1)}, u32[]{:S(2)}, u32[]{:S(2)}) async-start(bf16[32,128,64]{1,2,0:T(8,128)(2,1)} %bitcast.39), calls=%async_computation.5 | async-start | bytes 1048576 | tf_op jit(solution)/shard_map/all_to_all | solution.py:238
  148.9 3.1 %collective-permute-start.4 = (bf16[128,32]{0,1:T(8,128)(2,1)S(1)}, bf16[128,32]{0,1:T(8,128)(2,1)S(1)}, u32[]{:S(2)}, u32[]{:S(2)}) collective-permute-start(bf16[128,32]{0,1:T(8,128)(2,1)S(1)} %pad_maximum_fusion.11), channel_id=1, source_target_pairs={{0,1},{1,0},{2,3},{3,2},{4,5},{5,4},{6,7},{7,6},{8,9},{9,8},{10,11... | collective-permute-start | bytes 24584 | tf_op jit(solution)/shard_map/ppermute | solution.py:177
  166.5 22.0 %all-to-all-start.6 = ((bf16[16,2,512]{2,1,0:T(2,128)(2,1)}), bf16[16,2,512]{2,1,0:T(2,128)(2,1)S(1)}, u32[]{:S(2)}, u32[]{:S(2)}) async-start(bf16[16,2,512]{2,1,0:T(2,128)(2,1)} %reshape.516), calls=%async_computation.6 | async-start | bytes 65536 | tf_op jit(solution)/shard_map/all_to_all | solution.py:248
  190.1 0.6 copy-start.9

commit v9 on v8

--- a/solution.py
+++ b/solution.py
@@ -101,10 +101,12 @@
     prefix_all = first[:, state_split:].reshape(dp_count, prefix_rows, KVH, 2 * HD)
 
     state_shard = routed_here.reshape(row_count, width_here)
-    slot_ids = dp_index * local_reqs + jnp.arange(local_reqs, dtype=jnp.int32)
-    req_ids = jnp.take(request_order, slot_ids)
-    lengths_here = jnp.take(suffix_lengths, req_ids)
-    owner_here = jnp.take(group_owner, jnp.take(request_group[:, 0], req_ids))
+    req_ids = lax.dynamic_slice_in_dim(request_order, dp_index * local_reqs, local_reqs)
+    hit = jnp.arange(total_reqs, dtype=jnp.int32)[None, :] == req_ids[:, None]
+    lengths_here = jnp.sum(jnp.where(hit, suffix_lengths[None, :], 0), axis=1)
+    group_here = jnp.sum(jnp.where(hit, request_group[:, 0][None, :], 0), axis=1)
+    group_hit = jnp.arange(group_owner.shape[0], dtype=jnp.int32)[None, :] == group_here[:, None]
+    owner_here = jnp.sum(jnp.where(group_hit, group_owner[None, :], 0), axis=1)
     position = jnp.arange(L_MAX, dtype=jnp.int32)
     valid = (position[None, :] < lengths_here[:, None]).reshape(row_count)
     positions = (P_SIZE + position).astype(jnp.float32)
@@ -117,13 +119,13 @@
     w_key_chip = jnp.concatenate([w_key, w_qkv_sib[:, q_cols : q_cols + kv_cols]], axis=1)
     w_value_chip = jnp.concatenate([w_value, w_qkv_sib[:, q_cols + kv_cols :]], axis=1)
 
-    chosen = jnp.take(prefix_all, jnp.take(owner_here, np.arange(tp_count) % 2), axis=0)
+    chosen = jnp.take(prefix_all, jnp.tile(owner_here, tp_count // 2), axis=0)
     chosen = jnp.take_along_axis(
         chosen, jnp.asarray(kv_of_dest).reshape(tp_count, 1, 1, 1), axis=2
     ).reshape(tp_count, prefix_rows, 2 * HD)
 
     state_req = routed_here
-    sent = jnp.take(state_req, np.arange(tp_count) % 2, axis=0)
+    sent = jnp.tile(state_req, (tp_count // 2, 1, 1))
     got = lax.all_to_all(sent, "tensor", 0, 0, tiled=True)
     full_rows = got.transpose(1, 0, 2).reshape(L_MAX, tp_count * width_here)
     normed = rms_scale(full_rows.astype(jnp.float32), norm_attn)
@@ -226,7 +228,7 @@
     w_up_chip = jnp.concatenate([w_up, w_gu_sib[:, units:]], axis=1)
     w_down_chip = jnp.concatenate([w_down, w_down_sib], axis=0)
     middle_req = middle.reshape(local_reqs, L_MAX, width_here)
-    sent = jnp.take(middle_req, np.arange(tp_count) % 2, axis=0)
+    sent = jnp.tile(middle_req, (tp_count // 2, 1, 1))
     got = lax.all_to_all(sent, "tensor", 0, 0, tiled=True)
     middle_rows = got.transpose(1, 0, 2).reshape(L_MAX, tp_count * width_here)
     normed_two = rms_scale(middle_rows.astype(jnp.float32), norm_mlp)

time: 192 us -> 189 us (0.984)
  waiting for transfers between devices: 56.7 us -> 54.4 us
  local copies, waits for them, and re-layouts: 30.2 us -> 27.9 us
    gather x8 -> x1, local copies, waits for them, and re-layouts: 9.7 us -> 1.54 us  [shards(): chosen = jnp.take(prefix_all, jnp.tile(owner_here, tp_count // 2), axis=0)]
    all_to_all x3, waiting for transfers between devices: 37.1 us -> 34.8 us  [shards(): got = lax.all_to_all(sent, 'tensor', 0, 0, tiled=True)]
    another operation x0 -> x5, local copies, waits for them, and re-layouts: none -> 2.03 us  [the longest x1 0.93 us: shards(): sent = jnp.tile(state_req, (tp_count // 2, 1, 1))]
    unnamed x69 -> x61, local copies, waits for them, and re-layouts: 4.58 us -> 5.31 us
  transfers between devices with their start and end apart: 11 -> 11, of which waited for: 6 -> 6; matrix products, arithmetic and copies ran while one was open for 18% -> 20% of each run, Pallas kernels for 0% -> 0%
where the time goes in v9:
time: 189 us; the launch traced here: 187 us
  starting transfers between devices  57.9 us (31%)
  waiting for transfers between devices  54.4 us (29%)
  local copies, waits for them, and re-layouts  27.9 us (15%)
  blocking collectives  20.2 us (11%)
  other arithmetic  16.2 us (9%)
  matrix products  8.75 us (5%)
  between operations  2.15 us (1%)
    all_to_all x3, waiting for transfers between devices, shards(): got = lax.all_to_all(sent, 'tensor', 0, 0, tiled=True)  34.8 us
    all_to_all x1, blocking collectives, shards(): got = lax.all_to_all(sent, 'tensor', 0, 0, tiled=True)  20.2 us
    all_to_all x1, starting transfers between devices, shards(): lax.all_to_all(jnp.concatenate([state_part, prefix_part], axis=1), 'dp',...  16.2 us
    all_to_all x3, starting transfers between devices, shards(): got = lax.all_to_all(sent, 'tensor', 0, 0, tiled=True)  14.7 us
    all_to_all x1, starting transfers between devices, shards(): lax.all_to_all(result, 'dp', split_axis=1, concat_axis=0, tiled=True)  11.7 us
    all_to_all x1, waiting for transfers between devices, shards(): lax.all_to_all(result, 'dp', split_axis=1, concat_axis=0, tiled=True)  10.7 us
    all_to_all x1, waiting for transfers between devices, shards(): lax.all_to_all(jnp.concatenate([chosen.reshape(tp_count, -1), kv_sent.tra...  8.04 us
    unnamed x61, local copies, waits for them, and re-layouts  5.31 us
  transfers between devices with their start and end apart: 11, of which 6 were waited for; matrix products, arithmetic and copies ran while one was open for 20% of the time, Pallas kernels for 0%

profile of v9, /device:TPU:1, one launch (start us, length us, event | category | flops | bytes accessed | tf_op | source)
XLA Modules:
  0.0 187.4 jit_solution(15904722241290772378)
XLA Ops:
  0.7 0.8 compare_select_fusion.2
  2.2 0.9 select_reduce_fusion.1
  3.1 0.8 fusion.50
  4.1 1.2 compare_and_fusion
  6.1 0.8 copy.136
  7.5 0.9 reduce.4
  8.4 0.9 reshape.464
  9.3 16.2 %all-to-all-start = ((bf16[16,2,4608]{2,1,0:T(2,128)(2,1)}), bf16[16,2,4608]{2,1,0:T(2,128)(2,1)S(1)}, u32[]{:S(2)}, u32[]{:S(2)}) async-start(bf16[16,2,4608]{2,1,0:T(2,128)(2,1)} %reshape.464), calls=%async_computation | async-start | bytes 589824 | tf_op jit(solution)/shard_map/all_to_all | solution.py:90
  25.5 0.8 pad_maximum_fusion.4
  26.3 3.0 %collective-permute-start = (bf16[2048,96]{0,1:T(8,128)(2,1)}, bf16[2048,96]{0,1:T(8,128)(2,1)}, u32[]{:S(2)}, u32[]{:S(2)}) collective-permute-start(bf16[2048,96]{0,1:T(8,128)(2,1)} %pad_maximum_fusion.4), channel_id=1, source_target_pairs={{0,1},{1,0},{2,3},{3,2},{4,5},{5,4},{6,7},{7,6},{8,9},{9,8},{10,11... | collective-permute-start | bytes 1179656 | tf_op jit(solution)/shard_map/ppermute | solution.py:117
  29.3 1.9 %collective-permute-start.1 = (bf16[64,2048]{1,0:T(8,128)(2,1)}, bf16[64,2048]{1,0:T(8,128)(2,1)}, u32[]{:S(2)}, u32[]{:S(2)}) collective-permute-start(bf16[64,2048]{1,0:T(8,128)(2,1)} %param.27), channel_id=1, source_target_pairs={{0,1},{1,0},{2,3},{3,2},{4,5},{5,4},{6,7},{7,6},{8,9},{9,8},{10,11... | collective-permute-start | bytes 786440 | tf_op jit(solution)/shard_map/ppermute | solution.py:214
  31.2 1.5 pad_maximum_fusion
  32.7 2.4 %collective-permute-start.2 = (bf16[2048,512]{1,0:T(8,128)(2,1)}, bf16[2048,512]{1,0:T(8,128)(2,1)S(1)}, u32[]{:S(2)}, u32[]{:S(2)}) collective-permute-start(bf16[2048,512]{1,0:T(8,128)(2,1)} %pad_maximum_fusion), channel_id=1, source_target_pairs={{0,1},{1,0},{2,3},{3,2},{4,5},{5,4},{6,7},{7,6},{8,9},{9,8},{10,11... | collective-permute-start | bytes 6291464 | tf_op jit(solution)/shard_map/ppermute | solution.py:223
  39.5 1.7 slice.106
  41.8 0.9 tile.27
  42.7 7.3 %all-to-all-start.1 = ((bf16[32,128,64]{1,2,0:T(8,128)(2,1)}), bf16[32,128,64]{1,2,0:T(8,128)(2,1)S(1)}, u32[]{:S(2)}, u32[]{:S(2)}) async-start(bf16[32,128,64]{1,2,0:T(8,128)(2,1)} %bitcast.4), calls=%async_computation.1 | async-start | bytes 1048576 | tf_op jit(solution)/shard_map/all_to_all | solution.py:129
  50.0 1.1 pad_maximum_fusion.3
  51.1 1.5 fusion.70
  52.7 1.5 gather_fusion.1
  54.2 1.2 broadcast_select_fusion
  55.4 0.9 copy.100
  56.3 1.7 gather_fusion.3
  58.7 8.1 %all-to-all-done.1 = bf16[32,128,64]{1,2,0:T(8,128)(2,1)S(1)} async-done(((bf16[32,128,64]{1,2,0:T(8,128)(2,1)}), bf16[32,128,64]{1,2,0:T(8,128)(2,1)S(1)}, u32[]{:S(2)}, u32[]{:S(2)}) %all-to-all-start.1) | async-done | bytes 524320 | tf_op jit(solution)/shard_map/all_to_all | solution.py:129
  67.5 1.1 convolution_convert_fusion.2
  68.5 1.5 gather_fusion.2
  70.0 1.1 copy.101
  71.1 0.8 copy.102
  71.8 0.9 maximum_bitcast_fusion.1
  74.2 3.7 %all-to-all-start.2 = ((bf16[32,2,1024]{2,1,0:T(2,128)(2,1)}), bf16[32,2,1024]{2,1,0:T(2,128)(2,1)S(1)}, u32[]{:S(2)}, u32[]{:S(2)}) async-start(bf16[32,2,1024]{2,1,0:T(2,128)(2,1)} %reshape.466), calls=%async_computation.2 | async-start | bytes 262144 | tf_op jit(solution)/shard_map/all_to_all | solution.py:149
  78.5 8.0 %all-to-all-done.2 = bf16[32,2,1024]{2,1,0:T(2,128)(2,1)S(1)} async-done(((bf16[32,2,1024]{2,1,0:T(2,128)(2,1)}), bf16[32,2,1024]{2,1,0:T(2,128)(2,1)S(1)}, u32[]{:S(2)}, u32[]{:S(2)}) %all-to-all-start.2) | async-done | bytes 131104 | tf_op jit(solution)/shard_map/all_to_all | solution.py:149
  86.8 1.2 reshape.344
  90.2 1.3 convolution_convert_fusion.1
  91.9 20.2 %all_to_all.62 = bf16[32,128,64]{1,2,0:T(8,128)(2,1)S(1)} all-to-all(bf16[32,128,64]{1,2,0:T(8,128)(2,1)S(1)} %bitcast.124), channel_id=1, replica_groups=mesh['dp'=16,'tensor'=32] {'tensor'}, dimensions={0} | all-to-all | bytes 1048576 | tf_op jit(solution)/shard_map/all_to_all | solution.py:218
  112.1 0.9 tile.32
  113.1 3.7 %all-to-all-start.4 = ((bf16[32,128,64]{1,2,0:T(8,128)(2,1)}), bf16[32,128,64]{1,2,0:T(8,128)(2,1)S(1)}, u32[]{:S(2)}, u32[]{:S(2)}) async-start(bf16[32,128,64]{1,2,0:T(8,128)(2,1)} %bitcast.36), calls=%async_computation.4 | async-start | bytes 1048576 | tf_op jit(solution)/shard_map/all_to_all | solution.py:232
  116.8 2.2 %collective-permute-start.3 = (bf16[256,2048]{1,0:T(8,128)(2,1)}, bf16[256,2048]{1,0:T(8,128)(2,1)}, u32[]{:S(2)}, u32[]{:S(2)}) collective-permute-start(bf16[256,2048]{1,0:T(8,128)(2,1)} %param.31), channel_id=1, source_target_pairs={{0,1},{1,0},{2,3},{3,2},{4,5},{5,4},{6,7},{7,6},{8,9},{9,8},{10,11... | collective-permute-start | bytes 3145736 | tf_op jit(solution)/shard_map/ppermute | solution.py:223
  119.0 1.5 fusion.68
  120.5 13.1 %all-to-all-done.4 = bf16[32,128,64]{1,2,0:T(8,128)(2,1)S(1)} async-done(((bf16[32,128,64]{1,2,0:T(8,128)(2,1)}), bf16[32,128,64]{1,2,0:T(8,128)(2,1)S(1)}, u32[]{:S(2)}, u32[]{:S(2)}) %all-to-all-start.4) | async-done | bytes 524320 | tf_op jit(solution)/shard_map/all_to_all | solution.py:232
  134.2 2.9 %fusion.1 = f32[128,512]{1,0:T(8,128)} fusion(bf16[128,2048]{0,1:T(8,128)(2,1)S(1)} %fusion.16, bf16[2048,256]{1,0:T(8,128)(2,1)} %param.29, bf16[2048,256]{1,0:T(8,128)(2,1)} %get-tuple-element.28), kind=kOutput, calls=%fused_computation.10 | convolution fusion | flops 272629760 | bytes 2883584 | tf_op jit(solution)/shard_map/dot_general | solution.py:235
  137.1 2.5 %convolution_convert_fusion = bf16[128,2048]{1,0:T(8,128)(2,1)S(1)} fusion(bf16[256,2048]{1,0:T(8,128)(2,1)} %collective-permute-done.3, bf16[256,2048]{1,0:T(8,128)(2,1)} %param.31, f32[128,512]{1,0:T(8,128)} %fusion.1, bf16[128,2048]{0,1:T(8,128)(2,1)S(1)} %fusion.16, bf16[2048,256]{1,0:T(8,128)(2,1)S(1)} %copy-done.5, bf16[2048,256]{1,0:T(8,128)(2,1)S(1)} %copy-done.4), kind=kOutput, calls=%fused_computation.6 | convolution fusion | flops 545914880 | bytes 5505024 | tf_op jit(solution)/shard_map/dot_general | solution.py:238
  139.6 1.0 copy.112
  140.6 3.7 %all-to-all-start.5 = ((bf16[32,128,64]{1,2,0:T(8,128)(2,1)}), bf16[32,128,64]{1,2,0:T(8,128)(2,1)S(1)}, u32[]{:S(2)}, u32[]{:S(2)}) async-start(bf16[32,128,64]{1,2,0:T(8,128)(2,1)} %bitcast.40), calls=%async_computation.5 | async-start | bytes 1048576 | tf_op jit(solution)/shard_map/all_to_all | solution.py:240
  144.5 2.2 %collective-permute-start.4 = (bf16[128,32]{0,1:T(8,128)(2,1)S(1)}, bf16[128,32]{0,1:T(8,128)(2,1)S(1)}, u32[]{:S(2)}, u32[]{:S(2)}) collective-permute-start(bf16[128,32]{0,1:T(8,128)(2,1)S(1)} %pad_maximum_fusion.11), channel_id=1, source_target_pairs={{0,1},{1,0},{2,3},{3,2},{4,5},{5,4},{6,7},{7,6},{8,9},{9,8},{10,11... | collective-permute-start | bytes 24584 | tf_op jit(solution)/shard_map/ppermute | solution.py:179
  146.7 0.9 collective-permute-done.4
  147.6 13.5 %all-to-all-done.5 = bf16[32,128,64]{1,2,0:T(8,128)(2,1)S(1)} async-done(((bf16[32,128,64]{1,2,0:T(8,128)(2,1)}), bf16[32,128,64]{1,2,0:T(8,128)(2,1)S(1)}, u32[]{:S(2)}, u32[]{:S(2)}) %all-to-all-start.5) | async-done | bytes 524320 | tf_op jit(solution)/shard_map/all_to_all | solution.py:240
  162.1 11.7 %all-to-all-start.6 = ((bf16[16,2,512]{2,1,0:T(2,128)(2,1)}), bf16[16,2,512]{2,1,0:T(2,128)(2,1)S(1)}, u32[]{:S(2)}, u32[]{:S(2)}) async-start(bf16[16,2,512]{2,1,0:T(2,128)(2,1)} %reshape.468), calls=%async_computation.6 | async-start | bytes 65536 | tf_op jit(solution)/shard_map/all_to_all | solution.py:250
  174.4 10.7 %all-to-all-done.6 = bf16[16,2,512]{2,1,0:T(2,128)(2,1)S(1)} async-done(((bf16[16,2,512]{2,1,0:T(2,128)(2,1)}), bf16[16,2,512]{2,1,0:T(2,128)(2,1)S(1)}, u32[]{:S(2)}, u32[]{:S(2)}) %all-to-all-start.6) | async-done | bytes 32800 | tf_op jit(solution)/shard_map/all_to_all | solution.py:250
  185.3 1.5 scatter_fusion
  (133 shorter events, 15.8 us)
Async XLA Ops:
  0.6 4.6 %copy-start = (bf16[32,8,64]{2,1,0:T(8,128)(2,1)S(1)}, bf16[32,8,64]{2,1,0:T(8,128)(2,1)}, u32[]{:S(2)}) copy-start(bf16[32,8,64]{2,1,0:T(8,128)(2,1)} %param.17) | copy-start | bytes 98308
  0.6 24.8 %copy-start.1 = (bf16[2048,64]{0,1:T(8,128)(2,1)S(1)}, bf16[2048,64]{0,1:T(8,128)(2,1)}, u32[]{:S(2)}) copy-start(bf16[2048,64]{0,1:T(8,128)(2,1)} %param.24) | copy-start | bytes 786436
  0.7 24.8 %copy-start.9 = (bf16[2048,16]{0,1:T(8,128)(2,1)S(1)}, bf16[2048,16]{0,1:T(8,128)(2,1)}, u32[]{:S(2)}) copy-start(bf16[2048,16]{0,1:T(8,128)(2,1)} %param.26) | copy-start | bytes 196612
  0.7 30.6 %copy-start.2 = (bf16[2048,256]{1,0:T(8,128)(2,1)S(1)}, bf16[2048,256]{1,0:T(8,128)(2,1)}, u32[]{:S(2)}) copy-start(bf16[2048,256]{1,0:T(8,128)(2,1)} %param.29) | copy-start | bytes 3145732
  0.7 30.6 %copy-start.3 = (bf16[2048,256]{1,0:T(8,128)(2,1)S(1)}, bf16[2048,256]{1,0:T(8,128)(2,1)}, u32[]{:S(2)}) copy-start(bf16[2048,256]{1,0:T(8,128)(2,1)} %param.30) | copy-start | bytes 3145732
  1.5 4.3 %copy-start.17 = (s32[32]{0:T(128)}, s32[32]{0:T(128)S(1)}, u32[]{:S(2)}) copy-start(s32[32]{0:T(128)S(1)} %compare_select_fusion.2) | copy-start | bytes 388
  3.1 33.4 %copy-start.20 = (s32[2]{0:T(128)}, s32[2]{0:T(128)S(1)}, u32[]{:S(2)}) copy-start(s32[2]{0:T(128)S(1)} %get-tuple-element.26) | copy-start | bytes 28
  6.1 19.4 %copy-start.11 = (bf16[2048,16]{0,1:T(8,128)(2,1)S(1)}, bf16[2048,16]{0,1:T(8,128)(2,1)}, u32[]{:S(2)}) copy-start(bf16[2048,16]{0,1:T(8,128)(2,1)} %param.25) | copy-start | bytes 196612
  9.3 31.9 %all-to-all-start = ((bf16[16,2,4608]{2,1,0:T(2,128)(2,1)}), bf16[16,2,4608]{2,1,0:T(2,128)(2,1)S(1)}, u32[]{:S(2)}, u32[]{:S(2)}) async-start(bf16[16,2,4608]{2,1,0:T(2,128)(2,1)} %reshape.464), calls=%async_computation | async-start | bytes 589824 | tf_op jit(solution)/shard_map/all_to_all | solution.py:90
  26.3 9.5 %copy-start.15 = (bf16[2048]{0:T(1024)(128)(2,1)S(1)}, bf16[2048]{0:T(1024)(128)(2,1)}, u32[]{:S(2)}) copy-start(bf16[2048]{0:T(1024)(128)(2,1)} %param.23) | copy-start | bytes 12292
  26.3 10.2 %copy-start.19 = (s32[256]{0:T(256)S(1)}, s32[256]{0:T(256)}, u32[]{:S(2)}) copy-start(s32[256]{0:T(256)} %constant.245) | copy-start | bytes 3076
  26.3 13.2 %collective-permute-start = (bf16[2048,96]{0,1:T(8,128)(2,1)}, bf16[2048,96]{0,1:T(8,128)(2,1)}, u32[]{:S(2)}, u32[]{:S(2)}) collective-permute-start(bf16[2048,96]{0,1:T(8,128)(2,1)} %pad_maximum_fusion.4), channel_id=1, source_target_pairs={{0,1},{1,0},{2,3},{3,2},{4,5},{5,4},{6,7},{7,6},{8,9},{9,8},{10,11... | collective-permute-start | bytes 1179656 | tf_op jit(solution)/shard_map/ppermute | solution.py:117
  29.3 60.9 %collective-permute-start.1 = (bf16[64,2048]{1,0:T(8,128)(2,1)}, bf16[64,2048]{1,0:T(8,128)(2,1)}, u32[]{:S(2)}, u32[]{:S(2)}) collective-permute-start(bf16[64,2048]{1,0:T(8,128)(2,1)} %param.27), channel_id=1, source_target_pairs={{0,1},{1,0},{2,3},{3,2},{4,5},{5,4},{6,7},{7,6},{8,9},{9,8},{10,11... | collective-permute-start | bytes 786440 | tf_op jit(solution)/shard_map/ppermute | solution.py:214
  32.7 86.2 %collective-permute-start.2 = (bf16[2048,512]{1,0:T(8,128)(2,1)}, bf16[2048,512]{1,0:T(8,128)(2,1)S(1)}, u32[]{:S(2)}, u32[]{:S(2)}) collective-permute-start(bf16[2048,512]{1,0:T(8,128)(2,1)} %pad_maximum_fusion), channel_id=1, source_target_pairs={{0,1},{1,0},{2,3},{3,2},{4,5},{5,4},{6,7},{7,6},{8,9},{9,8},{10,11... | collective-permute-start | bytes 6291464 | tf_op jit(solution)/shard_map/ppermute | solution.py:223
  42.7 24.1 %all-to-all-start.1 = ((bf16[32,128,64]{1,2,0:T(8,128)(2,1)}), bf16[32,128,64]{1,2,0:T(8,128)(2,1)S(1)}, u32[]{:S(2)}, u32[]{:S(2)}) async-start(bf16[32,128,64]{1,2,0:T(8,128)(2,1)} %bitcast.4), calls=%async_computation.1 | async-start | bytes 1048576 | tf_op jit(solution)/shard_map/all_to_all | solution.py:129
  52.6 3.7 %copy-start.6 = (s32[32]{0:T(128)S(1)}, s32[32]{0:T(128)}, u32[]{:S(2)}) copy-start(s32[32]{0:T(128)} %constant.244) | copy-start | bytes 388
  54.2 13.2 %copy-start.10 = (bf16[2048,16]{0,1:T(8,128)(2,1)S(1)}, bf16[2048,16]{0,1:T(8,128)(2,1)}, u32[]{:S(2)}) copy-start(bf16[2048,16]{0,1:T(8,128)(2,1)} %param.26) | copy-start | bytes 196612
  54.2 13.2 %copy-start.12 = (bf16[2048,16]{0,1:T(8,128)(2,1)S(1)}, bf16[2048,16]{0,1:T(8,128)(2,1)}, u32[]{:S(2)}) copy-start(bf16[2048,16]{0,1:T(8,128)(2,1)} %param.25) | copy-start | bytes 196612
  54.2 13.2 %copy-start.14 = (bf16[2048,16]{0,1:T(8,128)(2,1)S(1)}, bf16[2048,16]{0,1:T(8,128)(2,1)}, u32[]{:S(2)}) copy-start(bf16[2048,16]{0,1:T(8,128)(2,1)} %get-tuple-element.31) | copy-start | bytes 196612
  67.1 10.8 %copy-start.8 = (f32[32,64]{1,0:T(8,128)S(1)}, f32[32,64]{1,0:T(8,128)}, u32[]{:S(2)}) copy-start(f32[32,64]{1,0:T(8,128)} %mul.206) | copy-start | bytes 24580
  74.2 12.4 %all-to-all-start.2 = ((bf16[32,2,1024]{2,1,0:T(2,128)(2,1)}), bf16[32,2,1024]{2,1,0:T(2,128)(2,1)S(1)}, u32[]{:S(2)}, u32[]{:S(2)}) async-start(bf16[32,2,1024]{2,1,0:T(2,128)(2,1)} %reshape.466), calls=%async_computation.2 | async-start | bytes 262144 | tf_op jit(solution)/shard_map/all_to_all | solution.py:149
  88.0 0.9 copy-start.22
  88.0 0.9 copy-start.23
  88.1 1.6 copy-start.13
  91.6 27.4 %copy-start.16 = (bf16[2048]{0:T(1024)(128)(2,1)S(1)}, bf16[2048]{0:T(1024)(128)(2,1)}, u32[]{:S(2)}) copy-start(bf16[2048]{0:T(1024)(128)(2,1)} %param.28) | copy-start | bytes 12292
  113.1 20.5 %all-to-all-start.4 = ((bf16[32,128,64]{1,2,0:T(8,128)(2,1)}), bf16[32,128,64]{1,2,0:T(8,128)(2,1)S(1)}, u32[]{:S(2)}, u32[]{:S(2)}) async-start(bf16[32,128,64]{1,2,0:T(8,128)(2,1)} %bitcast.36), calls=%async_computation.4 | async-start | bytes 1048576 | tf_op jit(solution)/shard_map/all_to_all | solution.py:232
  116.8 20.3 %collective-permute-start.3 = (bf16[256,2048]{1,0:T(8,128)(2,1)}, bf16[256,2048]{1,0:T(8,128)(2,1)}, u32[]{:S(2)}, u32[]{:S(2)}) collective-permute-start(bf16[256,2048]{1,0:T(8,128)(2,1)} %param.31), channel_id=1, source_target_pairs={{0,1},{1,0},{2,3},{3,2},{4,5},{5,4},{6,7},{7,6},{8,9},{9,8},{10,11... | collective-permute-start | bytes 3145736 | tf_op jit(solution)/shard_map/ppermute | solution.py:223
  134.2 2.9 %copy-start.4 = (bf16[2048,256]{1,0:T(8,128)(2,1)S(1)}, bf16[2048,256]{1,0:T(8,128)(2,1)}, u32[]{:S(2)}) copy-start(bf16[2048,256]{1,0:T(8,128)(2,1)} %param.30) | copy-start | bytes 3145732
  134.2 2.9 %copy-start.5 = (bf16[2048,256]{1,0:T(8,128)(2,1)S(1)}, bf16[2048,256]{1,0:T(8,128)(2,1)}, u32[]{:S(2)}) copy-start(bf16[2048,256]{1,0:T(8,128)(2,1)} %get-tuple-element.27) | copy-start | bytes 3145732
  139.6 4.8 %copy-start.21 = (s32[2]{0:T(128)S(1)}, s32[2]{0:T(128)}, u32[]{:S(2)}) copy-start(s32[2]{0:T(128)} %copy-done.20) | copy-start | bytes 28
  139.6 45.7 %copy-start.18 = (s32[32]{0:T(128)S(1)}, s32[32]{0:T(128)}, u32[]{:S(2)}) copy-start(s32[32]{0:T(128)} %copy-done.17) | copy-start | bytes 388
  140.6 20.5 %all-to-all-start.5 = ((bf16[32,128,64]{1,2,0:T(8,128)(2,1)}), bf16[32,128,64]{1,2,0:T(8,128)(2,1)S(1)}, u32[]{:S(2)}, u32[]{:S(2)}) async-start(bf16[32,128,64]{1,2,0:T(8,128)(2,1)} %bitcast.40), calls=%async_computation.5 | async-start | bytes 1048576 | tf_op jit(solution)/shard_map/all_to_all | solution.py:240
  144.5 3.1 %collective-permute-start.4 = (bf16[128,32]{0,1:T(8,128)(2,1)S(1)}, bf16[128,32]{0,1:T(8,128)(2,1)S(1)}, u32[]{:S(2)}, u32[]{:S(2)}) collective-permute-start(bf16[128,32]{0,1:T(8,128)(2,1)S(1)} %pad_maximum_fusion.11), channel_id=1, source_target_pairs={{0,1},{1,0},{2,3},{3,2},{4,5},{5,4},{6,7},{7,6},{8,9},{9,8},{10,11... | collective-permute-start | bytes 24584 | tf_op jit(solution)/shard_map/ppermute | solution.py:179
  162.1 23.0 %all-to-all-start.6 = ((bf16[16,2,512]{2,1,0:T(2,128)(2,1)}), bf16[16,2,512]{2,1,0:T(2,128)(2,1)S(1)}, u32[]{:S(2)}, u32[]{:S(2)}) async-start(bf16[16,2,512]{2,1,0:T(2,128)(2,1)} %reshape.468), calls=%async_computation.6 | async-start | bytes 65536 | tf_op jit(solution)/shard_map/all_to_all | solution.py:250
  186.8 0.6 copy-start.7

commit v10 on v9

--- a/solution.py
+++ b/solution.py
@@ -119,9 +119,12 @@
     w_key_chip = jnp.concatenate([w_key, w_qkv_sib[:, q_cols : q_cols + kv_cols]], axis=1)
     w_value_chip = jnp.concatenate([w_value, w_qkv_sib[:, q_cols + kv_cols :]], axis=1)
 
-    chosen = jnp.take(prefix_all, jnp.tile(owner_here, tp_count // 2), axis=0)
-    chosen = jnp.take_along_axis(
-        chosen, jnp.asarray(kv_of_dest).reshape(tp_count, 1, 1, 1), axis=2
+    per_kv = tp_count // KVH
+    chosen = jnp.stack(
+        [lax.dynamic_index_in_dim(prefix_all, owner_here[r], 0, keepdims=False) for r in range(local_reqs)]
+    ).transpose(2, 0, 1, 3)
+    chosen = jnp.broadcast_to(
+        chosen[:, None], (KVH, per_kv // local_reqs) + chosen.shape[1:]
     ).reshape(tp_count, prefix_rows, 2 * HD)
 
     state_req = routed_here
@@ -136,19 +139,14 @@
         normed, jnp.concatenate([w_key_chip, w_value_chip], axis=1), preferred_element_type=jnp.float32
     ).astype(jnp.bfloat16)
     chip_d = 2 * d_here
-    pick = (np.arange(d_here)[None, :] * KVH + kv_of_dest[:, None])
-    pick = np.concatenate(
-        [pick, kv_cols + pick, 2 * kv_cols + pick, 3 * kv_cols + pick], axis=1
-    )
-    kv_all = jnp.concatenate(
-        [kv_part[:, :kv_cols], kv_part[:, kv_cols : 2 * kv_cols],
-         kv_part[:, 2 * kv_cols : 3 * kv_cols], kv_part[:, 3 * kv_cols :]], axis=1
-    )
-    kv_sent = jnp.take(kv_all, pick.reshape(-1), axis=1).reshape(L_MAX, tp_count, 2 * chip_d)
+    kv_sent = kv_part.reshape(L_MAX, 4, d_here, KVH).transpose(3, 0, 1, 2).reshape(KVH, L_MAX, 2 * chip_d)
+    kv_sent = jnp.broadcast_to(kv_sent[:, None], (KVH, per_kv, L_MAX, 2 * chip_d)).reshape(
+        tp_count, L_MAX, 2 * chip_d
+    )
     prefix_split = chosen.shape[1] * chosen.shape[2]
     both = lax.all_to_all(
         jnp.concatenate(
-            [chosen.reshape(tp_count, -1), kv_sent.transpose(1, 0, 2).reshape(tp_count, -1)],
+            [chosen.reshape(tp_count, -1), kv_sent.reshape(tp_count, -1)],
             axis=1,
         ),
         "tensor", 0, 0, tiled=True,

time: 189 us -> 186 us (0.984)
  local copies, waits for them, and re-layouts: 27.9 us -> 19.6 us
  waiting for transfers between devices: 54.4 us -> 60.8 us
  other arithmetic: 16.2 us -> 11.7 us
  between operations: 2.15 us -> 6.27 us
    all_to_all x3, waiting for transfers between devices: 34.8 us -> 41.2 us  [shards(): got = lax.all_to_all(sent, 'tensor', 0, 0, tiled=True)]
    gather x4 -> x0, local copies, waits for them, and re-layouts: 5.79 us -> none  [the longest x2 2.56 us: shards(): jnp.take(kv_all, pick.reshape(-1), axis=1)]
    unnamed x61 -> x63, local copies, waits for them, and re-layouts: 5.31 us -> 5.31 us
  transfers between devices with their start and end apart: 11 -> 11, of which waited for: 6 -> 6; matrix products, arithmetic and copies ran while one was open for 20% -> 15% of each run, Pallas kernels for 0% -> 0%
where the time goes in v10:
time: 186 us; the launch traced here: 184 us
  waiting for transfers between devices  60.8 us (33%)
  starting transfers between devices  58.1 us (31%)
  blocking collectives  20.2 us (11%)
  local copies, waits for them, and re-layouts  19.6 us (11%)
  other arithmetic  11.7 us (6%)
  matrix products  7.75 us (4%)
  between operations  6.27 us (3%)
    all_to_all x3, waiting for transfers between devices, shards(): got = lax.all_to_all(sent, 'tensor', 0, 0, tiled=True)  41.2 us
    all_to_all x1, blocking collectives, shards(): got = lax.all_to_all(sent, 'tensor', 0, 0, tiled=True)  20.2 us
    all_to_all x1, starting transfers between devices, shards(): lax.all_to_all(jnp.concatenate([state_part, prefix_part], axis=1), 'dp',...  16.2 us
    all_to_all x3, starting transfers between devices, shards(): got = lax.all_to_all(sent, 'tensor', 0, 0, tiled=True)  14.7 us
    all_to_all x1, starting transfers between devices, shards(): lax.all_to_all(result, 'dp', split_axis=1, concat_axis=0, tiled=True)  11.7 us
    all_to_all x1, waiting for transfers between devices, shards(): lax.all_to_all(result, 'dp', split_axis=1, concat_axis=0, tiled=True)  10.7 us
    all_to_all x1, waiting for transfers between devices, shards(): lax.all_to_all(jnp.concatenate([chosen.reshape(tp_count, -1), kv_sent.res...  8.05 us
    unnamed x63, local copies, waits for them, and re-layouts  5.31 us
  transfers between devices with their start and end apart: 11, of which 6 were waited for; matrix products, arithmetic and copies ran while one was open for 15% of the time, Pallas kernels for 0%

profile of v10, /device:TPU:1, one launch (start us, length us, event | category | flops | bytes accessed | tf_op | source)
XLA Modules:
  0.0 184.4 jit_solution(12402220473626057883)
XLA Ops:
  0.7 0.8 compare_select_fusion
  1.5 0.7 compare_and_fusion
  2.2 0.6 gather_fusion
  3.0 0.7 copy.132
  4.3 0.8 reduce.4
  5.0 0.9 reshape.366
  6.0 16.2 %all-to-all-start = ((bf16[16,2,4608]{2,1,0:T(2,128)(2,1)}), bf16[16,2,4608]{2,1,0:T(2,128)(2,1)S(1)}, u32[]{:S(2)}, u32[]{:S(2)}) async-start(bf16[16,2,4608]{2,1,0:T(2,128)(2,1)} %reshape.366), calls=%async_computation | async-start | bytes 589824 | tf_op jit(solution)/shard_map/all_to_all | solution.py:90
  22.3 3.0 %collective-permute-start = (bf16[2048,96]{0,1:T(8,128)(2,1)S(1)}, bf16[2048,96]{0,1:T(8,128)(2,1)S(1)}, u32[]{:S(2)}, u32[]{:S(2)}) collective-permute-start(bf16[2048,96]{0,1:T(8,128)(2,1)S(1)} %pad_maximum_fusion.4), channel_id=1, source_target_pairs={{0,1},{1,0},{2,3},{3,2},{4,5},{5,4},{6,7},{7,6},{8,9},{9,8},{10,11... | collective-permute-start | bytes 1179656 | tf_op jit(solution)/shard_map/ppermute | solution.py:117
  25.3 1.9 %collective-permute-start.1 = (bf16[64,2048]{1,0:T(8,128)(2,1)}, bf16[64,2048]{1,0:T(8,128)(2,1)}, u32[]{:S(2)}, u32[]{:S(2)}) collective-permute-start(bf16[64,2048]{1,0:T(8,128)(2,1)} %param.25), channel_id=1, source_target_pairs={{0,1},{1,0},{2,3},{3,2},{4,5},{5,4},{6,7},{7,6},{8,9},{9,8},{10,11... | collective-permute-start | bytes 786440 | tf_op jit(solution)/shard_map/ppermute | solution.py:212
  27.3 1.5 pad_maximum_fusion
  28.7 2.4 %collective-permute-start.2 = (bf16[2048,512]{1,0:T(8,128)(2,1)}, bf16[2048,512]{1,0:T(8,128)(2,1)}, u32[]{:S(2)}, u32[]{:S(2)}) collective-permute-start(bf16[2048,512]{1,0:T(8,128)(2,1)} %pad_maximum_fusion), channel_id=1, source_target_pairs={{0,1},{1,0},{2,3},{3,2},{4,5},{5,4},{6,7},{7,6},{8,9},{9,8},{10,11... | collective-permute-start | bytes 6291464 | tf_op jit(solution)/shard_map/ppermute | solution.py:221
  31.6 0.7 fusion.72
  35.0 0.6 convert_element_type.134
  35.7 0.6 dynamic-slice.5
  38.3 0.5 add_convert_fusion.3
  39.3 0.6 fusion.39
  40.6 0.9 tile.16
  41.5 7.3 %all-to-all-start.1 = ((bf16[32,128,64]{1,2,0:T(8,128)(2,1)}), bf16[32,128,64]{1,2,0:T(8,128)(2,1)S(1)}, u32[]{:S(2)}, u32[]{:S(2)}) async-start(bf16[32,128,64]{1,2,0:T(8,128)(2,1)} %bitcast.4), calls=%async_computation.1 | async-start | bytes 1048576 | tf_op jit(solution)/shard_map/all_to_all | solution.py:132
  49.1 0.6 copy.130
  49.7 15.9 %all-to-all-done.1 = bf16[32,128,64]{1,2,0:T(8,128)(2,1)S(1)} async-done(((bf16[32,128,64]{1,2,0:T(8,128)(2,1)}), bf16[32,128,64]{1,2,0:T(8,128)(2,1)S(1)}, u32[]{:S(2)}, u32[]{:S(2)}) %all-to-all-start.1) | async-done | bytes 524320 | tf_op jit(solution)/shard_map/all_to_all | solution.py:132
  65.9 1.0 fusion.19
  67.6 1.5 reshape_reshape.15
  69.1 0.9 maximum_bitcast_fusion.1
  70.0 0.6 reduce.5
  70.6 0.7 reshape.368
  71.3 3.7 %all-to-all-start.2 = ((bf16[32,2,1024]{2,1,0:T(2,128)(2,1)}), bf16[32,2,1024]{2,1,0:T(2,128)(2,1)S(1)}, u32[]{:S(2)}, u32[]{:S(2)}) async-start(bf16[32,2,1024]{2,1,0:T(2,128)(2,1)} %reshape.368), calls=%async_computation.2 | async-start | bytes 262144 | tf_op jit(solution)/shard_map/all_to_all | solution.py:147
  75.6 8.0 %all-to-all-done.2 = bf16[32,2,1024]{2,1,0:T(2,128)(2,1)S(1)} async-done(((bf16[32,2,1024]{2,1,0:T(2,128)(2,1)}), bf16[32,2,1024]{2,1,0:T(2,128)(2,1)S(1)}, u32[]{:S(2)}, u32[]{:S(2)}) %all-to-all-start.2) | async-done | bytes 131104 | tf_op jit(solution)/shard_map/all_to_all | solution.py:147
  83.9 1.2 reshape.271
  87.4 1.3 convolution_convert_fusion.1
  89.0 20.2 %all_to_all.62 = bf16[32,128,64]{1,2,0:T(8,128)(2,1)S(1)} all-to-all(bf16[32,128,64]{1,2,0:T(8,128)(2,1)S(1)} %bitcast.128), channel_id=1, replica_groups=mesh['dp'=16,'tensor'=32] {'tensor'}, dimensions={0} | all-to-all | bytes 1048576 | tf_op jit(solution)/shard_map/all_to_all | solution.py:216
  109.2 0.9 tile.18
  110.2 3.7 %all-to-all-start.4 = ((bf16[32,128,64]{1,2,0:T(8,128)(2,1)}), bf16[32,128,64]{1,2,0:T(8,128)(2,1)S(1)}, u32[]{:S(2)}, u32[]{:S(2)}) async-start(bf16[32,128,64]{1,2,0:T(8,128)(2,1)} %bitcast.37), calls=%async_computation.4 | async-start | bytes 1048576 | tf_op jit(solution)/shard_map/all_to_all | solution.py:230
  113.9 2.3 %collective-permute-start.3 = (bf16[256,2048]{1,0:T(8,128)(2,1)}, bf16[256,2048]{1,0:T(8,128)(2,1)}, u32[]{:S(2)}, u32[]{:S(2)}) collective-permute-start(bf16[256,2048]{1,0:T(8,128)(2,1)} %param.29), channel_id=1, source_target_pairs={{0,1},{1,0},{2,3},{3,2},{4,5},{5,4},{6,7},{7,6},{8,9},{9,8},{10,11... | collective-permute-start | bytes 3145736 | tf_op jit(solution)/shard_map/ppermute | solution.py:221
  116.2 2.6 %fusion.68 = (bf16[2048,256]{1,0:T(8,128)(2,1)S(1)}, bf16[2048,256]{1,0:T(8,128)(2,1)}) fusion(bf16[2048,512]{1,0:T(8,128)(2,1)} %collective-permute-done.2), kind=kLoop, calls=%fused_computation.133 | loop fusion | bytes 4194304 | tf_op jit(solution)/shard_map/slice | solution.py:226
  118.9 11.8 %all-to-all-done.4 = bf16[32,128,64]{1,2,0:T(8,128)(2,1)S(1)} async-done(((bf16[32,128,64]{1,2,0:T(8,128)(2,1)}), bf16[32,128,64]{1,2,0:T(8,128)(2,1)S(1)}, u32[]{:S(2)}, u32[]{:S(2)}) %all-to-all-start.4) | async-done | bytes 524320 | tf_op jit(solution)/shard_map/all_to_all | solution.py:230
  131.3 2.6 %fusion.1 = f32[128,512]{1,0:T(8,128)} fusion(bf16[128,2048]{0,1:T(8,128)(2,1)S(1)} %fusion.17, bf16[2048,256]{1,0:T(8,128)(2,1)S(1)} %copy-done.2, bf16[2048,256]{1,0:T(8,128)(2,1)} %get-tuple-element.28), kind=kOutput, calls=%fused_computation.7 | convolution fusion | flops 272629760 | bytes 2883584 | tf_op jit(solution)/shard_map/dot_general | solution.py:233
  133.9 2.7 %convolution_convert_fusion = bf16[128,2048]{1,0:T(8,128)(2,1)S(1)} fusion(bf16[256,2048]{1,0:T(8,128)(2,1)} %collective-permute-done.3, bf16[256,2048]{1,0:T(8,128)(2,1)} %param.29, f32[128,512]{1,0:T(8,128)} %fusion.1, bf16[128,2048]{0,1:T(8,128)(2,1)} %copy-done.5, bf16[2048,256]{1,0:T(8,128)(2,1)S(1)} %get-tuple-element.27, ...), kind=kOutput, calls=%fused_computation.3 | convolution fusion | flops 545914880 | bytes 5505024 | tf_op jit(solution)/shard_map/dot_general | solution.py:236
  136.6 1.0 copy.108
  137.6 3.7 %all-to-all-start.5 = ((bf16[32,128,64]{1,2,0:T(8,128)(2,1)}), bf16[32,128,64]{1,2,0:T(8,128)(2,1)S(1)}, u32[]{:S(2)}, u32[]{:S(2)}) async-start(bf16[32,128,64]{1,2,0:T(8,128)(2,1)} %bitcast.41), calls=%async_computation.5 | async-start | bytes 1048576 | tf_op jit(solution)/shard_map/all_to_all | solution.py:238
  141.5 2.2 %collective-permute-start.4 = (bf16[128,32]{0,1:T(8,128)(2,1)S(1)}, bf16[128,32]{0,1:T(8,128)(2,1)S(1)}, u32[]{:S(2)}, u32[]{:S(2)}) collective-permute-start(bf16[128,32]{0,1:T(8,128)(2,1)S(1)} %pad_maximum_fusion.11), channel_id=1, source_target_pairs={{0,1},{1,0},{2,3},{3,2},{4,5},{5,4},{6,7},{7,6},{8,9},{9,8},{10,11... | collective-permute-start | bytes 24584 | tf_op jit(solution)/shard_map/ppermute | solution.py:177
  143.7 0.9 collective-permute-done.4
  144.6 13.5 %all-to-all-done.5 = bf16[32,128,64]{1,2,0:T(8,128)(2,1)S(1)} async-done(((bf16[32,128,64]{1,2,0:T(8,128)(2,1)}), bf16[32,128,64]{1,2,0:T(8,128)(2,1)S(1)}, u32[]{:S(2)}, u32[]{:S(2)}) %all-to-all-start.5) | async-done | bytes 524320 | tf_op jit(solution)/shard_map/all_to_all | solution.py:238
  158.4 0.7 reshape.370
  159.1 11.7 %all-to-all-start.6 = ((bf16[16,2,512]{2,1,0:T(2,128)(2,1)}), bf16[16,2,512]{2,1,0:T(2,128)(2,1)S(1)}, u32[]{:S(2)}, u32[]{:S(2)}) async-start(bf16[16,2,512]{2,1,0:T(2,128)(2,1)} %reshape.370), calls=%async_computation.6 | async-start | bytes 65536 | tf_op jit(solution)/shard_map/all_to_all | solution.py:248
  170.8 0.6 slice_select_fusion
  171.4 10.7 %all-to-all-done.6 = bf16[16,2,512]{2,1,0:T(2,128)(2,1)S(1)} async-done(((bf16[16,2,512]{2,1,0:T(2,128)(2,1)}), bf16[16,2,512]{2,1,0:T(2,128)(2,1)S(1)}, u32[]{:S(2)}, u32[]{:S(2)}) %all-to-all-start.6) | async-done | bytes 32800 | tf_op jit(solution)/shard_map/all_to_all | solution.py:248
  182.3 1.5 scatter_fusion
  183.8 0.6 copy-done.6
  (129 shorter events, 8.1 us)
Async XLA Ops:
  0.6 1.6 copy-start
  0.6 21.5 %copy-start.1 = (bf16[2048,64]{0,1:T(8,128)(2,1)S(1)}, bf16[2048,64]{0,1:T(8,128)(2,1)}, u32[]{:S(2)}) copy-start(bf16[2048,64]{0,1:T(8,128)(2,1)} %param.22) | copy-start | bytes 786436
  0.7 21.5 %copy-start.10 = (bf16[2048,16]{0,1:T(8,128)(2,1)S(1)}, bf16[2048,16]{0,1:T(8,128)(2,1)}, u32[]{:S(2)}) copy-start(bf16[2048,16]{0,1:T(8,128)(2,1)} %param.23) | copy-start | bytes 196612
  0.7 21.5 %copy-start.8 = (bf16[2048,16]{0,1:T(8,128)(2,1)S(1)}, bf16[2048,16]{0,1:T(8,128)(2,1)}, u32[]{:S(2)}) copy-start(bf16[2048,16]{0,1:T(8,128)(2,1)} %param.24) | copy-start | bytes 196612
  0.7 26.6 %copy-start.2 = (bf16[2048,256]{1,0:T(8,128)(2,1)S(1)}, bf16[2048,256]{1,0:T(8,128)(2,1)}, u32[]{:S(2)}) copy-start(bf16[2048,256]{1,0:T(8,128)(2,1)} %param.27) | copy-start | bytes 3145732
  0.7 26.6 %copy-start.3 = (bf16[2048,256]{1,0:T(8,128)(2,1)S(1)}, bf16[2048,256]{1,0:T(8,128)(2,1)}, u32[]{:S(2)}) copy-start(bf16[2048,256]{1,0:T(8,128)(2,1)} %param.28) | copy-start | bytes 3145732
  1.5 0.7 copy-start.15
  6.0 34.0 %all-to-all-start = ((bf16[16,2,4608]{2,1,0:T(2,128)(2,1)}), bf16[16,2,4608]{2,1,0:T(2,128)(2,1)S(1)}, u32[]{:S(2)}, u32[]{:S(2)}) async-start(bf16[16,2,4608]{2,1,0:T(2,128)(2,1)} %reshape.366), calls=%async_computation | async-start | bytes 589824 | tf_op jit(solution)/shard_map/all_to_all | solution.py:90
  22.2 8.9 %copy-start.23 = (s32[32]{0:T(128)S(1)}, s32[32]{0:T(128)}, u32[]{:S(2)}) copy-start(s32[32]{0:T(128)} %param.19) | copy-start | bytes 388
  22.3 9.0 %copy-start.17 = (s32[32,1]{0,1:T(1,128)S(1)}, s32[32,1]{0,1:T(1,128)}, u32[]{:S(2)}) copy-start(s32[32,1]{0,1:T(1,128)} %param.17) | copy-start | bytes 388
  22.3 9.0 %copy-start.18 = (s32[32]{0:T(128)S(1)}, s32[32]{0:T(128)}, u32[]{:S(2)}) copy-start(s32[32]{0:T(128)} %param.16) | copy-start | bytes 388
  22.3 9.2 %copy-start.24 = (s32[16]{0:T(128)S(1)}, s32[16]{0:T(128)}, u32[]{:S(2)}) copy-start(s32[16]{0:T(128)} %param.18) | copy-start | bytes 196
  22.3 12.7 %copy-start.13 = (bf16[2048]{0:T(1024)(128)(2,1)S(1)}, bf16[2048]{0:T(1024)(128)(2,1)}, u32[]{:S(2)}) copy-start(bf16[2048]{0:T(1024)(128)(2,1)} %param.21) | copy-start | bytes 12292
  22.3 17.7 %collective-permute-start = (bf16[2048,96]{0,1:T(8,128)(2,1)S(1)}, bf16[2048,96]{0,1:T(8,128)(2,1)S(1)}, u32[]{:S(2)}, u32[]{:S(2)}) collective-permute-start(bf16[2048,96]{0,1:T(8,128)(2,1)S(1)} %pad_maximum_fusion.4), channel_id=1, source_target_pairs={{0,1},{1,0},{2,3},{3,2},{4,5},{5,4},{6,7},{7,6},{8,9},{9,8},{10,11... | collective-permute-start | bytes 1179656 | tf_op jit(solution)/shard_map/ppermute | solution.py:117
  25.3 62.1 %collective-permute-start.1 = (bf16[64,2048]{1,0:T(8,128)(2,1)}, bf16[64,2048]{1,0:T(8,128)(2,1)}, u32[]{:S(2)}, u32[]{:S(2)}) collective-permute-start(bf16[64,2048]{1,0:T(8,128)(2,1)} %param.25), channel_id=1, source_target_pairs={{0,1},{1,0},{2,3},{3,2},{4,5},{5,4},{6,7},{7,6},{8,9},{9,8},{10,11... | collective-permute-start | bytes 786440 | tf_op jit(solution)/shard_map/ppermute | solution.py:212
  28.7 87.5 %collective-permute-start.2 = (bf16[2048,512]{1,0:T(8,128)(2,1)}, bf16[2048,512]{1,0:T(8,128)(2,1)}, u32[]{:S(2)}, u32[]{:S(2)}) collective-permute-start(bf16[2048,512]{1,0:T(8,128)(2,1)} %pad_maximum_fusion), channel_id=1, source_target_pairs={{0,1},{1,0},{2,3},{3,2},{4,5},{5,4},{6,7},{7,6},{8,9},{9,8},{10,11... | collective-permute-start | bytes 6291464 | tf_op jit(solution)/shard_map/ppermute | solution.py:221
  31.4 9.0 %copy-start.19 = (s32[2]{0:T(128)}, s32[2]{0:T(128)S(1)}, u32[]{:S(2)}) copy-start(s32[2]{0:T(128)S(1)} %get-tuple-element.26) | copy-start | bytes 28
  41.5 24.1 %all-to-all-start.1 = ((bf16[32,128,64]{1,2,0:T(8,128)(2,1)}), bf16[32,128,64]{1,2,0:T(8,128)(2,1)S(1)}, u32[]{:S(2)}, u32[]{:S(2)}) async-start(bf16[32,128,64]{1,2,0:T(8,128)(2,1)} %bitcast.4), calls=%async_computation.1 | async-start | bytes 1048576 | tf_op jit(solution)/shard_map/all_to_all | solution.py:132
  48.8 18.1 %copy-start.9 = (bf16[2048,16]{0,1:T(8,128)(2,1)S(1)}, bf16[2048,16]{0,1:T(8,128)(2,1)}, u32[]{:S(2)}) copy-start(bf16[2048,16]{0,1:T(8,128)(2,1)} %param.24) | copy-start | bytes 196612
  48.9 18.1 %copy-start.11 = (bf16[2048,16]{0,1:T(8,128)(2,1)S(1)}, bf16[2048,16]{0,1:T(8,128)(2,1)}, u32[]{:S(2)}) copy-start(bf16[2048,16]{0,1:T(8,128)(2,1)} %param.23) | copy-start | bytes 196612
  71.3 12.4 %all-to-all-start.2 = ((bf16[32,2,1024]{2,1,0:T(2,128)(2,1)}), bf16[32,2,1024]{2,1,0:T(2,128)(2,1)S(1)}, u32[]{:S(2)}, u32[]{:S(2)}) async-start(bf16[32,2,1024]{2,1,0:T(2,128)(2,1)} %reshape.368), calls=%async_computation.2 | async-start | bytes 262144 | tf_op jit(solution)/shard_map/all_to_all | solution.py:147
  85.1 0.9 copy-start.21
  85.1 0.9 copy-start.22
  85.2 1.6 copy-start.12
  85.9 1.5 copy-start.7
  88.7 27.5 %copy-start.14 = (bf16[2048]{0:T(1024)(128)(2,1)S(1)}, bf16[2048]{0:T(1024)(128)(2,1)}, u32[]{:S(2)}) copy-start(bf16[2048]{0:T(1024)(128)(2,1)} %param.26) | copy-start | bytes 12292
  110.2 20.5 %all-to-all-start.4 = ((bf16[32,128,64]{1,2,0:T(8,128)(2,1)}), bf16[32,128,64]{1,2,0:T(8,128)(2,1)S(1)}, u32[]{:S(2)}, u32[]{:S(2)}) async-start(bf16[32,128,64]{1,2,0:T(8,128)(2,1)} %bitcast.37), calls=%async_computation.4 | async-start | bytes 1048576 | tf_op jit(solution)/shard_map/all_to_all | solution.py:230
  113.9 20.1 %collective-permute-start.3 = (bf16[256,2048]{1,0:T(8,128)(2,1)}, bf16[256,2048]{1,0:T(8,128)(2,1)}, u32[]{:S(2)}, u32[]{:S(2)}) collective-permute-start(bf16[256,2048]{1,0:T(8,128)(2,1)} %param.29), channel_id=1, source_target_pairs={{0,1},{1,0},{2,3},{3,2},{4,5},{5,4},{6,7},{7,6},{8,9},{9,8},{10,11... | collective-permute-start | bytes 3145736 | tf_op jit(solution)/shard_map/ppermute | solution.py:221
  131.3 2.6 %copy-start.5 = (bf16[128,2048]{0,1:T(8,128)(2,1)}, bf16[128,2048]{0,1:T(8,128)(2,1)S(1)}, u32[]{:S(2)}) copy-start(bf16[128,2048]{0,1:T(8,128)(2,1)S(1)} %fusion.17) | copy-start | bytes 1572868
  131.3 2.6 %copy-start.4 = (bf16[2048,256]{1,0:T(8,128)(2,1)S(1)}, bf16[2048,256]{1,0:T(8,128)(2,1)}, u32[]{:S(2)}) copy-start(bf16[2048,256]{1,0:T(8,128)(2,1)} %param.28) | copy-start | bytes 3145732
  136.6 4.8 %copy-start.20 = (s32[2]{0:T(128)S(1)}, s32[2]{0:T(128)}, u32[]{:S(2)}) copy-start(s32[2]{0:T(128)} %copy-done.19) | copy-start | bytes 28
  136.6 45.7 %copy-start.16 = (s32[32]{0:T(128)S(1)}, s32[32]{0:T(128)}, u32[]{:S(2)}) copy-start(s32[32]{0:T(128)} %copy-done.15) | copy-start | bytes 388
  137.6 20.5 %all-to-all-start.5 = ((bf16[32,128,64]{1,2,0:T(8,128)(2,1)}), bf16[32,128,64]{1,2,0:T(8,128)(2,1)S(1)}, u32[]{:S(2)}, u32[]{:S(2)}) async-start(bf16[32,128,64]{1,2,0:T(8,128)(2,1)} %bitcast.41), calls=%async_computation.5 | async-start | bytes 1048576 | tf_op jit(solution)/shard_map/all_to_all | solution.py:238
  141.5 3.1 %collective-permute-start.4 = (bf16[128,32]{0,1:T(8,128)(2,1)S(1)}, bf16[128,32]{0,1:T(8,128)(2,1)S(1)}, u32[]{:S(2)}, u32[]{:S(2)}) collective-permute-start(bf16[128,32]{0,1:T(8,128)(2,1)S(1)} %pad_maximum_fusion.11), channel_id=1, source_target_pairs={{0,1},{1,0},{2,3},{3,2},{4,5},{5,4},{6,7},{7,6},{8,9},{9,8},{10,11... | collective-permute-start | bytes 24584 | tf_op jit(solution)/shard_map/ppermute | solution.py:177
  159.1 23.0 %all-to-all-start.6 = ((bf16[16,2,512]{2,1,0:T(2,128)(2,1)}), bf16[16,2,512]{2,1,0:T(2,128)(2,1)S(1)}, u32[]{:S(2)}, u32[]{:S(2)}) async-start(bf16[16,2,512]{2,1,0:T(2,128)(2,1)} %reshape.370), calls=%async_computation.6 | async-start | bytes 65536 | tf_op jit(solution)/shard_map/all_to_all | solution.py:248
  183.8 0.6 copy-start.6

commit v11 on v10

--- a/solution.py
+++ b/solution.py
@@ -1,10 +1,8 @@
 import jax
 import jax.numpy as jnp
-import numpy as np
 from jax import lax
 from jax.sharding import PartitionSpec as P
 
-H = 32
 KVH = 8
 HD = 64
 L_MAX = 128
@@ -33,22 +31,7 @@
     )
 
 
-def gather_rows(shard, axis_name, count):
-    sent = jnp.broadcast_to(shard[None], (count,) + shard.shape)
-    got = lax.all_to_all(sent, axis_name, 0, 0, tiled=True)
-    rows, width = shard.shape
-    return got.transpose(1, 0, 2).reshape(rows, count * width)
-
-
-def scatter_sum(terms, axis_name, count):
-    rows, width = terms.shape
-    share = width // count
-    sent = terms.astype(jnp.bfloat16).reshape(rows, count, share).transpose(1, 0, 2)
-    got = lax.all_to_all(sent, axis_name, 0, 0, tiled=True)
-    return jnp.sum(got.astype(jnp.float32), axis=0)
-
-
-def shards(
+def layer(
     suffix_states,
     suffix_lengths,
     request_group,
@@ -73,13 +56,10 @@
     local_reqs = total_reqs // dp_count
     row_count = local_reqs * L_MAX
     heads_here = w_query.shape[1] // HD
-    group_size = H // KVH
     assert heads_here == 1 and local_reqs == 2
     kv_cols = w_key.shape[1]
     d_here = kv_cols // KVH
     score_scale = HD ** (-0.5)
-    kv_of_dest = np.arange(tp_count) * heads_here // group_size
-    kv_here = tp_index * heads_here // group_size
 
     routed = jnp.take(suffix_states, request_order, axis=0)
     pos_here = routed.shape[1]
@@ -144,20 +124,14 @@
         tp_count, L_MAX, 2 * chip_d
     )
     prefix_split = chosen.shape[1] * chosen.shape[2]
-    both = lax.all_to_all(
-        jnp.concatenate(
-            [chosen.reshape(tp_count, -1), kv_sent.reshape(tp_count, -1)],
-            axis=1,
-        ),
-        "tensor", 0, 0, tiled=True,
-    )
+    packed = jnp.concatenate([chosen.reshape(tp_count, -1), kv_sent.reshape(tp_count, -1)], axis=1)
+    both = lax.all_to_all(packed, "tensor", 0, 0, tiled=True)
     picked = both[:, :prefix_split].reshape(tp_count, prefix_rows, 2 * HD)
     picked = picked.reshape(tp_count * prefix_rows, 2 * HD)
     prefix_keys = picked[:, :HD]
     prefix_values = picked[:, HD:]
     kv_got = both[:, prefix_split:].reshape(tp_count // 2, 2, L_MAX, 2 * chip_d)
     kv_got = jnp.take(kv_got, core, axis=1)
-    src_t = (np.arange(tp_count // 2) * 2)[:, None]
     keys4 = kv_got[:, :, : 2 * d_here].reshape(tp_count // 2, L_MAX, 2, d_here)
     vals4 = kv_got[:, :, 2 * d_here :].reshape(tp_count // 2, L_MAX, 2, d_here)
     flip = core == 1
@@ -269,4 +243,4 @@
         P("tensor", None),
     )
     out_specs = (P(None, "dp", "tensor"), P("dp", None, "tensor"), P("dp", None, "tensor"))
-    return jax.shard_map(shards, mesh=mesh, in_specs=in_specs, out_specs=out_specs, check_vma=False)
+    return jax.shard_map(layer, mesh=mesh, in_specs=in_specs, out_specs=out_specs, check_vma=False)

time: 186 us -> 186 us (level)
  no operation moved by 1% of the time
where the time goes in v11:
time: 186 us; the launch traced here: 184 us
  waiting for transfers between devices  60.8 us (33%)
  starting transfers between devices  58.1 us (31%)
  blocking collectives  20.2 us (11%)
  local copies, waits for them, and re-layouts  19.6 us (11%)
  other arithmetic  11.7 us (6%)
  matrix products  7.75 us (4%)
  between operations  6.27 us (3%)
    all_to_all x3, waiting for transfers between devices, layer(): got = lax.all_to_all(sent, 'tensor', 0, 0, tiled=True)  41.2 us
    all_to_all x1, blocking collectives, layer(): got = lax.all_to_all(sent, 'tensor', 0, 0, tiled=True)  20.2 us
    all_to_all x1, starting transfers between devices, layer(): lax.all_to_all(jnp.concatenate([state_part, prefix_part], axis=1), 'dp',...  16.2 us
    all_to_all x3, starting transfers between devices, layer(): got = lax.all_to_all(sent, 'tensor', 0, 0, tiled=True)  14.7 us
    all_to_all x1, starting transfers between devices, layer(): lax.all_to_all(result, 'dp', split_axis=1, concat_axis=0, tiled=True)  11.7 us
    all_to_all x1, waiting for transfers between devices, layer(): lax.all_to_all(result, 'dp', split_axis=1, concat_axis=0, tiled=True)  10.7 us
    all_to_all x1, waiting for transfers between devices, layer(): both = lax.all_to_all(packed, 'tensor', 0, 0, tiled=True)  8.05 us
    unnamed x63, local copies, waits for them, and re-layouts  5.31 us
  transfers between devices with their start and end apart: 11, of which 6 were waited for; matrix products, arithmetic and copies ran while one was open for 15% of the time, Pallas kernels for 0%

profile of v11, /device:TPU:1, one launch (start us, length us, event | category | flops | bytes accessed | tf_op | source)
XLA Modules:
  0.0 184.4 jit_solution(12402220473626057883)
XLA Ops:
  0.7 0.8 compare_select_fusion
  1.5 0.7 compare_and_fusion
  2.2 0.6 gather_fusion
  3.0 0.7 copy.132
  4.3 0.8 reduce.4
  5.0 0.9 reshape.366
  6.0 16.2 %all-to-all-start = ((bf16[16,2,4608]{2,1,0:T(2,128)(2,1)}), bf16[16,2,4608]{2,1,0:T(2,128)(2,1)S(1)}, u32[]{:S(2)}, u32[]{:S(2)}) async-start(bf16[16,2,4608]{2,1,0:T(2,128)(2,1)} %reshape.366), calls=%async_computation | async-start | bytes 589824 | tf_op jit(solution)/shard_map/all_to_all | solution.py:70
  22.3 3.0 %collective-permute-start = (bf16[2048,96]{0,1:T(8,128)(2,1)S(1)}, bf16[2048,96]{0,1:T(8,128)(2,1)S(1)}, u32[]{:S(2)}, u32[]{:S(2)}) collective-permute-start(bf16[2048,96]{0,1:T(8,128)(2,1)S(1)} %pad_maximum_fusion.4), channel_id=1, source_target_pairs={{0,1},{1,0},{2,3},{3,2},{4,5},{5,4},{6,7},{7,6},{8,9},{9,8},{10,11... | collective-permute-start | bytes 1179656 | tf_op jit(solution)/shard_map/ppermute | solution.py:97
  25.3 1.9 %collective-permute-start.1 = (bf16[64,2048]{1,0:T(8,128)(2,1)}, bf16[64,2048]{1,0:T(8,128)(2,1)}, u32[]{:S(2)}, u32[]{:S(2)}) collective-permute-start(bf16[64,2048]{1,0:T(8,128)(2,1)} %param.25), channel_id=1, source_target_pairs={{0,1},{1,0},{2,3},{3,2},{4,5},{5,4},{6,7},{7,6},{8,9},{9,8},{10,11... | collective-permute-start | bytes 786440 | tf_op jit(solution)/shard_map/ppermute | solution.py:186
  27.3 1.5 pad_maximum_fusion
  28.7 2.4 %collective-permute-start.2 = (bf16[2048,512]{1,0:T(8,128)(2,1)}, bf16[2048,512]{1,0:T(8,128)(2,1)}, u32[]{:S(2)}, u32[]{:S(2)}) collective-permute-start(bf16[2048,512]{1,0:T(8,128)(2,1)} %pad_maximum_fusion), channel_id=1, source_target_pairs={{0,1},{1,0},{2,3},{3,2},{4,5},{5,4},{6,7},{7,6},{8,9},{9,8},{10,11... | collective-permute-start | bytes 6291464 | tf_op jit(solution)/shard_map/ppermute | solution.py:195
  31.6 0.7 fusion.72
  35.0 0.6 convert_element_type.134
  35.7 0.6 dynamic-slice.5
  38.3 0.5 add_convert_fusion.3
  39.3 0.6 fusion.39
  40.6 0.9 tile.16
  41.5 7.3 %all-to-all-start.1 = ((bf16[32,128,64]{1,2,0:T(8,128)(2,1)}), bf16[32,128,64]{1,2,0:T(8,128)(2,1)S(1)}, u32[]{:S(2)}, u32[]{:S(2)}) async-start(bf16[32,128,64]{1,2,0:T(8,128)(2,1)} %bitcast.4), calls=%async_computation.1 | async-start | bytes 1048576 | tf_op jit(solution)/shard_map/all_to_all | solution.py:112
  49.1 0.6 copy.130
  49.7 15.9 %all-to-all-done.1 = bf16[32,128,64]{1,2,0:T(8,128)(2,1)S(1)} async-done(((bf16[32,128,64]{1,2,0:T(8,128)(2,1)}), bf16[32,128,64]{1,2,0:T(8,128)(2,1)S(1)}, u32[]{:S(2)}, u32[]{:S(2)}) %all-to-all-start.1) | async-done | bytes 524320 | tf_op jit(solution)/shard_map/all_to_all | solution.py:112
  65.9 1.0 fusion.19
  67.6 1.5 reshape_reshape.15
  69.1 0.9 maximum_bitcast_fusion.1
  70.0 0.6 reduce.5
  70.6 0.7 reshape.368
  71.3 3.7 %all-to-all-start.2 = ((bf16[32,2,1024]{2,1,0:T(2,128)(2,1)}), bf16[32,2,1024]{2,1,0:T(2,128)(2,1)S(1)}, u32[]{:S(2)}, u32[]{:S(2)}) async-start(bf16[32,2,1024]{2,1,0:T(2,128)(2,1)} %reshape.368), calls=%async_computation.2 | async-start | bytes 262144 | tf_op jit(solution)/shard_map/all_to_all | solution.py:128
  75.6 8.0 %all-to-all-done.2 = bf16[32,2,1024]{2,1,0:T(2,128)(2,1)S(1)} async-done(((bf16[32,2,1024]{2,1,0:T(2,128)(2,1)}), bf16[32,2,1024]{2,1,0:T(2,128)(2,1)S(1)}, u32[]{:S(2)}, u32[]{:S(2)}) %all-to-all-start.2) | async-done | bytes 131104 | tf_op jit(solution)/shard_map/all_to_all | solution.py:128
  83.9 1.2 reshape.271
  87.4 1.3 convolution_convert_fusion.1
  89.0 20.2 %all_to_all.62 = bf16[32,128,64]{1,2,0:T(8,128)(2,1)S(1)} all-to-all(bf16[32,128,64]{1,2,0:T(8,128)(2,1)S(1)} %bitcast.128), channel_id=1, replica_groups=mesh['dp'=16,'tensor'=32] {'tensor'}, dimensions={0} | all-to-all | bytes 1048576 | tf_op jit(solution)/shard_map/all_to_all | solution.py:190
  109.2 0.9 tile.18
  110.2 3.7 %all-to-all-start.4 = ((bf16[32,128,64]{1,2,0:T(8,128)(2,1)}), bf16[32,128,64]{1,2,0:T(8,128)(2,1)S(1)}, u32[]{:S(2)}, u32[]{:S(2)}) async-start(bf16[32,128,64]{1,2,0:T(8,128)(2,1)} %bitcast.37), calls=%async_computation.4 | async-start | bytes 1048576 | tf_op jit(solution)/shard_map/all_to_all | solution.py:204
  113.9 2.3 %collective-permute-start.3 = (bf16[256,2048]{1,0:T(8,128)(2,1)}, bf16[256,2048]{1,0:T(8,128)(2,1)}, u32[]{:S(2)}, u32[]{:S(2)}) collective-permute-start(bf16[256,2048]{1,0:T(8,128)(2,1)} %param.29), channel_id=1, source_target_pairs={{0,1},{1,0},{2,3},{3,2},{4,5},{5,4},{6,7},{7,6},{8,9},{9,8},{10,11... | collective-permute-start | bytes 3145736 | tf_op jit(solution)/shard_map/ppermute | solution.py:195
  116.2 2.6 %fusion.68 = (bf16[2048,256]{1,0:T(8,128)(2,1)S(1)}, bf16[2048,256]{1,0:T(8,128)(2,1)}) fusion(bf16[2048,512]{1,0:T(8,128)(2,1)} %collective-permute-done.2), kind=kLoop, calls=%fused_computation.133 | loop fusion | bytes 4194304 | tf_op jit(solution)/shard_map/slice | solution.py:200
  118.9 11.8 %all-to-all-done.4 = bf16[32,128,64]{1,2,0:T(8,128)(2,1)S(1)} async-done(((bf16[32,128,64]{1,2,0:T(8,128)(2,1)}), bf16[32,128,64]{1,2,0:T(8,128)(2,1)S(1)}, u32[]{:S(2)}, u32[]{:S(2)}) %all-to-all-start.4) | async-done | bytes 524320 | tf_op jit(solution)/shard_map/all_to_all | solution.py:204
  131.3 2.6 %fusion.1 = f32[128,512]{1,0:T(8,128)} fusion(bf16[128,2048]{0,1:T(8,128)(2,1)S(1)} %fusion.17, bf16[2048,256]{1,0:T(8,128)(2,1)S(1)} %copy-done.2, bf16[2048,256]{1,0:T(8,128)(2,1)} %get-tuple-element.28), kind=kOutput, calls=%fused_computation.7 | convolution fusion | flops 272629760 | bytes 2883584 | tf_op jit(solution)/shard_map/dot_general | solution.py:207
  133.9 2.7 %convolution_convert_fusion = bf16[128,2048]{1,0:T(8,128)(2,1)S(1)} fusion(bf16[256,2048]{1,0:T(8,128)(2,1)} %collective-permute-done.3, bf16[256,2048]{1,0:T(8,128)(2,1)} %param.29, f32[128,512]{1,0:T(8,128)} %fusion.1, bf16[128,2048]{0,1:T(8,128)(2,1)} %copy-done.5, bf16[2048,256]{1,0:T(8,128)(2,1)S(1)} %get-tuple-element.27, ...), kind=kOutput, calls=%fused_computation.3 | convolution fusion | flops 545914880 | bytes 5505024 | tf_op jit(solution)/shard_map/dot_general | solution.py:210
  136.6 1.0 copy.108
  137.6 3.7 %all-to-all-start.5 = ((bf16[32,128,64]{1,2,0:T(8,128)(2,1)}), bf16[32,128,64]{1,2,0:T(8,128)(2,1)S(1)}, u32[]{:S(2)}, u32[]{:S(2)}) async-start(bf16[32,128,64]{1,2,0:T(8,128)(2,1)} %bitcast.41), calls=%async_computation.5 | async-start | bytes 1048576 | tf_op jit(solution)/shard_map/all_to_all | solution.py:212
  141.5 2.2 %collective-permute-start.4 = (bf16[128,32]{0,1:T(8,128)(2,1)S(1)}, bf16[128,32]{0,1:T(8,128)(2,1)S(1)}, u32[]{:S(2)}, u32[]{:S(2)}) collective-permute-start(bf16[128,32]{0,1:T(8,128)(2,1)S(1)} %pad_maximum_fusion.11), channel_id=1, source_target_pairs={{0,1},{1,0},{2,3},{3,2},{4,5},{5,4},{6,7},{7,6},{8,9},{9,8},{10,11... | collective-permute-start | bytes 24584 | tf_op jit(solution)/shard_map/ppermute | solution.py:151
  143.7 0.9 collective-permute-done.4
  144.6 13.5 %all-to-all-done.5 = bf16[32,128,64]{1,2,0:T(8,128)(2,1)S(1)} async-done(((bf16[32,128,64]{1,2,0:T(8,128)(2,1)}), bf16[32,128,64]{1,2,0:T(8,128)(2,1)S(1)}, u32[]{:S(2)}, u32[]{:S(2)}) %all-to-all-start.5) | async-done | bytes 524320 | tf_op jit(solution)/shard_map/all_to_all | solution.py:212
  158.4 0.7 reshape.370
  159.1 11.7 %all-to-all-start.6 = ((bf16[16,2,512]{2,1,0:T(2,128)(2,1)}), bf16[16,2,512]{2,1,0:T(2,128)(2,1)S(1)}, u32[]{:S(2)}, u32[]{:S(2)}) async-start(bf16[16,2,512]{2,1,0:T(2,128)(2,1)} %reshape.370), calls=%async_computation.6 | async-start | bytes 65536 | tf_op jit(solution)/shard_map/all_to_all | solution.py:222
  170.8 0.6 slice_select_fusion
  171.4 10.7 %all-to-all-done.6 = bf16[16,2,512]{2,1,0:T(2,128)(2,1)S(1)} async-done(((bf16[16,2,512]{2,1,0:T(2,128)(2,1)}), bf16[16,2,512]{2,1,0:T(2,128)(2,1)S(1)}, u32[]{:S(2)}, u32[]{:S(2)}) %all-to-all-start.6) | async-done | bytes 32800 | tf_op jit(solution)/shard_map/all_to_all | solution.py:222
  182.3 1.5 scatter_fusion
  183.8 0.6 copy-done.6
  (129 shorter events, 8.1 us)
Async XLA Ops:
  0.6 1.6 copy-start
  0.6 21.5 %copy-start.1 = (bf16[2048,64]{0,1:T(8,128)(2,1)S(1)}, bf16[2048,64]{0,1:T(8,128)(2,1)}, u32[]{:S(2)}) copy-start(bf16[2048,64]{0,1:T(8,128)(2,1)} %param.22) | copy-start | bytes 786436
  0.7 21.5 %copy-start.10 = (bf16[2048,16]{0,1:T(8,128)(2,1)S(1)}, bf16[2048,16]{0,1:T(8,128)(2,1)}, u32[]{:S(2)}) copy-start(bf16[2048,16]{0,1:T(8,128)(2,1)} %param.23) | copy-start | bytes 196612
  0.7 21.5 %copy-start.8 = (bf16[2048,16]{0,1:T(8,128)(2,1)S(1)}, bf16[2048,16]{0,1:T(8,128)(2,1)}, u32[]{:S(2)}) copy-start(bf16[2048,16]{0,1:T(8,128)(2,1)} %param.24) | copy-start | bytes 196612
  0.7 26.6 %copy-start.2 = (bf16[2048,256]{1,0:T(8,128)(2,1)S(1)}, bf16[2048,256]{1,0:T(8,128)(2,1)}, u32[]{:S(2)}) copy-start(bf16[2048,256]{1,0:T(8,128)(2,1)} %param.27) | copy-start | bytes 3145732
  0.7 26.6 %copy-start.3 = (bf16[2048,256]{1,0:T(8,128)(2,1)S(1)}, bf16[2048,256]{1,0:T(8,128)(2,1)}, u32[]{:S(2)}) copy-start(bf16[2048,256]{1,0:T(8,128)(2,1)} %param.28) | copy-start | bytes 3145732
  1.5 0.7 copy-start.15
  6.0 34.0 %all-to-all-start = ((bf16[16,2,4608]{2,1,0:T(2,128)(2,1)}), bf16[16,2,4608]{2,1,0:T(2,128)(2,1)S(1)}, u32[]{:S(2)}, u32[]{:S(2)}) async-start(bf16[16,2,4608]{2,1,0:T(2,128)(2,1)} %reshape.366), calls=%async_computation | async-start | bytes 589824 | tf_op jit(solution)/shard_map/all_to_all | solution.py:70
  22.2 8.9 %copy-start.23 = (s32[32]{0:T(128)S(1)}, s32[32]{0:T(128)}, u32[]{:S(2)}) copy-start(s32[32]{0:T(128)} %param.19) | copy-start | bytes 388
  22.3 9.0 %copy-start.17 = (s32[32,1]{0,1:T(1,128)S(1)}, s32[32,1]{0,1:T(1,128)}, u32[]{:S(2)}) copy-start(s32[32,1]{0,1:T(1,128)} %param.17) | copy-start | bytes 388
  22.3 9.0 %copy-start.18 = (s32[32]{0:T(128)S(1)}, s32[32]{0:T(128)}, u32[]{:S(2)}) copy-start(s32[32]{0:T(128)} %param.16) | copy-start | bytes 388
  22.3 9.2 %copy-start.24 = (s32[16]{0:T(128)S(1)}, s32[16]{0:T(128)}, u32[]{:S(2)}) copy-start(s32[16]{0:T(128)} %param.18) | copy-start | bytes 196
  22.3 12.7 %copy-start.13 = (bf16[2048]{0:T(1024)(128)(2,1)S(1)}, bf16[2048]{0:T(1024)(128)(2,1)}, u32[]{:S(2)}) copy-start(bf16[2048]{0:T(1024)(128)(2,1)} %param.21) | copy-start | bytes 12292
  22.3 17.7 %collective-permute-start = (bf16[2048,96]{0,1:T(8,128)(2,1)S(1)}, bf16[2048,96]{0,1:T(8,128)(2,1)S(1)}, u32[]{:S(2)}, u32[]{:S(2)}) collective-permute-start(bf16[2048,96]{0,1:T(8,128)(2,1)S(1)} %pad_maximum_fusion.4), channel_id=1, source_target_pairs={{0,1},{1,0},{2,3},{3,2},{4,5},{5,4},{6,7},{7,6},{8,9},{9,8},{10,11... | collective-permute-start | bytes 1179656 | tf_op jit(solution)/shard_map/ppermute | solution.py:97
  25.3 62.1 %collective-permute-start.1 = (bf16[64,2048]{1,0:T(8,128)(2,1)}, bf16[64,2048]{1,0:T(8,128)(2,1)}, u32[]{:S(2)}, u32[]{:S(2)}) collective-permute-start(bf16[64,2048]{1,0:T(8,128)(2,1)} %param.25), channel_id=1, source_target_pairs={{0,1},{1,0},{2,3},{3,2},{4,5},{5,4},{6,7},{7,6},{8,9},{9,8},{10,11... | collective-permute-start | bytes 786440 | tf_op jit(solution)/shard_map/ppermute | solution.py:186
  28.7 87.5 %collective-permute-start.2 = (bf16[2048,512]{1,0:T(8,128)(2,1)}, bf16[2048,512]{1,0:T(8,128)(2,1)}, u32[]{:S(2)}, u32[]{:S(2)}) collective-permute-start(bf16[2048,512]{1,0:T(8,128)(2,1)} %pad_maximum_fusion), channel_id=1, source_target_pairs={{0,1},{1,0},{2,3},{3,2},{4,5},{5,4},{6,7},{7,6},{8,9},{9,8},{10,11... | collective-permute-start | bytes 6291464 | tf_op jit(solution)/shard_map/ppermute | solution.py:195
  31.4 9.0 %copy-start.19 = (s32[2]{0:T(128)}, s32[2]{0:T(128)S(1)}, u32[]{:S(2)}) copy-start(s32[2]{0:T(128)S(1)} %get-tuple-element.26) | copy-start | bytes 28
  41.5 24.1 %all-to-all-start.1 = ((bf16[32,128,64]{1,2,0:T(8,128)(2,1)}), bf16[32,128,64]{1,2,0:T(8,128)(2,1)S(1)}, u32[]{:S(2)}, u32[]{:S(2)}) async-start(bf16[32,128,64]{1,2,0:T(8,128)(2,1)} %bitcast.4), calls=%async_computation.1 | async-start | bytes 1048576 | tf_op jit(solution)/shard_map/all_to_all | solution.py:112
  48.8 18.1 %copy-start.9 = (bf16[2048,16]{0,1:T(8,128)(2,1)S(1)}, bf16[2048,16]{0,1:T(8,128)(2,1)}, u32[]{:S(2)}) copy-start(bf16[2048,16]{0,1:T(8,128)(2,1)} %param.24) | copy-start | bytes 196612
  48.9 18.1 %copy-start.11 = (bf16[2048,16]{0,1:T(8,128)(2,1)S(1)}, bf16[2048,16]{0,1:T(8,128)(2,1)}, u32[]{:S(2)}) copy-start(bf16[2048,16]{0,1:T(8,128)(2,1)} %param.23) | copy-start | bytes 196612
  71.3 12.4 %all-to-all-start.2 = ((bf16[32,2,1024]{2,1,0:T(2,128)(2,1)}), bf16[32,2,1024]{2,1,0:T(2,128)(2,1)S(1)}, u32[]{:S(2)}, u32[]{:S(2)}) async-start(bf16[32,2,1024]{2,1,0:T(2,128)(2,1)} %reshape.368), calls=%async_computation.2 | async-start | bytes 262144 | tf_op jit(solution)/shard_map/all_to_all | solution.py:128
  85.1 0.9 copy-start.21
  85.1 0.9 copy-start.22
  85.2 1.6 copy-start.12
  85.9 1.5 copy-start.7
  88.7 27.5 %copy-start.14 = (bf16[2048]{0:T(1024)(128)(2,1)S(1)}, bf16[2048]{0:T(1024)(128)(2,1)}, u32[]{:S(2)}) copy-start(bf16[2048]{0:T(1024)(128)(2,1)} %param.26) | copy-start | bytes 12292
  110.2 20.5 %all-to-all-start.4 = ((bf16[32,128,64]{1,2,0:T(8,128)(2,1)}), bf16[32,128,64]{1,2,0:T(8,128)(2,1)S(1)}, u32[]{:S(2)}, u32[]{:S(2)}) async-start(bf16[32,128,64]{1,2,0:T(8,128)(2,1)} %bitcast.37), calls=%async_computation.4 | async-start | bytes 1048576 | tf_op jit(solution)/shard_map/all_to_all | solution.py:204
  113.9 20.1 %collective-permute-start.3 = (bf16[256,2048]{1,0:T(8,128)(2,1)}, bf16[256,2048]{1,0:T(8,128)(2,1)}, u32[]{:S(2)}, u32[]{:S(2)}) collective-permute-start(bf16[256,2048]{1,0:T(8,128)(2,1)} %param.29), channel_id=1, source_target_pairs={{0,1},{1,0},{2,3},{3,2},{4,5},{5,4},{6,7},{7,6},{8,9},{9,8},{10,11... | collective-permute-start | bytes 3145736 | tf_op jit(solution)/shard_map/ppermute | solution.py:195
  131.3 2.6 %copy-start.5 = (bf16[128,2048]{0,1:T(8,128)(2,1)}, bf16[128,2048]{0,1:T(8,128)(2,1)S(1)}, u32[]{:S(2)}) copy-start(bf16[128,2048]{0,1:T(8,128)(2,1)S(1)} %fusion.17) | copy-start | bytes 1572868
  131.3 2.6 %copy-start.4 = (bf16[2048,256]{1,0:T(8,128)(2,1)S(1)}, bf16[2048,256]{1,0:T(8,128)(2,1)}, u32[]{:S(2)}) copy-start(bf16[2048,256]{1,0:T(8,128)(2,1)} %param.28) | copy-start | bytes 3145732
  136.6 4.8 %copy-start.20 = (s32[2]{0:T(128)S(1)}, s32[2]{0:T(128)}, u32[]{:S(2)}) copy-start(s32[2]{0:T(128)} %copy-done.19) | copy-start | bytes 28
  136.6 45.7 %copy-start.16 = (s32[32]{0:T(128)S(1)}, s32[32]{0:T(128)}, u32[]{:S(2)}) copy-start(s32[32]{0:T(128)} %copy-done.15) | copy-start | bytes 388
  137.6 20.5 %all-to-all-start.5 = ((bf16[32,128,64]{1,2,0:T(8,128)(2,1)}), bf16[32,128,64]{1,2,0:T(8,128)(2,1)S(1)}, u32[]{:S(2)}, u32[]{:S(2)}) async-start(bf16[32,128,64]{1,2,0:T(8,128)(2,1)} %bitcast.41), calls=%async_computation.5 | async-start | bytes 1048576 | tf_op jit(solution)/shard_map/all_to_all | solution.py:212
  141.5 3.1 %collective-permute-start.4 = (bf16[128,32]{0,1:T(8,128)(2,1)S(1)}, bf16[128,32]{0,1:T(8,128)(2,1)S(1)}, u32[]{:S(2)}, u32[]{:S(2)}) collective-permute-start(bf16[128,32]{0,1:T(8,128)(2,1)S(1)} %pad_maximum_fusion.11), channel_id=1, source_target_pairs={{0,1},{1,0},{2,3},{3,2},{4,5},{5,4},{6,7},{7,6},{8,9},{9,8},{10,11... | collective-permute-start | bytes 24584 | tf_op jit(solution)/shard_map/ppermute | solution.py:151
  159.1 23.0 %all-to-all-start.6 = ((bf16[16,2,512]{2,1,0:T(2,128)(2,1)}), bf16[16,2,512]{2,1,0:T(2,128)(2,1)S(1)}, u32[]{:S(2)}, u32[]{:S(2)}) async-start(bf16[16,2,512]{2,1,0:T(2,128)(2,1)} %reshape.370), calls=%async_computation.6 | async-start | bytes 65536 | tf_op jit(solution)/shard_map/all_to_all | solution.py:222
  183.8 0.6 copy-start.6

commit v12 on v11

--- a/solution.py
+++ b/solution.py
@@ -220,7 +220,12 @@
         .reshape(local_reqs, L_MAX, width_here)
     )
     returned = lax.all_to_all(result, "dp", split_axis=1, concat_axis=0, tiled=True)
-    hidden_out = jnp.zeros_like(returned).at[request_order].set(returned)
+    order_hit = (
+        jnp.arange(total_reqs, dtype=jnp.int32)[:, None] == request_order[None, :]
+    ).astype(jnp.bfloat16)
+    hidden_out = jnp.dot(
+        order_hit, returned.reshape(total_reqs, -1), preferred_element_type=jnp.float32
+    ).astype(jnp.bfloat16).reshape(returned.shape)
     return (hidden_out, keys_out, values_out)
 
 

time: 186 us -> 184 us (0.989)
    unnamed x63 -> x59, local copies, waits for them, and re-layouts: 5.31 us -> 4.69 us
where the time goes in v12:
time: 184 us; the launch traced here: 183 us
  waiting for transfers between devices  60.8 us (33%)
  starting transfers between devices  58.1 us (32%)
  blocking collectives  20.2 us (11%)
  local copies, waits for them, and re-layouts  18.3 us (10%)
  other arithmetic  11.7 us (6%)
  matrix products  7.86 us (4%)
  between operations  6.25 us (3%)
    all_to_all x3, waiting for transfers between devices, layer(): got = lax.all_to_all(sent, 'tensor', 0, 0, tiled=True)  41.2 us
    all_to_all x1, blocking collectives, layer(): got = lax.all_to_all(sent, 'tensor', 0, 0, tiled=True)  20.2 us
    all_to_all x1, starting transfers between devices, layer(): lax.all_to_all(jnp.concatenate([state_part, prefix_part], axis=1), 'dp',...  16.2 us
    all_to_all x3, starting transfers between devices, layer(): got = lax.all_to_all(sent, 'tensor', 0, 0, tiled=True)  14.7 us
    all_to_all x1, starting transfers between devices, layer(): lax.all_to_all(result, 'dp', split_axis=1, concat_axis=0, tiled=True)  11.7 us
    all_to_all x1, waiting for transfers between devices, layer(): lax.all_to_all(result, 'dp', split_axis=1, concat_axis=0, tiled=True)  10.7 us
    all_to_all x1, waiting for transfers between devices, layer(): both = lax.all_to_all(packed, 'tensor', 0, 0, tiled=True)  8.05 us
    ppermute x2, starting transfers between devices, layer(): lax.ppermute((jnp.concatenate([w_gate, w_up], axis=1), w_down), 'tensor',...  4.74 us
  transfers between devices with their start and end apart: 11, of which 6 were waited for; matrix products, arithmetic and copies ran while one was open for 15% of the time, Pallas kernels for 0%

profile of v12, /device:TPU:1, one launch (start us, length us, event | category | flops | bytes accessed | tf_op | source)
XLA Modules:
  0.0 183.3 jit_solution(5216724660277528833)
XLA Ops:
  0.7 0.8 compare_select_fusion
  1.5 0.7 compare_and_fusion
  2.2 0.6 gather_fusion
  3.0 0.7 copy.130
  4.3 0.8 reduce.4
  5.0 0.9 reshape.367
  6.0 16.2 %all-to-all-start = ((bf16[16,2,4608]{2,1,0:T(2,128)(2,1)}), bf16[16,2,4608]{2,1,0:T(2,128)(2,1)S(1)}, u32[]{:S(2)}, u32[]{:S(2)}) async-start(bf16[16,2,4608]{2,1,0:T(2,128)(2,1)} %reshape.367), calls=%async_computation | async-start | bytes 589824 | tf_op jit(solution)/shard_map/all_to_all | solution.py:70
  22.3 3.0 %collective-permute-start = (bf16[2048,96]{0,1:T(8,128)(2,1)S(1)}, bf16[2048,96]{0,1:T(8,128)(2,1)S(1)}, u32[]{:S(2)}, u32[]{:S(2)}) collective-permute-start(bf16[2048,96]{0,1:T(8,128)(2,1)S(1)} %pad_maximum_fusion.4), channel_id=1, source_target_pairs={{0,1},{1,0},{2,3},{3,2},{4,5},{5,4},{6,7},{7,6},{8,9},{9,8},{10,11... | collective-permute-start | bytes 1179656 | tf_op jit(solution)/shard_map/ppermute | solution.py:97
  25.3 1.9 %collective-permute-start.1 = (bf16[64,2048]{1,0:T(8,128)(2,1)}, bf16[64,2048]{1,0:T(8,128)(2,1)}, u32[]{:S(2)}, u32[]{:S(2)}) collective-permute-start(bf16[64,2048]{1,0:T(8,128)(2,1)} %param.25), channel_id=1, source_target_pairs={{0,1},{1,0},{2,3},{3,2},{4,5},{5,4},{6,7},{7,6},{8,9},{9,8},{10,11... | collective-permute-start | bytes 786440 | tf_op jit(solution)/shard_map/ppermute | solution.py:186
  27.2 1.5 pad_maximum_fusion
  28.7 2.4 %collective-permute-start.2 = (bf16[2048,512]{1,0:T(8,128)(2,1)}, bf16[2048,512]{1,0:T(8,128)(2,1)}, u32[]{:S(2)}, u32[]{:S(2)}) collective-permute-start(bf16[2048,512]{1,0:T(8,128)(2,1)} %pad_maximum_fusion), channel_id=1, source_target_pairs={{0,1},{1,0},{2,3},{3,2},{4,5},{5,4},{6,7},{7,6},{8,9},{9,8},{10,11... | collective-permute-start | bytes 6291464 | tf_op jit(solution)/shard_map/ppermute | solution.py:195
  31.6 0.7 fusion.73
  35.0 0.6 convert_element_type.138
  35.7 0.6 dynamic-slice.5
  38.2 0.5 add_convert_fusion.3
  38.8 0.5 negate_power_fusion
  39.3 0.6 fusion.39
  40.6 0.9 tile.16
  41.5 7.3 %all-to-all-start.1 = ((bf16[32,128,64]{1,2,0:T(8,128)(2,1)}), bf16[32,128,64]{1,2,0:T(8,128)(2,1)S(1)}, u32[]{:S(2)}, u32[]{:S(2)}) async-start(bf16[32,128,64]{1,2,0:T(8,128)(2,1)} %bitcast.4), calls=%async_computation.1 | async-start | bytes 1048576 | tf_op jit(solution)/shard_map/all_to_all | solution.py:112
  49.1 0.6 copy.128
  49.7 15.9 %all-to-all-done.1 = bf16[32,128,64]{1,2,0:T(8,128)(2,1)S(1)} async-done(((bf16[32,128,64]{1,2,0:T(8,128)(2,1)}), bf16[32,128,64]{1,2,0:T(8,128)(2,1)S(1)}, u32[]{:S(2)}, u32[]{:S(2)}) %all-to-all-start.1) | async-done | bytes 524320 | tf_op jit(solution)/shard_map/all_to_all | solution.py:112
  65.9 1.0 fusion.19
  67.6 1.5 reshape_reshape.15
  69.1 0.9 maximum_bitcast_fusion.1
  70.0 0.6 reduce.5
  70.6 0.7 reshape.369
  71.3 3.7 %all-to-all-start.2 = ((bf16[32,2,1024]{2,1,0:T(2,128)(2,1)}), bf16[32,2,1024]{2,1,0:T(2,128)(2,1)S(1)}, u32[]{:S(2)}, u32[]{:S(2)}) async-start(bf16[32,2,1024]{2,1,0:T(2,128)(2,1)} %reshape.369), calls=%async_computation.2 | async-start | bytes 262144 | tf_op jit(solution)/shard_map/all_to_all | solution.py:128
  75.6 8.0 %all-to-all-done.2 = bf16[32,2,1024]{2,1,0:T(2,128)(2,1)S(1)} async-done(((bf16[32,2,1024]{2,1,0:T(2,128)(2,1)}), bf16[32,2,1024]{2,1,0:T(2,128)(2,1)S(1)}, u32[]{:S(2)}, u32[]{:S(2)}) %all-to-all-start.2) | async-done | bytes 131104 | tf_op jit(solution)/shard_map/all_to_all | solution.py:128
  83.9 1.2 reshape.279
  87.4 1.3 convolution_convert_fusion.1
  88.9 20.2 %all_to_all.59 = bf16[32,128,64]{1,2,0:T(8,128)(2,1)S(1)} all-to-all(bf16[32,128,64]{1,2,0:T(8,128)(2,1)S(1)} %bitcast.130), channel_id=1, replica_groups=mesh['dp'=16,'tensor'=32] {'tensor'}, dimensions={0} | all-to-all | bytes 1048576 | tf_op jit(solution)/shard_map/all_to_all | solution.py:190
  109.2 0.9 tile.18
  110.2 3.7 %all-to-all-start.4 = ((bf16[32,128,64]{1,2,0:T(8,128)(2,1)}), bf16[32,128,64]{1,2,0:T(8,128)(2,1)S(1)}, u32[]{:S(2)}, u32[]{:S(2)}) async-start(bf16[32,128,64]{1,2,0:T(8,128)(2,1)} %bitcast.37), calls=%async_computation.4 | async-start | bytes 1048576 | tf_op jit(solution)/shard_map/all_to_all | solution.py:204
  113.8 2.3 %collective-permute-start.3 = (bf16[256,2048]{1,0:T(8,128)(2,1)}, bf16[256,2048]{1,0:T(8,128)(2,1)}, u32[]{:S(2)}, u32[]{:S(2)}) collective-permute-start(bf16[256,2048]{1,0:T(8,128)(2,1)} %param.29), channel_id=1, source_target_pairs={{0,1},{1,0},{2,3},{3,2},{4,5},{5,4},{6,7},{7,6},{8,9},{9,8},{10,11... | collective-permute-start | bytes 3145736 | tf_op jit(solution)/shard_map/ppermute | solution.py:195
  116.2 2.6 %fusion.69 = (bf16[2048,256]{1,0:T(8,128)(2,1)S(1)}, bf16[2048,256]{1,0:T(8,128)(2,1)}) fusion(bf16[2048,512]{1,0:T(8,128)(2,1)} %collective-permute-done.2), kind=kLoop, calls=%fused_computation.135 | loop fusion | bytes 4194304 | tf_op jit(solution)/shard_map/slice | solution.py:200
  118.9 11.8 %all-to-all-done.4 = bf16[32,128,64]{1,2,0:T(8,128)(2,1)S(1)} async-done(((bf16[32,128,64]{1,2,0:T(8,128)(2,1)}), bf16[32,128,64]{1,2,0:T(8,128)(2,1)S(1)}, u32[]{:S(2)}, u32[]{:S(2)}) %all-to-all-start.4) | async-done | bytes 524320 | tf_op jit(solution)/shard_map/all_to_all | solution.py:204
  131.3 2.6 %fusion.1 = f32[128,512]{1,0:T(8,128)} fusion(bf16[128,2048]{0,1:T(8,128)(2,1)S(1)} %fusion.17, bf16[2048,256]{1,0:T(8,128)(2,1)S(1)} %copy-done.2, bf16[2048,256]{1,0:T(8,128)(2,1)} %get-tuple-element.28), kind=kOutput, calls=%fused_computation.6 | convolution fusion | flops 272629760 | bytes 2883584 | tf_op jit(solution)/shard_map/dot_general | solution.py:207
  133.9 2.7 %convolution_convert_fusion = bf16[128,2048]{1,0:T(8,128)(2,1)S(1)} fusion(bf16[256,2048]{1,0:T(8,128)(2,1)} %collective-permute-done.3, bf16[256,2048]{1,0:T(8,128)(2,1)} %param.29, f32[128,512]{1,0:T(8,128)} %fusion.1, bf16[128,2048]{0,1:T(8,128)(2,1)} %copy-done.5, bf16[2048,256]{1,0:T(8,128)(2,1)S(1)} %get-tuple-element.27, ...), kind=kOutput, calls=%fused_computation.2 | convolution fusion | flops 545914880 | bytes 5505024 | tf_op jit(solution)/shard_map/dot_general | solution.py:210
  136.6 1.0 copy.106
  137.6 3.7 %all-to-all-start.5 = ((bf16[32,128,64]{1,2,0:T(8,128)(2,1)}), bf16[32,128,64]{1,2,0:T(8,128)(2,1)S(1)}, u32[]{:S(2)}, u32[]{:S(2)}) async-start(bf16[32,128,64]{1,2,0:T(8,128)(2,1)} %bitcast.41), calls=%async_computation.5 | async-start | bytes 1048576 | tf_op jit(solution)/shard_map/all_to_all | solution.py:212
  141.5 2.2 %collective-permute-start.4 = (bf16[128,32]{0,1:T(8,128)(2,1)S(1)}, bf16[128,32]{0,1:T(8,128)(2,1)S(1)}, u32[]{:S(2)}, u32[]{:S(2)}) collective-permute-start(bf16[128,32]{0,1:T(8,128)(2,1)S(1)} %pad_maximum_fusion.11), channel_id=1, source_target_pairs={{0,1},{1,0},{2,3},{3,2},{4,5},{5,4},{6,7},{7,6},{8,9},{9,8},{10,11... | collective-permute-start | bytes 24584 | tf_op jit(solution)/shard_map/ppermute | solution.py:151
  143.7 0.9 collective-permute-done.4
  144.6 13.5 %all-to-all-done.5 = bf16[32,128,64]{1,2,0:T(8,128)(2,1)S(1)} async-done(((bf16[32,128,64]{1,2,0:T(8,128)(2,1)}), bf16[32,128,64]{1,2,0:T(8,128)(2,1)S(1)}, u32[]{:S(2)}, u32[]{:S(2)}) %all-to-all-start.5) | async-done | bytes 524320 | tf_op jit(solution)/shard_map/all_to_all | solution.py:212
  158.4 0.7 reshape.371
  159.1 11.7 %all-to-all-start.6 = ((bf16[16,2,512]{2,1,0:T(2,128)(2,1)}), bf16[16,2,512]{2,1,0:T(2,128)(2,1)S(1)}, u32[]{:S(2)}, u32[]{:S(2)}) async-start(bf16[16,2,512]{2,1,0:T(2,128)(2,1)} %reshape.371), calls=%async_computation.6 | async-start | bytes 65536 | tf_op jit(solution)/shard_map/all_to_all | solution.py:222
  170.8 0.6 slice_select_fusion
  171.4 10.7 %all-to-all-done.6 = bf16[16,2,512]{2,1,0:T(2,128)(2,1)S(1)} async-done(((bf16[16,2,512]{2,1,0:T(2,128)(2,1)}), bf16[16,2,512]{2,1,0:T(2,128)(2,1)S(1)}, u32[]{:S(2)}, u32[]{:S(2)}) %all-to-all-start.6) | async-done | bytes 32800 | tf_op jit(solution)/shard_map/all_to_all | solution.py:222
  182.5 0.7 reshape.287
  (126 shorter events, 7.8 us)
Async XLA Ops:
  0.6 1.6 copy-start
  0.6 21.5 %copy-start.1 = (bf16[2048,64]{0,1:T(8,128)(2,1)S(1)}, bf16[2048,64]{0,1:T(8,128)(2,1)}, u32[]{:S(2)}) copy-start(bf16[2048,64]{0,1:T(8,128)(2,1)} %param.22) | copy-start | bytes 786436
  0.7 21.5 %copy-start.9 = (bf16[2048,16]{0,1:T(8,128)(2,1)S(1)}, bf16[2048,16]{0,1:T(8,128)(2,1)}, u32[]{:S(2)}) copy-start(bf16[2048,16]{0,1:T(8,128)(2,1)} %param.23) | copy-start | bytes 196612
  0.7 21.5 %copy-start.7 = (bf16[2048,16]{0,1:T(8,128)(2,1)S(1)}, bf16[2048,16]{0,1:T(8,128)(2,1)}, u32[]{:S(2)}) copy-start(bf16[2048,16]{0,1:T(8,128)(2,1)} %param.24) | copy-start | bytes 196612
  0.7 26.6 %copy-start.2 = (bf16[2048,256]{1,0:T(8,128)(2,1)S(1)}, bf16[2048,256]{1,0:T(8,128)(2,1)}, u32[]{:S(2)}) copy-start(bf16[2048,256]{1,0:T(8,128)(2,1)} %param.27) | copy-start | bytes 3145732
  0.7 26.6 %copy-start.3 = (bf16[2048,256]{1,0:T(8,128)(2,1)S(1)}, bf16[2048,256]{1,0:T(8,128)(2,1)}, u32[]{:S(2)}) copy-start(bf16[2048,256]{1,0:T(8,128)(2,1)} %param.28) | copy-start | bytes 3145732
  6.0 34.0 %all-to-all-start = ((bf16[16,2,4608]{2,1,0:T(2,128)(2,1)}), bf16[16,2,4608]{2,1,0:T(2,128)(2,1)S(1)}, u32[]{:S(2)}, u32[]{:S(2)}) async-start(bf16[16,2,4608]{2,1,0:T(2,128)(2,1)} %reshape.367), calls=%async_computation | async-start | bytes 589824 | tf_op jit(solution)/shard_map/all_to_all | solution.py:70
  22.2 8.9 %copy-start.14 = (s32[32]{0:T(128)S(1)}, s32[32]{0:T(128)}, u32[]{:S(2)}) copy-start(s32[32]{0:T(128)} %param.19) | copy-start | bytes 388
  22.2 9.0 %copy-start.16 = (s32[32,1]{0,1:T(1,128)S(1)}, s32[32,1]{0,1:T(1,128)}, u32[]{:S(2)}) copy-start(s32[32,1]{0,1:T(1,128)} %param.17) | copy-start | bytes 388
  22.3 9.0 %copy-start.17 = (s32[32]{0:T(128)S(1)}, s32[32]{0:T(128)}, u32[]{:S(2)}) copy-start(s32[32]{0:T(128)} %param.16) | copy-start | bytes 388
  22.3 9.2 %copy-start.22 = (s32[16]{0:T(128)S(1)}, s32[16]{0:T(128)}, u32[]{:S(2)}) copy-start(s32[16]{0:T(128)} %param.18) | copy-start | bytes 196
  22.3 12.7 %copy-start.12 = (bf16[2048]{0:T(1024)(128)(2,1)S(1)}, bf16[2048]{0:T(1024)(128)(2,1)}, u32[]{:S(2)}) copy-start(bf16[2048]{0:T(1024)(128)(2,1)} %param.21) | copy-start | bytes 12292
  22.3 17.7 %collective-permute-start = (bf16[2048,96]{0,1:T(8,128)(2,1)S(1)}, bf16[2048,96]{0,1:T(8,128)(2,1)S(1)}, u32[]{:S(2)}, u32[]{:S(2)}) collective-permute-start(bf16[2048,96]{0,1:T(8,128)(2,1)S(1)} %pad_maximum_fusion.4), channel_id=1, source_target_pairs={{0,1},{1,0},{2,3},{3,2},{4,5},{5,4},{6,7},{7,6},{8,9},{9,8},{10,11... | collective-permute-start | bytes 1179656 | tf_op jit(solution)/shard_map/ppermute | solution.py:97
  25.3 62.1 %collective-permute-start.1 = (bf16[64,2048]{1,0:T(8,128)(2,1)}, bf16[64,2048]{1,0:T(8,128)(2,1)}, u32[]{:S(2)}, u32[]{:S(2)}) collective-permute-start(bf16[64,2048]{1,0:T(8,128)(2,1)} %param.25), channel_id=1, source_target_pairs={{0,1},{1,0},{2,3},{3,2},{4,5},{5,4},{6,7},{7,6},{8,9},{9,8},{10,11... | collective-permute-start | bytes 786440 | tf_op jit(solution)/shard_map/ppermute | solution.py:186
  28.7 87.5 %collective-permute-start.2 = (bf16[2048,512]{1,0:T(8,128)(2,1)}, bf16[2048,512]{1,0:T(8,128)(2,1)}, u32[]{:S(2)}, u32[]{:S(2)}) collective-permute-start(bf16[2048,512]{1,0:T(8,128)(2,1)} %pad_maximum_fusion), channel_id=1, source_target_pairs={{0,1},{1,0},{2,3},{3,2},{4,5},{5,4},{6,7},{7,6},{8,9},{9,8},{10,11... | collective-permute-start | bytes 6291464 | tf_op jit(solution)/shard_map/ppermute | solution.py:195
  31.4 9.0 %copy-start.18 = (s32[2]{0:T(128)}, s32[2]{0:T(128)S(1)}, u32[]{:S(2)}) copy-start(s32[2]{0:T(128)S(1)} %get-tuple-element.26) | copy-start | bytes 28
  41.5 24.1 %all-to-all-start.1 = ((bf16[32,128,64]{1,2,0:T(8,128)(2,1)}), bf16[32,128,64]{1,2,0:T(8,128)(2,1)S(1)}, u32[]{:S(2)}, u32[]{:S(2)}) async-start(bf16[32,128,64]{1,2,0:T(8,128)(2,1)} %bitcast.4), calls=%async_computation.1 | async-start | bytes 1048576 | tf_op jit(solution)/shard_map/all_to_all | solution.py:112
  48.8 18.1 %copy-start.8 = (bf16[2048,16]{0,1:T(8,128)(2,1)S(1)}, bf16[2048,16]{0,1:T(8,128)(2,1)}, u32[]{:S(2)}) copy-start(bf16[2048,16]{0,1:T(8,128)(2,1)} %param.24) | copy-start | bytes 196612
  48.9 18.1 %copy-start.10 = (bf16[2048,16]{0,1:T(8,128)(2,1)S(1)}, bf16[2048,16]{0,1:T(8,128)(2,1)}, u32[]{:S(2)}) copy-start(bf16[2048,16]{0,1:T(8,128)(2,1)} %param.23) | copy-start | bytes 196612
  71.3 12.4 %all-to-all-start.2 = ((bf16[32,2,1024]{2,1,0:T(2,128)(2,1)}), bf16[32,2,1024]{2,1,0:T(2,128)(2,1)S(1)}, u32[]{:S(2)}, u32[]{:S(2)}) async-start(bf16[32,2,1024]{2,1,0:T(2,128)(2,1)} %reshape.369), calls=%async_computation.2 | async-start | bytes 262144 | tf_op jit(solution)/shard_map/all_to_all | solution.py:128
  85.1 0.9 copy-start.20
  85.1 0.9 copy-start.21
  85.2 1.6 copy-start.11
  85.9 1.5 copy-start.6
  88.7 27.5 %copy-start.13 = (bf16[2048]{0:T(1024)(128)(2,1)S(1)}, bf16[2048]{0:T(1024)(128)(2,1)}, u32[]{:S(2)}) copy-start(bf16[2048]{0:T(1024)(128)(2,1)} %param.26) | copy-start | bytes 12292
  110.2 20.5 %all-to-all-start.4 = ((bf16[32,128,64]{1,2,0:T(8,128)(2,1)}), bf16[32,128,64]{1,2,0:T(8,128)(2,1)S(1)}, u32[]{:S(2)}, u32[]{:S(2)}) async-start(bf16[32,128,64]{1,2,0:T(8,128)(2,1)} %bitcast.37), calls=%async_computation.4 | async-start | bytes 1048576 | tf_op jit(solution)/shard_map/all_to_all | solution.py:204
  113.8 20.1 %collective-permute-start.3 = (bf16[256,2048]{1,0:T(8,128)(2,1)}, bf16[256,2048]{1,0:T(8,128)(2,1)}, u32[]{:S(2)}, u32[]{:S(2)}) collective-permute-start(bf16[256,2048]{1,0:T(8,128)(2,1)} %param.29), channel_id=1, source_target_pairs={{0,1},{1,0},{2,3},{3,2},{4,5},{5,4},{6,7},{7,6},{8,9},{9,8},{10,11... | collective-permute-start | bytes 3145736 | tf_op jit(solution)/shard_map/ppermute | solution.py:195
  131.3 2.6 %copy-start.5 = (bf16[128,2048]{0,1:T(8,128)(2,1)}, bf16[128,2048]{0,1:T(8,128)(2,1)S(1)}, u32[]{:S(2)}) copy-start(bf16[128,2048]{0,1:T(8,128)(2,1)S(1)} %fusion.17) | copy-start | bytes 1572868
  131.3 2.6 %copy-start.4 = (bf16[2048,256]{1,0:T(8,128)(2,1)S(1)}, bf16[2048,256]{1,0:T(8,128)(2,1)}, u32[]{:S(2)}) copy-start(bf16[2048,256]{1,0:T(8,128)(2,1)} %param.28) | copy-start | bytes 3145732
  136.6 4.8 %copy-start.19 = (s32[2]{0:T(128)S(1)}, s32[2]{0:T(128)}, u32[]{:S(2)}) copy-start(s32[2]{0:T(128)} %copy-done.18) | copy-start | bytes 28
  136.6 45.8 %copy-start.15 = (s32[32]{0:T(128)S(1)}, s32[32]{0:T(128)}, u32[]{:S(2)}) copy-start(s32[32]{0:T(128)} %param.19) | copy-start | bytes 388
  137.6 20.5 %all-to-all-start.5 = ((bf16[32,128,64]{1,2,0:T(8,128)(2,1)}), bf16[32,128,64]{1,2,0:T(8,128)(2,1)S(1)}, u32[]{:S(2)}, u32[]{:S(2)}) async-start(bf16[32,128,64]{1,2,0:T(8,128)(2,1)} %bitcast.41), calls=%async_computation.5 | async-start | bytes 1048576 | tf_op jit(solution)/shard_map/all_to_all | solution.py:212
  141.5 3.1 %collective-permute-start.4 = (bf16[128,32]{0,1:T(8,128)(2,1)S(1)}, bf16[128,32]{0,1:T(8,128)(2,1)S(1)}, u32[]{:S(2)}, u32[]{:S(2)}) collective-permute-start(bf16[128,32]{0,1:T(8,128)(2,1)S(1)} %pad_maximum_fusion.11), channel_id=1, source_target_pairs={{0,1},{1,0},{2,3},{3,2},{4,5},{5,4},{6,7},{7,6},{8,9},{9,8},{10,11... | collective-permute-start | bytes 24584 | tf_op jit(solution)/shard_map/ppermute | solution.py:151
  159.1 23.0 %all-to-all-start.6 = ((bf16[16,2,512]{2,1,0:T(2,128)(2,1)}), bf16[16,2,512]{2,1,0:T(2,128)(2,1)S(1)}, u32[]{:S(2)}, u32[]{:S(2)}) async-start(bf16[16,2,512]{2,1,0:T(2,128)(2,1)} %reshape.371), calls=%async_computation.6 | async-start | bytes 65536 | tf_op jit(solution)/shard_map/all_to_all | solution.py:222

commit v13 on v12

--- a/solution.py
+++ b/solution.py
@@ -61,7 +61,12 @@
     d_here = kv_cols // KVH
     score_scale = HD ** (-0.5)
 
-    routed = jnp.take(suffix_states, request_order, axis=0)
+    slot_hit = (
+        request_order[:, None] == jnp.arange(suffix_states.shape[0], dtype=jnp.int32)[None, :]
+    ).astype(jnp.bfloat16)
+    routed = jnp.dot(
+        slot_hit, suffix_states.reshape(suffix_states.shape[0], -1), preferred_element_type=jnp.float32
+    ).astype(jnp.bfloat16).reshape(suffix_states.shape)
     pos_here = routed.shape[1]
     width_here = routed.shape[2]
     state_part = routed.reshape(dp_count, local_reqs * pos_here * width_here)
@@ -131,7 +136,7 @@
     prefix_keys = picked[:, :HD]
     prefix_values = picked[:, HD:]
     kv_got = both[:, prefix_split:].reshape(tp_count // 2, 2, L_MAX, 2 * chip_d)
-    kv_got = jnp.take(kv_got, core, axis=1)
+    kv_got = lax.dynamic_index_in_dim(kv_got, core, 1, keepdims=False)
     keys4 = kv_got[:, :, : 2 * d_here].reshape(tp_count // 2, L_MAX, 2, d_here)
     vals4 = kv_got[:, :, 2 * d_here :].reshape(tp_count // 2, L_MAX, 2, d_here)
     flip = core == 1
@@ -160,7 +165,7 @@
     keys_out = jnp.where(valid3, kv_two[:, :, :out_width], 0.0).astype(jnp.bfloat16)
     values_out = jnp.where(valid3, kv_two[:, :, out_width:], 0.0).astype(jnp.bfloat16)
 
-    length_me = jnp.take(lengths_here, core)
+    length_me = lax.dynamic_index_in_dim(lengths_here, core, 0, keepdims=False)
     prefix_scores = jnp.einsum(
         "htd,pd->htp", query, prefix_keys, preferred_element_type=jnp.float32
     ) * score_scale

time: 184 us -> 183 us (level)
    unnamed x59 -> x57, local copies, waits for them, and re-layouts: 4.69 us -> 4.05 us
  transfers between devices with their start and end apart: 11 -> 11, of which waited for: 6 -> 6; matrix products, arithmetic and copies ran while one was open for 15% -> 14% of each run, Pallas kernels for 0% -> 0%
where the time goes in v13:
time: 183 us; the launch traced here: 182 us
  waiting for transfers between devices  61.6 us (34%)
  starting transfers between devices  57.9 us (32%)
  blocking collectives  20.2 us (11%)
  local copies, waits for them, and re-layouts  17.7 us (10%)
  other arithmetic  10.1 us (6%)
  matrix products  8.71 us (5%)
  between operations  5.44 us (3%)
    all_to_all x3, waiting for transfers between devices, layer(): got = lax.all_to_all(sent, 'tensor', 0, 0, tiled=True)  42 us
    all_to_all x1, blocking collectives, layer(): got = lax.all_to_all(sent, 'tensor', 0, 0, tiled=True)  20.2 us
    all_to_all x1, starting transfers between devices, layer(): lax.all_to_all(jnp.concatenate([state_part, prefix_part], axis=1), 'dp',...  16.2 us
    all_to_all x3, starting transfers between devices, layer(): got = lax.all_to_all(sent, 'tensor', 0, 0, tiled=True)  14.7 us
    all_to_all x1, starting transfers between devices, layer(): lax.all_to_all(result, 'dp', split_axis=1, concat_axis=0, tiled=True)  11.7 us
    all_to_all x1, waiting for transfers between devices, layer(): lax.all_to_all(result, 'dp', split_axis=1, concat_axis=0, tiled=True)  10.7 us
    all_to_all x1, waiting for transfers between devices, layer(): both = lax.all_to_all(packed, 'tensor', 0, 0, tiled=True)  8.03 us
    ppermute x2, starting transfers between devices, layer(): lax.ppermute((jnp.concatenate([w_gate, w_up], axis=1), w_down), 'tensor',...  4.56 us
  transfers between devices with their start and end apart: 11, of which 6 were waited for; matrix products, arithmetic and copies ran while one was open for 14% of the time, Pallas kernels for 0%

profile of v13, /device:TPU:1, one launch (start us, length us, event | category | flops | bytes accessed | tf_op | source)
XLA Modules:
  0.0 181.6 jit_solution(15262928498392486463)
XLA Ops:
  0.7 1.1 reshape.269
  1.8 0.8 convolution_convert_fusion.3
  2.7 0.7 copy.114
  3.4 0.6 broadcast.170
  4.0 0.8 reduce.4
  4.8 0.9 reshape.292
  5.8 16.2 %all-to-all-start = ((bf16[16,2,4608]{2,1,0:T(2,128)(2,1)}), bf16[16,2,4608]{2,1,0:T(2,128)(2,1)S(1)}, u32[]{:S(2)}, u32[]{:S(2)}) async-start(bf16[16,2,4608]{2,1,0:T(2,128)(2,1)} %reshape.292), calls=%async_computation | async-start | bytes 589824 | tf_op jit(solution)/shard_map/all_to_all | solution.py:75
  22.1 3.0 %collective-permute-start = (bf16[2048,96]{0,1:T(8,128)(2,1)S(1)}, bf16[2048,96]{0,1:T(8,128)(2,1)S(1)}, u32[]{:S(2)}, u32[]{:S(2)}) collective-permute-start(bf16[2048,96]{0,1:T(8,128)(2,1)S(1)} %pad_maximum_fusion.4), channel_id=1, source_target_pairs={{0,1},{1,0},{2,3},{3,2},{4,5},{5,4},{6,7},{7,6},{8,9},{9,8},{10,11... | collective-permute-start | bytes 1179656 | tf_op jit(solution)/shard_map/ppermute | solution.py:102
  25.1 1.9 %collective-permute-start.1 = (bf16[64,2048]{1,0:T(8,128)(2,1)}, bf16[64,2048]{1,0:T(8,128)(2,1)}, u32[]{:S(2)}, u32[]{:S(2)}) collective-permute-start(bf16[64,2048]{1,0:T(8,128)(2,1)} %param.25), channel_id=1, source_target_pairs={{0,1},{1,0},{2,3},{3,2},{4,5},{5,4},{6,7},{7,6},{8,9},{9,8},{10,11... | collective-permute-start | bytes 786440 | tf_op jit(solution)/shard_map/ppermute | solution.py:191
  27.0 1.5 pad_maximum_fusion
  28.5 2.4 %collective-permute-start.2 = (bf16[2048,512]{1,0:T(8,128)(2,1)}, bf16[2048,512]{1,0:T(8,128)(2,1)}, u32[]{:S(2)}, u32[]{:S(2)}) collective-permute-start(bf16[2048,512]{1,0:T(8,128)(2,1)} %pad_maximum_fusion), channel_id=1, source_target_pairs={{0,1},{1,0},{2,3},{3,2},{4,5},{5,4},{6,7},{7,6},{8,9},{9,8},{10,11... | collective-permute-start | bytes 6291464 | tf_op jit(solution)/shard_map/ppermute | solution.py:200
  31.4 0.6 fusion.74
  34.6 0.6 convert_element_type.143
  36.6 0.6 dynamic_slice.31
  37.2 0.5 add_convert_fusion.3
  37.7 0.6 negate_power_fusion
  38.3 0.6 iota_compare_fusion.7
  38.9 0.6 fusion.39
  40.2 0.9 tile.16
  41.2 7.3 %all-to-all-start.1 = ((bf16[32,128,64]{1,2,0:T(8,128)(2,1)}), bf16[32,128,64]{1,2,0:T(8,128)(2,1)S(1)}, u32[]{:S(2)}, u32[]{:S(2)}) async-start(bf16[32,128,64]{1,2,0:T(8,128)(2,1)} %bitcast.4), calls=%async_computation.1 | async-start | bytes 1048576 | tf_op jit(solution)/shard_map/all_to_all | solution.py:117
  48.7 16.5 %all-to-all-done.1 = bf16[32,128,64]{1,2,0:T(8,128)(2,1)S(1)} async-done(((bf16[32,128,64]{1,2,0:T(8,128)(2,1)}), bf16[32,128,64]{1,2,0:T(8,128)(2,1)S(1)}, u32[]{:S(2)}, u32[]{:S(2)}) %all-to-all-start.1) | async-done | bytes 524320 | tf_op jit(solution)/shard_map/all_to_all | solution.py:117
  65.6 1.0 fusion.19
  67.3 1.5 reshape_reshape.19
  68.8 0.7 reduce.5
  69.4 0.7 reshape.294
  70.2 3.7 %all-to-all-start.2 = ((bf16[32,2,1024]{2,1,0:T(2,128)(2,1)}), bf16[32,2,1024]{2,1,0:T(2,128)(2,1)S(1)}, u32[]{:S(2)}, u32[]{:S(2)}) async-start(bf16[32,2,1024]{2,1,0:T(2,128)(2,1)} %reshape.294), calls=%async_computation.2 | async-start | bytes 262144 | tf_op jit(solution)/shard_map/all_to_all | solution.py:133
  74.5 8.0 %all-to-all-done.2 = bf16[32,2,1024]{2,1,0:T(2,128)(2,1)S(1)} async-done(((bf16[32,2,1024]{2,1,0:T(2,128)(2,1)}), bf16[32,2,1024]{2,1,0:T(2,128)(2,1)S(1)}, u32[]{:S(2)}, u32[]{:S(2)}) %all-to-all-start.2) | async-done | bytes 131104 | tf_op jit(solution)/shard_map/all_to_all | solution.py:133
  82.8 1.2 reshape.273
  85.7 1.3 convolution_convert_fusion.1
  87.3 20.2 %all_to_all.59 = bf16[32,128,64]{1,2,0:T(8,128)(2,1)S(1)} all-to-all(bf16[32,128,64]{1,2,0:T(8,128)(2,1)S(1)} %bitcast.130), channel_id=1, replica_groups=mesh['dp'=16,'tensor'=32] {'tensor'}, dimensions={0} | all-to-all | bytes 1048576 | tf_op jit(solution)/shard_map/all_to_all | solution.py:195
  107.5 0.9 tile.18
  108.5 3.7 %all-to-all-start.4 = ((bf16[32,128,64]{1,2,0:T(8,128)(2,1)}), bf16[32,128,64]{1,2,0:T(8,128)(2,1)S(1)}, u32[]{:S(2)}, u32[]{:S(2)}) async-start(bf16[32,128,64]{1,2,0:T(8,128)(2,1)} %bitcast.38), calls=%async_computation.4 | async-start | bytes 1048576 | tf_op jit(solution)/shard_map/all_to_all | solution.py:209
  112.2 2.2 %collective-permute-start.3 = (bf16[256,2048]{1,0:T(8,128)(2,1)}, bf16[256,2048]{1,0:T(8,128)(2,1)}, u32[]{:S(2)}, u32[]{:S(2)}) collective-permute-start(bf16[256,2048]{1,0:T(8,128)(2,1)} %param.29), channel_id=1, source_target_pairs={{0,1},{1,0},{2,3},{3,2},{4,5},{5,4},{6,7},{7,6},{8,9},{9,8},{10,11... | collective-permute-start | bytes 3145736 | tf_op jit(solution)/shard_map/ppermute | solution.py:200
  114.4 2.6 %fusion.70 = (bf16[2048,256]{1,0:T(8,128)(2,1)S(1)}, bf16[2048,256]{1,0:T(8,128)(2,1)}) fusion(bf16[2048,512]{1,0:T(8,128)(2,1)} %collective-permute-done.2), kind=kLoop, calls=%fused_computation.132 | loop fusion | bytes 4194304 | tf_op jit(solution)/shard_map/slice | solution.py:205
  117.0 11.9 %all-to-all-done.4 = bf16[32,128,64]{1,2,0:T(8,128)(2,1)S(1)} async-done(((bf16[32,128,64]{1,2,0:T(8,128)(2,1)}), bf16[32,128,64]{1,2,0:T(8,128)(2,1)S(1)}, u32[]{:S(2)}, u32[]{:S(2)}) %all-to-all-start.4) | async-done | bytes 524320 | tf_op jit(solution)/shard_map/all_to_all | solution.py:209
  129.3 0.3 fusion.17
  129.6 2.6 %fusion.1 = f32[128,512]{1,0:T(8,128)} fusion(bf16[128,2048]{0,1:T(8,128)(2,1)S(1)} %fusion.17, bf16[2048,256]{1,0:T(8,128)(2,1)S(1)} %copy-done.1, bf16[2048,256]{1,0:T(8,128)(2,1)} %get-tuple-element.6), kind=kOutput, calls=%fused_computation.5 | convolution fusion | flops 272629760 | bytes 2883584 | tf_op jit(solution)/shard_map/dot_general | solution.py:212
  132.2 2.7 %convolution_convert_fusion = bf16[128,2048]{1,0:T(8,128)(2,1)S(1)} fusion(bf16[256,2048]{1,0:T(8,128)(2,1)} %collective-permute-done.3, bf16[256,2048]{1,0:T(8,128)(2,1)} %param.29, f32[128,512]{1,0:T(8,128)} %fusion.1, bf16[128,2048]{0,1:T(8,128)(2,1)} %copy-done.4, bf16[2048,256]{1,0:T(8,128)(2,1)S(1)} %get-tuple-element.5, ...), kind=kOutput, calls=%fused_computation.1 | convolution fusion | flops 545914880 | bytes 5505024 | tf_op jit(solution)/shard_map/dot_general | solution.py:215
  134.9 1.0 copy.90
  135.9 3.7 %all-to-all-start.5 = ((bf16[32,128,64]{1,2,0:T(8,128)(2,1)}), bf16[32,128,64]{1,2,0:T(8,128)(2,1)S(1)}, u32[]{:S(2)}, u32[]{:S(2)}) async-start(bf16[32,128,64]{1,2,0:T(8,128)(2,1)} %bitcast.42), calls=%async_computation.5 | async-start | bytes 1048576 | tf_op jit(solution)/shard_map/all_to_all | solution.py:217
  139.8 2.2 %collective-permute-start.4 = (bf16[128,32]{0,1:T(8,128)(2,1)S(1)}, bf16[128,32]{0,1:T(8,128)(2,1)S(1)}, u32[]{:S(2)}, u32[]{:S(2)}) collective-permute-start(bf16[128,32]{0,1:T(8,128)(2,1)S(1)} %pad_maximum_fusion.11), channel_id=1, source_target_pairs={{0,1},{1,0},{2,3},{3,2},{4,5},{5,4},{6,7},{7,6},{8,9},{9,8},{10,11... | collective-permute-start | bytes 24584 | tf_op jit(solution)/shard_map/ppermute | solution.py:156
  142.0 0.9 collective-permute-done.4
  142.9 13.5 %all-to-all-done.5 = bf16[32,128,64]{1,2,0:T(8,128)(2,1)S(1)} async-done(((bf16[32,128,64]{1,2,0:T(8,128)(2,1)}), bf16[32,128,64]{1,2,0:T(8,128)(2,1)S(1)}, u32[]{:S(2)}, u32[]{:S(2)}) %all-to-all-start.5) | async-done | bytes 524320 | tf_op jit(solution)/shard_map/all_to_all | solution.py:217
  156.7 0.7 reshape.296
  157.4 11.7 %all-to-all-start.6 = ((bf16[16,2,512]{2,1,0:T(2,128)(2,1)}), bf16[16,2,512]{2,1,0:T(2,128)(2,1)S(1)}, u32[]{:S(2)}, u32[]{:S(2)}) async-start(bf16[16,2,512]{2,1,0:T(2,128)(2,1)} %reshape.296), calls=%async_computation.6 | async-start | bytes 65536 | tf_op jit(solution)/shard_map/all_to_all | solution.py:227
  169.1 0.6 slice_select_fusion
  169.7 10.7 %all-to-all-done.6 = bf16[16,2,512]{2,1,0:T(2,128)(2,1)S(1)} async-done(((bf16[16,2,512]{2,1,0:T(2,128)(2,1)}), bf16[16,2,512]{2,1,0:T(2,128)(2,1)S(1)}, u32[]{:S(2)}, u32[]{:S(2)}) %all-to-all-start.6) | async-done | bytes 32800 | tf_op jit(solution)/shard_map/all_to_all | solution.py:227
  180.8 0.7 reshape.281
  (118 shorter events, 6.2 us)
Async XLA Ops:
  0.6 21.3 %copy-start = (bf16[2048,64]{0,1:T(8,128)(2,1)S(1)}, bf16[2048,64]{0,1:T(8,128)(2,1)}, u32[]{:S(2)}) copy-start(bf16[2048,64]{0,1:T(8,128)(2,1)} %param.22) | copy-start | bytes 786436
  0.6 21.3 %copy-start.8 = (bf16[2048,16]{0,1:T(8,128)(2,1)S(1)}, bf16[2048,16]{0,1:T(8,128)(2,1)}, u32[]{:S(2)}) copy-start(bf16[2048,16]{0,1:T(8,128)(2,1)} %param.23) | copy-start | bytes 196612
  0.7 21.3 %copy-start.6 = (bf16[2048,16]{0,1:T(8,128)(2,1)S(1)}, bf16[2048,16]{0,1:T(8,128)(2,1)}, u32[]{:S(2)}) copy-start(bf16[2048,16]{0,1:T(8,128)(2,1)} %param.24) | copy-start | bytes 196612
  0.7 26.4 %copy-start.1 = (bf16[2048,256]{1,0:T(8,128)(2,1)S(1)}, bf16[2048,256]{1,0:T(8,128)(2,1)}, u32[]{:S(2)}) copy-start(bf16[2048,256]{1,0:T(8,128)(2,1)} %param.27) | copy-start | bytes 3145732
  0.7 26.4 %copy-start.2 = (bf16[2048,256]{1,0:T(8,128)(2,1)S(1)}, bf16[2048,256]{1,0:T(8,128)(2,1)}, u32[]{:S(2)}) copy-start(bf16[2048,256]{1,0:T(8,128)(2,1)} %param.28) | copy-start | bytes 3145732
  5.8 33.8 %all-to-all-start = ((bf16[16,2,4608]{2,1,0:T(2,128)(2,1)}), bf16[16,2,4608]{2,1,0:T(2,128)(2,1)S(1)}, u32[]{:S(2)}, u32[]{:S(2)}) async-start(bf16[16,2,4608]{2,1,0:T(2,128)(2,1)} %reshape.292), calls=%async_computation | async-start | bytes 589824 | tf_op jit(solution)/shard_map/all_to_all | solution.py:75
  22.0 8.9 %copy-start.13 = (s32[32]{0:T(128)S(1)}, s32[32]{0:T(128)}, u32[]{:S(2)}) copy-start(s32[32]{0:T(128)} %param.19) | copy-start | bytes 388
  22.0 9.0 %copy-start.15 = (s32[32,1]{0,1:T(1,128)S(1)}, s32[32,1]{0,1:T(1,128)}, u32[]{:S(2)}) copy-start(s32[32,1]{0,1:T(1,128)} %param.17) | copy-start | bytes 388
  22.0 9.0 %copy-start.16 = (s32[32]{0:T(128)S(1)}, s32[32]{0:T(128)}, u32[]{:S(2)}) copy-start(s32[32]{0:T(128)} %param.16) | copy-start | bytes 388
  22.1 9.2 %copy-start.21 = (s32[16]{0:T(128)S(1)}, s32[16]{0:T(128)}, u32[]{:S(2)}) copy-start(s32[16]{0:T(128)} %param.18) | copy-start | bytes 196
  22.1 12.5 %copy-start.11 = (bf16[2048]{0:T(1024)(128)(2,1)S(1)}, bf16[2048]{0:T(1024)(128)(2,1)}, u32[]{:S(2)}) copy-start(bf16[2048]{0:T(1024)(128)(2,1)} %param.21) | copy-start | bytes 12292
  22.1 17.5 %collective-permute-start = (bf16[2048,96]{0,1:T(8,128)(2,1)S(1)}, bf16[2048,96]{0,1:T(8,128)(2,1)S(1)}, u32[]{:S(2)}, u32[]{:S(2)}) collective-permute-start(bf16[2048,96]{0,1:T(8,128)(2,1)S(1)} %pad_maximum_fusion.4), channel_id=1, source_target_pairs={{0,1},{1,0},{2,3},{3,2},{4,5},{5,4},{6,7},{7,6},{8,9},{9,8},{10,11... | collective-permute-start | bytes 1179656 | tf_op jit(solution)/shard_map/ppermute | solution.py:102
  25.1 60.6 %collective-permute-start.1 = (bf16[64,2048]{1,0:T(8,128)(2,1)}, bf16[64,2048]{1,0:T(8,128)(2,1)}, u32[]{:S(2)}, u32[]{:S(2)}) collective-permute-start(bf16[64,2048]{1,0:T(8,128)(2,1)} %param.25), channel_id=1, source_target_pairs={{0,1},{1,0},{2,3},{3,2},{4,5},{5,4},{6,7},{7,6},{8,9},{9,8},{10,11... | collective-permute-start | bytes 786440 | tf_op jit(solution)/shard_map/ppermute | solution.py:191
  28.5 85.8 %collective-permute-start.2 = (bf16[2048,512]{1,0:T(8,128)(2,1)}, bf16[2048,512]{1,0:T(8,128)(2,1)}, u32[]{:S(2)}, u32[]{:S(2)}) collective-permute-start(bf16[2048,512]{1,0:T(8,128)(2,1)} %pad_maximum_fusion), channel_id=1, source_target_pairs={{0,1},{1,0},{2,3},{3,2},{4,5},{5,4},{6,7},{7,6},{8,9},{9,8},{10,11... | collective-permute-start | bytes 6291464 | tf_op jit(solution)/shard_map/ppermute | solution.py:200
  31.2 8.9 %copy-start.17 = (s32[2]{0:T(128)}, s32[2]{0:T(128)S(1)}, u32[]{:S(2)}) copy-start(s32[2]{0:T(128)S(1)} %get-tuple-element.4) | copy-start | bytes 28
  41.2 24.1 %all-to-all-start.1 = ((bf16[32,128,64]{1,2,0:T(8,128)(2,1)}), bf16[32,128,64]{1,2,0:T(8,128)(2,1)S(1)}, u32[]{:S(2)}, u32[]{:S(2)}) async-start(bf16[32,128,64]{1,2,0:T(8,128)(2,1)} %bitcast.4), calls=%async_computation.1 | async-start | bytes 1048576 | tf_op jit(solution)/shard_map/all_to_all | solution.py:117
  48.5 18.1 %copy-start.7 = (bf16[2048,16]{0,1:T(8,128)(2,1)S(1)}, bf16[2048,16]{0,1:T(8,128)(2,1)}, u32[]{:S(2)}) copy-start(bf16[2048,16]{0,1:T(8,128)(2,1)} %param.24) | copy-start | bytes 196612
  48.5 18.1 %copy-start.9 = (bf16[2048,16]{0,1:T(8,128)(2,1)S(1)}, bf16[2048,16]{0,1:T(8,128)(2,1)}, u32[]{:S(2)}) copy-start(bf16[2048,16]{0,1:T(8,128)(2,1)} %param.23) | copy-start | bytes 196612
  70.2 12.4 %all-to-all-start.2 = ((bf16[32,2,1024]{2,1,0:T(2,128)(2,1)}), bf16[32,2,1024]{2,1,0:T(2,128)(2,1)S(1)}, u32[]{:S(2)}, u32[]{:S(2)}) async-start(bf16[32,2,1024]{2,1,0:T(2,128)(2,1)} %reshape.294), calls=%async_computation.2 | async-start | bytes 262144 | tf_op jit(solution)/shard_map/all_to_all | solution.py:133
  74.5 9.8 %copy-start.19 = (f32[128]{0:T(128)S(1)}, f32[128]{0:T(128)}, u32[]{:S(2)}) copy-start(f32[128]{0:T(128)} %add_convert_fusion.3) | copy-start | bytes 1540
  74.5 9.8 %copy-start.20 = (f32[32]{0:T(128)S(1)}, f32[32]{0:T(128)}, u32[]{:S(2)}) copy-start(f32[32]{0:T(128)} %negate_power_fusion) | copy-start | bytes 388
  82.7 2.4 %copy-start.10 = (pred[128,128]{1,0:T(8,128)(4,1)S(1)}, pred[128,128]{1,0:T(8,128)(4,1)}, u32[]{:S(2)}) copy-start(pred[128,128]{1,0:T(8,128)(4,1)} %fusion.39) | copy-start | bytes 49156
  84.2 1.5 copy-start.5
  87.0 27.4 %copy-start.12 = (bf16[2048]{0:T(1024)(128)(2,1)S(1)}, bf16[2048]{0:T(1024)(128)(2,1)}, u32[]{:S(2)}) copy-start(bf16[2048]{0:T(1024)(128)(2,1)} %param.26) | copy-start | bytes 12292
  108.5 20.5 %all-to-all-start.4 = ((bf16[32,128,64]{1,2,0:T(8,128)(2,1)}), bf16[32,128,64]{1,2,0:T(8,128)(2,1)S(1)}, u32[]{:S(2)}, u32[]{:S(2)}) async-start(bf16[32,128,64]{1,2,0:T(8,128)(2,1)} %bitcast.38), calls=%async_computation.4 | async-start | bytes 1048576 | tf_op jit(solution)/shard_map/all_to_all | solution.py:209
  112.2 20.1 %collective-permute-start.3 = (bf16[256,2048]{1,0:T(8,128)(2,1)}, bf16[256,2048]{1,0:T(8,128)(2,1)}, u32[]{:S(2)}, u32[]{:S(2)}) collective-permute-start(bf16[256,2048]{1,0:T(8,128)(2,1)} %param.29), channel_id=1, source_target_pairs={{0,1},{1,0},{2,3},{3,2},{4,5},{5,4},{6,7},{7,6},{8,9},{9,8},{10,11... | collective-permute-start | bytes 3145736 | tf_op jit(solution)/shard_map/ppermute | solution.py:200
  129.6 2.6 %copy-start.4 = (bf16[128,2048]{0,1:T(8,128)(2,1)}, bf16[128,2048]{0,1:T(8,128)(2,1)S(1)}, u32[]{:S(2)}) copy-start(bf16[128,2048]{0,1:T(8,128)(2,1)S(1)} %fusion.17) | copy-start | bytes 1572868
  129.6 2.6 %copy-start.3 = (bf16[2048,256]{1,0:T(8,128)(2,1)S(1)}, bf16[2048,256]{1,0:T(8,128)(2,1)}, u32[]{:S(2)}) copy-start(bf16[2048,256]{1,0:T(8,128)(2,1)} %param.28) | copy-start | bytes 3145732
  134.9 4.8 %copy-start.18 = (s32[2]{0:T(128)S(1)}, s32[2]{0:T(128)}, u32[]{:S(2)}) copy-start(s32[2]{0:T(128)} %copy-done.17) | copy-start | bytes 28
  134.9 45.8 %copy-start.14 = (s32[32]{0:T(128)S(1)}, s32[32]{0:T(128)}, u32[]{:S(2)}) copy-start(s32[32]{0:T(128)} %param.19) | copy-start | bytes 388
  135.9 20.5 %all-to-all-start.5 = ((bf16[32,128,64]{1,2,0:T(8,128)(2,1)}), bf16[32,128,64]{1,2,0:T(8,128)(2,1)S(1)}, u32[]{:S(2)}, u32[]{:S(2)}) async-start(bf16[32,128,64]{1,2,0:T(8,128)(2,1)} %bitcast.42), calls=%async_computation.5 | async-start | bytes 1048576 | tf_op jit(solution)/shard_map/all_to_all | solution.py:217
  139.8 3.1 %collective-permute-start.4 = (bf16[128,32]{0,1:T(8,128)(2,1)S(1)}, bf16[128,32]{0,1:T(8,128)(2,1)S(1)}, u32[]{:S(2)}, u32[]{:S(2)}) collective-permute-start(bf16[128,32]{0,1:T(8,128)(2,1)S(1)} %pad_maximum_fusion.11), channel_id=1, source_target_pairs={{0,1},{1,0},{2,3},{3,2},{4,5},{5,4},{6,7},{7,6},{8,9},{9,8},{10,11... | collective-permute-start | bytes 24584 | tf_op jit(solution)/shard_map/ppermute | solution.py:156
  157.4 23.0 %all-to-all-start.6 = ((bf16[16,2,512]{2,1,0:T(2,128)(2,1)}), bf16[16,2,512]{2,1,0:T(2,128)(2,1)S(1)}, u32[]{:S(2)}, u32[]{:S(2)}) async-start(bf16[16,2,512]{2,1,0:T(2,128)(2,1)} %reshape.296), calls=%async_computation.6 | async-start | bytes 65536 | tf_op jit(solution)/shard_map/all_to_all | solution.py:227

commit v14 on v13

--- a/solution.py
+++ b/solution.py
@@ -136,7 +136,7 @@
     prefix_keys = picked[:, :HD]
     prefix_values = picked[:, HD:]
     kv_got = both[:, prefix_split:].reshape(tp_count // 2, 2, L_MAX, 2 * chip_d)
-    kv_got = lax.dynamic_index_in_dim(kv_got, core, 1, keepdims=False)
+    kv_got = jnp.take(kv_got, core, axis=1)
     keys4 = kv_got[:, :, : 2 * d_here].reshape(tp_count // 2, L_MAX, 2, d_here)
     vals4 = kv_got[:, :, 2 * d_here :].reshape(tp_count // 2, L_MAX, 2, d_here)
     flip = core == 1
@@ -165,7 +165,7 @@
     keys_out = jnp.where(valid3, kv_two[:, :, :out_width], 0.0).astype(jnp.bfloat16)
     values_out = jnp.where(valid3, kv_two[:, :, out_width:], 0.0).astype(jnp.bfloat16)
 
-    length_me = lax.dynamic_index_in_dim(lengths_here, core, 0, keepdims=False)
+    length_me = jnp.take(lengths_here, core)
     prefix_scores = jnp.einsum(
         "htd,pd->htp", query, prefix_keys, preferred_element_type=jnp.float32
     ) * score_scale
@@ -228,9 +228,9 @@
     order_hit = (
         jnp.arange(total_reqs, dtype=jnp.int32)[:, None] == request_order[None, :]
     ).astype(jnp.bfloat16)
-    hidden_out = jnp.dot(
-        order_hit, returned.reshape(total_reqs, -1), preferred_element_type=jnp.float32
-    ).astype(jnp.bfloat16).reshape(returned.shape)
+    hidden_out = jnp.einsum(
+        "rs,spf->rpf", order_hit, returned, preferred_element_type=jnp.float32
+    ).astype(jnp.bfloat16)
     return (hidden_out, keys_out, values_out)
 
 

time: 183 us -> 183 us (level)
    unnamed x57 -> x58, local copies, waits for them, and re-layouts: 4.05 us -> 4.71 us
where the time goes in v14:
time: 183 us; the launch traced here: 182 us
  waiting for transfers between devices  61.4 us (34%)
  starting transfers between devices  58.1 us (32%)
  blocking collectives  20.2 us (11%)
  local copies, waits for them, and re-layouts  18 us (10%)
  other arithmetic  9.49 us (5%)
  matrix products  8.73 us (5%)
  between operations  5.85 us (3%)
    all_to_all x3, waiting for transfers between devices, layer(): got = lax.all_to_all(sent, 'tensor', 0, 0, tiled=True)  41.8 us
    all_to_all x1, blocking collectives, layer(): got = lax.all_to_all(sent, 'tensor', 0, 0, tiled=True)  20.2 us
    all_to_all x1, starting transfers between devices, layer(): lax.all_to_all(jnp.concatenate([state_part, prefix_part], axis=1), 'dp',...  16.2 us
    all_to_all x3, starting transfers between devices, layer(): got = lax.all_to_all(sent, 'tensor', 0, 0, tiled=True)  14.7 us
    all_to_all x1, starting transfers between devices, layer(): lax.all_to_all(result, 'dp', split_axis=1, concat_axis=0, tiled=True)  11.7 us
    all_to_all x1, waiting for transfers between devices, layer(): lax.all_to_all(result, 'dp', split_axis=1, concat_axis=0, tiled=True)  10.7 us
    all_to_all x1, waiting for transfers between devices, layer(): both = lax.all_to_all(packed, 'tensor', 0, 0, tiled=True)  8.05 us
    ppermute x2, starting transfers between devices, layer(): lax.ppermute((jnp.concatenate([w_gate, w_up], axis=1), w_down), 'tensor',...  4.74 us
  transfers between devices with their start and end apart: 11, of which 6 were waited for; matrix products, arithmetic and copies ran while one was open for 14% of the time, Pallas kernels for 0%

profile of v14, /device:TPU:1, one launch (start us, length us, event | category | flops | bytes accessed | tf_op | source)
XLA Modules:
  0.0 181.8 jit_solution(18252236940682001713)
XLA Ops:
  0.7 1.1 reshape.263
  1.8 0.8 convolution_convert_fusion.3
  2.7 0.7 copy.139
  3.4 0.6 broadcast.207
  4.0 0.8 reduce.4
  4.8 0.9 reshape.345
  5.8 16.2 %all-to-all-start = ((bf16[16,2,4608]{2,1,0:T(2,128)(2,1)}), bf16[16,2,4608]{2,1,0:T(2,128)(2,1)S(1)}, u32[]{:S(2)}, u32[]{:S(2)}) async-start(bf16[16,2,4608]{2,1,0:T(2,128)(2,1)} %reshape.345), calls=%async_computation | async-start | bytes 589824 | tf_op jit(solution)/shard_map/all_to_all | solution.py:75
  22.1 3.0 %collective-permute-start = (bf16[2048,96]{0,1:T(8,128)(2,1)S(1)}, bf16[2048,96]{0,1:T(8,128)(2,1)S(1)}, u32[]{:S(2)}, u32[]{:S(2)}) collective-permute-start(bf16[2048,96]{0,1:T(8,128)(2,1)S(1)} %pad_maximum_fusion.4), channel_id=1, source_target_pairs={{0,1},{1,0},{2,3},{3,2},{4,5},{5,4},{6,7},{7,6},{8,9},{9,8},{10,11... | collective-permute-start | bytes 1179656 | tf_op jit(solution)/shard_map/ppermute | solution.py:102
  25.1 1.9 %collective-permute-start.1 = (bf16[64,2048]{1,0:T(8,128)(2,1)}, bf16[64,2048]{1,0:T(8,128)(2,1)}, u32[]{:S(2)}, u32[]{:S(2)}) collective-permute-start(bf16[64,2048]{1,0:T(8,128)(2,1)} %param.25), channel_id=1, source_target_pairs={{0,1},{1,0},{2,3},{3,2},{4,5},{5,4},{6,7},{7,6},{8,9},{9,8},{10,11... | collective-permute-start | bytes 786440 | tf_op jit(solution)/shard_map/ppermute | solution.py:191
  27.0 1.5 pad_maximum_fusion
  28.5 2.4 %collective-permute-start.2 = (bf16[2048,512]{1,0:T(8,128)(2,1)}, bf16[2048,512]{1,0:T(8,128)(2,1)}, u32[]{:S(2)}, u32[]{:S(2)}) collective-permute-start(bf16[2048,512]{1,0:T(8,128)(2,1)} %pad_maximum_fusion), channel_id=1, source_target_pairs={{0,1},{1,0},{2,3},{3,2},{4,5},{5,4},{6,7},{7,6},{8,9},{9,8},{10,11... | collective-permute-start | bytes 6291464 | tf_op jit(solution)/shard_map/ppermute | solution.py:200
  31.4 0.6 fusion.76
  34.5 0.6 convert_element_type.143
  35.1 0.6 dynamic-slice.5
  37.6 0.6 add_convert_fusion.3
  38.2 0.5 negate_power_fusion
  38.7 0.6 fusion.39
  40.0 0.9 tile.16
  40.9 7.3 %all-to-all-start.1 = ((bf16[32,128,64]{1,2,0:T(8,128)(2,1)}), bf16[32,128,64]{1,2,0:T(8,128)(2,1)S(1)}, u32[]{:S(2)}, u32[]{:S(2)}) async-start(bf16[32,128,64]{1,2,0:T(8,128)(2,1)} %bitcast.5), calls=%async_computation.1 | async-start | bytes 1048576 | tf_op jit(solution)/shard_map/all_to_all | solution.py:117
  48.5 16.5 %all-to-all-done.1 = bf16[32,128,64]{1,2,0:T(8,128)(2,1)S(1)} async-done(((bf16[32,128,64]{1,2,0:T(8,128)(2,1)}), bf16[32,128,64]{1,2,0:T(8,128)(2,1)S(1)}, u32[]{:S(2)}, u32[]{:S(2)}) %all-to-all-start.1) | async-done | bytes 524320 | tf_op jit(solution)/shard_map/all_to_all | solution.py:117
  65.3 1.0 fusion.19
  67.0 1.5 reshape_reshape.19
  68.5 0.7 reduce.5
  69.2 0.7 reshape.347
  69.9 3.7 %all-to-all-start.2 = ((bf16[32,2,1024]{2,1,0:T(2,128)(2,1)}), bf16[32,2,1024]{2,1,0:T(2,128)(2,1)S(1)}, u32[]{:S(2)}, u32[]{:S(2)}) async-start(bf16[32,2,1024]{2,1,0:T(2,128)(2,1)} %reshape.347), calls=%async_computation.2 | async-start | bytes 262144 | tf_op jit(solution)/shard_map/all_to_all | solution.py:133
  73.6 0.3 multiply_convert_fusion
  74.2 8.0 %all-to-all-done.2 = bf16[32,2,1024]{2,1,0:T(2,128)(2,1)S(1)} async-done(((bf16[32,2,1024]{2,1,0:T(2,128)(2,1)}), bf16[32,2,1024]{2,1,0:T(2,128)(2,1)S(1)}, u32[]{:S(2)}, u32[]{:S(2)}) %all-to-all-start.2) | async-done | bytes 131104 | tf_op jit(solution)/shard_map/all_to_all | solution.py:133
  82.5 1.2 reshape.267
  86.0 1.3 convolution_convert_fusion.1
  87.6 20.2 %all_to_all.62 = bf16[32,128,64]{1,2,0:T(8,128)(2,1)S(1)} all-to-all(bf16[32,128,64]{1,2,0:T(8,128)(2,1)S(1)} %bitcast.133), channel_id=1, replica_groups=mesh['dp'=16,'tensor'=32] {'tensor'}, dimensions={0} | all-to-all | bytes 1048576 | tf_op jit(solution)/shard_map/all_to_all | solution.py:195
  107.8 0.9 tile.18
  108.8 3.7 %all-to-all-start.4 = ((bf16[32,128,64]{1,2,0:T(8,128)(2,1)}), bf16[32,128,64]{1,2,0:T(8,128)(2,1)S(1)}, u32[]{:S(2)}, u32[]{:S(2)}) async-start(bf16[32,128,64]{1,2,0:T(8,128)(2,1)} %bitcast.38), calls=%async_computation.4 | async-start | bytes 1048576 | tf_op jit(solution)/shard_map/all_to_all | solution.py:209
  112.5 2.3 %collective-permute-start.3 = (bf16[256,2048]{1,0:T(8,128)(2,1)}, bf16[256,2048]{1,0:T(8,128)(2,1)}, u32[]{:S(2)}, u32[]{:S(2)}) collective-permute-start(bf16[256,2048]{1,0:T(8,128)(2,1)} %param.29), channel_id=1, source_target_pairs={{0,1},{1,0},{2,3},{3,2},{4,5},{5,4},{6,7},{7,6},{8,9},{9,8},{10,11... | collective-permute-start | bytes 3145736 | tf_op jit(solution)/shard_map/ppermute | solution.py:200
  114.8 2.6 %fusion.72 = (bf16[2048,256]{1,0:T(8,128)(2,1)S(1)}, bf16[2048,256]{1,0:T(8,128)(2,1)}) fusion(bf16[2048,512]{1,0:T(8,128)(2,1)} %collective-permute-done.2), kind=kLoop, calls=%fused_computation.134 | loop fusion | bytes 4194304 | tf_op jit(solution)/shard_map/slice | solution.py:205
  117.5 11.8 %all-to-all-done.4 = bf16[32,128,64]{1,2,0:T(8,128)(2,1)S(1)} async-done(((bf16[32,128,64]{1,2,0:T(8,128)(2,1)}), bf16[32,128,64]{1,2,0:T(8,128)(2,1)S(1)}, u32[]{:S(2)}, u32[]{:S(2)}) %all-to-all-start.4) | async-done | bytes 524320 | tf_op jit(solution)/shard_map/all_to_all | solution.py:209
  129.6 0.3 fusion.17
  129.9 2.6 %fusion.1 = f32[128,512]{1,0:T(8,128)} fusion(bf16[128,2048]{0,1:T(8,128)(2,1)S(1)} %fusion.17, bf16[2048,256]{1,0:T(8,128)(2,1)S(1)} %copy-done.1, bf16[2048,256]{1,0:T(8,128)(2,1)} %get-tuple-element.46), kind=kOutput, calls=%fused_computation.5 | convolution fusion | flops 272629760 | bytes 2883584 | tf_op jit(solution)/shard_map/dot_general | solution.py:212
  132.5 2.7 %convolution_convert_fusion = bf16[128,2048]{1,0:T(8,128)(2,1)S(1)} fusion(bf16[256,2048]{1,0:T(8,128)(2,1)} %collective-permute-done.3, bf16[256,2048]{1,0:T(8,128)(2,1)} %param.29, f32[128,512]{1,0:T(8,128)} %fusion.1, bf16[128,2048]{0,1:T(8,128)(2,1)} %copy-done.4, bf16[2048,256]{1,0:T(8,128)(2,1)S(1)} %get-tuple-element.45, ...), kind=kOutput, calls=%fused_computation.1 | convolution fusion | flops 545914880 | bytes 5505024 | tf_op jit(solution)/shard_map/dot_general | solution.py:215
  135.2 1.0 copy.114
  136.2 3.7 %all-to-all-start.5 = ((bf16[32,128,64]{1,2,0:T(8,128)(2,1)}), bf16[32,128,64]{1,2,0:T(8,128)(2,1)S(1)}, u32[]{:S(2)}, u32[]{:S(2)}) async-start(bf16[32,128,64]{1,2,0:T(8,128)(2,1)} %bitcast.42), calls=%async_computation.5 | async-start | bytes 1048576 | tf_op jit(solution)/shard_map/all_to_all | solution.py:217
  140.1 2.2 %collective-permute-start.4 = (bf16[128,32]{0,1:T(8,128)(2,1)S(1)}, bf16[128,32]{0,1:T(8,128)(2,1)S(1)}, u32[]{:S(2)}, u32[]{:S(2)}) collective-permute-start(bf16[128,32]{0,1:T(8,128)(2,1)S(1)} %pad_maximum_fusion.11), channel_id=1, source_target_pairs={{0,1},{1,0},{2,3},{3,2},{4,5},{5,4},{6,7},{7,6},{8,9},{9,8},{10,11... | collective-permute-start | bytes 24584 | tf_op jit(solution)/shard_map/ppermute | solution.py:156
  142.3 0.9 collective-permute-done.4
  143.2 13.5 %all-to-all-done.5 = bf16[32,128,64]{1,2,0:T(8,128)(2,1)S(1)} async-done(((bf16[32,128,64]{1,2,0:T(8,128)(2,1)}), bf16[32,128,64]{1,2,0:T(8,128)(2,1)S(1)}, u32[]{:S(2)}, u32[]{:S(2)}) %all-to-all-start.5) | async-done | bytes 524320 | tf_op jit(solution)/shard_map/all_to_all | solution.py:217
  157.0 0.7 reshape.349
  157.7 11.7 %all-to-all-start.6 = ((bf16[16,2,512]{2,1,0:T(2,128)(2,1)}), bf16[16,2,512]{2,1,0:T(2,128)(2,1)S(1)}, u32[]{:S(2)}, u32[]{:S(2)}) async-start(bf16[16,2,512]{2,1,0:T(2,128)(2,1)} %reshape.349), calls=%async_computation.6 | async-start | bytes 65536 | tf_op jit(solution)/shard_map/all_to_all | solution.py:227
  169.4 0.6 slice_select_fusion
  170.1 10.7 %all-to-all-done.6 = bf16[16,2,512]{2,1,0:T(2,128)(2,1)S(1)} async-done(((bf16[16,2,512]{2,1,0:T(2,128)(2,1)}), bf16[16,2,512]{2,1,0:T(2,128)(2,1)S(1)}, u32[]{:S(2)}, u32[]{:S(2)}) %all-to-all-start.6) | async-done | bytes 32800 | tf_op jit(solution)/shard_map/all_to_all | solution.py:227
  181.1 0.7 copy.118
  (120 shorter events, 6.4 us)
Async XLA Ops:
  0.6 21.3 %copy-start = (bf16[2048,64]{0,1:T(8,128)(2,1)S(1)}, bf16[2048,64]{0,1:T(8,128)(2,1)}, u32[]{:S(2)}) copy-start(bf16[2048,64]{0,1:T(8,128)(2,1)} %param.22) | copy-start | bytes 786436
  0.6 21.3 %copy-start.8 = (bf16[2048,16]{0,1:T(8,128)(2,1)S(1)}, bf16[2048,16]{0,1:T(8,128)(2,1)}, u32[]{:S(2)}) copy-start(bf16[2048,16]{0,1:T(8,128)(2,1)} %param.23) | copy-start | bytes 196612
  0.7 21.3 %copy-start.6 = (bf16[2048,16]{0,1:T(8,128)(2,1)S(1)}, bf16[2048,16]{0,1:T(8,128)(2,1)}, u32[]{:S(2)}) copy-start(bf16[2048,16]{0,1:T(8,128)(2,1)} %param.24) | copy-start | bytes 196612
  0.7 26.4 %copy-start.1 = (bf16[2048,256]{1,0:T(8,128)(2,1)S(1)}, bf16[2048,256]{1,0:T(8,128)(2,1)}, u32[]{:S(2)}) copy-start(bf16[2048,256]{1,0:T(8,128)(2,1)} %param.27) | copy-start | bytes 3145732
  0.7 26.4 %copy-start.2 = (bf16[2048,256]{1,0:T(8,128)(2,1)S(1)}, bf16[2048,256]{1,0:T(8,128)(2,1)}, u32[]{:S(2)}) copy-start(bf16[2048,256]{1,0:T(8,128)(2,1)} %param.28) | copy-start | bytes 3145732
  5.8 33.6 %all-to-all-start = ((bf16[16,2,4608]{2,1,0:T(2,128)(2,1)}), bf16[16,2,4608]{2,1,0:T(2,128)(2,1)S(1)}, u32[]{:S(2)}, u32[]{:S(2)}) async-start(bf16[16,2,4608]{2,1,0:T(2,128)(2,1)} %reshape.345), calls=%async_computation | async-start | bytes 589824 | tf_op jit(solution)/shard_map/all_to_all | solution.py:75
  22.0 8.9 %copy-start.13 = (s32[32]{0:T(128)S(1)}, s32[32]{0:T(128)}, u32[]{:S(2)}) copy-start(s32[32]{0:T(128)} %param.19) | copy-start | bytes 388
  22.0 9.0 %copy-start.15 = (s32[32,1]{0,1:T(1,128)S(1)}, s32[32,1]{0,1:T(1,128)}, u32[]{:S(2)}) copy-start(s32[32,1]{0,1:T(1,128)} %param.17) | copy-start | bytes 388
  22.0 9.0 %copy-start.16 = (s32[32]{0:T(128)S(1)}, s32[32]{0:T(128)}, u32[]{:S(2)}) copy-start(s32[32]{0:T(128)} %param.16) | copy-start | bytes 388
  22.1 9.2 %copy-start.21 = (s32[16]{0:T(128)S(1)}, s32[16]{0:T(128)}, u32[]{:S(2)}) copy-start(s32[16]{0:T(128)} %param.18) | copy-start | bytes 196
  22.1 12.4 %copy-start.11 = (bf16[2048]{0:T(1024)(128)(2,1)S(1)}, bf16[2048]{0:T(1024)(128)(2,1)}, u32[]{:S(2)}) copy-start(bf16[2048]{0:T(1024)(128)(2,1)} %param.21) | copy-start | bytes 12292
  22.1 17.2 %collective-permute-start = (bf16[2048,96]{0,1:T(8,128)(2,1)S(1)}, bf16[2048,96]{0,1:T(8,128)(2,1)S(1)}, u32[]{:S(2)}, u32[]{:S(2)}) collective-permute-start(bf16[2048,96]{0,1:T(8,128)(2,1)S(1)} %pad_maximum_fusion.4), channel_id=1, source_target_pairs={{0,1},{1,0},{2,3},{3,2},{4,5},{5,4},{6,7},{7,6},{8,9},{9,8},{10,11... | collective-permute-start | bytes 1179656 | tf_op jit(solution)/shard_map/ppermute | solution.py:102
  25.1 60.9 %collective-permute-start.1 = (bf16[64,2048]{1,0:T(8,128)(2,1)}, bf16[64,2048]{1,0:T(8,128)(2,1)}, u32[]{:S(2)}, u32[]{:S(2)}) collective-permute-start(bf16[64,2048]{1,0:T(8,128)(2,1)} %param.25), channel_id=1, source_target_pairs={{0,1},{1,0},{2,3},{3,2},{4,5},{5,4},{6,7},{7,6},{8,9},{9,8},{10,11... | collective-permute-start | bytes 786440 | tf_op jit(solution)/shard_map/ppermute | solution.py:191
  28.5 86.3 %collective-permute-start.2 = (bf16[2048,512]{1,0:T(8,128)(2,1)}, bf16[2048,512]{1,0:T(8,128)(2,1)}, u32[]{:S(2)}, u32[]{:S(2)}) collective-permute-start(bf16[2048,512]{1,0:T(8,128)(2,1)} %pad_maximum_fusion), channel_id=1, source_target_pairs={{0,1},{1,0},{2,3},{3,2},{4,5},{5,4},{6,7},{7,6},{8,9},{9,8},{10,11... | collective-permute-start | bytes 6291464 | tf_op jit(solution)/shard_map/ppermute | solution.py:200
  31.2 8.6 %copy-start.17 = (s32[2]{0:T(128)}, s32[2]{0:T(128)S(1)}, u32[]{:S(2)}) copy-start(s32[2]{0:T(128)S(1)} %get-tuple-element.44) | copy-start | bytes 28
  40.9 24.1 %all-to-all-start.1 = ((bf16[32,128,64]{1,2,0:T(8,128)(2,1)}), bf16[32,128,64]{1,2,0:T(8,128)(2,1)S(1)}, u32[]{:S(2)}, u32[]{:S(2)}) async-start(bf16[32,128,64]{1,2,0:T(8,128)(2,1)} %bitcast.5), calls=%async_computation.1 | async-start | bytes 1048576 | tf_op jit(solution)/shard_map/all_to_all | solution.py:117
  48.2 18.1 %copy-start.7 = (bf16[2048,16]{0,1:T(8,128)(2,1)S(1)}, bf16[2048,16]{0,1:T(8,128)(2,1)}, u32[]{:S(2)}) copy-start(bf16[2048,16]{0,1:T(8,128)(2,1)} %param.24) | copy-start | bytes 196612
  48.2 18.1 %copy-start.9 = (bf16[2048,16]{0,1:T(8,128)(2,1)S(1)}, bf16[2048,16]{0,1:T(8,128)(2,1)}, u32[]{:S(2)}) copy-start(bf16[2048,16]{0,1:T(8,128)(2,1)} %param.23) | copy-start | bytes 196612
  69.9 12.4 %all-to-all-start.2 = ((bf16[32,2,1024]{2,1,0:T(2,128)(2,1)}), bf16[32,2,1024]{2,1,0:T(2,128)(2,1)S(1)}, u32[]{:S(2)}, u32[]{:S(2)}) async-start(bf16[32,2,1024]{2,1,0:T(2,128)(2,1)} %reshape.347), calls=%async_computation.2 | async-start | bytes 262144 | tf_op jit(solution)/shard_map/all_to_all | solution.py:133
  83.7 0.9 copy-start.19
  83.7 0.9 copy-start.20
  83.8 1.6 copy-start.10
  84.5 1.5 copy-start.5
  87.3 27.5 %copy-start.12 = (bf16[2048]{0:T(1024)(128)(2,1)S(1)}, bf16[2048]{0:T(1024)(128)(2,1)}, u32[]{:S(2)}) copy-start(bf16[2048]{0:T(1024)(128)(2,1)} %param.26) | copy-start | bytes 12292
  108.8 20.5 %all-to-all-start.4 = ((bf16[32,128,64]{1,2,0:T(8,128)(2,1)}), bf16[32,128,64]{1,2,0:T(8,128)(2,1)S(1)}, u32[]{:S(2)}, u32[]{:S(2)}) async-start(bf16[32,128,64]{1,2,0:T(8,128)(2,1)} %bitcast.38), calls=%async_computation.4 | async-start | bytes 1048576 | tf_op jit(solution)/shard_map/all_to_all | solution.py:209
  112.5 20.1 %collective-permute-start.3 = (bf16[256,2048]{1,0:T(8,128)(2,1)}, bf16[256,2048]{1,0:T(8,128)(2,1)}, u32[]{:S(2)}, u32[]{:S(2)}) collective-permute-start(bf16[256,2048]{1,0:T(8,128)(2,1)} %param.29), channel_id=1, source_target_pairs={{0,1},{1,0},{2,3},{3,2},{4,5},{5,4},{6,7},{7,6},{8,9},{9,8},{10,11... | collective-permute-start | bytes 3145736 | tf_op jit(solution)/shard_map/ppermute | solution.py:200
  129.9 2.6 %copy-start.4 = (bf16[128,2048]{0,1:T(8,128)(2,1)}, bf16[128,2048]{0,1:T(8,128)(2,1)S(1)}, u32[]{:S(2)}) copy-start(bf16[128,2048]{0,1:T(8,128)(2,1)S(1)} %fusion.17) | copy-start | bytes 1572868
  129.9 2.6 %copy-start.3 = (bf16[2048,256]{1,0:T(8,128)(2,1)S(1)}, bf16[2048,256]{1,0:T(8,128)(2,1)}, u32[]{:S(2)}) copy-start(bf16[2048,256]{1,0:T(8,128)(2,1)} %param.28) | copy-start | bytes 3145732
  135.2 4.8 %copy-start.18 = (s32[2]{0:T(128)S(1)}, s32[2]{0:T(128)}, u32[]{:S(2)}) copy-start(s32[2]{0:T(128)} %copy-done.17) | copy-start | bytes 28
  135.2 45.7 %copy-start.14 = (s32[32]{0:T(128)S(1)}, s32[32]{0:T(128)}, u32[]{:S(2)}) copy-start(s32[32]{0:T(128)} %param.19) | copy-start | bytes 388
  136.2 20.5 %all-to-all-start.5 = ((bf16[32,128,64]{1,2,0:T(8,128)(2,1)}), bf16[32,128,64]{1,2,0:T(8,128)(2,1)S(1)}, u32[]{:S(2)}, u32[]{:S(2)}) async-start(bf16[32,128,64]{1,2,0:T(8,128)(2,1)} %bitcast.42), calls=%async_computation.5 | async-start | bytes 1048576 | tf_op jit(solution)/shard_map/all_to_all | solution.py:217
  140.1 3.1 %collective-permute-start.4 = (bf16[128,32]{0,1:T(8,128)(2,1)S(1)}, bf16[128,32]{0,1:T(8,128)(2,1)S(1)}, u32[]{:S(2)}, u32[]{:S(2)}) collective-permute-start(bf16[128,32]{0,1:T(8,128)(2,1)S(1)} %pad_maximum_fusion.11), channel_id=1, source_target_pairs={{0,1},{1,0},{2,3},{3,2},{4,5},{5,4},{6,7},{7,6},{8,9},{9,8},{10,11... | collective-permute-start | bytes 24584 | tf_op jit(solution)/shard_map/ppermute | solution.py:156
  157.7 23.0 %all-to-all-start.6 = ((bf16[16,2,512]{2,1,0:T(2,128)(2,1)}), bf16[16,2,512]{2,1,0:T(2,128)(2,1)S(1)}, u32[]{:S(2)}, u32[]{:S(2)}) async-start(bf16[16,2,512]{2,1,0:T(2,128)(2,1)} %reshape.349), calls=%async_computation.6 | async-start | bytes 65536 | tf_op jit(solution)/shard_map/all_to_all | solution.py:227
